TPU v7x, 32 devices: a whole 2x2x4 slice. The times are simulated.
32 devices in a mesh: dp: 8 (over y, x, core), tensor: 4 (over z).
Axes of the slice: x: 2, y: 2, z: 4, core: 2. Of those that a mesh axis runs over, the one named last changes fastest.
Arguments:
- inputs: bfloat16 [16384, 768], P(('dp', 'tensor')), may hold values from -6 to 6
- cotangent: bfloat16 [16384, 768], P(('dp', 'tensor')), may hold values from -6 to 6
- lengths: int32 [128], P('dp'), may hold values from 25 to 128
- block_kind: int32 [32], P('dp'), may hold values from 0 to 1
- w_qkv: bfloat16 [2, 3, 768, 768], P(None, None, None, 'tensor'), may hold values from -0.3125 to 0.3125
- qv_bias: bfloat16 [2, 2, 768], P(None, None, 'tensor'), may hold values from -3 to 3
- w_out: bfloat16 [2, 768, 768], P(None, 'tensor'), may hold values from -0.625 to 0.625
- resid_bias: bfloat16 [2, 2, 768], replicated, may hold values from -3 to 3
- norm_gain: bfloat16 [2, 2, 768], replicated, may hold values from 0.5 to 1.5
- norm_shift: bfloat16 [2, 2, 768], replicated, may hold values from -2 to 2
- w_up: bfloat16 [2, 768, 3072], P(None, None, 'tensor'), may hold values from -0.21875 to 0.21875
- up_bias: bfloat16 [2, 3072], P(None, 'tensor'), may hold values from -3 to 3
- w_down: bfloat16 [2, 3072, 768], P(None, 'tensor'), may hold values from -0.15625 to 0.15625
Outputs:
- layer_out: bfloat16 [16384, 768], P(('dp', 'tensor'))
- input_grad: float32 [16384, 768], P(('dp', 'tensor'))
- grad_w_qkv: float32 [2, 3, 768, 768], P(None, None, None, 'tensor')
- grad_qv_bias: float32 [2, 2, 768], P(None, None, 'tensor')
- grad_w_out: float32 [2, 768, 768], P(None, 'tensor')
- grad_resid_bias: float32 [2, 2, 768], replicated
- grad_norm_gain: float32 [2, 2, 768], replicated
- grad_norm_shift: float32 [2, 2, 768], replicated
- grad_w_up: float32 [2, 768, 3072], P(None, None, 'tensor')
- grad_up_bias: float32 [2, 3072], P(None, 'tensor')
- grad_w_down: float32 [2, 3072, 768], P(None, 'tensor')
Inputs may be any that keep to these rules, and one draw needn't show every extreme that they name: lengths[s] is the number of real tokens of chain s; positions from lengths[s] on are padding and are never attended to. `block_kind`: block b holds chains b * 4 to (b+1) * 4 - 1, all heavy (0) or all light (1).
All inputs are finite; a program needn't handle non-finite values.
Results may differ from a plain program's by a relative error of at most 0.019.
The roundings to bfloat16 on the way count: a program that leaves them out, or rounds other values in their place, can miss the bound.
Values may be sent and summed in bfloat16 or wider, within the bound.
No kernel may reach another device: no remote copies, remote signals or barrier semaphores. Data moves between devices by JAX's collectives and lax.ppermute only.
A program may use at most 128 MiB of HBM per device.

v0:
```python
import jax
import jax.numpy as jnp
from jax import lax
from jax.sharding import PartitionSpec as P

HEAD_DIM = 64
CHAIN = 128
BLOCK_SEQS = 4


EPSILON = 1e-05
SQRT_HALF = 0.7071067811865476
INV_ROOT_TWO_PI = 0.3989422804014327


def norm_forward(row_data, gain_rows, shift_rows):
    mean_row = jnp.mean(row_data, axis=-1, keepdims=True)
    centred = row_data - mean_row
    var_row = jnp.mean(centred * centred, axis=-1, keepdims=True)
    inv_std = lax.rsqrt(var_row + EPSILON)
    unit_rows = centred * inv_std
    return (unit_rows * gain_rows + shift_rows, unit_rows, inv_std)


def norm_backward(grad_rows, gain_rows, unit_rows, inv_std):
    scaled = grad_rows * gain_rows
    mean_first = jnp.mean(scaled, axis=-1, keepdims=True)
    mean_second = jnp.mean(scaled * unit_rows, axis=-1, keepdims=True)
    return inv_std * (scaled - mean_first - unit_rows * mean_second)


def type_sum(kind_hot, values):
    return jnp.einsum("rt,rd->td", kind_hot, values, precision=lax.Precision.HIGHEST)


def gelu_slope(values):
    return 0.5 * (1.0 + lax.erf(values * SQRT_HALF)) + values * INV_ROOT_TWO_PI * jnp.exp(
        -0.5 * values * values
    )


def split_heads(row_data, heads_here):
    return row_data.reshape(BLOCK_SEQS, CHAIN, heads_here, HEAD_DIM)


def ffn_apply(up_w, ubias_w, down_w, row_blocks, kinds):

    def step(carry, packed):
        row_data, block_type = packed
        pre_act = jnp.dot(row_data, up_w[block_type], preferred_element_type=jnp.float32) + ubias_w[
            block_type
        ].astype(jnp.float32)
        activ = jax.nn.gelu(pre_act, approximate=False).astype(jnp.bfloat16)
        return (
            carry,
            (
                pre_act,
                activ,
                jnp.dot(activ, down_w[block_type], preferred_element_type=jnp.float32),
            ),
        )

    return lax.scan(step, 0, (row_blocks, kinds))[1]


def ffn_grad(up_w, ubias_w, down_w, row_blocks, grad_blocks, pre_blocks, activ_blocks, kinds):

    def step(accums, packed):
        acc_up, acc_ubias, acc_down = accums
        row_data, grad_rows, pre_act, activ, block_type = packed
        acc_down = acc_down.at[block_type].add(
            jnp.einsum("rf,rd->fd", activ, grad_rows, preferred_element_type=jnp.float32)
        )
        d_activ = jnp.einsum(
            "rd,fd->rf", grad_rows, down_w[block_type], preferred_element_type=jnp.float32
        ).astype(jnp.bfloat16)
        d_pre = (d_activ.astype(jnp.float32) * gelu_slope(pre_act)).astype(jnp.bfloat16)
        acc_up = acc_up.at[block_type].add(
            jnp.einsum("rd,rf->df", row_data, d_pre, preferred_element_type=jnp.float32)
        )
        acc_ubias = acc_ubias.at[block_type].add(jnp.sum(d_pre.astype(jnp.float32), axis=0))
        partial_back = jnp.einsum(
            "rf,df->rd", d_pre, up_w[block_type], preferred_element_type=jnp.float32
        )
        return ((acc_up, acc_ubias, acc_down), partial_back)

    zeros_ffn = (
        jnp.zeros(up_w.shape, jnp.float32),
        jnp.zeros(ubias_w.shape, jnp.float32),
        jnp.zeros(down_w.shape, jnp.float32),
    )
    return lax.scan(step, zeros_ffn, (row_blocks, grad_blocks, pre_blocks, activ_blocks, kinds))


def local(
    inputs,
    cotangent,
    lengths,
    block_kind,
    w_qkv,
    qv_bias,
    w_out,
    resid_bias,
    norm_gain,
    norm_shift,
    w_up,
    up_bias,
    w_down,
):
    tok_dev = inputs.shape[0]
    group_rows = tok_dev * lax.axis_size("tensor")
    block_rows = BLOCK_SEQS * CHAIN
    n_blocks = group_rows // block_rows
    heads_here = w_qkv.shape[3] // HEAD_DIM
    score_scale = HEAD_DIM ** (-0.5)
    highest = lax.Precision.HIGHEST
    row_block = (lax.axis_index("tensor") * tok_dev + jnp.arange(tok_dev)) // block_rows
    block_hot = row_block[:, None] == jnp.arange(n_blocks)[None, :]
    row_kind = jnp.sum(jnp.where(block_hot, block_kind[None, :], 0), axis=1)
    kind_hot = (row_kind[:, None] == jnp.arange(2)[None, :]).astype(jnp.float32)

    def pick(kind_table):
        return jnp.dot(kind_hot, kind_table.astype(jnp.float32), precision=highest)

    key_valid = jnp.arange(CHAIN)[None, :] < lengths[:, None]
    valid_blocks = key_valid.reshape(n_blocks, BLOCK_SEQS, CHAIN)

    def scores_of(query_rows, key_rows, valid_keys):
        raw_scores = (
            jnp.einsum(
                "sqhd,skhd->shqk",
                split_heads(query_rows, heads_here),
                split_heads(key_rows, heads_here),
                preferred_element_type=jnp.float32,
            )
            * score_scale
        )
        return jnp.where(valid_keys[:, None, None, :], raw_scores, -1e30)

    gathered = lax.all_gather(inputs, "tensor", axis=0, tiled=True)
    input_blocks = gathered.reshape(n_blocks, block_rows, -1)

    def attend_forward(accums, packed):
        row_data, valid_keys, block_type = packed
        projected = jnp.einsum(
            "rd,jde->jre", row_data, w_qkv[block_type], preferred_element_type=jnp.float32
        )
        bias_pair = qv_bias[block_type].astype(jnp.float32)
        query_rows = (projected[0] + bias_pair[0]).astype(jnp.bfloat16)
        key_rows = projected[1].astype(jnp.bfloat16)
        value_rows = (projected[2] + bias_pair[1]).astype(jnp.bfloat16)
        scores = scores_of(query_rows, key_rows, valid_keys)
        row_max = jnp.max(scores, axis=-1, keepdims=True)
        log_total = row_max[..., 0] + jnp.log(jnp.sum(jnp.exp(scores - row_max), axis=-1))
        attn_probs = jnp.exp(scores - log_total[..., None]).astype(jnp.bfloat16)
        mixed = jnp.einsum(
            "shqk,skhd->sqhd",
            attn_probs,
            split_heads(value_rows, heads_here),
            preferred_element_type=jnp.float32,
        )
        mixed = mixed.reshape(block_rows, -1).astype(jnp.bfloat16)
        partial_out = jnp.dot(mixed, w_out[block_type], preferred_element_type=jnp.float32)
        return (
            accums,
            (jnp.stack([query_rows, key_rows, value_rows]), log_total, mixed, partial_out),
        )

    unused, (kept_proj, kept_total, kept_mixed, attn_parts) = lax.scan(
        attend_forward, 0, (input_blocks, valid_blocks, block_kind)
    )
    attn_rows = lax.psum_scatter(
        attn_parts.reshape(group_rows, -1), "tensor", scatter_dimension=0, tiled=True
    )
    hidden_one = inputs.astype(jnp.float32) + attn_rows + pick(resid_bias[:, 0])
    gain_one = pick(norm_gain[:, 0])
    normed, unit_one, inv_one = norm_forward(hidden_one, gain_one, pick(norm_shift[:, 0]))
    normed_low = normed.astype(jnp.bfloat16)
    gathered_norm = lax.all_gather(normed_low, "tensor", axis=0, tiled=True)
    norm_blocks = gathered_norm.reshape(n_blocks, block_rows, -1)
    kept_pre, kept_activ, ffn_parts = ffn_apply(w_up, up_bias, w_down, norm_blocks, block_kind)
    ffn_rows = lax.psum_scatter(
        ffn_parts.reshape(group_rows, -1), "tensor", scatter_dimension=0, tiled=True
    )
    hidden_two = normed + ffn_rows + pick(resid_bias[:, 1])
    gain_two = pick(norm_gain[:, 1])
    output_rows, unit_two, inv_two = norm_forward(hidden_two, gain_two, pick(norm_shift[:, 1]))
    layer_out = output_rows.astype(jnp.bfloat16)
    grad_out = cotangent.astype(jnp.float32)
    d_two = norm_backward(grad_out, gain_two, unit_two, inv_two)
    d_two_low = d_two.astype(jnp.bfloat16)
    gathered_two = lax.all_gather(d_two_low, "tensor", axis=0, tiled=True)
    two_blocks = gathered_two.reshape(n_blocks, block_rows, -1)
    (acc_up, acc_ubias, acc_down), ffn_back_parts = ffn_grad(
        w_up, up_bias, w_down, norm_blocks, two_blocks, kept_pre, kept_activ, block_kind
    )
    d_normed = (
        lax.psum_scatter(
            ffn_back_parts.reshape(group_rows, -1), "tensor", scatter_dimension=0, tiled=True
        )
        + d_two
    )
    up_total, ubias_total, down_total = (acc_up, acc_ubias, acc_down)
    d_one = norm_backward(d_normed, gain_one, unit_one, inv_one)
    gain_grads = jnp.stack(
        [type_sum(kind_hot, d_normed * unit_one), type_sum(kind_hot, grad_out * unit_two)], axis=1
    )
    shift_grads = jnp.stack([type_sum(kind_hot, d_normed), type_sum(kind_hot, grad_out)], axis=1)
    rbias_grads = jnp.stack([type_sum(kind_hot, d_one), type_sum(kind_hot, d_two)], axis=1)
    gathered_one = lax.all_gather(d_one.astype(jnp.bfloat16), "tensor", axis=0, tiled=True)
    one_blocks = gathered_one.reshape(n_blocks, block_rows, -1)

    def attend_backward(accums, packed):
        acc_qkv, acc_qv, acc_out = accums
        row_data, grad_rows, valid_keys, kept_rows, log_total, mixed, block_type = packed
        acc_out = acc_out.at[block_type].add(
            jnp.einsum("re,rd->ed", mixed, grad_rows, preferred_element_type=jnp.float32)
        )
        d_mixed = jnp.einsum(
            "rd,ed->re", grad_rows, w_out[block_type], preferred_element_type=jnp.float32
        ).astype(jnp.bfloat16)
        scores = scores_of(kept_rows[0], kept_rows[1], valid_keys)
        attn_probs = jnp.exp(scores - log_total[..., None])
        d_mixed_heads = split_heads(d_mixed, heads_here)
        d_value = jnp.einsum(
            "shqk,sqhd->skhd",
            attn_probs.astype(jnp.bfloat16),
            d_mixed_heads,
            preferred_element_type=jnp.float32,
        )
        d_value = d_value.reshape(block_rows, -1).astype(jnp.bfloat16)
        d_probs = jnp.einsum(
            "sqhd,skhd->shqk",
            d_mixed_heads,
            split_heads(kept_rows[2], heads_here),
            preferred_element_type=jnp.float32,
        )
        prob_dot = jnp.sum(attn_probs * d_probs, axis=-1, keepdims=True)
        d_scores = (attn_probs * (d_probs - prob_dot)).astype(jnp.bfloat16)
        d_query = (
            jnp.einsum(
                "shqk,skhd->sqhd",
                d_scores,
                split_heads(kept_rows[1], heads_here),
                preferred_element_type=jnp.float32,
            )
            * score_scale
        )
        d_key = (
            jnp.einsum(
                "shqk,sqhd->skhd",
                d_scores,
                split_heads(kept_rows[0], heads_here),
                preferred_element_type=jnp.float32,
            )
            * score_scale
        )
        d_query = d_query.reshape(block_rows, -1).astype(jnp.bfloat16)
        d_key = d_key.reshape(block_rows, -1).astype(jnp.bfloat16)
        d_proj = jnp.stack([d_query, d_key, d_value])
        acc_qkv = acc_qkv.at[block_type].add(
            jnp.einsum("rd,jre->jde", row_data, d_proj, preferred_element_type=jnp.float32)
        )
        bias_sums = jnp.stack(
            [
                jnp.sum(d_query.astype(jnp.float32), axis=0),
                jnp.sum(d_value.astype(jnp.float32), axis=0),
            ]
        )
        acc_qv = acc_qv.at[block_type].add(bias_sums)
        partial_back = jnp.einsum(
            "jre,jde->rd", d_proj, w_qkv[block_type], preferred_element_type=jnp.float32
        )
        return ((acc_qkv, acc_qv, acc_out), partial_back)

    zeros_attn = (
        jnp.zeros(w_qkv.shape, jnp.float32),
        jnp.zeros(qv_bias.shape, jnp.float32),
        jnp.zeros(w_out.shape, jnp.float32),
    )
    (acc_qkv, acc_qv, acc_out), qkv_back_parts = lax.scan(
        attend_backward,
        zeros_attn,
        (input_blocks, one_blocks, valid_blocks, kept_proj, kept_total, kept_mixed, block_kind),
    )
    input_grad = (
        lax.psum_scatter(
            qkv_back_parts.reshape(group_rows, -1).astype(jnp.bfloat16),
            "tensor",
            scatter_dimension=0,
            tiled=True,
        ).astype(jnp.float32)
        + d_one
    )
    qkv_total, qv_total, out_total, up_total, ubias_total, down_total = lax.psum(
        (acc_qkv, acc_qv, acc_out, up_total, ubias_total, down_total), "dp"
    )
    rbias_total, gain_total, shift_total = lax.psum(
        (rbias_grads, gain_grads, shift_grads), ("dp", "tensor")
    )
    return (
        layer_out,
        input_grad,
        qkv_total,
        qv_total,
        out_total,
        rbias_total,
        gain_total,
        shift_total,
        up_total,
        ubias_total,
        down_total,
    )


def solution(mesh):
    return jax.shard_map(
        local,
        mesh=mesh,
        in_specs=(
            P(("dp", "tensor"), None),
            P(("dp", "tensor"), None),
            P("dp"),
            P("dp"),
            P(None, None, None, "tensor"),
            P(None, None, "tensor"),
            P(None, "tensor", None),
            P(),
            P(),
            P(),
            P(None, None, "tensor"),
            P(None, "tensor"),
            P(None, "tensor", None),
        ),
        out_specs=(
            P(("dp", "tensor"), None),
            P(("dp", "tensor"), None),
            P(None, None, None, "tensor"),
            P(None, None, "tensor"),
            P(None, "tensor", None),
            P(),
            P(),
            P(),
            P(None, None, "tensor"),
            P(None, "tensor"),
            P(None, "tensor", None),
        ),
        check_vma=False,
    )
```

profile of v0, /device:TPU:0, one launch (start us, length us, event | category | flops | bytes accessed | tf_op | source)
XLA Modules:
  0.0 1168.2 jit_solution(15813986910202748736)
XLA Ops:
  8.8 67.0 %all-gather.5.cloned.1.call-done = bf16[2048,768]{1,0:T(8,128)(2,1)} async-done(((bf16[512,768]{1,0:T(8,128)(2,1)}), bf16[2048,768]{1,0:T(8,128)(2,1)}) %all-gather.5.cloned.1.call-update) | async-done | bytes 3145744 | tf_op jit(solution)/shard_map/all_gather | solution.py:140
  75.8 3.2 broadcast.348.clone
  79.0 39.6 %while.68 = (s32[]{:T(128)}, bf16[4,3,512,192]{2,3,1,0:T(8,128)(2,1)}, f32[4,4,3,128]{3,2,1,0:T(4,128)S(1)}, bf16[4,512,192]{1,2,0:T(8,128)(2,1)S(1)}, f32[4,512...) while((s32[]{:T(128)}, ...), condition=%wide.region_3.4_spmd, body=%wide.region_0.3_spmd.sunk | while | flops 658340736 | bytes 15210975 | solution.py:169
  81.5 2.1 convolution_bitcast_fusion.7
  86.3 2.6 bitcast_dynamic-update-slice_fusion.15
  91.4 2.1 convolution_bitcast_fusion.7
  96.2 2.5 bitcast_dynamic-update-slice_fusion.15
  101.2 2.1 convolution_bitcast_fusion.7
  106.0 2.6 bitcast_dynamic-update-slice_fusion.15
  115.9 2.6 bitcast_dynamic-update-slice_fusion.15
  120.6 107.5 %reduce-scatter.5.cloned.1.call-done = f32[512,768]{1,0:T(8,128)} async-done(((f32[2048,768]{1,0:T(8,128)}), f32[512,768]{1,0:T(8,128)}) %reduce-scatter.5.cloned.1.call-update) | async-done | bytes 1572880 | tf_op jit(solution)/shard_map/reduce_scatter | solution.py:172
  228.1 2.1 fusion.155
  232.6 64.0 %all-gather.7.cloned.1.call-done = bf16[2048,768]{1,0:T(8,128)(2,1)} async-done(((bf16[512,768]{1,0:T(8,128)(2,1)}), bf16[2048,768]{1,0:T(8,128)(2,1)}) %all-gather.7.cloned.1.call-update) | async-done | bytes 3145744 | tf_op jit(solution)/shard_map/all_gather | solution.py:179
  296.6 3.2 broadcast.348.clone.1
  299.8 3.1 broadcast.348.clone.2
  303.0 48.6 %while.69 = (s32[]{:T(128)}, f32[4,512,768]{2,1,0:T(8,128)}, bf16[4,512,768]{2,1,0:T(8,128)(2,1)}, f32[4,512,768]{2,1,0:T(8,128)}, bf16[4,512,768]{2,1,0:T(8,128...) while((s32[]{:T(128)}, f32[4,512,768]{2,1,0:T(8,128)}, ...), condition=%wide.region_9.10_spmd, body=%wide.region_8.9_spmd.sunk | while | flops 1233912576 | bytes 21243096 | solution.py:63
  305.5 3.5 bitcast_dynamic-update-slice_fusion.16
  309.0 4.2 bitcast_dynamic-update-slice_fusion.17
  317.6 3.4 bitcast_dynamic-update-slice_fusion.16
  321.1 4.2 bitcast_dynamic-update-slice_fusion.17
  329.8 3.5 bitcast_dynamic-update-slice_fusion.16
  333.3 4.2 bitcast_dynamic-update-slice_fusion.17
  342.0 3.5 bitcast_dynamic-update-slice_fusion.16
  345.5 4.2 bitcast_dynamic-update-slice_fusion.17
  351.7 109.5 %reduce-scatter.7.cloned.1.call-done = f32[512,768]{1,0:T(8,128)} async-done(((f32[2048,768]{1,0:T(8,128)}), f32[512,768]{1,0:T(8,128)}) %reduce-scatter.7.cloned.1.call-update) | async-done | bytes 1572880 | tf_op jit(solution)/shard_map/reduce_scatter | solution.py:182
  461.2 2.4 fusion.157
  467.7 63.9 %all-gather.9.cloned.1.call-done = bf16[2048,768]{1,0:T(8,128)(2,1)} async-done(((bf16[512,768]{1,0:T(8,128)(2,1)}), bf16[2048,768]{1,0:T(8,128)(2,1)}) %all-gather.9.cloned.1.call-update) | async-done | bytes 3145744 | tf_op jit(solution)/shard_map/all_gather | solution.py:192
  531.5 2.5 broadcast.352
  534.0 2.5 broadcast.352.clone
  536.5 3.1 broadcast.348
  539.7 79.0 %while.70 = (s32[]{:T(128)}, f32[2,768,768]{2,1,0:T(8,128)}, f32[2,768]{1,0:T(2,128)S(1)}, f32[2,768,768]{2,1,0:T(8,128)}, f32[4,512,768]{2,1,0:T(8,128)}, /*ind...) while((s32[]{:T(128)}, f32[2,768,768]{2,1,0:T(8,128)}, ...), condition=%wide.region_19.20_spmd, body=%wide.region_15.19_spmd.sunk | while | flops 2423784192 | bytes 36199780 | solution.py:92
  542.2 3.1 convert_reduce_fusion.9
  546.1 4.7 fusion.226
  552.1 5.3 fusion.227
  561.9 3.1 convert_reduce_fusion.9
  565.8 4.7 fusion.226
  571.8 5.3 fusion.227
  577.1 2.1 bitcast_dynamic-update-slice_fusion.19
  581.7 3.1 convert_reduce_fusion.9
  585.6 4.7 fusion.226
  591.7 5.3 fusion.227
  601.4 3.1 convert_reduce_fusion.9
  605.3 4.7 fusion.226
  611.4 5.3 fusion.227
  619.2 109.0 %reduce-scatter.9.cloned.1.call-done = f32[512,768]{1,0:T(8,128)} async-done(((f32[2048,768]{1,0:T(8,128)}), f32[512,768]{1,0:T(8,128)}) %reduce-scatter.9.cloned.1.call-update) | async-done | bytes 1572880 | tf_op jit(solution)/shard_map/reduce_scatter | solution.py:198
  728.3 2.9 fusion.146
  735.0 62.2 %all-gather.11.cloned.1.call-done = bf16[2048,768]{1,0:T(8,128)(2,1)} async-done(((bf16[512,768]{1,0:T(8,128)(2,1)}), bf16[2048,768]{1,0:T(8,128)(2,1)}) %all-gather.11.cloned.1.call-update) | async-done | bytes 3145744 | tf_op jit(solution)/shard_map/all_gather | solution.py:210
  797.2 2.1 broadcast_in_dim.122
  800.4 95.7 %while.71 = (s32[]{:T(128)}, f32[2,3,768,192]{2,3,1,0:T(8,128)}, f32[2,2,192]{2,1,0:T(2,128)S(1)}, f32[2,192,768]{2,1,0:T(8,128)}, bf16[4,512,768]{2,1,0:T(8,128...) while((s32[]{:T(128)}, f32[2,3,768,192]{2,3,1,0:T(8,128)}, ...), condition=%wide.region_29.30_spmd, body=%wide.region_23.29_spmd.sunk | while | flops 1337720064 | bytes 39173132 | solution.py:281
  813.6 4.2 fusion.244
  819.4 3.2 fusion.245
  837.6 4.2 fusion.244
  843.3 3.2 fusion.245
  861.5 4.2 fusion.244
  867.2 3.2 fusion.245
  885.4 4.2 fusion.244
  891.2 3.2 fusion.245
  905.5 43.0 %all-reduce = (f32[2,2,768]{2,0,1:T(2,128)S(1)}, f32[2,2,768]{2,0,1:T(2,128)S(1)}, f32[2,2,768]{2,0,1:T(2,128)S(1)}) all-reduce(f32[2,2,768]{2,0,1:T(2,128)S(1)} %pad_maximum_fusion, f32[2,2,768]{2,0,1:T(2,128)S(1)} %pad_maximum_fusion.1, f32[2,2,768]{2,0,1:T(2,128)S(1)} %pad_maximum_fusion.2), channel_id=1, replica_groups=mesh['dp'=8,'tensor'=4] {'dp','tensor'}, use_global_device_ids=true, to_apply=%region_34.35 | all-reduce | flops 9216 | bytes 73728 | tf_op jit(solution)/shard_map/psum | solution.py:298
  950.3 24.0 %all-reduce.1 = (f32[2,2,192]{2,1,0:T(2,128)}, f32[2,768]{1,0:T(2,128)}) all-reduce(f32[2,2,192]{2,1,0:T(2,128)S(1)} %get-tuple-element.342, f32[2,768]{1,0:T(2,128)S(1)} %copy-done.25), channel_id=1, replica_groups=mesh['dp'=8,'tensor'=4] {'dp'}, use_global_device_ids=true, to_apply=%region_32.33 | all-reduce | flops 2304 | bytes 18432 | tf_op jit(solution)/shard_map/psum | solution.py:295
  974.3 2.4 convert_add_fusion
  976.7 173.9 %all-reduce.5.cloned.1.call-done = (f32[2,3,768,192]{2,3,1,0:T(8,128)}, f32[2,192,768]{2,1,0:T(8,128)}, f32[2,768,768]{2,1,0:T(8,128)}, f32[2,768,768]{2,1,0:T(8,128)}) async-done(((f32[2,3,768,192]{2,3,1,0:T(8,128)}, f32[2,192,768]{2,1,0:T(8,128)}, f32[2,768,768]{2,1,0:T(8,128)}, f32[2,768,768]{2,1,0:T(8,128)}), (f32[2,3,768,192]{2,3,1,0:T(8,128)}, f32[2,192,768]{2,1,0:T(8,128)}, f32[2,768,768]{2,1,0:T(8,128)}, ...) | async-done | bytes 14155792 | tf_op jit(solution)/shard_map/psum | solution.py:295
  1150.6 4.3 copy.275
  1156.0 2.4 copy.277
  1159.5 2.2 copy.278
  (511 shorter events, 128.3 us)
Async XLA Ops:
  7.2 68.6 %all-gather.5.cloned.1.call-start = ((), (), s32[]{:S(2)}) async-start(), calls=%async_computation.4 | async-start | bytes 3932160 | tf_op jit(solution)/shard_map/all_gather | solution.py:140
  7.9 220.2 %reduce-scatter.5.cloned.1.call-start = ((), (), s32[]{:S(2)}) async-start(), calls=%async_computation.5 | async-start | bytes 7864320 | tf_op jit(solution)/shard_map/reduce_scatter | solution.py:172
  75.8 3.2 copy-start.44
  75.8 3.2 copy-start.48
  119.5 177.2 %all-gather.7.cloned.1.call-start = ((), (), s32[]{:S(2)}) async-start(), calls=%async_computation.6 | async-start | bytes 3932160 | tf_op jit(solution)/shard_map/all_gather | solution.py:179
  120.6 109.9 %copy-start.17 = (f32[512,768]{1,0:T(8,128)}, f32[512,768]{1,0:T(8,128)S(1)}, u32[]{:S(2)}) copy-start(f32[512,768]{1,0:T(8,128)S(1)} %fusion.116) | copy-start | bytes 4718596
  230.2 501.0 %copy-start = (f32[512,768]{1,0:T(8,128)}, f32[512,768]{1,0:T(8,128)S(1)}, u32[]{:S(2)}) copy-start(f32[512,768]{1,0:T(8,128)S(1)} %get-tuple-element.566) | copy-start | bytes 4718596
  230.2 501.0 %copy-start.29 = (f32[512]{0:T(512)}, f32[512]{0:T(512)S(1)}, u32[]{:S(2)}) copy-start(f32[512]{0:T(512)S(1)} %broadcast_multiply_fusion.5) | copy-start | bytes 6148
  230.6 500.7 %copy-start.33 = (f32[512]{0:T(512)}, f32[512]{0:T(512)S(1)}, u32[]{:S(2)}) copy-start(f32[512]{0:T(512)S(1)} %add_rsqrt_fusion.1) | copy-start | bytes 6148
  232.5 228.7 %reduce-scatter.7.cloned.1.call-start = ((), (), s32[]{:S(2)}) async-start(), calls=%async_computation.7 | async-start | bytes 7864320 | tf_op jit(solution)/shard_map/reduce_scatter | solution.py:182
  299.8 3.1 copy-start.26
  309.0 4.2 copy-start.51
  321.1 4.2 copy-start.51
  333.3 4.2 copy-start.51
  345.5 4.2 copy-start.51
  351.6 179.9 %all-gather.9.cloned.1.call-start = ((), (), s32[]{:S(2)}) async-start(), calls=%async_computation.8 | async-start | bytes 3932160 | tf_op jit(solution)/shard_map/all_gather | solution.py:192
  467.5 260.8 %reduce-scatter.9.cloned.1.call-start = ((), (), s32[]{:S(2)}) async-start(), calls=%async_computation.9 | async-start | bytes 7864320 | tf_op jit(solution)/shard_map/reduce_scatter | solution.py:198
  536.5 3.1 copy-start.37
  536.5 3.1 copy-start.46
  545.3 5.5 copy-start.9
  552.1 5.3 copy-start.10
  552.1 5.3 copy-start.11
  565.0 5.5 copy-start.9
  571.8 5.3 copy-start.10
  571.8 5.3 copy-start.11
  584.8 5.5 copy-start.9
  591.6 5.3 copy-start.10
  591.6 5.3 copy-start.11
  604.5 5.5 copy-start.9
  611.4 5.3 copy-start.10
  611.4 5.3 copy-start.11
  619.2 177.9 %all-gather.11.cloned.1.call-start = ((), (), s32[]{:S(2)}) async-start(), calls=%async_computation.10 | async-start | bytes 3932160 | tf_op jit(solution)/shard_map/all_gather | solution.py:210
  733.1 241.2 %reduce-scatter.11.cloned.1.call-start = ((), (), s32[]{:S(2)}) async-start(), calls=%async_computation.11 | async-start | bytes 3932160 | tf_op jit(solution)/shard_map/reduce_scatter | solution.py:287
  800.4 3.8 copy-start.38
  800.4 5.4 copy-start.49
  800.4 5.8 copy-start.35
  805.8 3.3 copy-start.2
  813.6 4.4 copy-start.39
  818.0 4.5 copy-start.20
  824.3 3.8 copy-start.38
  824.3 5.5 copy-start.49
  824.3 5.8 copy-start.35
  829.7 3.3 copy-start.2
  837.6 4.4 copy-start.39
  841.9 4.5 copy-start.20
  848.2 3.8 copy-start.38
  848.2 5.5 copy-start.49
  848.2 5.8 copy-start.35
  853.6 3.3 copy-start.2
  861.5 4.4 copy-start.39
  865.8 4.5 copy-start.20
  872.1 3.8 copy-start.38
  872.1 5.5 copy-start.49
  872.1 5.8 copy-start.35
  877.6 3.3 copy-start.2
  885.4 4.4 copy-start.39
  889.8 4.5 copy-start.20
  896.0 254.5 %all-reduce.5.cloned.1.call-start = ((), (), s32[]{:S(2)}) async-start(), calls=%async_computation.12 | async-start | bytes 28311552 | tf_op jit(solution)/shard_map/psum | solution.py:295
  904.6 45.6 %copy-start.25 = (f32[2,768]{1,0:T(2,128)S(1)}, f32[2,768]{1,0:T(2,128)}, u32[]{:S(2)}) copy-start(f32[2,768]{1,0:T(2,128)} %copy-done.24) | copy-start | bytes 18436
  904.7 69.6 %copy-start.15 = (f32[512,768]{1,0:T(8,128)S(1)}, f32[512,768]{1,0:T(8,128)}, u32[]{:S(2)}) copy-start(f32[512,768]{1,0:T(8,128)} %get-tuple-element.534) | copy-start | bytes 4718596
  1150.6 4.4 copy-start.23
  1150.6 5.4 copy-start.21
  1155.0 4.2 slice-start
  1156.0 3.6 slice-start.1
  (53 other events, 88.7 us)
Sparse Core Ops, SparseCore 0:
  9.6 66.1 all-gather.4
  118.7 109.3 reduce-scatter.4
  232.6 63.9 all-gather.6
  351.7 109.4 reduce-scatter.6
  467.6 63.9 all-gather.8
  618.8 109.4 reduce-scatter.8
  733.2 63.9 all-gather.10
  896.2 59.9 reduce-scatter.10
  961.4 189.1 all-reduce.4
where the time goes:
time: 1170 us
  waiting for transfers between devices  758 us (65%)
  matrix products  172 us (15%)
  local copies, waits for them, and re-layouts  73.4 us (6%)
  blocking collectives  67 us (6%)
  other arithmetic  50 us (4%)
  loops' own time  32.5 us (3%)
  between operations  14.2 us (1%)
    psum x1, waiting for transfers between devices, local(): lax.psum((acc_qkv, acc_qv, acc_out, up_total, ubias_total, down_total), '...  174 us
    reduce_scatter x1, waiting for transfers between devices, local(): lax.psum_scatter(ffn_parts.reshape(group_rows, -1), 'tensor', scatter_dim...  110 us
    reduce_scatter x1, waiting for transfers between devices, local(): lax.psum_scatter(ffn_back_parts.reshape(group_rows, -1), 'tensor', scatte...  109 us
    reduce_scatter x1, waiting for transfers between devices, local(): lax.psum_scatter(attn_parts.reshape(group_rows, -1), 'tensor', scatter_di...  107 us
    all_gather x1, waiting for transfers between devices, local(): gathered = lax.all_gather(inputs, 'tensor', axis=0, tiled=True)  67 us
    all_gather x1, waiting for transfers between devices, local(): gathered_norm = lax.all_gather(normed_low, 'tensor', axis=0, tiled=True)  64 us
    all_gather x1, waiting for transfers between devices, local(): gathered_two = lax.all_gather(d_two_low, 'tensor', axis=0, tiled=True)  63.9 us
    all_gather x1, waiting for transfers between devices, local(): lax.all_gather(d_one.astype(jnp.bfloat16), 'tensor', axis=0, tiled=True)  62.2 us
  transfers between devices with their start and end apart: 9, of which 8 were waited for; matrix products, arithmetic and copies ran while one was open for 1% of the time, Pallas kernels for 0%

commit v1 on v0

--- a/solution.py
+++ b/solution.py
@@ -180,8 +180,11 @@
     norm_blocks = gathered_norm.reshape(n_blocks, block_rows, -1)
     kept_pre, kept_activ, ffn_parts = ffn_apply(w_up, up_bias, w_down, norm_blocks, block_kind)
     ffn_rows = lax.psum_scatter(
-        ffn_parts.reshape(group_rows, -1), "tensor", scatter_dimension=0, tiled=True
-    )
+        ffn_parts.reshape(group_rows, -1).astype(jnp.bfloat16),
+        "tensor",
+        scatter_dimension=0,
+        tiled=True,
+    ).astype(jnp.float32)
     hidden_two = normed + ffn_rows + pick(resid_bias[:, 1])
     gain_two = pick(norm_gain[:, 1])
     output_rows, unit_two, inv_two = norm_forward(hidden_two, gain_two, pick(norm_shift[:, 1]))
@@ -196,8 +199,11 @@
     )
     d_normed = (
         lax.psum_scatter(
-            ffn_back_parts.reshape(group_rows, -1), "tensor", scatter_dimension=0, tiled=True
-        )
+            ffn_back_parts.reshape(group_rows, -1).astype(jnp.bfloat16),
+            "tensor",
+            scatter_dimension=0,
+            tiled=True,
+        ).astype(jnp.float32)
         + d_two
     )
     up_total, ubias_total, down_total = (acc_up, acc_ubias, acc_down)
@@ -292,12 +298,17 @@
         ).astype(jnp.float32)
         + d_one
     )
-    qkv_total, qv_total, out_total, up_total, ubias_total, down_total = lax.psum(
-        (acc_qkv, acc_qv, acc_out, up_total, ubias_total, down_total), "dp"
-    )
-    rbias_total, gain_total, shift_total = lax.psum(
-        (rbias_grads, gain_grads, shift_grads), ("dp", "tensor")
-    )
+    qkv_low, out_low, up_low, down_low = lax.psum(
+        tuple(v.astype(jnp.bfloat16) for v in (acc_qkv, acc_out, up_total, down_total)), "dp"
+    )
+    qkv_total, out_total, up_total, down_total = (
+        v.astype(jnp.float32) for v in (qkv_low, out_low, up_low, down_low)
+    )
+    small_grads = jnp.sum(
+        lax.all_gather(jnp.stack([rbias_grads, gain_grads, shift_grads]), "tensor"), axis=0
+    )
+    qv_total, ubias_total, small_total = lax.psum((acc_qv, ubias_total, small_grads), "dp")
+    rbias_total, gain_total, shift_total = small_total[0], small_total[1], small_total[2]
     return (
         layer_out,
         input_grad,

time: 1170 us -> 982 us (0.84)
  waiting for transfers between devices: 758 us -> 584 us
  blocking collectives: 67 us -> 38.2 us
  other arithmetic: 50 us -> 71 us
  matrix products: 172 us -> 160 us
    psum x1, waiting for transfers between devices: 174 us -> 62.3 us  [local(): lax.psum(tuple((v.astype(jnp.bfloat16) for v in (acc_qkv, acc_out, up_tot...]
    reduce_scatter x2, waiting for transfers between devices: 219 us -> 118 us  [the longest x1 59.2 us: local(): lax.psum_scatter(ffn_parts.reshape(group_rows, -1).astype(jnp.bfloat16),...]
    reduce_scatter x1, waiting for transfers between devices: 0.01 us -> 52.9 us  [local(): lax.psum_scatter(qkv_back_parts.reshape(group_rows, -1).astype(jnp.bfloat...]
    psum x2 -> x1, blocking collectives: 67 us -> 24.6 us  [local(): lax.psum((acc_qv, ubias_total, small_grads), 'dp')]
    convert_element_type x0 -> x8, other arithmetic: none -> 22.3 us  [the longest x4 12.3 us: local(): v.astype(jnp.bfloat16)]
    while x152 -> x192, local copies, waits for them, and re-layouts: 7.24 us -> 24.8 us
    all_gather x0 -> x1, blocking collectives: none -> 13.6 us  [local(): lax.all_gather(jnp.stack([rbias_grads, gain_grads, shift_grads]), 'tensor')]
  transfers between devices with their start and end apart: 9 -> 9, of which waited for: 8 -> 9; matrix products, arithmetic and copies ran while one was open for 1% -> 4% of each run, Pallas kernels for 0% -> 0%
where the time goes in v1:
time: 982 us; the launch traced here: 979 us
  waiting for transfers between devices  584 us (59%)
  matrix products  160 us (16%)
  local copies, waits for them, and re-layouts  78.3 us (8%)
  other arithmetic  71 us (7%)
  blocking collectives  38.2 us (4%)
  loops' own time  32.7 us (3%)
  between operations  14.2 us (1%)
    reduce_scatter x1, waiting for transfers between devices, local(): lax.psum_scatter(attn_parts.reshape(group_rows, -1), 'tensor', scatter_di...  108 us
    all_gather x1, waiting for transfers between devices, local(): gathered = lax.all_gather(inputs, 'tensor', axis=0, tiled=True)  67 us
    psum x1, waiting for transfers between devices, local(): lax.psum(tuple((v.astype(jnp.bfloat16) for v in (acc_qkv, acc_out, up_tot...  62.3 us
    all_gather x1, waiting for transfers between devices, local(): gathered_norm = lax.all_gather(normed_low, 'tensor', axis=0, tiled=True)  60.5 us
    all_gather x1, waiting for transfers between devices, local(): gathered_two = lax.all_gather(d_two_low, 'tensor', axis=0, tiled=True)  59.5 us
    reduce_scatter x1, waiting for transfers between devices, local(): lax.psum_scatter(ffn_parts.reshape(group_rows, -1).astype(jnp.bfloat16),...  59.2 us
    reduce_scatter x1, waiting for transfers between devices, local(): lax.psum_scatter(ffn_back_parts.reshape(group_rows, -1).astype(jnp.bfloat...  58.6 us
    all_gather x1, waiting for transfers between devices, local(): lax.all_gather(d_one.astype(jnp.bfloat16), 'tensor', axis=0, tiled=True)  55.5 us
  transfers between devices with their start and end apart: 9, of which 9 were waited for; matrix products, arithmetic and copies ran while one was open for 4% of the time, Pallas kernels for 0%

profile of v1, /device:TPU:0, one launch (start us, length us, event | category | flops | bytes accessed | tf_op | source)
XLA Modules:
  0.0 979.4 jit_solution(18382728737028988269)
XLA Ops:
  8.8 67.0 %all-gather.6.cloned.1.call-done = bf16[2048,768]{1,0:T(8,128)(2,1)} async-done(((bf16[512,768]{1,0:T(8,128)(2,1)}), bf16[2048,768]{1,0:T(8,128)(2,1)}) %all-gather.6.cloned.1.call-update) | async-done | bytes 3145744 | tf_op jit(solution)/shard_map/all_gather | solution.py:140
  75.8 3.2 broadcast.348.clone
  78.9 39.6 %while.68 = (s32[]{:T(128)}, bf16[4,3,512,192]{2,3,1,0:T(8,128)(2,1)}, f32[4,4,3,128]{3,2,1,0:T(4,128)S(1)}, bf16[4,512,192]{1,2,0:T(8,128)(2,1)S(1)}, f32[4,512...) while((s32[]{:T(128)}, ...), condition=%wide.region_3.4_spmd, body=%wide.region_0.3_spmd.sunk | while | flops 658340736 | bytes 15210975 | solution.py:169
  86.3 2.6 bitcast_dynamic-update-slice_fusion.15
  91.4 2.1 convolution_bitcast_fusion.7
  96.2 2.5 bitcast_dynamic-update-slice_fusion.15
  106.0 2.6 bitcast_dynamic-update-slice_fusion.15
  115.9 2.6 bitcast_dynamic-update-slice_fusion.15
  120.8 107.8 %reduce-scatter.5.cloned.1.call-done = f32[512,768]{1,0:T(8,128)} async-done(((f32[2048,768]{1,0:T(8,128)}), f32[512,768]{1,0:T(8,128)}) %reduce-scatter.5.cloned.1.call-update) | async-done | bytes 1572880 | tf_op jit(solution)/shard_map/reduce_scatter | solution.py:172
  228.7 2.1 fusion.156
  236.7 60.5 %all-gather.8.cloned.1.call-done = bf16[2048,768]{1,0:T(8,128)(2,1)} async-done(((bf16[512,768]{1,0:T(8,128)(2,1)}), bf16[2048,768]{1,0:T(8,128)(2,1)}) %all-gather.8.cloned.1.call-update) | async-done | bytes 3145744 | tf_op jit(solution)/shard_map/all_gather | solution.py:179
  297.2 3.2 broadcast.348
  300.4 51.2 %while.69 = (s32[]{:T(128)}, f32[4,512,768]{2,1,0:T(8,128)}, bf16[4,512,768]{2,1,0:T(8,128)(2,1)}, bf16[4,512,768]{2,1,0:T(8,128)(2,1)}, bf16[4,512,768]{2,1,0:T...) while((s32[]{:T(128)}, f32[4,512,768]{2,1,0:T(8,128)}, ...), condition=%wide.region_9.10_spmd, body=%wide.region_8.9_spmd.sunk | while | flops 1233912576 | bytes 46408972 | solution.py:63
  302.9 3.6 bitcast_dynamic-update-slice_fusion.16
  306.6 4.2 bitcast_dynamic-update-slice_fusion.17
  315.8 3.6 bitcast_dynamic-update-slice_fusion.16
  319.4 4.2 bitcast_dynamic-update-slice_fusion.17
  328.5 3.6 bitcast_dynamic-update-slice_fusion.16
  332.2 4.2 bitcast_dynamic-update-slice_fusion.17
  341.3 3.6 bitcast_dynamic-update-slice_fusion.16
  345.0 4.2 bitcast_dynamic-update-slice_fusion.17
  351.7 59.2 %reduce-scatter.7.cloned.1.call-done = bf16[512,768]{1,0:T(8,128)(2,1)} async-done(((bf16[2048,768]{1,0:T(8,128)(2,1)}), bf16[512,768]{1,0:T(8,128)(2,1)}) %reduce-scatter.7.cloned.1.call-update) | async-done | bytes 786448 | tf_op jit(solution)/shard_map/reduce_scatter | solution.py:182
  410.8 2.1 fusion.158
  417.1 3.8 copy.267
  420.9 59.5 %all-gather.10.cloned.1.call-done = bf16[2048,768]{1,0:T(8,128)(2,1)} async-done(((bf16[512,768]{1,0:T(8,128)(2,1)}), bf16[2048,768]{1,0:T(8,128)(2,1)}) %all-gather.10.cloned.1.call-update) | async-done | bytes 3145744 | tf_op jit(solution)/shard_map/all_gather | solution.py:195
  480.3 2.5 broadcast.352
  482.8 2.5 broadcast.352.clone
  485.3 82.3 %while.70 = (s32[]{:T(128)}, f32[2,768,768]{2,1,0:T(8,128)}, f32[2,768]{1,0:T(2,128)S(1)}, f32[2,768,768]{2,1,0:T(8,128)}, bf16[4,512,768]{2,1,0:T(8,128)(2,1)},...) while((s32[]{:T(128)}, f32[2,768,768]{2,1,0:T(8,128)}, ...), condition=%wide.region_19.20_spmd, body=%wide.region_15.19_spmd.sunk | while | flops 2423784192 | bytes 61365152 | solution.py:92
  487.8 3.1 convert_reduce_fusion.9
  491.7 4.7 fusion.227
  497.9 5.4 fusion.228
  508.4 3.1 convert_reduce_fusion.9
  512.3 4.7 fusion.227
  518.5 5.4 fusion.228
  529.0 3.1 convert_reduce_fusion.9
  532.9 4.7 fusion.227
  539.0 5.4 fusion.228
  549.5 3.1 convert_reduce_fusion.9
  553.4 4.7 fusion.227
  559.6 5.4 fusion.228
  568.2 58.6 %reduce-scatter.9.cloned.1.call-done = bf16[512,768]{1,0:T(8,128)(2,1)} async-done(((bf16[2048,768]{1,0:T(8,128)(2,1)}), bf16[512,768]{1,0:T(8,128)(2,1)}) %reduce-scatter.9.cloned.1.call-update) | async-done | bytes 786448 | tf_op jit(solution)/shard_map/reduce_scatter | solution.py:201
  626.8 2.7 fusion.145
  631.5 4.0 convert_element_type.232
  635.5 4.0 convert_element_type.234
  639.4 55.5 %all-gather.12.cloned.1.call-done = bf16[2048,768]{1,0:T(8,128)(2,1)} async-done(((bf16[512,768]{1,0:T(8,128)(2,1)}), bf16[2048,768]{1,0:T(8,128)(2,1)}) %all-gather.12.cloned.1.call-update) | async-done | bytes 3145744 | tf_op jit(solution)/shard_map/all_gather | solution.py:216
  694.9 2.1 broadcast_in_dim.122
  698.1 93.0 %while.71 = (s32[]{:T(128)}, f32[2,3,768,192]{2,3,1,0:T(8,128)}, f32[2,2,192]{2,1,0:T(2,128)S(1)}, f32[2,192,768]{2,1,0:T(8,128)}, bf16[4,512,768]{2,1,0:T(8,128...) while((s32[]{:T(128)}, f32[2,3,768,192]{2,3,1,0:T(8,128)}, ...), condition=%wide.region_29.30_spmd, body=%wide.region_23.29_spmd.sunk | while | flops 1337720064 | bytes 39959592 | solution.py:287
  710.7 4.2 fusion.245
  716.5 3.2 fusion.246
  733.9 4.2 fusion.245
  739.7 3.2 fusion.246
  757.2 4.2 fusion.245
  763.0 3.2 fusion.246
  780.4 4.2 fusion.245
  786.2 3.2 fusion.246
  791.1 3.5 convert_element_type.228
  805.2 13.6 %all-gather = f32[12,2,2,768]{3,2,1,0:T(2,128)S(1)} all-gather(f32[3,2,2,768]{3,2,1,0:T(2,128)S(1)} %copy.99), channel_id=2, replica_groups=mesh['dp'=8,'tensor'=4] {'tensor'}, dimensions={0}, use_global_device_ids=true | all-gather | bytes 184320 | tf_op jit(solution)/shard_map/all_gather | solution.py:308
  818.9 24.6 %all-reduce = (f32[2,2,192]{2,1,0:T(2,128)}, f32[3,2,2,768]{3,1,2,0:T(2,128)S(1)}, f32[2,768]{1,0:T(2,128)}) all-reduce(f32[2,2,192]{2,1,0:T(2,128)S(1)} %get-tuple-element.342, f32[3,2,2,768]{3,1,2,0:T(2,128)S(1)} %copy.115, f32[2,768]{1,0:T(2,128)S(1)} %copy-done.33), channel_id=1, replica_groups=mesh['dp'=8,'tensor'=4] {'dp'}, use_global_device_ids=true, to_apply=%region_32.33 | all-reduce | flops 11520 | bytes 92160 | tf_op jit(solution)/shard_map/psum | solution.py:310
  845.3 62.3 %all-reduce.4.cloned.1.call-done = (bf16[2,3,768,192]{2,3,1,0:T(8,128)(2,1)}, bf16[2,192,768]{2,1,0:T(8,128)(2,1)}, bf16[2,768,768]{2,1,0:T(8,128)(2,1)}, bf16[2,768,768]{2,1,0:T(8,128)(2,1)}) async-done(((bf16[2,3,768,192]{2,3,1,0:T(8,128)(2,1)}, bf16[2,192,768]{2,1,0:T(8,128)(2,1)}, bf16[2,768,768]{2,1,0:T(8,128)(2,1)}, bf16[2,768,768]{2,1,0:T(8,128)(2,1)}), (bf16[2,3,768,192]{2,3,1,0:T(8,128)(2,1)}, ...) | async-done | bytes 7077904 | tf_op jit(solution)/shard_map/psum | solution.py:301
  907.6 3.7 convert_element_type.229
  912.5 2.5 convert_element_type.233
  915.0 2.5 convert_element_type.235
  917.6 52.9 %reduce-scatter.11.cloned.1.call-done = bf16[512,768]{1,0:T(8,128)(2,1)} async-done(((bf16[2048,768]{1,0:T(8,128)(2,1)}), bf16[512,768]{1,0:T(8,128)(2,1)}) %reduce-scatter.11.cloned.1.call-update) | async-done | bytes 786448 | tf_op jit(solution)/shard_map/reduce_scatter | solution.py:293
  970.5 2.4 convert_add_fusion
  (561 shorter events, 138.4 us)
Async XLA Ops:
  7.2 68.6 %all-gather.6.cloned.1.call-start = ((), (), s32[]{:S(2)}) async-start(), calls=%async_computation.4 | async-start | bytes 3932160 | tf_op jit(solution)/shard_map/all_gather | solution.py:140
  7.9 220.8 %reduce-scatter.5.cloned.1.call-start = ((), (), s32[]{:S(2)}) async-start(), calls=%async_computation.5 | async-start | bytes 7864320 | tf_op jit(solution)/shard_map/reduce_scatter | solution.py:172
  75.8 3.2 copy-start.52
  75.8 3.2 copy-start.56
  119.5 177.7 %all-gather.8.cloned.1.call-start = ((), (), s32[]{:S(2)}) async-start(), calls=%async_computation.6 | async-start | bytes 3932160 | tf_op jit(solution)/shard_map/all_gather | solution.py:179
  120.8 110.3 %copy-start.19 = (f32[512,768]{1,0:T(8,128)}, f32[512,768]{1,0:T(8,128)S(1)}, u32[]{:S(2)}) copy-start(f32[512,768]{1,0:T(8,128)S(1)} %fusion.117) | copy-start | bytes 4718596
  230.8 398.7 %copy-start = (f32[512,768]{1,0:T(8,128)}, f32[512,768]{1,0:T(8,128)S(1)}, u32[]{:S(2)}) copy-start(f32[512,768]{1,0:T(8,128)S(1)} %get-tuple-element.573) | copy-start | bytes 4718596
  230.8 398.7 %copy-start.37 = (f32[512]{0:T(512)}, f32[512]{0:T(512)S(1)}, u32[]{:S(2)}) copy-start(f32[512]{0:T(512)S(1)} %broadcast_multiply_fusion.5) | copy-start | bytes 6148
  231.1 398.4 %copy-start.46 = (f32[512]{0:T(512)}, f32[512]{0:T(512)S(1)}, u32[]{:S(2)}) copy-start(f32[512]{0:T(512)S(1)} %add_rsqrt_fusion.1) | copy-start | bytes 6148
  233.1 177.7 %reduce-scatter.7.cloned.1.call-start = ((), (), s32[]{:S(2)}) async-start(), calls=%async_computation.7 | async-start | bytes 3932160 | tf_op jit(solution)/shard_map/reduce_scatter | solution.py:182
  302.9 7.8 copy-start.59
  306.6 4.2 copy-start.22
  315.8 7.8 copy-start.59
  319.3 4.2 copy-start.22
  328.5 7.8 copy-start.59
  332.1 4.2 copy-start.22
  341.3 7.8 copy-start.59
  345.0 4.2 copy-start.22
  351.6 128.7 %all-gather.10.cloned.1.call-start = ((), (), s32[]{:S(2)}) async-start(), calls=%async_computation.8 | async-start | bytes 3932160 | tf_op jit(solution)/shard_map/all_gather | solution.py:195
  416.8 210.0 %reduce-scatter.9.cloned.1.call-start = ((), (), s32[]{:S(2)}) async-start(), calls=%async_computation.9 | async-start | bytes 3932160 | tf_op jit(solution)/shard_map/reduce_scatter | solution.py:201
  491.0 5.5 copy-start.12
  497.9 5.5 copy-start.13
  497.9 5.5 copy-start.14
  497.9 5.5 copy-start.20
  511.5 5.5 copy-start.12
  518.4 5.5 copy-start.13
  518.4 5.5 copy-start.14
  518.5 5.5 copy-start.20
  532.1 5.5 copy-start.12
  539.0 5.5 copy-start.13
  539.0 5.5 copy-start.14
  539.0 5.5 copy-start.20
  552.6 5.5 copy-start.12
  559.6 5.5 copy-start.13
  559.6 5.5 copy-start.14
  559.6 5.5 copy-start.20
  568.2 126.7 %all-gather.12.cloned.1.call-start = ((), (), s32[]{:S(2)}) async-start(), calls=%async_computation.10 | async-start | bytes 3932160 | tf_op jit(solution)/shard_map/all_gather | solution.py:216
  631.4 276.2 %all-reduce.4.cloned.1.call-start = ((), (), s32[]{:S(2)}) async-start(), calls=%async_computation.12 | async-start | bytes 14155776 | tf_op jit(solution)/shard_map/psum | solution.py:301
  698.1 5.4 copy-start.44
  698.1 5.4 copy-start.57
  698.1 5.8 copy-start.41
  710.7 4.4 copy-start.45
  715.1 4.5 copy-start.26
  721.3 5.5 copy-start.44
  721.3 5.5 copy-start.57
  721.3 5.8 copy-start.41
  733.9 4.4 copy-start.45
  738.3 4.5 copy-start.26
  744.6 5.5 copy-start.44
  744.6 5.5 copy-start.57
  744.6 5.8 copy-start.41
  757.2 4.4 copy-start.45
  761.6 4.5 copy-start.26
  767.8 5.5 copy-start.44
  767.8 5.5 copy-start.57
  767.8 5.8 copy-start.41
  780.4 4.4 copy-start.45
  784.8 4.5 copy-start.26
  791.1 3.5 copy-start.11
  795.5 175.0 %reduce-scatter.11.cloned.1.call-start = ((), (), s32[]{:S(2)}) async-start(), calls=%async_computation.11 | async-start | bytes 3932160 | tf_op jit(solution)/shard_map/reduce_scatter | solution.py:293
  804.0 14.9 %copy-start.33 = (f32[2,768]{1,0:T(2,128)S(1)}, f32[2,768]{1,0:T(2,128)}, u32[]{:S(2)}) copy-start(f32[2,768]{1,0:T(2,128)} %copy-done.32) | copy-start | bytes 18436
  907.6 3.7 copy-start.31
  907.6 4.8 copy-start.29
  915.0 55.5 %copy-start.18 = (f32[512,768]{1,0:T(8,128)S(1)}, f32[512,768]{1,0:T(8,128)}, u32[]{:S(2)}) copy-start(f32[512,768]{1,0:T(8,128)} %get-tuple-element.535) | copy-start | bytes 4718596
  (74 other events, 113.5 us)
Sparse Core Ops, SparseCore 0:
  9.6 66.1 all-gather.5
  119.2 109.4 reduce-scatter.4
  233.2 63.9 all-gather.7
  351.7 59.0 reduce-scatter.6
  416.9 63.3 all-gather.9
  567.7 59.0 reduce-scatter.8
  631.5 63.3 all-gather.11
  795.6 111.9 all-reduce.3
  909.9 60.4 reduce-scatter.10

commit v2 on v0

v2 whole, which is shorter than its diff:
```python
import jax
import jax.numpy as jnp
from jax import lax
from jax.sharding import PartitionSpec as P

HEAD_DIM = 64
CHAIN = 128
BLOCK_SEQS = 4
STREAMS = 2


EPSILON = 1e-05
SQRT_HALF = 0.7071067811865476
INV_ROOT_TWO_PI = 0.3989422804014327


def norm_forward(row_data, gain_rows, shift_rows):
    mean_row = jnp.mean(row_data, axis=-1, keepdims=True)
    centred = row_data - mean_row
    var_row = jnp.mean(centred * centred, axis=-1, keepdims=True)
    inv_std = lax.rsqrt(var_row + EPSILON)
    unit_rows = centred * inv_std
    return (unit_rows * gain_rows + shift_rows, unit_rows, inv_std)


def norm_backward(grad_rows, gain_rows, unit_rows, inv_std):
    scaled = grad_rows * gain_rows
    mean_first = jnp.mean(scaled, axis=-1, keepdims=True)
    mean_second = jnp.mean(scaled * unit_rows, axis=-1, keepdims=True)
    return inv_std * (scaled - mean_first - unit_rows * mean_second)


def type_sum(kind_hot, values):
    return jnp.einsum("rt,rd->td", kind_hot, values, precision=lax.Precision.HIGHEST)


def gelu_slope(values):
    return 0.5 * (1.0 + lax.erf(values * SQRT_HALF)) + values * INV_ROOT_TWO_PI * jnp.exp(
        -0.5 * values * values
    )


def gather_rows(local_rows):
    return lax.all_gather(local_rows, "tensor", axis=0, tiled=False)


def scatter_sum(seg_parts):
    n_seg, seg_rows, width = seg_parts.shape
    summed = lax.psum_scatter(
        seg_parts.reshape(n_seg * seg_rows, width).astype(jnp.bfloat16),
        "tensor",
        scatter_dimension=0,
        tiled=True,
    )
    return summed.astype(jnp.float32)


def masked(seg_rows, seg_hot):
    return seg_rows[:, None] * seg_hot[:, :, None, None].astype(seg_rows.dtype)


def kind_sums(seg_hot, seg_totals):
    return jnp.einsum(
        "st,se->te", seg_hot, seg_totals, precision=lax.Precision.HIGHEST
    )


def stream(
    inputs,
    cotangent,
    seg_kind,
    seg_lens,
    row_kind,
    w_qkv,
    qv_bias,
    w_out,
    resid_bias,
    norm_gain,
    norm_shift,
    w_up,
    up_bias,
    w_down,
):
    n_seg, chains = seg_lens.shape
    seg_rows = chains * CHAIN
    heads_here = w_qkv.shape[3] // HEAD_DIM
    score_scale = HEAD_DIM ** (-0.5)
    highest = lax.Precision.HIGHEST
    seg_hot = (seg_kind[:, None] == jnp.arange(2)[None, :]).astype(jnp.float32)
    kind_hot = (row_kind[:, None] == jnp.arange(2)[None, :]).astype(jnp.float32)

    def pick(kind_table):
        return jnp.dot(kind_hot, kind_table.astype(jnp.float32), precision=highest)

    def heads(rows):
        return rows.reshape(n_seg, chains, CHAIN, heads_here, HEAD_DIM)

    key_valid = jnp.arange(CHAIN)[None, None, :] < seg_lens[:, :, None]

    qkv_sel = w_qkv[seg_kind]
    qvb_sel = qv_bias[seg_kind].astype(jnp.float32)
    out_sel = w_out[seg_kind]
    up_sel = w_up[seg_kind]
    ubias_sel = up_bias[seg_kind].astype(jnp.float32)
    down_sel = w_down[seg_kind]

    input_segs = gather_rows(inputs)
    projected = jnp.einsum(
        "srd,sjde->jsre", input_segs, qkv_sel, preferred_element_type=jnp.float32
    )
    query_rows = (projected[0] + qvb_sel[:, None, 0]).astype(jnp.bfloat16)
    key_rows = projected[1].astype(jnp.bfloat16)
    value_rows = (projected[2] + qvb_sel[:, None, 1]).astype(jnp.bfloat16)

    def probs_of():
        raw_scores = (
            jnp.einsum(
                "scqhd,sckhd->schqk",
                heads(query_rows),
                heads(key_rows),
                preferred_element_type=jnp.float32,
            )
            * score_scale
        )
        return jnp.where(key_valid[:, :, None, None, :], raw_scores, -1e30)

    scores = probs_of()
    row_max = jnp.max(scores, axis=-1, keepdims=True)
    log_total = row_max[..., 0] + jnp.log(jnp.sum(jnp.exp(scores - row_max), axis=-1))
    attn_probs = jnp.exp(scores - log_total[..., None])
    probs_low = attn_probs.astype(jnp.bfloat16)
    mixed = jnp.einsum(
        "schqk,sckhd->scqhd", probs_low, heads(value_rows), preferred_element_type=jnp.float32
    )
    mixed = mixed.reshape(n_seg, seg_rows, -1).astype(jnp.bfloat16)
    attn_parts = jnp.einsum("sre,sed->srd", mixed, out_sel, preferred_element_type=jnp.float32)
    attn_rows = scatter_sum(attn_parts)

    hidden_one = inputs.astype(jnp.float32) + attn_rows + pick(resid_bias[:, 0])
    gain_one = pick(norm_gain[:, 0])
    normed, unit_one, inv_one = norm_forward(hidden_one, gain_one, pick(norm_shift[:, 0]))
    normed_low = normed.astype(jnp.bfloat16)
    norm_segs = gather_rows(normed_low)
    pre_act = (
        jnp.einsum("srd,sdf->srf", norm_segs, up_sel, preferred_element_type=jnp.float32)
        + ubias_sel[:, None]
    )
    activ = jax.nn.gelu(pre_act, approximate=False).astype(jnp.bfloat16)
    ffn_parts = jnp.einsum("srf,sfd->srd", activ, down_sel, preferred_element_type=jnp.float32)
    ffn_rows = scatter_sum(ffn_parts)

    hidden_two = normed + ffn_rows + pick(resid_bias[:, 1])
    gain_two = pick(norm_gain[:, 1])
    output_rows, unit_two, inv_two = norm_forward(hidden_two, gain_two, pick(norm_shift[:, 1]))
    layer_out = output_rows.astype(jnp.bfloat16)
    grad_out = cotangent.astype(jnp.float32)
    d_two = norm_backward(grad_out, gain_two, unit_two, inv_two)
    two_segs = gather_rows(d_two.astype(jnp.bfloat16))

    grad_down = jnp.einsum(
        "strf,srd->tfd", masked(activ, seg_hot), two_segs, preferred_element_type=jnp.float32
    )
    d_activ = jnp.einsum(
        "srd,sfd->srf", two_segs, down_sel, preferred_element_type=jnp.float32
    ).astype(jnp.bfloat16)
    d_pre = (d_activ.astype(jnp.float32) * gelu_slope(pre_act)).astype(jnp.bfloat16)
    grad_up = jnp.einsum(
        "strd,srf->tdf", masked(norm_segs, seg_hot), d_pre, preferred_element_type=jnp.float32
    )
    grad_ubias = kind_sums(seg_hot, jnp.sum(d_pre.astype(jnp.float32), axis=1))
    ffn_back = jnp.einsum("srf,sdf->srd", d_pre, up_sel, preferred_element_type=jnp.float32)
    d_normed = scatter_sum(ffn_back) + d_two

    d_one = norm_backward(d_normed, gain_one, unit_one, inv_one)
    gain_grads = jnp.stack(
        [type_sum(kind_hot, d_normed * unit_one), type_sum(kind_hot, grad_out * unit_two)], axis=1
    )
    shift_grads = jnp.stack([type_sum(kind_hot, d_normed), type_sum(kind_hot, grad_out)], axis=1)
    rbias_grads = jnp.stack([type_sum(kind_hot, d_one), type_sum(kind_hot, d_two)], axis=1)
    one_segs = gather_rows(d_one.astype(jnp.bfloat16))

    grad_out_w = jnp.einsum(
        "stre,srd->ted", masked(mixed, seg_hot), one_segs, preferred_element_type=jnp.float32
    )
    d_mixed = jnp.einsum(
        "srd,sed->sre", one_segs, out_sel, preferred_element_type=jnp.float32
    ).astype(jnp.bfloat16)
    d_mixed_heads = heads(d_mixed)
    d_value = jnp.einsum(
        "schqk,scqhd->sckhd", probs_low, d_mixed_heads, preferred_element_type=jnp.float32
    )
    d_value = d_value.reshape(n_seg, seg_rows, -1).astype(jnp.bfloat16)
    d_probs = jnp.einsum(
        "scqhd,sckhd->schqk", d_mixed_heads, heads(value_rows), preferred_element_type=jnp.float32
    )
    prob_dot = jnp.sum(attn_probs * d_probs, axis=-1, keepdims=True)
    d_scores = (attn_probs * (d_probs - prob_dot)).astype(jnp.bfloat16)
    d_query = (
        jnp.einsum(
            "schqk,sckhd->scqhd", d_scores, heads(key_rows), preferred_element_type=jnp.float32
        )
        * score_scale
    )
    d_key = (
        jnp.einsum(
            "schqk,scqhd->sckhd", d_scores, heads(query_rows), preferred_element_type=jnp.float32
        )
        * score_scale
    )
    d_query = d_query.reshape(n_seg, seg_rows, -1).astype(jnp.bfloat16)
    d_key = d_key.reshape(n_seg, seg_rows, -1).astype(jnp.bfloat16)
    d_proj = jnp.stack([d_query, d_key, d_value])
    grad_qkv = jnp.einsum(
        "strd,jsre->tjde", masked(input_segs, seg_hot), d_proj, preferred_element_type=jnp.float32
    )
    grad_qv = jnp.stack(
        [
            kind_sums(seg_hot, jnp.sum(d_query.astype(jnp.float32), axis=1)),
            kind_sums(seg_hot, jnp.sum(d_value.astype(jnp.float32), axis=1)),
        ],
        axis=1,
    )
    qkv_back = jnp.einsum("jsre,sjde->srd", d_proj, qkv_sel, preferred_element_type=jnp.float32)
    input_grad = scatter_sum(qkv_back) + d_one
    small = jnp.stack([rbias_grads, gain_grads, shift_grads])
    return (
        layer_out,
        input_grad,
        (grad_qkv, grad_qv, grad_out_w, grad_up, grad_ubias, grad_down),
        small,
    )


def local(
    inputs,
    cotangent,
    lengths,
    block_kind,
    w_qkv,
    qv_bias,
    w_out,
    resid_bias,
    norm_gain,
    norm_shift,
    w_up,
    up_bias,
    w_down,
):
    tok_dev = inputs.shape[0]
    n_tensor = lax.axis_size("tensor")
    rank = lax.axis_index("tensor")
    block_rows = BLOCK_SEQS * CHAIN
    assert block_rows % tok_dev == 0
    dev_chains = tok_dev // CHAIN
    chains = dev_chains // STREAMS
    seg_rows = chains * CHAIN
    weights = (w_qkv, qv_bias, w_out, resid_bias, norm_gain, norm_shift, w_up, up_bias, w_down)
    outs, ins, grads, smalls = [], [], [], []
    for part in range(STREAMS):
        first_row = jnp.arange(n_tensor) * tok_dev + part * seg_rows
        seg_kind = block_kind[first_row // block_rows]
        chain_ids = (
            jnp.arange(n_tensor)[:, None] * dev_chains + part * chains + jnp.arange(chains)[None, :]
        )
        seg_lens = lengths[chain_ids]
        own_rows = rank * tok_dev + part * seg_rows + jnp.arange(seg_rows)
        row_kind = block_kind[own_rows // block_rows]
        rows = slice(part * seg_rows, (part + 1) * seg_rows)
        out_part, in_part, grad_part, small_part = stream(
            inputs[rows], cotangent[rows], seg_kind, seg_lens, row_kind, *weights
        )
        outs.append(out_part)
        ins.append(in_part)
        grads.append(grad_part)
        smalls.append(small_part)
    layer_out = jnp.concatenate(outs, axis=0)
    input_grad = jnp.concatenate(ins, axis=0)
    grad_qkv, grad_qv, grad_out_w, grad_up, grad_ubias, grad_down = (
        sum(parts[1:], parts[0]) for parts in zip(*grads)
    )
    small = sum(smalls[1:], smalls[0])
    qkv_low, out_low, up_low, down_low = lax.psum(
        tuple(v.astype(jnp.bfloat16) for v in (grad_qkv, grad_out_w, grad_up, grad_down)), "dp"
    )
    qkv_total, out_total, up_total, down_total = (
        v.astype(jnp.float32) for v in (qkv_low, out_low, up_low, down_low)
    )
    small_grads = jnp.sum(lax.all_gather(small, "tensor"), axis=0)
    qv_total, ubias_total, small_total = lax.psum((grad_qv, grad_ubias, small_grads), "dp")
    return (
        layer_out,
        input_grad,
        qkv_total,
        qv_total,
        out_total,
        small_total[0],
        small_total[1],
        small_total[2],
        up_total,
        ubias_total,
        down_total,
    )


def solution(mesh):
    return jax.shard_map(
        local,
        mesh=mesh,
        in_specs=(
            P(("dp", "tensor"), None),
            P(("dp", "tensor"), None),
            P("dp"),
            P("dp"),
            P(None, None, None, "tensor"),
            P(None, None, "tensor"),
            P(None, "tensor", None),
            P(),
            P(),
            P(),
            P(None, None, "tensor"),
            P(None, "tensor"),
            P(None, "tensor", None),
        ),
        out_specs=(
            P(("dp", "tensor"), None),
            P(("dp", "tensor"), None),
            P(None, None, None, "tensor"),
            P(None, None, "tensor"),
            P(None, "tensor", None),
            P(),
            P(),
            P(),
            P(None, None, "tensor"),
            P(None, "tensor"),
            P(None, "tensor", None),
        ),
        check_vma=False,
    )
```

time: 1170 us -> 759 us (0.65)
  waiting for transfers between devices: 758 us -> 404 us
  loops' own time: 32.5 us -> 0 us
  blocking collectives: 67 us -> 38.7 us
  matrix products: 172 us -> 145 us
  local copies, waits for them, and re-layouts: 73.4 us -> 96.7 us
    reduce_scatter x4 -> x8, waiting for transfers between devices: 326 us -> 112 us  [scatter_sum(): lax.psum_scatter(seg_parts.reshape(n_seg * seg_rows, width).astype(jnp.bf...]
    psum x1, waiting for transfers between devices: 174 us -> 101 us  [local(): lax.psum(tuple((v.astype(jnp.bfloat16) for v in (grad_qkv, grad_out_w, gr...]
    all_gather x4 -> x8, waiting for transfers between devices: 257 us -> 189 us  [gather_rows(): return lax.all_gather(local_rows, 'tensor', axis=0, tiled=False)]
    dot_general x76 -> x42, matrix products: 158 us -> 112 us  [the longest x2 12.7 us: stream(): jnp.einsum('srd,sfd->srf', two_segs, down_sel, preferred_element_type=jnp...]
    psum x2 -> x1, blocking collectives: 67 us -> 23.7 us  [local(): lax.psum((grad_qv, grad_ubias, small_grads), 'dp')]
    gather x0 -> x19, local copies, waits for them, and re-layouts: none -> 33.2 us  [the longest x2 8.16 us: stream(): qkv_sel = w_qkv[seg_kind]]
    another operation x4 -> x0, loops' own time: 32.5 us -> none  [the longest x1 8.63 us: local(): lax.scan(attend_backward, zeros_attn, (input_blocks, one_blocks, valid_bl...]
    convert_element_type x10 -> x16, other arithmetic: 4.19 us -> 28.3 us  [the longest x2 14.6 us: stream(): activ = jax.nn.gelu(pre_act, approximate=False).astype(jnp.bfloat16)]
  transfers between devices with their start and end apart: 9 -> 17, of which waited for: 8 -> 15; matrix products, arithmetic and copies ran while one was open for 1% -> 35% of each run, Pallas kernels for 0% -> 0%
where the time goes in v2:
time: 759 us; the launch traced here: 748 us
  waiting for transfers between devices  404 us (53%)
  matrix products  145 us (19%)
  local copies, waits for them, and re-layouts  96.7 us (13%)
  other arithmetic  45.4 us (6%)
  blocking collectives  38.7 us (5%)
  between operations  15.8 us (2%)
    all_gather x8, waiting for transfers between devices, gather_rows(): return lax.all_gather(local_rows, 'tensor', axis=0, tiled=False)  189 us
    reduce_scatter x8, waiting for transfers between devices, scatter_sum(): lax.psum_scatter(seg_parts.reshape(n_seg * seg_rows, width).astype(jnp.bf...  112 us
    psum x1, waiting for transfers between devices, local(): lax.psum(tuple((v.astype(jnp.bfloat16) for v in (grad_qkv, grad_out_w, gr...  101 us
    psum x1, blocking collectives, local(): lax.psum((grad_qv, grad_ubias, small_grads), 'dp')  23.7 us
    dot_general x12, matrix products, pick(): return jnp.dot(kind_hot, kind_table.astype(jnp.float32), precision=highest)  17.4 us
    dot_general x12, matrix products, type_sum(): jnp.einsum('rt,rd->td', kind_hot, values, precision=lax.Precision.HIGHEST)  15.9 us
  transfers between devices with their start and end apart: 17, of which 15 were waited for; matrix products, arithmetic and copies ran while one was open for 35% of the time, Pallas kernels for 0%

profile of v2, /device:TPU:0, one launch (start us, length us, event | category | flops | bytes accessed | tf_op | source)
XLA Modules:
  0.0 748.4 jit_solution(5101154546540024199)
XLA Ops:
  15.7 4.0 gather_fusion.9
  19.8 30.1 %all-gather.21.cloned.1.call-done = bf16[1024,768]{1,0:T(8,128)(2,1)} async-done(((bf16[256,768]{1,0:T(8,128)(2,1)}), bf16[1024,768]{1,0:T(8,128)(2,1)}) %all-gather.21.cloned.1.call-update) | async-done | bytes 1572880 | tf_op jit(solution)/shard_map/all_gather | solution.py:44
  49.9 3.6 convolution_bitcast_fusion
  56.8 2.8 fusion.212
  59.7 2.4 squeeze.55
  62.1 2.4 squeeze.56
  70.6 3.2 convolution_convert_fusion.6
  77.4 4.1 gather_fusion.1
  83.3 4.7 all-gather.17.cloned.1.call-done
  88.0 3.6 convolution_bitcast_fusion.1
  93.2 2.5 fusion.211
  102.1 3.2 convolution_convert_fusion.7
  106.0 2.6 compare_select_fusion.4
  110.5 14.8 %reduce-scatter.13.cloned.1.call-done = bf16[256,768]{1,0:T(8,128)(2,1)} async-done(((bf16[1024,768]{1,0:T(8,128)(2,1)}), bf16[256,768]{1,0:T(8,128)(2,1)}) %reduce-scatter.13.cloned.1.call-update) | async-done | bytes 393232 | tf_op jit(solution)/shard_map/reduce_scatter | solution.py:49
  127.0 2.5 fusion.220
  131.4 3.2 gather_fusion.15
  134.6 3.2 gather_fusion.7
  137.7 5.0 gather_fusion.13
  142.7 3.1 gather_fusion.5
  145.9 2.6 compare_select_fusion.7
  148.8 12.9 %reduce-scatter.9.cloned.1.call-done = bf16[256,768]{1,0:T(8,128)(2,1)} async-done(((bf16[1024,768]{1,0:T(8,128)(2,1)}), bf16[256,768]{1,0:T(8,128)(2,1)}) %reduce-scatter.9.cloned.1.call-update) | async-done | bytes 393232 | tf_op jit(solution)/shard_map/reduce_scatter | solution.py:49
  164.9 34.6 %all-gather.23.cloned.1.call-done = bf16[1024,768]{1,0:T(8,128)(2,1)} async-done(((bf16[256,768]{1,0:T(8,128)(2,1)}), bf16[1024,768]{1,0:T(8,128)(2,1)}) %all-gather.23.cloned.1.call-update) | async-done | bytes 1572880 | tf_op jit(solution)/shard_map/all_gather | solution.py:44
  199.6 5.1 fusion.93
  204.7 7.3 fusion.8
  212.0 2.5 convolution_convert_fusion.4
  214.8 22.1 %all-gather.19.cloned.1.call-done = bf16[1024,768]{1,0:T(8,128)(2,1)} async-done(((bf16[256,768]{1,0:T(8,128)(2,1)}), bf16[1024,768]{1,0:T(8,128)(2,1)}) %all-gather.19.cloned.1.call-update) | async-done | bytes 1572880 | tf_op jit(solution)/shard_map/all_gather | solution.py:44
  236.9 5.1 fusion.92
  242.0 7.3 fusion.5
  249.3 2.6 convolution_convert_fusion.5
  253.2 21.0 %reduce-scatter.15.cloned.1.call-done = bf16[256,768]{1,0:T(8,128)(2,1)} async-done(((bf16[1024,768]{1,0:T(8,128)(2,1)}), bf16[256,768]{1,0:T(8,128)(2,1)}) %reduce-scatter.15.cloned.1.call-update) | async-done | bytes 393232 | tf_op jit(solution)/shard_map/reduce_scatter | solution.py:49
  276.0 34.7 %reduce-scatter.11.cloned.1.call-done = bf16[256,768]{1,0:T(8,128)(2,1)} async-done(((bf16[1024,768]{1,0:T(8,128)(2,1)}), bf16[256,768]{1,0:T(8,128)(2,1)}) %reduce-scatter.11.cloned.1.call-update) | async-done | bytes 393232 | tf_op jit(solution)/shard_map/reduce_scatter | solution.py:49
  317.2 35.4 %all-gather.25.cloned.1.call-done = bf16[1024,768]{1,0:T(8,128)(2,1)} async-done(((bf16[256,768]{1,0:T(8,128)(2,1)}), bf16[1024,768]{1,0:T(8,128)(2,1)}) %all-gather.25.cloned.1.call-update) | async-done | bytes 1572880 | tf_op jit(solution)/shard_map/all_gather | solution.py:44
  352.5 6.4 convert_reduce_fusion.1
  358.9 5.7 convolution_convert_fusion.2
  364.9 24.9 %all-gather.29.cloned.1.call-done = bf16[1024,768]{1,0:T(8,128)(2,1)} async-done(((bf16[256,768]{1,0:T(8,128)(2,1)}), bf16[1024,768]{1,0:T(8,128)(2,1)}) %all-gather.29.cloned.1.call-update) | async-done | bytes 1572880 | tf_op jit(solution)/shard_map/all_gather | solution.py:44
  389.9 6.4 convert_reduce_fusion
  396.2 5.5 convolution_convert_fusion
  404.2 22.3 %reduce-scatter.17.cloned.1.call-done = bf16[256,768]{1,0:T(8,128)(2,1)} async-done(((bf16[1024,768]{1,0:T(8,128)(2,1)}), bf16[256,768]{1,0:T(8,128)(2,1)}) %reduce-scatter.17.cloned.1.call-update) | async-done | bytes 393232 | tf_op jit(solution)/shard_map/reduce_scatter | solution.py:49
  432.2 2.6 copy.139
  434.7 2.6 copy.136
  437.4 2.6 copy.145
  439.9 2.6 copy.144
  442.5 2.6 copy.147
  445.2 2.6 copy.146
  447.8 2.3 convolution_bitcast_fusion.9
  457.1 6.5 reduce-scatter.21.cloned.1.call-done
  471.3 29.7 %all-gather.27.cloned.1.call-done = bf16[1024,768]{1,0:T(8,128)(2,1)} async-done(((bf16[256,768]{1,0:T(8,128)(2,1)}), bf16[1024,768]{1,0:T(8,128)(2,1)}) %all-gather.27.cloned.1.call-update) | async-done | bytes 1572880 | tf_op jit(solution)/shard_map/all_gather | solution.py:44
  501.0 3.2 convolution_convert_fusion.13
  517.4 4.8 bitcast_convert_fusion.1
  522.7 4.7 fusion.27
  527.4 3.9 fusion.1
  531.3 7.1 all-gather.31.cloned.1.call-done
  538.4 3.2 convolution_convert_fusion.12
  554.2 4.7 bitcast_convert_fusion
  559.9 4.7 fusion.23
  564.7 3.9 fusion
  573.9 3.4 fusion.49
  583.6 15.0 %all_gather.68 = f32[4,3,2,2,768]{4,3,2,1,0:T(2,128)S(1)} all-gather(f32[1,3,2,2,768]{4,3,2,1,0:T(2,128)S(1)} %copy.142), channel_id=1, replica_groups=mesh['dp'=8,'tensor'=4] {'tensor'}, dimensions={0}, use_global_device_ids=true | all-gather | bytes 184320 | tf_op jit(solution)/shard_map/all_gather | solution.py:288
  599.6 23.7 %all-reduce = (f32[2,2,192]{2,0,1:T(2,128)S(1)}, f32[3,2,2,768]{3,1,2,0:T(2,128)S(1)}, f32[2,768]{1,0:T(2,128)}) all-reduce(f32[2,2,192]{2,0,1:T(2,128)S(1)} %maximum_add_fusion.1, f32[3,2,2,768]{3,1,2,0:T(2,128)S(1)} %copy.189, f32[2,768]{1,0:T(2,128)S(1)} %copy-done.108), channel_id=1, replica_groups=mesh['dp'=8,'tensor'=4] {'dp'}, use_global_device_ids=true, to_apply=%region_35.36 | all-reduce | flops 11520 | bytes 92160 | tf_op jit(solution)/shard_map/psum | solution.py:289
  629.2 101.5 %all-reduce.4.cloned.1.call-done = (bf16[2,3,768,192]{2,3,0,1:T(8,128)(2,1)}, bf16[2,192,768]{2,1,0:T(8,128)(2,1)}, bf16[2,768,768]{2,1,0:T(8,128)(2,1)}, bf16[2,768,768]{2,1,0:T(8,128)(2,1)}) async-done(((bf16[2,3,768,192]{2,3,0,1:T(8,128)(2,1)}, bf16[2,192,768]{2,1,0:T(8,128)(2,1)}, bf16[2,768,768]{2,1,0:T(8,128)(2,1)}, bf16[2,768,768]{2,1,0:T(8,128)(2,1)}), (bf16[2,3,768,192]{2,3,0,1:T(8,128)(2,1)}, ...) | async-done | bytes 7077904 | tf_op jit(solution)/shard_map/psum | solution.py:282
  730.7 2.3 convert_element_type.525
  733.0 3.6 copy.148
  736.5 2.5 convert_element_type.527
  739.1 2.5 convert_element_type.531
  (457 shorter events, 118.5 us)
Async XLA Ops:
  7.2 124.2 %copy-start = (bf16[2,768,768]{2,1,0:T(8,128)(2,1)S(1)}, bf16[2,768,768]{2,1,0:T(8,128)(2,1)}, u32[]{:S(2)}) copy-start(bf16[2,768,768]{2,1,0:T(8,128)(2,1)} %param.25) | copy-start | bytes 7077892
  7.2 6.8 copy-start.15
  7.2 42.7 %all-gather.21.cloned.1.call-start = ((), (), s32[]{:S(2)}) async-start(), calls=%async_computation.18 | async-start | bytes 1966080 | tf_op jit(solution)/shard_map/all_gather | solution.py:44
  9.5 78.5 %all-gather.17.cloned.1.call-start = ((), (), s32[]{:S(2)}) async-start(), calls=%async_computation.16 | async-start | bytes 1966080 | tf_op jit(solution)/shard_map/all_gather | solution.py:44
  10.2 115.0 %reduce-scatter.13.cloned.1.call-start = ((), (), s32[]{:S(2)}) async-start(), calls=%async_computation.10 | async-start | bytes 1966080 | tf_op jit(solution)/shard_map/reduce_scatter | solution.py:49
  11.8 7.9 %copy-start.100 = (s32[1024]{0:T(1024)}, s32[1024]{0:T(1024)S(1)}, u32[]{:S(2)}) copy-start(s32[1024]{0:T(1024)S(1)} %pad_clamp_fusion.1) | copy-start | bytes 12292
  13.9 52.8 %copy-start.73 = (f32[4,3,64]{2,1,0:T(4,128)}, f32[4,3,64]{2,1,0:T(4,128)S(1)}, u32[]{:S(2)}) copy-start(f32[4,3,64]{2,1,0:T(4,128)S(1)} %add.467) | copy-start | bytes 9220
  14.0 50.5 %copy-start.71 = (f32[4,3,64]{2,1,0:T(4,128)}, f32[4,3,64]{2,1,0:T(4,128)S(1)}, u32[]{:S(2)}) copy-start(f32[4,3,64]{2,1,0:T(4,128)S(1)} %add.475) | copy-start | bytes 9220
  56.8 7.7 %copy-start.33 = (bf16[4,2,128,3,64]{2,1,4,3,0:T(2,128)(2,1)}, bf16[4,2,128,3,64]{2,1,4,3,0:T(2,128)(2,1)S(1)}, u32[]{:S(2)}) copy-start(bf16[4,2,128,3,64]{2,1,4,3,0:T(2,128)(2,1)S(1)} %convert_element_type.452) | copy-start | bytes 1179652
  70.6 6.8 copy-start.48
  73.8 87.9 %reduce-scatter.9.cloned.1.call-start = ((), (), s32[]{:S(2)}) async-start(), calls=%async_computation.8 | async-start | bytes 1966080 | tf_op jit(solution)/shard_map/reduce_scatter | solution.py:49
  83.2 15.3 %copy-start.74 = (f32[4,3,64]{2,1,0:T(4,128)}, f32[4,3,64]{2,1,0:T(4,128)S(1)}, u32[]{:S(2)}) copy-start(f32[4,3,64]{2,1,0:T(4,128)S(1)} %add.447) | copy-start | bytes 9220
  101.4 7.2 copy-start.97
  101.8 6.8 copy-start.98
  101.8 6.9 copy-start.99
  102.1 23.2 %copy-start.50 = (bf16[4,256,192]{1,2,0:T(8,128)(2,1)}, bf16[4,256,192]{1,2,0:T(8,128)(2,1)S(1)}, u32[]{:S(2)}) copy-start(bf16[4,256,192]{1,2,0:T(8,128)(2,1)S(1)} %convert_element_type.437) | copy-start | bytes 1179652
  105.3 94.3 %all-gather.23.cloned.1.call-start = ((), (), s32[]{:S(2)}) async-start(), calls=%async_computation.19 | async-start | bytes 1966080 | tf_op jit(solution)/shard_map/all_gather | solution.py:44
  108.6 345.7 %copy-start.67 = (s32[256,1]{0,1:T(1,128)}, s32[256,1]{0,1:T(1,128)S(1)}, u32[]{:S(2)}) copy-start(s32[256,1]{0,1:T(1,128)S(1)} %compare_select_fusion.4) | copy-start | bytes 3076
  109.3 20.7 %copy-start.41 = (bf16[2,768]{1,0:T(2,128)(2,1)S(1)}, bf16[2,768]{1,0:T(2,128)(2,1)}, u32[]{:S(2)}) copy-start(bf16[2,768]{1,0:T(2,128)(2,1)} %param.24) | copy-start | bytes 9220
  126.7 338.7 %copy-start.77 = (f32[256]{0:T(256)}, f32[256]{0:T(256)S(1)}, u32[]{:S(2)}) copy-start(f32[256]{0:T(256)S(1)} %broadcast_multiply_fusion.9) | copy-start | bytes 3076
  127.0 7.6 %copy-start.86 = (f32[256]{0:T(256)}, f32[256]{0:T(256)S(1)}, u32[]{:S(2)}) copy-start(f32[256]{0:T(256)S(1)} %add_rsqrt_fusion.1) | copy-start | bytes 3076
  129.5 107.5 %all-gather.19.cloned.1.call-start = ((), (), s32[]{:S(2)}) async-start(), calls=%async_computation.17 | async-start | bytes 1966080 | tf_op jit(solution)/shard_map/all_gather | solution.py:44
  148.5 306.9 %copy-start.69 = (s32[256,1]{0,1:T(1,128)}, s32[256,1]{0,1:T(1,128)S(1)}, u32[]{:S(2)}) copy-start(s32[256,1]{0,1:T(1,128)S(1)} %compare_select_fusion.7) | copy-start | bytes 3076
  148.8 55.9 %copy-start.27 = (f32[256,768]{1,0:T(8,128)}, f32[256,768]{1,0:T(8,128)S(1)}, u32[]{:S(2)}) copy-start(f32[256,768]{1,0:T(8,128)S(1)} %fusion.133) | copy-start | bytes 2359300
  163.2 265.2 %copy-start.79 = (f32[256]{0:T(256)}, f32[256]{0:T(256)S(1)}, u32[]{:S(2)}) copy-start(f32[256]{0:T(256)S(1)} %broadcast_multiply_fusion.11) | copy-start | bytes 3076
  163.5 264.9 %copy-start.88 = (f32[256]{0:T(256)}, f32[256]{0:T(256)S(1)}, u32[]{:S(2)}) copy-start(f32[256]{0:T(256)S(1)} %add_rsqrt_fusion.3) | copy-start | bytes 3076
  164.9 109.3 %reduce-scatter.15.cloned.1.call-start = ((), (), s32[]{:S(2)}) async-start(), calls=%async_computation.11 | async-start | bytes 1966080 | tf_op jit(solution)/shard_map/reduce_scatter | solution.py:49
  199.6 12.4 %slice-start = ((s8[4718592]{0:T(1024)(128)(4,1)}), s8[4194304]{0:T(1024)(128)(4,1)S(1)}, s32[]{:S(2)}) async-start(s8[4718592]{0:T(1024)(128)(4,1)} %bitcast.330), calls=%async_computation.25 | async-start | bytes 8388608
  199.6 12.4 %slice-start.1 = ((s8[4718592]{0:T(1024)(128)(4,1)}), s8[524288]{0:T(1024)(128)(4,1)S(1)}, s32[]{:S(2)}) async-start(s8[4718592]{0:T(1024)(128)(4,1)} %bitcast.330), calls=%async_computation.26 | async-start | bytes 1048576
  204.7 9.9 %copy-start.39 = (f32[4,256,768]{2,1,0:T(8,128)}, f32[4,256,768]{2,1,0:T(8,128)S(1)}, u32[]{:S(2)}) copy-start(f32[4,256,768]{2,1,0:T(8,128)S(1)} %get-tuple-element.106) | copy-start | bytes 9437188
  214.6 96.2 %reduce-scatter.11.cloned.1.call-start = ((), (), s32[]{:S(2)}) async-start(), calls=%async_computation.9 | async-start | bytes 1966080 | tf_op jit(solution)/shard_map/reduce_scatter | solution.py:49
  236.9 12.4 %slice-start.2 = ((s8[4718592]{0:T(1024)(128)(4,1)}), s8[4194304]{0:T(1024)(128)(4,1)S(1)}, s32[]{:S(2)}) async-start(s8[4718592]{0:T(1024)(128)(4,1)} %bitcast.332), calls=%async_computation.27 | async-start | bytes 8388608
  236.9 12.4 %slice-start.3 = ((s8[4718592]{0:T(1024)(128)(4,1)}), s8[524288]{0:T(1024)(128)(4,1)S(1)}, s32[]{:S(2)}) async-start(s8[4718592]{0:T(1024)(128)(4,1)} %bitcast.332), calls=%async_computation.28 | async-start | bytes 1048576
  242.0 9.9 %copy-start.40 = (f32[4,256,768]{2,1,0:T(8,128)}, f32[4,256,768]{2,1,0:T(8,128)S(1)}, u32[]{:S(2)}) copy-start(f32[4,256,768]{2,1,0:T(8,128)S(1)} %get-tuple-element.115) | copy-start | bytes 9437188
  251.9 100.6 %all-gather.25.cloned.1.call-start = ((), (), s32[]{:S(2)}) async-start(), calls=%async_computation.20 | async-start | bytes 1966080 | tf_op jit(solution)/shard_map/all_gather | solution.py:44
  276.0 174.0 %copy-start.90 = (f32[256]{0:T(256)}, f32[256]{0:T(256)S(1)}, u32[]{:S(2)}) copy-start(f32[256]{0:T(256)S(1)} %add_rsqrt_fusion) | copy-start | bytes 3076
  312.5 139.7 %copy-start.81 = (f32[256]{0:T(256)}, f32[256]{0:T(256)S(1)}, u32[]{:S(2)}) copy-start(f32[256]{0:T(256)S(1)} %broadcast_multiply_fusion.10) | copy-start | bytes 3076
  312.8 139.4 %copy-start.91 = (f32[256]{0:T(256)}, f32[256]{0:T(256)S(1)}, u32[]{:S(2)}) copy-start(f32[256]{0:T(256)S(1)} %add_rsqrt_fusion.2) | copy-start | bytes 3076
  316.5 73.4 %all-gather.29.cloned.1.call-start = ((), (), s32[]{:S(2)}) async-start(), calls=%async_computation.22 | async-start | bytes 1966080 | tf_op jit(solution)/shard_map/all_gather | solution.py:44
  317.1 109.4 %reduce-scatter.17.cloned.1.call-start = ((), (), s32[]{:S(2)}) async-start(), calls=%async_computation.12 | async-start | bytes 1966080 | tf_op jit(solution)/shard_map/reduce_scatter | solution.py:49
  364.7 98.9 %reduce-scatter.21.cloned.1.call-start = ((), (), s32[]{:S(2)}) async-start(), calls=%async_computation.14 | async-start | bytes 1966080 | tf_op jit(solution)/shard_map/reduce_scatter | solution.py:49
  396.2 7.5 %copy-start.104 = (s32[4]{0:T(128)S(1)}, s32[4]{0:T(128)}, u32[]{:S(2)}) copy-start(s32[4]{0:T(128)} %copy-done.103) | copy-start | bytes 52
  401.8 99.2 %all-gather.27.cloned.1.call-start = ((), (), s32[]{:S(2)}) async-start(), calls=%async_computation.21 | async-start | bytes 1966080 | tf_op jit(solution)/shard_map/all_gather | solution.py:44
  429.7 108.7 %all-gather.31.cloned.1.call-start = ((), (), s32[]{:S(2)}) async-start(), calls=%async_computation.23 | async-start | bytes 1966080 | tf_op jit(solution)/shard_map/all_gather | solution.py:44
  447.8 6.6 copy-start.92
  447.8 7.6 %copy-start.19 = (f32[256,768]{1,0:T(8,128)S(1)}, f32[256,768]{1,0:T(8,128)}, u32[]{:S(2)}) copy-start(f32[256,768]{1,0:T(8,128)} %copy-done.18) | copy-start | bytes 2359300
  455.4 10.1 %copy-start.87 = (f32[256]{0:T(256)S(1)}, f32[256]{0:T(256)}, u32[]{:S(2)}) copy-start(f32[256]{0:T(256)} %copy-done.86) | copy-start | bytes 3076
  466.8 38.5 %copy-start.7 = (f32[4,2,3,128,128]{3,4,2,1,0:T(8,128)S(1)}, f32[4,2,3,128,128]{3,4,2,1,0:T(8,128)}, u32[]{:S(2)}) copy-start(f32[4,2,3,128,128]{3,4,2,1,0:T(8,128)} %copy-done.6) | copy-start | bytes 4718596
  466.8 38.5 %copy-start.55 = (f32[4,2,3,128]{3,2,1,0:T(4,128)S(1)}, f32[4,2,3,128]{3,2,1,0:T(4,128)}, u32[]{:S(2)}) copy-start(f32[4,2,3,128]{3,2,1,0:T(4,128)} %copy-done.54) | copy-start | bytes 36868
  466.8 159.0 %reduce-scatter.19.cloned.1.call-start = ((), (), s32[]{:S(2)}) async-start(), calls=%async_computation.13 | async-start | bytes 1966080 | tf_op jit(solution)/shard_map/reduce_scatter | solution.py:49
  514.7 7.4 copy-start.58
  522.2 104.7 %reduce-scatter.23.cloned.1.call-start = ((), (), s32[]{:S(2)}) async-start(), calls=%async_computation.15 | async-start | bytes 1966080 | tf_op jit(solution)/shard_map/reduce_scatter | solution.py:49
  531.3 11.3 %copy-start.5 = (f32[4,2,3,128,128]{3,4,2,1,0:T(8,128)S(1)}, f32[4,2,3,128,128]{3,4,2,1,0:T(8,128)}, u32[]{:S(2)}) copy-start(f32[4,2,3,128,128]{3,4,2,1,0:T(8,128)} %copy-done.4) | copy-start | bytes 4718596
  531.3 11.4 %copy-start.53 = (f32[4,2,3,128]{3,2,1,0:T(4,128)S(1)}, f32[4,2,3,128]{3,2,1,0:T(4,128)}, u32[]{:S(2)}) copy-start(f32[4,2,3,128]{3,2,1,0:T(4,128)} %copy-done.52) | copy-start | bytes 36868
  551.5 7.4 copy-start.63
  558.9 171.7 %all-reduce.4.cloned.1.call-start = ((), (), s32[]{:S(2)}) async-start(), calls=%async_computation.24 | async-start | bytes 14155776 | tf_op jit(solution)/shard_map/psum | solution.py:282
  581.5 17.2 %copy-start.82 = (f32[4,3,64]{2,1,0:T(4,128)S(1)}, f32[4,3,64]{2,1,0:T(4,128)}, u32[]{:S(2)}) copy-start(f32[4,3,64]{2,1,0:T(4,128)} %get-tuple-element.123) | copy-start | bytes 9220
  581.5 17.3 %copy-start.83 = (f32[4,3,64]{2,1,0:T(4,128)S(1)}, f32[4,3,64]{2,1,0:T(4,128)}, u32[]{:S(2)}) copy-start(f32[4,3,64]{2,1,0:T(4,128)} %get-tuple-element.125) | copy-start | bytes 9220
  581.5 17.4 %copy-start.84 = (f32[4,3,64]{2,1,0:T(4,128)S(1)}, f32[4,3,64]{2,1,0:T(4,128)}, u32[]{:S(2)}) copy-start(f32[4,3,64]{2,1,0:T(4,128)} %get-tuple-element.127) | copy-start | bytes 9220
  581.5 17.6 %copy-start.106 = (s32[4]{0:T(128)S(1)}, s32[4]{0:T(128)}, u32[]{:S(2)}) copy-start(s32[4]{0:T(128)} %copy-done.103) | copy-start | bytes 52
  581.5 17.8 %copy-start.111 = (s32[4]{0:T(128)S(1)}, s32[4]{0:T(128)}, u32[]{:S(2)}) copy-start(s32[4]{0:T(128)} %copy-done.109) | copy-start | bytes 52
  581.5 18.1 %copy-start.108 = (f32[2,768]{1,0:T(2,128)S(1)}, f32[2,768]{1,0:T(2,128)}, u32[]{:S(2)}) copy-start(f32[2,768]{1,0:T(2,128)} %convolution_add_fusion.8) | copy-start | bytes 18436
  581.5 44.2 %copy-start.24 = (f32[256,768]{1,0:T(8,128)S(1)}, f32[256,768]{1,0:T(8,128)}, u32[]{:S(2)}) copy-start(f32[256,768]{1,0:T(8,128)} %get-tuple-element.70) | copy-start | bytes 2359300
  582.5 44.4 %copy-start.26 = (f32[256,768]{1,0:T(8,128)S(1)}, f32[256,768]{1,0:T(8,128)}, u32[]{:S(2)}) copy-start(f32[256,768]{1,0:T(8,128)} %get-tuple-element.75) | copy-start | bytes 2359300
  (79 other events, 268.3 us)
Sparse Core Ops, SparseCore 0:
  10.2 39.7 all-gather.20
  52.1 35.8 all-gather.16
  90.9 34.2 reduce-scatter.12
  127.4 34.2 reduce-scatter.8
  163.7 35.8 all-gather.22
  201.0 35.8 all-gather.18
  239.8 34.2 reduce-scatter.14
  276.5 34.2 reduce-scatter.10
  316.7 35.8 all-gather.24
  354.0 35.8 all-gather.28
  392.2 34.2 reduce-scatter.16
  429.3 34.2 reduce-scatter.20
  465.2 35.8 all-gather.26
  502.5 35.8 all-gather.30
  540.5 34.2 reduce-scatter.18
  577.6 36.7 reduce-scatter.22
  619.1 111.5 all-reduce.3

commit v3 on v2

--- a/solution.py
+++ b/solution.py
@@ -63,6 +63,53 @@
     return jnp.einsum(
         "st,se->te", seg_hot, seg_totals, precision=lax.Precision.HIGHEST
     )
+
+
+def dp_perm(n, bit):
+    return [(j, j ^ bit) for j in range(n)]
+
+
+def dp_sum_low(parts):
+    shapes = [p.shape for p in parts]
+    flat = jnp.concatenate([p.reshape(-1) for p in parts])
+    n_dp = lax.axis_size("dp")
+    idx = lax.axis_index("dp")
+    steps = n_dp.bit_length() - 1
+    assert 1 << steps == n_dp and flat.shape[0] % n_dp == 0
+    cur = flat
+    for b in range(steps):
+        half = cur.shape[0] // 2
+        low_half, high_half = cur[:half], cur[half:]
+        upper = ((idx >> b) & 1) == 1
+        keep = jnp.where(upper, high_half, low_half)
+        send = jnp.where(upper, low_half, high_half)
+        got = lax.ppermute(send.astype(jnp.bfloat16), "dp", dp_perm(n_dp, 1 << b))
+        cur = keep + got.astype(jnp.float32)
+    cur = cur.astype(jnp.bfloat16)
+    for b in reversed(range(steps)):
+        got = lax.ppermute(cur, "dp", dp_perm(n_dp, 1 << b))
+        upper = ((idx >> b) & 1) == 1
+        cur = jnp.where(upper, jnp.concatenate([got, cur]), jnp.concatenate([cur, got]))
+    cur = cur.astype(jnp.float32)
+    outs, start = [], 0
+    for shape in shapes:
+        size = 1
+        for extent in shape:
+            size *= extent
+        outs.append(cur[start : start + size].reshape(shape))
+        start += size
+    return outs
+
+
+def exact_sum(values, axis):
+    n_ax = lax.axis_size(axis)
+    steps = n_ax.bit_length() - 1
+    assert 1 << steps == n_ax
+    for b in range(steps):
+        values = tuple(
+            v + g for v, g in zip(values, lax.ppermute(values, axis, dp_perm(n_ax, 1 << b)))
+        )
+    return values
 
 
 def stream(
@@ -279,14 +326,10 @@
         sum(parts[1:], parts[0]) for parts in zip(*grads)
     )
     small = sum(smalls[1:], smalls[0])
-    qkv_low, out_low, up_low, down_low = lax.psum(
-        tuple(v.astype(jnp.bfloat16) for v in (grad_qkv, grad_out_w, grad_up, grad_down)), "dp"
-    )
-    qkv_total, out_total, up_total, down_total = (
-        v.astype(jnp.float32) for v in (qkv_low, out_low, up_low, down_low)
-    )
-    small_grads = jnp.sum(lax.all_gather(small, "tensor"), axis=0)
-    qv_total, ubias_total, small_total = lax.psum((grad_qv, grad_ubias, small_grads), "dp")
+    up_total, down_total = dp_sum_low((grad_up, grad_down))
+    qkv_total, out_total = dp_sum_low((grad_qkv, grad_out_w))
+    (small_grads,) = exact_sum((small,), "tensor")
+    qv_total, ubias_total, small_total = exact_sum((grad_qv, grad_ubias, small_grads), "dp")
     return (
         layer_out,
         input_grad,

time: 759 us -> 756 us (level)
  waiting for transfers between devices: 404 us -> 313 us
  local copies, waits for them, and re-layouts: 96.7 us -> 154 us
  other arithmetic: 45.4 us -> 98.1 us
  blocking collectives: 38.7 us -> 0 us
  starting transfers between devices: 2.44 us -> 22.1 us
    psum x1 -> x0, waiting for transfers between devices: 101 us -> none  [local(): lax.psum(tuple((v.astype(jnp.bfloat16) for v in (grad_qkv, grad_out_w, gr...]
    ppermute x0 -> x23, waiting for transfers between devices: none -> 38.3 us  [the longest x11 25.4 us: exact_sum(): lax.ppermute(values, axis, dp_perm(n_ax, 1 << b))]
    psum x1 -> x0, blocking collectives: 23.7 us -> none  [local(): lax.psum((grad_qv, grad_ubias, small_grads), 'dp')]
    concatenate x0 -> x8, local copies, waits for them, and re-layouts: none -> 22.8 us  [dp_sum_low(): jnp.concatenate([got, cur])]
    ppermute x0 -> x23, starting transfers between devices: none -> 20.3 us  [the longest x11 8.23 us: exact_sum(): lax.ppermute(values, axis, dp_perm(n_ax, 1 << b))]
    select_n x0 -> x8, other arithmetic: none -> 19.5 us  [dp_sum_low(): jnp.where(upper, jnp.concatenate([got, cur]), jnp.concatenate([cur, got]))]
    add x0 -> x15, other arithmetic: none -> 15.6 us  [the longest x4 11.6 us: dp_sum_low(): cur = keep + got.astype(jnp.float32)]
    all_gather x1 -> x0, blocking collectives: 15 us -> none  [local(): small_grads = jnp.sum(lax.all_gather(small, 'tensor'), axis=0)]
  transfers between devices with their start and end apart: 17 -> 39, of which waited for: 15 -> 19; matrix products, arithmetic and copies ran while one was open for 35% -> 47% of each run, Pallas kernels for 0% -> 0%
where the time goes in v3:
time: 756 us; the launch traced here: 745 us
  waiting for transfers between devices  313 us (41%)
  local copies, waits for them, and re-layouts  154 us (20%)
  matrix products  140 us (19%)
  other arithmetic  98.1 us (13%)
  starting transfers between devices  22.1 us (3%)
  between operations  16.3 us (2%)
    all_gather x8, waiting for transfers between devices, gather_rows(): return lax.all_gather(local_rows, 'tensor', axis=0, tiled=False)  176 us
    reduce_scatter x8, waiting for transfers between devices, scatter_sum(): lax.psum_scatter(seg_parts.reshape(n_seg * seg_rows, width).astype(jnp.bf...  97.3 us
    ppermute x11, waiting for transfers between devices, exact_sum(): lax.ppermute(values, axis, dp_perm(n_ax, 1 << b))  25.4 us
    concatenate x8, local copies, waits for them, and re-layouts, dp_sum_low(): jnp.concatenate([got, cur])  22.8 us
    select_n x8, other arithmetic, dp_sum_low(): jnp.where(upper, jnp.concatenate([got, cur]), jnp.concatenate([cur, got]))  19.5 us
    unnamed x293, local copies, waits for them, and re-layouts  16.7 us
    dot_general x12, matrix products, pick(): return jnp.dot(kind_hot, kind_table.astype(jnp.float32), precision=highest)  16.6 us
    dot_general x12, matrix products, type_sum(): jnp.einsum('rt,rd->td', kind_hot, values, precision=lax.Precision.HIGHEST)  15.2 us
  transfers between devices with their start and end apart: 39, of which 19 were waited for; matrix products, arithmetic and copies ran while one was open for 47% of the time, Pallas kernels for 0%

profile of v3, /device:TPU:0, one launch (start us, length us, event | category | flops | bytes accessed | tf_op | source)
XLA Modules:
  0.0 744.7 jit_solution(16518775606192012519)
XLA Ops:
  15.7 4.0 gather_fusion.9
  19.8 30.1 %all-gather.21.cloned.1.call-done = bf16[1024,768]{1,0:T(8,128)(2,1)} async-done(((bf16[256,768]{1,0:T(8,128)(2,1)}), bf16[1024,768]{1,0:T(8,128)(2,1)}) %all-gather.21.cloned.1.call-update) | async-done | bytes 1572880 | tf_op jit(solution)/shard_map/all_gather | solution.py:44
  49.9 3.6 convolution_bitcast_fusion
  56.8 2.8 fusion.214
  70.7 3.2 convolution_convert_fusion.6
  77.4 4.1 gather_fusion.1
  83.2 4.8 all-gather.17.cloned.1.call-done
  88.0 3.6 convolution_bitcast_fusion.1
  103.8 3.1 convolution_convert_fusion.7
  113.1 12.1 %reduce-scatter.13.cloned.1.call-done = bf16[256,768]{1,0:T(8,128)(2,1)} async-done(((bf16[1024,768]{1,0:T(8,128)(2,1)}), bf16[256,768]{1,0:T(8,128)(2,1)}) %reduce-scatter.13.cloned.1.call-update) | async-done | bytes 393232 | tf_op jit(solution)/shard_map/reduce_scatter | solution.py:49
  132.9 3.2 gather_fusion.15
  136.1 3.2 gather_fusion.7
  139.3 5.0 gather_fusion.13
  144.2 3.1 gather_fusion.5
  152.3 9.4 %reduce-scatter.9.cloned.1.call-done = bf16[256,768]{1,0:T(8,128)(2,1)} async-done(((bf16[1024,768]{1,0:T(8,128)(2,1)}), bf16[256,768]{1,0:T(8,128)(2,1)}) %reduce-scatter.9.cloned.1.call-update) | async-done | bytes 393232 | tf_op jit(solution)/shard_map/reduce_scatter | solution.py:49
  164.9 34.7 %all-gather.23.cloned.1.call-done = bf16[1024,768]{1,0:T(8,128)(2,1)} async-done(((bf16[256,768]{1,0:T(8,128)(2,1)}), bf16[1024,768]{1,0:T(8,128)(2,1)}) %all-gather.23.cloned.1.call-update) | async-done | bytes 1572880 | tf_op jit(solution)/shard_map/all_gather | solution.py:44
  199.6 5.1 fusion.92
  204.7 7.3 fusion.7
  215.2 21.8 %all-gather.19.cloned.1.call-done = bf16[1024,768]{1,0:T(8,128)(2,1)} async-done(((bf16[256,768]{1,0:T(8,128)(2,1)}), bf16[1024,768]{1,0:T(8,128)(2,1)}) %all-gather.19.cloned.1.call-update) | async-done | bytes 1572880 | tf_op jit(solution)/shard_map/all_gather | solution.py:44
  236.9 5.1 fusion.91
  242.0 7.3 fusion.4
  253.2 21.0 %reduce-scatter.15.cloned.1.call-done = bf16[256,768]{1,0:T(8,128)(2,1)} async-done(((bf16[1024,768]{1,0:T(8,128)(2,1)}), bf16[256,768]{1,0:T(8,128)(2,1)}) %reduce-scatter.15.cloned.1.call-update) | async-done | bytes 393232 | tf_op jit(solution)/shard_map/reduce_scatter | solution.py:49
  276.9 33.9 %reduce-scatter.11.cloned.1.call-done = bf16[256,768]{1,0:T(8,128)(2,1)} async-done(((bf16[1024,768]{1,0:T(8,128)(2,1)}), bf16[256,768]{1,0:T(8,128)(2,1)}) %reduce-scatter.11.cloned.1.call-update) | async-done | bytes 393232 | tf_op jit(solution)/shard_map/reduce_scatter | solution.py:49
  322.4 2.6 copy.101
  330.2 22.4 %all-gather.25.cloned.1.call-done = bf16[1024,768]{1,0:T(8,128)(2,1)} async-done(((bf16[256,768]{1,0:T(8,128)(2,1)}), bf16[1024,768]{1,0:T(8,128)(2,1)}) %all-gather.25.cloned.1.call-update) | async-done | bytes 1572880 | tf_op jit(solution)/shard_map/all_gather | solution.py:44
  352.7 7.5 %convert_reduce_fusion.1 = (f32[4,768]{1,0:T(4,128)}, bf16[4,256,768]{2,1,0:T(8,128)(2,1)}) fusion(f32[4,256,768]{2,1,0:T(8,128)} %copy-done.51, f32[4,768]{1,0:T(4,128)} %copy-done.91, bf16[4,256,768]{2,1,0:T(8,128)(2,1)} %bitcast.336, bf16[4,768,768]{2,1,0:T(8,128)(2,1)} %gather_fusion.7), kind=kOutput, calls=%fused_computation.60 | convolution fusion | flops 1219752960 | bytes 11034624 | tf_op jit(solution)/shard_map/srd,sfd->srf/dot_general | solution.py:210
  360.1 29.9 %all-gather.29.cloned.1.call-done = bf16[1024,768]{1,0:T(8,128)(2,1)} async-done(((bf16[256,768]{1,0:T(8,128)(2,1)}), bf16[1024,768]{1,0:T(8,128)(2,1)}) %all-gather.29.cloned.1.call-update) | async-done | bytes 1572880 | tf_op jit(solution)/shard_map/all_gather | solution.py:44
  390.0 6.4 convert_reduce_fusion
  396.4 5.5 convolution_convert_fusion
  402.2 4.7 fusion.22
  406.9 2.7 fusion.26
  409.7 2.8 bitcast_add_fusion
  412.5 4.7 broadcast_select_fusion
  419.3 5.3 convert_element_type.554
  442.1 5.7 select_n.322
  447.8 5.4 convolution_convert_fusion.2
  453.3 4.6 convert_add_fusion
  457.9 3.7 select_convert_fusion.1
  467.0 20.9 %reduce-scatter.17.cloned.1.call-done = bf16[256,768]{1,0:T(8,128)(2,1)} async-done(((bf16[1024,768]{1,0:T(8,128)(2,1)}), bf16[256,768]{1,0:T(8,128)(2,1)}) %reduce-scatter.17.cloned.1.call-update) | async-done | bytes 393232 | tf_op jit(solution)/shard_map/reduce_scatter | solution.py:49
  496.5 3.7 collective-permute-done.9
  501.8 3.4 collective-permute-done.10
  508.8 3.0 convert_add_fusion.1
  518.3 10.4 %collective-permute-done.22 = f32[2,768]{1,0:T(2,128)S(1)} collective-permute-done((f32[2,768]{1,0:T(2,128)S(1)}, f32[2,768]{1,0:T(2,128)S(1)}, u32[]{:S(2)}, u32[]{:S(2)}) %collective-permute-start.22) | collective-permute-done | bytes 6176 | tf_op jit(solution)/shard_map/ppermute | solution.py:110
  533.2 2.7 concatenate.123
  537.4 5.7 all-gather.27.cloned.1.call-done
  550.8 3.2 convert_reduce_fusion.4
  553.9 27.1 %all-gather.31.cloned.1.call-done = bf16[1024,768]{1,0:T(8,128)(2,1)} async-done(((bf16[256,768]{1,0:T(8,128)(2,1)}), bf16[1024,768]{1,0:T(8,128)(2,1)}) %all-gather.31.cloned.1.call-update) | async-done | bytes 1572880 | tf_op jit(solution)/shard_map/all_gather | solution.py:44
  603.7 4.1 fusion.18
  610.0 3.4 copy.98
  613.5 4.5 reshape.749
  620.5 2.6 maximum_select_fusion.5
  633.4 2.9 maximum_select_fusion.6
  641.7 2.7 bitcast_convert_fusion.1
  644.5 7.9 %collective-permute-done.7 = f32[2,2,192]{2,0,1:T(2,128)} collective-permute-done((f32[2,2,192]{2,0,1:T(2,128)}, f32[2,2,192]{2,0,1:T(2,128)}, u32[]{:S(2)}, u32[]{:S(2)}) %collective-permute-start.7) | collective-permute-done | bytes 3104 | tf_op jit(solution)/shard_map/ppermute | solution.py:110
  655.1 9.4 %collective-permute-done.1 = bf16[294912]{0:T(1024)(128)(2,1)} collective-permute-done((bf16[294912]{0:T(1024)(128)(2,1)}, bf16[294912]{0:T(1024)(128)(2,1)}, u32[]{:S(2)}, u32[]{:S(2)}) %collective-permute-start.1) | collective-permute-done | bytes 589856 | tf_op jit(solution)/shard_map/ppermute | solution.py:86
  673.8 3.4 collective-permute-done.2
  680.2 5.3 maximum_select_fusion.1
  685.5 3.4 concatenate.121
  697.8 5.4 concatenate.120
  703.1 2.8 fusion
  708.2 4.4 fusion.212
  723.3 3.0 reshape.754
  726.4 5.8 copy.103
  732.1 3.4 concatenate.106
  (577 shorter events, 228.8 us)
Async XLA Ops:
  7.2 125.8 %copy-start = (bf16[2,768,768]{2,1,0:T(8,128)(2,1)S(1)}, bf16[2,768,768]{2,1,0:T(8,128)(2,1)}, u32[]{:S(2)}) copy-start(bf16[2,768,768]{2,1,0:T(8,128)(2,1)} %param.25) | copy-start | bytes 7077892
  7.2 42.7 %all-gather.21.cloned.1.call-start = ((), (), s32[]{:S(2)}) async-start(), calls=%async_computation.18 | async-start | bytes 1966080 | tf_op jit(solution)/shard_map/all_gather | solution.py:44
  9.5 78.5 %all-gather.17.cloned.1.call-start = ((), (), s32[]{:S(2)}) async-start(), calls=%async_computation.16 | async-start | bytes 1966080 | tf_op jit(solution)/shard_map/all_gather | solution.py:44
  10.2 115.0 %reduce-scatter.13.cloned.1.call-start = ((), (), s32[]{:S(2)}) async-start(), calls=%async_computation.10 | async-start | bytes 1966080 | tf_op jit(solution)/shard_map/reduce_scatter | solution.py:49
  13.9 52.8 %copy-start.86 = (f32[4,3,64]{2,1,0:T(4,128)}, f32[4,3,64]{2,1,0:T(4,128)S(1)}, u32[]{:S(2)}) copy-start(f32[4,3,64]{2,1,0:T(4,128)S(1)} %add.499) | copy-start | bytes 9220
  14.0 50.5 %copy-start.84 = (f32[4,3,64]{2,1,0:T(4,128)}, f32[4,3,64]{2,1,0:T(4,128)S(1)}, u32[]{:S(2)}) copy-start(f32[4,3,64]{2,1,0:T(4,128)S(1)} %add.507) | copy-start | bytes 9220
  73.9 87.8 %reduce-scatter.9.cloned.1.call-start = ((), (), s32[]{:S(2)}) async-start(), calls=%async_computation.8 | async-start | bytes 1966080 | tf_op jit(solution)/shard_map/reduce_scatter | solution.py:49
  83.2 15.4 %copy-start.87 = (f32[4,3,64]{2,1,0:T(4,128)}, f32[4,3,64]{2,1,0:T(4,128)S(1)}, u32[]{:S(2)}) copy-start(f32[4,3,64]{2,1,0:T(4,128)S(1)} %add.479) | copy-start | bytes 9220
  106.9 92.7 %all-gather.23.cloned.1.call-start = ((), (), s32[]{:S(2)}) async-start(), calls=%async_computation.19 | async-start | bytes 1966080 | tf_op jit(solution)/shard_map/all_gather | solution.py:44
  111.3 13.9 %copy-start.116 = (bf16[2,1,768]{2,1,0:T(2,128)(2,1)}, bf16[2,1,768]{2,1,0:T(2,128)(2,1)S(1)}, u32[]{:S(2)}) copy-start(bf16[2,1,768]{2,1,0:T(2,128)(2,1)S(1)} %get-tuple-element.78) | copy-start | bytes 9220
  111.9 18.4 %copy-start.53 = (bf16[2,768]{1,0:T(2,128)(2,1)S(1)}, bf16[2,768]{1,0:T(2,128)(2,1)}, u32[]{:S(2)}) copy-start(bf16[2,768]{1,0:T(2,128)(2,1)} %param.24) | copy-start | bytes 9220
  130.0 106.9 %all-gather.19.cloned.1.call-start = ((), (), s32[]{:S(2)}) async-start(), calls=%async_computation.17 | async-start | bytes 1966080 | tf_op jit(solution)/shard_map/all_gather | solution.py:44
  147.3 16.1 %copy-start.115 = (bf16[2,1,768]{2,1,0:T(2,128)(2,1)S(1)}, bf16[2,1,768]{2,1,0:T(2,128)(2,1)}, u32[]{:S(2)}) copy-start(bf16[2,1,768]{2,1,0:T(2,128)(2,1)} %get-tuple-element.75) | copy-start | bytes 9220
  148.1 56.6 %copy-start.90 = (f32[4,768]{1,0:T(4,128)}, f32[4,768]{1,0:T(4,128)S(1)}, u32[]{:S(2)}) copy-start(f32[4,768]{1,0:T(4,128)S(1)} %convert_element_type.486) | copy-start | bytes 36868
  148.8 93.3 %copy-start.91 = (f32[4,768]{1,0:T(4,128)}, f32[4,768]{1,0:T(4,128)S(1)}, u32[]{:S(2)}) copy-start(f32[4,768]{1,0:T(4,128)S(1)} %convert_element_type.467) | copy-start | bytes 36868
  152.3 52.4 %copy-start.33 = (f32[256,768]{1,0:T(8,128)}, f32[256,768]{1,0:T(8,128)S(1)}, u32[]{:S(2)}) copy-start(f32[256,768]{1,0:T(8,128)S(1)} %fusion.134) | copy-start | bytes 2359300
  163.5 41.2 %copy-start.102 = (f32[256]{0:T(256)}, f32[256]{0:T(256)S(1)}, u32[]{:S(2)}) copy-start(f32[256]{0:T(256)S(1)} %add_rsqrt_fusion.3) | copy-start | bytes 3076
  164.9 109.3 %reduce-scatter.15.cloned.1.call-start = ((), (), s32[]{:S(2)}) async-start(), calls=%async_computation.11 | async-start | bytes 1966080 | tf_op jit(solution)/shard_map/reduce_scatter | solution.py:49
  199.6 12.4 %slice-start = ((s8[4718592]{0:T(1024)(128)(4,1)}), s8[4194304]{0:T(1024)(128)(4,1)S(1)}, s32[]{:S(2)}) async-start(s8[4718592]{0:T(1024)(128)(4,1)} %bitcast.322), calls=%async_computation.24 | async-start | bytes 8388608
  199.6 12.4 %slice-start.1 = ((s8[4718592]{0:T(1024)(128)(4,1)}), s8[524288]{0:T(1024)(128)(4,1)S(1)}, s32[]{:S(2)}) async-start(s8[4718592]{0:T(1024)(128)(4,1)} %bitcast.322), calls=%async_computation.25 | async-start | bytes 1048576
  214.6 96.2 %reduce-scatter.11.cloned.1.call-start = ((), (), s32[]{:S(2)}) async-start(), calls=%async_computation.9 | async-start | bytes 1966080 | tf_op jit(solution)/shard_map/reduce_scatter | solution.py:49
  236.9 12.4 %slice-start.3 = ((s8[4718592]{0:T(1024)(128)(4,1)}), s8[524288]{0:T(1024)(128)(4,1)S(1)}, s32[]{:S(2)}) async-start(s8[4718592]{0:T(1024)(128)(4,1)} %bitcast.324), calls=%async_computation.27 | async-start | bytes 1048576
  249.4 24.8 %copy-start.52 = (f32[256,768]{1,0:T(8,128)S(1)}, f32[256,768]{1,0:T(8,128)}, u32[]{:S(2)}) copy-start(f32[256,768]{1,0:T(8,128)} %get-tuple-element.89) | copy-start | bytes 2359300
  251.9 100.7 %all-gather.25.cloned.1.call-start = ((), (), s32[]{:S(2)}) async-start(), calls=%async_computation.20 | async-start | bytes 1966080 | tf_op jit(solution)/shard_map/all_gather | solution.py:44
  316.6 73.4 %all-gather.29.cloned.1.call-start = ((), (), s32[]{:S(2)}) async-start(), calls=%async_computation.22 | async-start | bytes 1966080 | tf_op jit(solution)/shard_map/all_gather | solution.py:44
  317.2 146.1 %reduce-scatter.21.cloned.1.call-start = ((), (), s32[]{:S(2)}) async-start(), calls=%async_computation.14 | async-start | bytes 1966080 | tf_op jit(solution)/shard_map/reduce_scatter | solution.py:49
  401.9 86.0 %reduce-scatter.17.cloned.1.call-start = ((), (), s32[]{:S(2)}) async-start(), calls=%async_computation.12 | async-start | bytes 1966080 | tf_op jit(solution)/shard_map/reduce_scatter | solution.py:49
  424.6 28.7 %collective-permute-start.14 = (bf16[1179648]{0:T(1024)(128)(2,1)}, bf16[1179648]{0:T(1024)(128)(2,1)}, u32[]{:S(2)}, u32[]{:S(2)}) collective-permute-start(bf16[1179648]{0:T(1024)(128)(2,1)} %convert_element_type.554), channel_id=1, source_target_pairs={{0,4},{4,0},{8,12},{12,8},{16,20},{20,16},{24,28},{28,24},{1,5},{5... | collective-permute-start | bytes 7077896 | tf_op jit(solution)/shard_map/ppermute | solution.py:86
  453.3 89.9 %all-gather.27.cloned.1.call-start = ((), (), s32[]{:S(2)}) async-start(), calls=%async_computation.21 | async-start | bytes 1966080 | tf_op jit(solution)/shard_map/all_gather | solution.py:44
  461.7 47.1 %collective-permute-start.15 = (bf16[589824]{0:T(1024)(128)(2,1)}, bf16[589824]{0:T(1024)(128)(2,1)}, u32[]{:S(2)}, u32[]{:S(2)}) collective-permute-start(bf16[589824]{0:T(1024)(128)(2,1)} %select_convert_fusion.1), channel_id=1, source_target_pairs={{0,8},{4,12},{8,0},{12,4},{16,24},{20,28},{24,16},{28,20},{1,9},{5... | collective-permute-start | bytes 3538952 | tf_op jit(solution)/shard_map/ppermute | solution.py:86
  496.2 4.0 collective-permute-start.9
  500.3 4.9 collective-permute-start.10
  501.7 4.7 collective-permute-start.20
  505.3 2.8 collective-permute-start.11
  506.5 8.1 %collective-permute-start.21 = (f32[2,768]{1,0:T(2,128)S(1)}, f32[2,768]{1,0:T(2,128)}, u32[]{:S(2)}, u32[]{:S(2)}) collective-permute-start(f32[2,768]{1,0:T(2,128)S(1)} %add.557), channel_id=1, source_target_pairs={{0,8},{4,12},{8,0},{12,4},{16,24},{20,28},{24,16},{28,20},{1,9},{5... | collective-permute-start | bytes 18440 | tf_op jit(solution)/shard_map/ppermute | solution.py:110
  508.0 73.0 %all-gather.31.cloned.1.call-start = ((), (), s32[]{:S(2)}) async-start(), calls=%async_computation.23 | async-start | bytes 1966080 | tf_op jit(solution)/shard_map/all_gather | solution.py:44
  508.1 7.7 %collective-permute-start.12 = (f32[3,2,2,768]{3,1,2,0:T(2,128)S(1)}, f32[3,2,2,768]{3,1,2,0:T(2,128)S(1)}, u32[]{:S(2)}, u32[]{:S(2)}) collective-permute-start(f32[3,2,2,768]{3,1,2,0:T(2,128)S(1)} %add.548), channel_id=1, source_target_pairs={{0,8},{4,12},{8,0},{12,4},{16,24},{20,28},{24,16},{28,20},{1,9},{5... | collective-permute-start | bytes 110600 | tf_op jit(solution)/shard_map/ppermute | solution.py:110
  512.7 18.5 %collective-permute-start.16 = (bf16[294912]{0:T(1024)(128)(2,1)}, bf16[294912]{0:T(1024)(128)(2,1)}, u32[]{:S(2)}, u32[]{:S(2)}) collective-permute-start(bf16[294912]{0:T(1024)(128)(2,1)} %select_convert_fusion.3), channel_id=1, source_target_pairs={{0,16},{4,20},{8,24},{12,28},{16,0},{20,4},{24,8},{28,12},{1,17},{... | collective-permute-start | bytes 1769480 | tf_op jit(solution)/shard_map/ppermute | solution.py:86
  515.2 13.4 %collective-permute-start.22 = (f32[2,768]{1,0:T(2,128)S(1)}, f32[2,768]{1,0:T(2,128)S(1)}, u32[]{:S(2)}, u32[]{:S(2)}) collective-permute-start(f32[2,768]{1,0:T(2,128)S(1)} %add.558), channel_id=1, source_target_pairs={{0,16},{4,20},{8,24},{12,28},{16,0},{20,4},{24,8},{28,12},{1,17},{... | collective-permute-start | bytes 18440 | tf_op jit(solution)/shard_map/ppermute | solution.py:110
  515.8 13.5 %collective-permute-start.13 = (f32[3,2,2,768]{3,1,2,0:T(2,128)S(1)}, f32[3,2,2,768]{3,1,2,0:T(2,128)S(1)}, u32[]{:S(2)}, u32[]{:S(2)}) collective-permute-start(f32[3,2,2,768]{3,1,2,0:T(2,128)S(1)} %add.549), channel_id=1, source_target_pairs={{0,16},{4,20},{8,24},{12,28},{16,0},{20,4},{24,8},{28,12},{1,17},{... | collective-permute-start | bytes 110600 | tf_op jit(solution)/shard_map/ppermute | solution.py:110
  529.3 188.3 %reduce-scatter.19.cloned.1.call-start = ((), (), s32[]{:S(2)}) async-start(), calls=%async_computation.13 | async-start | bytes 1966080 | tf_op jit(solution)/shard_map/reduce_scatter | solution.py:49
  533.2 12.4 %copy-start.7 = (f32[4,2,3,128,128]{3,4,2,1,0:T(8,128)S(1)}, f32[4,2,3,128,128]{3,4,2,1,0:T(8,128)}, u32[]{:S(2)}) copy-start(f32[4,2,3,128,128]{3,4,2,1,0:T(8,128)} %copy-done.6) | copy-start | bytes 4718596
  533.2 12.4 %copy-start.37 = (f32[4,2,128,3,64]{2,1,4,3,0:T(2,128)S(1)}, f32[4,2,128,3,64]{2,1,4,3,0:T(2,128)}, u32[]{:S(2)}) copy-start(f32[4,2,128,3,64]{2,1,4,3,0:T(2,128)} %squeeze.47) | copy-start | bytes 2359300
  533.2 12.4 %copy-start.72 = (f32[4,2,3,128]{3,2,1,0:T(4,128)S(1)}, f32[4,2,3,128]{3,2,1,0:T(4,128)}, u32[]{:S(2)}) copy-start(f32[4,2,3,128]{3,2,1,0:T(4,128)} %copy-done.71) | copy-start | bytes 36868
  535.9 84.6 %collective-permute-start.17 = (bf16[294912]{0:T(1024)(128)(2,1)}, bf16[294912]{0:T(1024)(128)(2,1)}, u32[]{:S(2)}, u32[]{:S(2)}) collective-permute-start(bf16[294912]{0:T(1024)(128)(2,1)} %add_convert_fusion), channel_id=1, source_target_pairs={{0,16},{4,20},{8,24},{12,28},{16,0},{20,4},{24,8},{28,12},{1,17},{... | collective-permute-start | bytes 1769480 | tf_op jit(solution)/shard_map/ppermute | solution.py:90
  550.8 32.9 %copy-start.5 = (f32[4,2,3,128,128]{3,4,2,1,0:T(8,128)S(1)}, f32[4,2,3,128,128]{3,4,2,1,0:T(8,128)}, u32[]{:S(2)}) copy-start(f32[4,2,3,128,128]{3,4,2,1,0:T(8,128)} %copy-done.4) | copy-start | bytes 4718596
  550.8 32.9 %copy-start.70 = (f32[4,2,3,128]{3,2,1,0:T(4,128)S(1)}, f32[4,2,3,128]{3,2,1,0:T(4,128)}, u32[]{:S(2)}) copy-start(f32[4,2,3,128]{3,2,1,0:T(4,128)} %copy-done.69) | copy-start | bytes 36868
  620.5 17.1 %collective-permute-start = (bf16[589824]{0:T(1024)(128)(2,1)}, bf16[589824]{0:T(1024)(128)(2,1)}, u32[]{:S(2)}, u32[]{:S(2)}) collective-permute-start(bf16[589824]{0:T(1024)(128)(2,1)} %select_convert_fusion.2), channel_id=1, source_target_pairs={{0,4},{4,0},{8,12},{12,8},{16,20},{20,16},{24,28},{28,24},{1,5},{5... | collective-permute-start | bytes 3538952 | tf_op jit(solution)/shard_map/ppermute | solution.py:86
  623.1 57.0 %collective-permute-start.18 = (bf16[589824]{0:T(1024)(128)(2,1)}, bf16[589824]{0:T(1024)(128)(2,1)}, u32[]{:S(2)}, u32[]{:S(2)}) collective-permute-start(bf16[589824]{0:T(1024)(128)(2,1)} %maximum_select_fusion.5), channel_id=1, source_target_pairs={{0,8},{4,12},{8,0},{12,4},{16,24},{20,28},{24,16},{28,20},{1,9},{5... | collective-permute-start | bytes 3538952 | tf_op jit(solution)/shard_map/ppermute | solution.py:90
  633.1 3.2 collective-permute-start.6
  636.9 15.5 %collective-permute-start.7 = (f32[2,2,192]{2,0,1:T(2,128)}, f32[2,2,192]{2,0,1:T(2,128)}, u32[]{:S(2)}, u32[]{:S(2)}) collective-permute-start(f32[2,2,192]{2,0,1:T(2,128)} %fusion.277), channel_id=1, source_target_pairs={{0,8},{4,12},{8,0},{12,4},{16,24},{20,28},{24,16},{28,20},{1,9},{5... | collective-permute-start | bytes 9224 | tf_op jit(solution)/shard_map/ppermute | solution.py:110
  640.5 24.0 %collective-permute-start.1 = (bf16[294912]{0:T(1024)(128)(2,1)}, bf16[294912]{0:T(1024)(128)(2,1)}, u32[]{:S(2)}, u32[]{:S(2)}) collective-permute-start(bf16[294912]{0:T(1024)(128)(2,1)} %select_convert_fusion.4), channel_id=1, source_target_pairs={{0,8},{4,12},{8,0},{12,4},{16,24},{20,28},{24,16},{28,20},{1,9},{5... | collective-permute-start | bytes 1769480 | tf_op jit(solution)/shard_map/ppermute | solution.py:86
  644.4 25.4 %copy-start.11 = (bf16[4,3,768,192]{2,3,1,0:T(8,128)(2,1)S(1)}, bf16[4,3,768,192]{2,3,1,0:T(8,128)(2,1)}, u32[]{:S(2)}) copy-start(bf16[4,3,768,192]{2,3,1,0:T(8,128)(2,1)} %gather_fusion.9) | copy-start | bytes 10616836
  644.4 74.2 %reduce-scatter.23.cloned.1.call-start = ((), (), s32[]{:S(2)}) async-start(), calls=%async_computation.15 | async-start | bytes 1966080 | tf_op jit(solution)/shard_map/reduce_scatter | solution.py:49
  644.5 25.3 %copy-start.75 = (bf16[1,4,256,192]{2,3,1,0:T(8,128)(2,1)S(1)}, bf16[1,4,256,192]{2,3,1,0:T(8,128)(2,1)}, u32[]{:S(2)}) copy-start(bf16[1,4,256,192]{2,3,1,0:T(8,128)(2,1)} %convert_element_type.534) | copy-start | bytes 1179652
  644.5 25.3 %copy-start.76 = (bf16[1,4,256,192]{2,3,1,0:T(8,128)(2,1)S(1)}, bf16[1,4,256,192]{2,3,1,0:T(8,128)(2,1)}, u32[]{:S(2)}) copy-start(bf16[1,4,256,192]{2,3,1,0:T(8,128)(2,1)} %convert_element_type.528) | copy-start | bytes 1179652
  644.5 25.3 %copy-start.77 = (bf16[1,4,256,192]{2,3,1,0:T(8,128)(2,1)S(1)}, bf16[1,4,256,192]{2,3,1,0:T(8,128)(2,1)}, u32[]{:S(2)}) copy-start(bf16[1,4,256,192]{2,3,1,0:T(8,128)(2,1)} %convert_element_type.531) | copy-start | bytes 1179652
  653.7 18.8 %collective-permute-start.8 = (f32[2,2,192]{2,0,1:T(2,128)}, f32[2,2,192]{2,0,1:T(2,128)S(1)}, u32[]{:S(2)}, u32[]{:S(2)}) collective-permute-start(f32[2,2,192]{2,0,1:T(2,128)} %fusion.279), channel_id=1, source_target_pairs={{0,16},{4,20},{8,24},{12,28},{16,0},{20,4},{24,8},{28,12},{1,17},{... | collective-permute-start | bytes 9224 | tf_op jit(solution)/shard_map/ppermute | solution.py:110
  668.3 8.9 %collective-permute-start.2 = (bf16[147456]{0:T(1024)(128)(2,1)}, bf16[147456]{0:T(1024)(128)(2,1)}, u32[]{:S(2)}, u32[]{:S(2)}) collective-permute-start(bf16[147456]{0:T(1024)(128)(2,1)} %select_convert_fusion.5), channel_id=1, source_target_pairs={{0,16},{4,20},{8,24},{12,28},{16,0},{20,4},{24,8},{28,12},{1,17},{... | collective-permute-start | bytes 884744 | tf_op jit(solution)/shard_map/ppermute | solution.py:86
  678.6 12.7 %copy-start.40 = (bf16[1,768,768]{2,1,0:T(8,128)(2,1)S(1)}, bf16[1,768,768]{2,1,0:T(8,128)(2,1)}, u32[]{:S(2)}) copy-start(bf16[1,768,768]{2,1,0:T(8,128)(2,1)} %maximum_select_fusion.6) | copy-start | bytes 3538948
  678.6 10.2 %collective-permute-start.3 = (bf16[147456]{0:T(1024)(128)(2,1)S(1)}, bf16[147456]{0:T(1024)(128)(2,1)S(1)}, u32[]{:S(2)}, u32[]{:S(2)}) collective-permute-start(bf16[147456]{0:T(1024)(128)(2,1)S(1)} %add_convert_fusion.1), channel_id=1, source_target_pairs={{0,16},{4,20},{8,24},{12,28},{16,0},{20,4},{24,8},{28,12},{1,17},{... | collective-permute-start | bytes 884744 | tf_op jit(solution)/shard_map/ppermute | solution.py:90
  685.5 12.3 %collective-permute-start.19 = (bf16[1179648]{0:T(1024)(128)(2,1)}, bf16[1179648]{0:T(1024)(128)(2,1)}, u32[]{:S(2)}, u32[]{:S(2)}) collective-permute-start(bf16[1179648]{0:T(1024)(128)(2,1)} %maximum_select_fusion.1), channel_id=1, source_target_pairs={{0,4},{4,0},{8,12},{12,8},{16,20},{20,16},{24,28},{28,24},{1,5},{5... | collective-permute-start | bytes 7077896 | tf_op jit(solution)/shard_map/ppermute | solution.py:90
  689.8 16.1 %collective-permute-start.4 = (bf16[294912]{0:T(1024)(128)(2,1)}, bf16[294912]{0:T(1024)(128)(2,1)}, u32[]{:S(2)}, u32[]{:S(2)}) collective-permute-start(bf16[294912]{0:T(1024)(128)(2,1)} %maximum_select_fusion.7), channel_id=1, source_target_pairs={{0,8},{4,12},{8,0},{12,4},{16,24},{20,28},{24,16},{28,20},{1,9},{5... | collective-permute-start | bytes 1769480 | tf_op jit(solution)/shard_map/ppermute | solution.py:90
  707.9 13.0 %collective-permute-start.5 = (bf16[589824]{0:T(1024)(128)(2,1)S(1)}, bf16[589824]{0:T(1024)(128)(2,1)}, u32[]{:S(2)}, u32[]{:S(2)}) collective-permute-start(bf16[589824]{0:T(1024)(128)(2,1)S(1)} %maximum_select_fusion.3), channel_id=1, source_target_pairs={{0,4},{4,0},{8,12},{12,8},{16,20},{20,16},{24,28},{28,24},{1,5},{5... | collective-permute-start | bytes 3538952 | tf_op jit(solution)/shard_map/ppermute | solution.py:90
  (119 other events, 519.0 us)
Sparse Core Ops, SparseCore 0:
  10.2 39.7 all-gather.20
  52.1 35.8 all-gather.16
  90.9 34.2 reduce-scatter.12
  127.4 34.2 reduce-scatter.8
  163.7 35.8 all-gather.22
  201.0 35.8 all-gather.18
  239.8 34.2 reduce-scatter.14
  276.5 34.2 reduce-scatter.10
  316.8 35.8 all-gather.24
  354.1 35.8 all-gather.28
  402.0 34.2 reduce-scatter.20
  453.4 34.4 reduce-scatter.16
  508.1 34.9 all-gather.26
  545.1 35.8 all-gather.30
  644.5 33.6 reduce-scatter.18
  681.0 34.2 reduce-scatter.22

commit v4 on v3

--- a/solution.py
+++ b/solution.py
@@ -71,34 +71,26 @@
 
 def dp_sum_low(parts):
     shapes = [p.shape for p in parts]
-    flat = jnp.concatenate([p.reshape(-1) for p in parts])
     n_dp = lax.axis_size("dp")
     idx = lax.axis_index("dp")
     steps = n_dp.bit_length() - 1
-    assert 1 << steps == n_dp and flat.shape[0] % n_dp == 0
-    cur = flat
+    cur = [p.reshape(-1, p.shape[-1]) for p in parts]
+    assert 1 << steps == n_dp and all(c.shape[0] % n_dp == 0 for c in cur)
     for b in range(steps):
-        half = cur.shape[0] // 2
-        low_half, high_half = cur[:half], cur[half:]
         upper = ((idx >> b) & 1) == 1
-        keep = jnp.where(upper, high_half, low_half)
-        send = jnp.where(upper, low_half, high_half)
-        got = lax.ppermute(send.astype(jnp.bfloat16), "dp", dp_perm(n_dp, 1 << b))
-        cur = keep + got.astype(jnp.float32)
-    cur = cur.astype(jnp.bfloat16)
+        halves = [(c[: c.shape[0] // 2], c[c.shape[0] // 2 :]) for c in cur]
+        sends = tuple(jnp.where(upper, lo, hi).astype(jnp.bfloat16) for lo, hi in halves)
+        gots = lax.ppermute(sends, "dp", dp_perm(n_dp, 1 << b))
+        cur = [jnp.where(upper, hi, lo) + g.astype(jnp.float32) for (lo, hi), g in zip(halves, gots)]
+    cur = [c.astype(jnp.bfloat16) for c in cur]
     for b in reversed(range(steps)):
-        got = lax.ppermute(cur, "dp", dp_perm(n_dp, 1 << b))
         upper = ((idx >> b) & 1) == 1
-        cur = jnp.where(upper, jnp.concatenate([got, cur]), jnp.concatenate([cur, got]))
-    cur = cur.astype(jnp.float32)
-    outs, start = [], 0
-    for shape in shapes:
-        size = 1
-        for extent in shape:
-            size *= extent
-        outs.append(cur[start : start + size].reshape(shape))
-        start += size
-    return outs
+        gots = lax.ppermute(tuple(cur), "dp", dp_perm(n_dp, 1 << b))
+        cur = [
+            jnp.where(upper, jnp.concatenate([g, c]), jnp.concatenate([c, g]))
+            for c, g in zip(cur, gots)
+        ]
+    return [c.astype(jnp.float32).reshape(shape) for c, shape in zip(cur, shapes)]
 
 
 def exact_sum(values, axis):

time: 756 us -> 691 us (0.914)
  local copies, waits for them, and re-layouts: 154 us -> 114 us
  waiting for transfers between devices: 313 us -> 296 us
  other arithmetic: 98.1 us -> 86.9 us
  starting transfers between devices: 22.1 us -> 31.6 us
    ppermute x12 -> x24, waiting for transfers between devices: 12.9 us -> 59.9 us  [the longest x12 43.1 us: dp_sum_low(): gots = lax.ppermute(sends, 'dp', dp_perm(n_dp, 1 << b))]
    all_gather x8, waiting for transfers between devices: 176 us -> 150 us  [gather_rows(): return lax.all_gather(local_rows, 'tensor', axis=0, tiled=False)]
    reduce_scatter x8, waiting for transfers between devices: 97.3 us -> 73.2 us  [scatter_sum(): lax.psum_scatter(seg_parts.reshape(n_seg * seg_rows, width).astype(jnp.bf...]
    concatenate x8 -> x0, local copies, waits for them, and re-layouts: 22.8 us -> none  [dp_sum_low(): jnp.concatenate([got, cur])]
    ppermute x11, waiting for transfers between devices: 25.4 us -> 11.6 us  [exact_sum(): lax.ppermute(values, axis, dp_perm(n_ax, 1 << b))]
    ppermute x12 -> x24, starting transfers between devices: 12 us -> 20.9 us  [the longest x12 10.8 us: dp_sum_low(): gots = lax.ppermute(tuple(cur), 'dp', dp_perm(n_dp, 1 << b))]
    reshape x3 -> x0, local copies, waits for them, and re-layouts: 8.61 us -> none  [the longest x2 5.57 us: dp_sum_low(): flat = jnp.concatenate([p.reshape(-1) for p in parts])]
    unnamed x293 -> x295, local copies, waits for them, and re-layouts: 16.7 us -> 23.5 us
  transfers between devices with their start and end apart: 39 -> 51, of which waited for: 19 -> 25; matrix products, arithmetic and copies ran while one was open for 47% -> 44% of each run, Pallas kernels for 0% -> 0%
where the time goes in v4:
time: 691 us; the launch traced here: 680 us
  waiting for transfers between devices  296 us (43%)
  matrix products  135 us (20%)
  local copies, waits for them, and re-layouts  114 us (16%)
  other arithmetic  86.9 us (13%)
  starting transfers between devices  31.6 us (5%)
  between operations  16.5 us (2%)
    all_gather x8, waiting for transfers between devices, gather_rows(): return lax.all_gather(local_rows, 'tensor', axis=0, tiled=False)  150 us
    reduce_scatter x8, waiting for transfers between devices, scatter_sum(): lax.psum_scatter(seg_parts.reshape(n_seg * seg_rows, width).astype(jnp.bf...  73.2 us
    ppermute x12, waiting for transfers between devices, dp_sum_low(): gots = lax.ppermute(sends, 'dp', dp_perm(n_dp, 1 << b))  43.1 us
    unnamed x295, local copies, waits for them, and re-layouts  23.5 us
    dot_general x12, matrix products, pick(): return jnp.dot(kind_hot, kind_table.astype(jnp.float32), precision=highest)  17.6 us
    ppermute x12, waiting for transfers between devices, dp_sum_low(): gots = lax.ppermute(tuple(cur), 'dp', dp_perm(n_dp, 1 << b))  16.8 us
    dot_general x12, matrix products, type_sum(): jnp.einsum('rt,rd->td', kind_hot, values, precision=lax.Precision.HIGHEST)  16.1 us
    select_n x11, other arithmetic, dp_sum_low(): jnp.where(upper, jnp.concatenate([g, c]), jnp.concatenate([c, g]))  15.4 us
  transfers between devices with their start and end apart: 51, of which 25 were waited for; matrix products, arithmetic and copies ran while one was open for 44% of the time, Pallas kernels for 0%

profile of v4, /device:TPU:0, one launch (start us, length us, event | category | flops | bytes accessed | tf_op | source)
XLA Modules:
  0.0 680.2 jit_solution(316841999800847631)
XLA Ops:
  16.2 4.0 gather_fusion.9
  20.3 29.6 %all-gather.21.cloned.1.call-done = bf16[1024,768]{1,0:T(8,128)(2,1)} async-done(((bf16[256,768]{1,0:T(8,128)(2,1)}), bf16[1024,768]{1,0:T(8,128)(2,1)}) %all-gather.21.cloned.1.call-update) | async-done | bytes 1572880 | tf_op jit(solution)/shard_map/all_gather | solution.py:44
  49.9 3.6 convolution_bitcast_fusion
  56.8 2.8 fusion.212
  70.5 3.2 convolution_convert_fusion.6
  77.1 4.1 gather_fusion.1
  82.4 5.6 all-gather.17.cloned.1.call-done
  88.0 3.6 convolution_bitcast_fusion.1
  93.2 2.8 fusion.211
  105.6 3.1 convolution_convert_fusion.7
  115.1 10.2 %reduce-scatter.13.cloned.1.call-done = bf16[256,768]{1,0:T(8,128)(2,1)} async-done(((bf16[1024,768]{1,0:T(8,128)(2,1)}), bf16[256,768]{1,0:T(8,128)(2,1)}) %reduce-scatter.13.cloned.1.call-update) | async-done | bytes 393232 | tf_op jit(solution)/shard_map/reduce_scatter | solution.py:49
  132.9 3.2 gather_fusion.15
  136.1 3.2 gather_fusion.7
  139.3 5.0 gather_fusion.13
  144.3 3.2 gather_fusion.5
  153.0 8.7 %reduce-scatter.9.cloned.1.call-done = bf16[256,768]{1,0:T(8,128)(2,1)} async-done(((bf16[1024,768]{1,0:T(8,128)(2,1)}), bf16[256,768]{1,0:T(8,128)(2,1)}) %reduce-scatter.9.cloned.1.call-update) | async-done | bytes 393232 | tf_op jit(solution)/shard_map/reduce_scatter | solution.py:49
  164.9 34.7 %all-gather.23.cloned.1.call-done = bf16[1024,768]{1,0:T(8,128)(2,1)} async-done(((bf16[256,768]{1,0:T(8,128)(2,1)}), bf16[1024,768]{1,0:T(8,128)(2,1)}) %all-gather.23.cloned.1.call-update) | async-done | bytes 1572880 | tf_op jit(solution)/shard_map/all_gather | solution.py:44
  199.6 5.1 fusion.92
  204.7 8.0 %fusion.6 = bf16[4,256,768]{2,1,0:T(8,128)(2,1)S(1)} fusion(f32[4,256,768]{2,1,0:T(8,128)S(1)} %get-tuple-element.88, f32[4,768]{1,0:T(4,128)} %copy-done.84, u8[256,768]{1,0:T(8,128)(4,1)S(1)} %get-tuple-element.36, u8[256,768]{1,0:T(8,128)(4,1)S(1)} %get-tuple-element.35), kind=kLoop, calls=%fused_computation.29 | loop fusion | flops 55836672 | bytes 5124096 | tf_op jit(solution)/shard_map/convert_element_type | solution.py:187
  215.9 21.0 %all-gather.19.cloned.1.call-done = bf16[1024,768]{1,0:T(8,128)(2,1)} async-done(((bf16[256,768]{1,0:T(8,128)(2,1)}), bf16[1024,768]{1,0:T(8,128)(2,1)}) %all-gather.19.cloned.1.call-update) | async-done | bytes 1572880 | tf_op jit(solution)/shard_map/all_gather | solution.py:44
  236.9 5.1 fusion.91
  242.1 7.3 %fusion.3 = bf16[4,256,768]{2,1,0:T(8,128)(2,1)S(1)} fusion(f32[4,256,768]{2,1,0:T(8,128)S(1)} %get-tuple-element.97, f32[4,768]{1,0:T(4,128)S(1)} %copy-done.86, u8[256,768]{1,0:T(8,128)(4,1)S(1)} %get-tuple-element.34, u8[256,768]{1,0:T(8,128)(4,1)S(1)} %get-tuple-element.33), kind=kLoop, calls=%fused_computation.26 | loop fusion | flops 55836672 | bytes 5124096 | tf_op jit(solution)/shard_map/convert_element_type | solution.py:187
  249.4 2.6 convolution_convert_fusion.5
  254.0 20.2 %reduce-scatter.15.cloned.1.call-done = bf16[256,768]{1,0:T(8,128)(2,1)} async-done(((bf16[1024,768]{1,0:T(8,128)(2,1)}), bf16[256,768]{1,0:T(8,128)(2,1)}) %reduce-scatter.15.cloned.1.call-update) | async-done | bytes 393232 | tf_op jit(solution)/shard_map/reduce_scatter | solution.py:49
  276.6 34.2 %reduce-scatter.11.cloned.1.call-done = bf16[256,768]{1,0:T(8,128)(2,1)} async-done(((bf16[1024,768]{1,0:T(8,128)(2,1)}), bf16[256,768]{1,0:T(8,128)(2,1)}) %reduce-scatter.11.cloned.1.call-update) | async-done | bytes 393232 | tf_op jit(solution)/shard_map/reduce_scatter | solution.py:49
  323.6 2.7 copy.95
  326.4 2.6 copy.92
  329.0 2.6 copy.101
  331.6 2.6 copy.100
  334.2 2.6 copy.103
  336.8 2.6 copy.102
  347.1 5.7 all-gather.25.cloned.1.call-done
  352.8 6.9 %convert_reduce_fusion.1 = (f32[4,768]{1,0:T(4,128)S(1)}, bf16[4,256,768]{2,1,0:T(8,128)(2,1)}) fusion(f32[4,256,768]{2,1,0:T(8,128)} %copy-done.48, f32[4,768]{1,0:T(4,128)} %convert_element_type.539, bf16[4,256,768]{2,1,0:T(8,128)(2,1)} %bitcast.424, bf16[4,768,768]{2,1,0:T(8,128)(2,1)} %gather_fusion.7), kind=kOutput, calls=%fused_computation.60 | convolution fusion | flops 1219752960 | bytes 11034624 | tf_op jit(solution)/shard_map/srd,sfd->srf/dot_general | solution.py:202
  359.7 30.4 %all-gather.29.cloned.1.call-done = bf16[1024,768]{1,0:T(8,128)(2,1)} async-done(((bf16[256,768]{1,0:T(8,128)(2,1)}), bf16[1024,768]{1,0:T(8,128)(2,1)}) %all-gather.29.cloned.1.call-update) | async-done | bytes 1572880 | tf_op jit(solution)/shard_map/all_gather | solution.py:44
  390.1 5.8 convert_reduce_fusion
  395.9 5.5 convolution_convert_fusion
  401.7 4.7 fusion.25
  406.4 2.7 bitcast_add_fusion.1
  413.2 2.7 fusion.21
  415.9 2.8 bitcast_add_fusion
  422.2 2.6 convolution_convert_fusion.2
  425.4 3.3 bitcast_add_fusion.4
  433.0 12.0 %collective-permute-done.21 = bf16[384,768]{1,0:T(8,128)(2,1)S(1)} collective-permute-done((bf16[384,768]{1,0:T(8,128)(2,1)S(1)}, bf16[384,768]{1,0:T(8,128)(2,1)S(1)}, u32[]{:S(2)}, u32[]{:S(2)}) %collective-permute-start.21) | collective-permute-done | bytes 589856 | tf_op jit(solution)/shard_map/ppermute | solution.py:83
  446.8 10.4 %collective-permute-done.30 = bf16[384,768]{1,0:T(8,128)(2,1)S(1)} collective-permute-done((bf16[384,768]{1,0:T(8,128)(2,1)S(1)}, bf16[384,768]{1,0:T(8,128)(2,1)S(1)}, u32[]{:S(2)}, u32[]{:S(2)}) %collective-permute-start.30) | collective-permute-done | bytes 589856 | tf_op jit(solution)/shard_map/ppermute | solution.py:83
  462.8 4.6 collective-permute-done.31
  469.7 4.0 collective-permute-done.23
  492.9 3.1 maximum_select_fusion.3
  496.0 2.9 collective-permute-done.15
  501.4 5.1 collective-permute-done.16
  512.2 2.9 collective-permute-done.18
  516.6 2.7 maximum_select_fusion.4
  521.2 3.7 maximum_select_fusion
  534.7 22.8 %all-gather.31.cloned.1.call-done = bf16[1024,768]{1,0:T(8,128)(2,1)} async-done(((bf16[256,768]{1,0:T(8,128)(2,1)}), bf16[1024,768]{1,0:T(8,128)(2,1)}) %all-gather.31.cloned.1.call-update) | async-done | bytes 1572880 | tf_op jit(solution)/shard_map/all_gather | solution.py:44
  570.1 4.8 bitcast_convert_fusion.1
  581.7 3.5 fusion.17
  595.7 2.7 bitcast_convert_fusion
  602.8 10.8 %collective-permute-done.1 = bf16[1152,192]{0,1:T(8,128)(2,1)S(1)} collective-permute-done((bf16[1152,192]{0,1:T(8,128)(2,1)S(1)}, bf16[1152,192]{0,1:T(8,128)(2,1)S(1)}, u32[]{:S(2)}, u32[]{:S(2)}) %collective-permute-start.1) | collective-permute-done | bytes 442400 | tf_op jit(solution)/shard_map/ppermute | solution.py:83
  616.1 4.6 collective-permute-done.2
  623.0 4.3 collective-permute-done.3
  631.4 5.2 collective-permute-done.4
  640.1 3.2 collective-permute-done.13
  643.4 2.8 maximum_select_fusion.1
  655.5 6.6 reshape.743
  662.2 5.4 copy.104
  (610 shorter events, 212.7 us)
Async XLA Ops:
  7.2 125.8 %copy-start = (bf16[2,768,768]{2,1,0:T(8,128)(2,1)S(1)}, bf16[2,768,768]{2,1,0:T(8,128)(2,1)}, u32[]{:S(2)}) copy-start(bf16[2,768,768]{2,1,0:T(8,128)(2,1)} %param.25) | copy-start | bytes 7077892
  7.2 42.7 %all-gather.21.cloned.1.call-start = ((), (), s32[]{:S(2)}) async-start(), calls=%async_computation.18 | async-start | bytes 1966080 | tf_op jit(solution)/shard_map/all_gather | solution.py:44
  9.5 78.5 %all-gather.17.cloned.1.call-start = ((), (), s32[]{:S(2)}) async-start(), calls=%async_computation.16 | async-start | bytes 1966080 | tf_op jit(solution)/shard_map/all_gather | solution.py:44
  10.2 115.0 %reduce-scatter.13.cloned.1.call-start = ((), (), s32[]{:S(2)}) async-start(), calls=%async_computation.10 | async-start | bytes 1966080 | tf_op jit(solution)/shard_map/reduce_scatter | solution.py:49
  14.4 52.4 %copy-start.80 = (f32[4,3,64]{2,1,0:T(4,128)}, f32[4,3,64]{2,1,0:T(4,128)S(1)}, u32[]{:S(2)}) copy-start(f32[4,3,64]{2,1,0:T(4,128)S(1)} %add.517) | copy-start | bytes 9220
  14.5 50.0 %copy-start.78 = (f32[4,3,64]{2,1,0:T(4,128)}, f32[4,3,64]{2,1,0:T(4,128)S(1)}, u32[]{:S(2)}) copy-start(f32[4,3,64]{2,1,0:T(4,128)S(1)} %add.525) | copy-start | bytes 9220
  73.7 88.0 %reduce-scatter.9.cloned.1.call-start = ((), (), s32[]{:S(2)}) async-start(), calls=%async_computation.8 | async-start | bytes 1966080 | tf_op jit(solution)/shard_map/reduce_scatter | solution.py:49
  82.2 20.8 %copy-start.83 = (f32[4,3,64]{2,1,0:T(4,128)}, f32[4,3,64]{2,1,0:T(4,128)S(1)}, u32[]{:S(2)}) copy-start(f32[4,3,64]{2,1,0:T(4,128)S(1)} %add.490) | copy-start | bytes 9220
  108.8 90.8 %all-gather.23.cloned.1.call-start = ((), (), s32[]{:S(2)}) async-start(), calls=%async_computation.19 | async-start | bytes 1966080 | tf_op jit(solution)/shard_map/all_gather | solution.py:44
  130.0 106.9 %all-gather.19.cloned.1.call-start = ((), (), s32[]{:S(2)}) async-start(), calls=%async_computation.17 | async-start | bytes 1966080 | tf_op jit(solution)/shard_map/all_gather | solution.py:44
  148.2 51.4 %copy-start.84 = (f32[4,768]{1,0:T(4,128)}, f32[4,768]{1,0:T(4,128)S(1)}, u32[]{:S(2)}) copy-start(f32[4,768]{1,0:T(4,128)S(1)} %convert_element_type.558) | copy-start | bytes 36868
  153.0 51.7 %copy-start.32 = (f32[256,768]{1,0:T(8,128)}, f32[256,768]{1,0:T(8,128)S(1)}, u32[]{:S(2)}) copy-start(f32[256,768]{1,0:T(8,128)S(1)} %fusion.133) | copy-start | bytes 2359300
  163.5 41.2 %copy-start.100 = (f32[256]{0:T(256)}, f32[256]{0:T(256)S(1)}, u32[]{:S(2)}) copy-start(f32[256]{0:T(256)S(1)} %add_rsqrt_fusion.3) | copy-start | bytes 3076
  164.9 109.3 %reduce-scatter.15.cloned.1.call-start = ((), (), s32[]{:S(2)}) async-start(), calls=%async_computation.11 | async-start | bytes 1966080 | tf_op jit(solution)/shard_map/reduce_scatter | solution.py:49
  215.3 95.4 %reduce-scatter.11.cloned.1.call-start = ((), (), s32[]{:S(2)}) async-start(), calls=%async_computation.9 | async-start | bytes 1966080 | tf_op jit(solution)/shard_map/reduce_scatter | solution.py:49
  252.1 100.7 %all-gather.25.cloned.1.call-start = ((), (), s32[]{:S(2)}) async-start(), calls=%async_computation.20 | async-start | bytes 1966080 | tf_op jit(solution)/shard_map/all_gather | solution.py:44
  275.8 35.0 %copy-start.89 = (f32[256]{0:T(256)}, f32[256]{0:T(256)S(1)}, u32[]{:S(2)}) copy-start(f32[256]{0:T(256)S(1)} %broadcast_multiply_fusion.8) | copy-start | bytes 3076
  316.8 73.4 %all-gather.29.cloned.1.call-start = ((), (), s32[]{:S(2)}) async-start(), calls=%async_computation.22 | async-start | bytes 1966080 | tf_op jit(solution)/shard_map/all_gather | solution.py:44
  317.4 158.9 %reduce-scatter.21.cloned.1.call-start = ((), (), s32[]{:S(2)}) async-start(), calls=%async_computation.14 | async-start | bytes 1966080 | tf_op jit(solution)/shard_map/reduce_scatter | solution.py:49
  352.8 37.3 %copy-start.85 = (f32[4,768]{1,0:T(4,128)S(1)}, f32[4,768]{1,0:T(4,128)}, u32[]{:S(2)}) copy-start(f32[4,768]{1,0:T(4,128)} %copy-done.84) | copy-start | bytes 36868
  401.4 78.3 %reduce-scatter.17.cloned.1.call-start = ((), (), s32[]{:S(2)}) async-start(), calls=%async_computation.12 | async-start | bytes 1966080 | tf_op jit(solution)/shard_map/reduce_scatter | solution.py:49
  410.4 15.0 %collective-permute-start.20 = (bf16[768,768]{1,0:T(8,128)(2,1)}, bf16[768,768]{1,0:T(8,128)(2,1)}, u32[]{:S(2)}, u32[]{:S(2)}) collective-permute-start(bf16[768,768]{1,0:T(8,128)(2,1)} %fusion.77), channel_id=1, source_target_pairs={{0,4},{4,0},{8,12},{12,8},{16,20},{20,16},{24,28},{28,24},{1,5},{5... | collective-permute-start | bytes 3538952 | tf_op jit(solution)/shard_map/ppermute | solution.py:83
  422.2 8.2 %collective-permute-start.29 = (bf16[768,768]{1,0:T(8,128)(2,1)}, bf16[768,768]{1,0:T(8,128)(2,1)}, u32[]{:S(2)}, u32[]{:S(2)}) collective-permute-start(bf16[768,768]{1,0:T(8,128)(2,1)} %fusion.78), channel_id=1, source_target_pairs={{0,4},{4,0},{8,12},{12,8},{16,20},{20,16},{24,28},{28,24},{1,5},{5... | collective-permute-start | bytes 3538952 | tf_op jit(solution)/shard_map/ppermute | solution.py:83
  424.8 100.1 %all-gather.27.cloned.1.call-start = ((), (), s32[]{:S(2)}) async-start(), calls=%async_computation.21 | async-start | bytes 1966080 | tf_op jit(solution)/shard_map/all_gather | solution.py:44
  428.8 16.3 %collective-permute-start.21 = (bf16[384,768]{1,0:T(8,128)(2,1)S(1)}, bf16[384,768]{1,0:T(8,128)(2,1)S(1)}, u32[]{:S(2)}, u32[]{:S(2)}) collective-permute-start(bf16[384,768]{1,0:T(8,128)(2,1)S(1)} %select_convert_fusion.4), channel_id=1, source_target_pairs={{0,8},{4,12},{8,0},{12,4},{16,24},{20,28},{24,16},{28,20},{1,9},{5... | collective-permute-start | bytes 1769480 | tf_op jit(solution)/shard_map/ppermute | solution.py:83
  432.1 25.1 %collective-permute-start.30 = (bf16[384,768]{1,0:T(8,128)(2,1)S(1)}, bf16[384,768]{1,0:T(8,128)(2,1)S(1)}, u32[]{:S(2)}, u32[]{:S(2)}) collective-permute-start(bf16[384,768]{1,0:T(8,128)(2,1)S(1)} %select_convert_fusion.3), channel_id=1, source_target_pairs={{0,8},{4,12},{8,0},{12,4},{16,24},{20,28},{24,16},{28,20},{1,9},{5... | collective-permute-start | bytes 1769480 | tf_op jit(solution)/shard_map/ppermute | solution.py:83
  432.9 27.9 %collective-permute-start.26 = (f32[2,768]{1,0:T(2,128)S(1)}, f32[2,768]{1,0:T(2,128)S(1)}, u32[]{:S(2)}, u32[]{:S(2)}) collective-permute-start(f32[2,768]{1,0:T(2,128)S(1)} %convolution_add_fusion.8), channel_id=1, source_target_pairs={{0,4},{4,0},{8,12},{12,8},{16,20},{20,16},{24,28},{28,24},{1,5},{5... | collective-permute-start | bytes 18440 | tf_op jit(solution)/shard_map/ppermute | solution.py:102
  445.3 13.7 %collective-permute-start.22 = (bf16[192,768]{1,0:T(8,128)(2,1)S(1)}, bf16[192,768]{1,0:T(8,128)(2,1)S(1)}, u32[]{:S(2)}, u32[]{:S(2)}) collective-permute-start(bf16[192,768]{1,0:T(8,128)(2,1)S(1)} %select_convert_fusion.7), channel_id=1, source_target_pairs={{0,16},{4,20},{8,24},{12,28},{16,0},{20,4},{24,8},{28,12},{1,17},{... | collective-permute-start | bytes 884744 | tf_op jit(solution)/shard_map/ppermute | solution.py:83
  457.4 18.8 %copy-start.9 = (f32[256,768]{1,0:T(8,128)S(1)}, f32[256,768]{1,0:T(8,128)}, u32[]{:S(2)}) copy-start(f32[256,768]{1,0:T(8,128)} %get-tuple-element.66) | copy-start | bytes 2359300
  457.5 9.9 %collective-permute-start.31 = (bf16[192,768]{1,0:T(8,128)(2,1)S(1)}, bf16[192,768]{1,0:T(8,128)(2,1)S(1)}, u32[]{:S(2)}, u32[]{:S(2)}) collective-permute-start(bf16[192,768]{1,0:T(8,128)(2,1)S(1)} %select_convert_fusion.6), channel_id=1, source_target_pairs={{0,16},{4,20},{8,24},{12,28},{16,0},{20,4},{24,8},{28,12},{1,17},{... | collective-permute-start | bytes 884744 | tf_op jit(solution)/shard_map/ppermute | solution.py:83
  459.1 14.6 %collective-permute-start.23 = (bf16[192,768]{1,0:T(8,128)(2,1)S(1)}, bf16[192,768]{1,0:T(8,128)(2,1)S(1)}, u32[]{:S(2)}, u32[]{:S(2)}) collective-permute-start(bf16[192,768]{1,0:T(8,128)(2,1)S(1)} %add_convert_fusion.1), channel_id=1, source_target_pairs={{0,16},{4,20},{8,24},{12,28},{16,0},{20,4},{24,8},{28,12},{1,17},{... | collective-permute-start | bytes 884744 | tf_op jit(solution)/shard_map/ppermute | solution.py:88
  461.4 45.6 %collective-permute-start.27 = (f32[2,768]{1,0:T(2,128)}, f32[2,768]{1,0:T(2,128)}, u32[]{:S(2)}, u32[]{:S(2)}) collective-permute-start(f32[2,768]{1,0:T(2,128)} %add.577), channel_id=1, source_target_pairs={{0,8},{4,12},{8,0},{12,4},{16,24},{20,28},{24,16},{28,20},{1,9},{5... | collective-permute-start | bytes 18440 | tf_op jit(solution)/shard_map/ppermute | solution.py:102
  468.2 30.8 %collective-permute-start.32 = (bf16[192,768]{1,0:T(8,128)(2,1)}, bf16[192,768]{1,0:T(8,128)(2,1)}, u32[]{:S(2)}, u32[]{:S(2)}) collective-permute-start(bf16[192,768]{1,0:T(8,128)(2,1)} %add_convert_fusion), channel_id=1, source_target_pairs={{0,16},{4,20},{8,24},{12,28},{16,0},{20,4},{24,8},{28,12},{1,17},{... | collective-permute-start | bytes 884744 | tf_op jit(solution)/shard_map/ppermute | solution.py:88
  474.8 18.2 %collective-permute-start.24 = (bf16[384,768]{1,0:T(8,128)(2,1)}, bf16[384,768]{1,0:T(8,128)(2,1)}, u32[]{:S(2)}, u32[]{:S(2)}) collective-permute-start(bf16[384,768]{1,0:T(8,128)(2,1)} %maximum_select_fusion.7), channel_id=1, source_target_pairs={{0,8},{4,12},{8,0},{12,4},{16,24},{20,28},{24,16},{28,20},{1,9},{5... | collective-permute-start | bytes 1769480 | tf_op jit(solution)/shard_map/ppermute | solution.py:88
  483.5 74.0 %all-gather.31.cloned.1.call-start = ((), (), s32[]{:S(2)}) async-start(), calls=%async_computation.23 | async-start | bytes 1966080 | tf_op jit(solution)/shard_map/all_gather | solution.py:44
  492.3 6.6 collective-permute-start.15
  496.0 25.2 %collective-permute-start.25 = (bf16[768,768]{1,0:T(8,128)(2,1)}, bf16[768,768]{1,0:T(8,128)(2,1)}, u32[]{:S(2)}, u32[]{:S(2)}) collective-permute-start(bf16[768,768]{1,0:T(8,128)(2,1)} %maximum_select_fusion.3), channel_id=1, source_target_pairs={{0,4},{4,0},{8,12},{12,8},{16,20},{20,16},{24,28},{28,24},{1,5},{5... | collective-permute-start | bytes 3538952 | tf_op jit(solution)/shard_map/ppermute | solution.py:88
  499.0 7.5 %collective-permute-start.16 = (f32[3,2,2,768]{3,1,2,0:T(2,128)S(1)}, f32[3,2,2,768]{3,1,2,0:T(2,128)S(1)}, u32[]{:S(2)}, u32[]{:S(2)}) collective-permute-start(f32[3,2,2,768]{3,1,2,0:T(2,128)S(1)} %fusion.274), channel_id=1, source_target_pairs={{0,2},{1,3},{2,0},{3,1},{4,6},{5,7},{6,4},{7,5},{8,10},{9,11},{10,... | collective-permute-start | bytes 110600 | tf_op jit(solution)/shard_map/ppermute | solution.py:102
  500.4 16.2 %collective-permute-start.33 = (bf16[384,768]{1,0:T(8,128)(2,1)S(1)}, bf16[384,768]{1,0:T(8,128)(2,1)}, u32[]{:S(2)}, u32[]{:S(2)}) collective-permute-start(bf16[384,768]{1,0:T(8,128)(2,1)S(1)} %maximum_select_fusion.8), channel_id=1, source_target_pairs={{0,8},{4,12},{8,0},{12,4},{16,24},{20,28},{24,16},{28,20},{1,9},{5... | collective-permute-start | bytes 1769480 | tf_op jit(solution)/shard_map/ppermute | solution.py:88
  506.5 2.6 collective-permute-start.17
  507.7 3.6 collective-permute-start.28
  509.2 5.8 collective-permute-start.18
  512.0 155.6 %reduce-scatter.19.cloned.1.call-start = ((), (), s32[]{:S(2)}) async-start(), calls=%async_computation.13 | async-start | bytes 1966080 | tf_op jit(solution)/shard_map/reduce_scatter | solution.py:49
  515.1 4.3 collective-permute-start.19
  519.3 124.1 %collective-permute-start.34 = (bf16[768,768]{1,0:T(8,128)(2,1)}, bf16[768,768]{1,0:T(8,128)(2,1)}, u32[]{:S(2)}, u32[]{:S(2)}) collective-permute-start(bf16[768,768]{1,0:T(8,128)(2,1)} %maximum_select_fusion.4), channel_id=1, source_target_pairs={{0,4},{4,0},{8,12},{12,8},{16,20},{20,16},{24,28},{28,24},{1,5},{5... | collective-permute-start | bytes 3538952 | tf_op jit(solution)/shard_map/ppermute | solution.py:88
  532.7 28.2 %copy-start.5 = (f32[4,2,3,128,128]{3,4,2,1,0:T(8,128)S(1)}, f32[4,2,3,128,128]{3,4,2,1,0:T(8,128)}, u32[]{:S(2)}) copy-start(f32[4,2,3,128,128]{3,4,2,1,0:T(8,128)} %copy-done.4) | copy-start | bytes 4718596
  532.7 28.2 %copy-start.65 = (f32[4,2,3,128]{3,2,1,0:T(4,128)S(1)}, f32[4,2,3,128]{3,2,1,0:T(4,128)}, u32[]{:S(2)}) copy-start(f32[4,2,3,128]{3,2,1,0:T(4,128)} %copy-done.64) | copy-start | bytes 36868
  574.9 94.6 %reduce-scatter.23.cloned.1.call-start = ((), (), s32[]{:S(2)}) async-start(), calls=%async_computation.15 | async-start | bytes 1966080 | tf_op jit(solution)/shard_map/reduce_scatter | solution.py:49
  581.7 47.5 %collective-permute-start.6 = (f32[2,2,192]{2,0,1:T(2,128)}, f32[2,2,192]{2,0,1:T(2,128)S(1)}, u32[]{:S(2)}, u32[]{:S(2)}) collective-permute-start(f32[2,2,192]{2,0,1:T(2,128)} %maximum_add_fusion.1), channel_id=1, source_target_pairs={{0,4},{4,0},{8,12},{12,8},{16,20},{20,16},{24,28},{28,24},{1,5},{5... | collective-permute-start | bytes 9224 | tf_op jit(solution)/shard_map/ppermute | solution.py:102
  589.4 9.0 %collective-permute-start = (bf16[2304,192]{0,1:T(8,128)(2,1)}, bf16[2304,192]{0,1:T(8,128)(2,1)}, u32[]{:S(2)}, u32[]{:S(2)}) collective-permute-start(bf16[2304,192]{0,1:T(8,128)(2,1)} %bitcast.163), channel_id=1, source_target_pairs={{0,4},{4,0},{8,12},{12,8},{16,20},{20,16},{24,28},{28,24},{1,5},{5... | collective-permute-start | bytes 2654216 | tf_op jit(solution)/shard_map/ppermute | solution.py:83
  592.4 9.6 %collective-permute-start.9 = (bf16[192,768]{1,0:T(8,128)(2,1)}, bf16[192,768]{1,0:T(8,128)(2,1)S(1)}, u32[]{:S(2)}, u32[]{:S(2)}) collective-permute-start(bf16[192,768]{1,0:T(8,128)(2,1)} %fusion.121), channel_id=1, source_target_pairs={{0,4},{4,0},{8,12},{12,8},{16,20},{20,16},{24,28},{28,24},{1,5},{5... | collective-permute-start | bytes 884744 | tf_op jit(solution)/shard_map/ppermute | solution.py:83
  600.5 13.1 %collective-permute-start.1 = (bf16[1152,192]{0,1:T(8,128)(2,1)S(1)}, bf16[1152,192]{0,1:T(8,128)(2,1)S(1)}, u32[]{:S(2)}, u32[]{:S(2)}) collective-permute-start(bf16[1152,192]{0,1:T(8,128)(2,1)S(1)} %select_convert_fusion.5), channel_id=1, source_target_pairs={{0,8},{4,12},{8,0},{12,4},{16,24},{20,28},{24,16},{28,20},{1,9},{5... | collective-permute-start | bytes 1327112 | tf_op jit(solution)/shard_map/ppermute | solution.py:83
  602.2 27.0 %copy-start.98 = (f32[2,1,192]{2,0,1:T(2,128)S(1)}, f32[2,1,192]{2,0,1:T(2,128)}, u32[]{:S(2)}) copy-start(f32[2,1,192]{2,0,1:T(2,128)} %convolution_bitcast_fusion.16) | copy-start | bytes 4612
  602.2 13.9 %collective-permute-start.10 = (bf16[96,768]{1,0:T(8,128)(2,1)S(1)}, bf16[96,768]{1,0:T(8,128)(2,1)S(1)}, u32[]{:S(2)}, u32[]{:S(2)}) collective-permute-start(bf16[96,768]{1,0:T(8,128)(2,1)S(1)} %select_convert_fusion.10), channel_id=1, source_target_pairs={{0,8},{4,12},{8,0},{12,4},{16,24},{20,28},{24,16},{28,20},{1,9},{5... | collective-permute-start | bytes 442376 | tf_op jit(solution)/shard_map/ppermute | solution.py:83
  613.9 6.8 collective-permute-start.2
  620.9 6.5 collective-permute-start.3
  622.4 7.4 %collective-permute-start.11 = (bf16[48,768]{1,0:T(8,128)(2,1)S(1)}, bf16[48,768]{1,0:T(8,128)(2,1)S(1)}, u32[]{:S(2)}, u32[]{:S(2)}) collective-permute-start(bf16[48,768]{1,0:T(8,128)(2,1)S(1)} %select_convert_fusion.11), channel_id=1, source_target_pairs={{0,16},{4,20},{8,24},{12,28},{16,0},{20,4},{24,8},{28,12},{1,17},{... | collective-permute-start | bytes 221192 | tf_op jit(solution)/shard_map/ppermute | solution.py:83
  627.6 9.0 %collective-permute-start.4 = (bf16[1152,192]{0,1:T(8,128)(2,1)S(1)}, bf16[1152,192]{0,1:T(8,128)(2,1)S(1)}, u32[]{:S(2)}, u32[]{:S(2)}) collective-permute-start(bf16[1152,192]{0,1:T(8,128)(2,1)S(1)} %maximum_select_fusion.9), channel_id=1, source_target_pairs={{0,8},{4,12},{8,0},{12,4},{16,24},{20,28},{24,16},{28,20},{1,9},{5... | collective-permute-start | bytes 1327112 | tf_op jit(solution)/shard_map/ppermute | solution.py:88
  629.2 9.3 %collective-permute-start.7 = (f32[2,2,192]{2,0,1:T(2,128)S(1)}, f32[2,2,192]{2,0,1:T(2,128)S(1)}, u32[]{:S(2)}, u32[]{:S(2)}) collective-permute-start(f32[2,2,192]{2,0,1:T(2,128)S(1)} %fusion.275), channel_id=1, source_target_pairs={{0,8},{4,12},{8,0},{12,4},{16,24},{20,28},{24,16},{28,20},{1,9},{5... | collective-permute-start | bytes 9224 | tf_op jit(solution)/shard_map/ppermute | solution.py:102
  629.8 7.1 %collective-permute-start.12 = (bf16[48,768]{1,0:T(8,128)(2,1)S(1)}, bf16[48,768]{1,0:T(8,128)(2,1)S(1)}, u32[]{:S(2)}, u32[]{:S(2)}) collective-permute-start(bf16[48,768]{1,0:T(8,128)(2,1)S(1)} %add_convert_fusion.3), channel_id=1, source_target_pairs={{0,16},{4,20},{8,24},{12,28},{16,0},{20,4},{24,8},{28,12},{1,17},{... | collective-permute-start | bytes 221192 | tf_op jit(solution)/shard_map/ppermute | solution.py:88
  636.8 16.4 %collective-permute-start.5 = (bf16[2304,192]{0,1:T(8,128)(2,1)S(1)}, bf16[2304,192]{0,1:T(8,128)(2,1)S(1)}, u32[]{:S(2)}, u32[]{:S(2)}) collective-permute-start(bf16[2304,192]{0,1:T(8,128)(2,1)S(1)} %maximum_select_fusion.5), channel_id=1, source_target_pairs={{0,4},{4,0},{8,12},{12,8},{16,20},{20,16},{24,28},{28,24},{1,5},{5... | collective-permute-start | bytes 2654216 | tf_op jit(solution)/shard_map/ppermute | solution.py:88
  637.0 6.3 collective-permute-start.13
  638.5 12.8 %collective-permute-start.8 = (f32[2,2,192]{2,0,1:T(2,128)S(1)}, f32[2,2,192]{2,0,1:T(2,128)S(1)}, u32[]{:S(2)}, u32[]{:S(2)}) collective-permute-start(f32[2,2,192]{2,0,1:T(2,128)S(1)} %fusion.277), channel_id=1, source_target_pairs={{0,16},{4,20},{8,24},{12,28},{16,0},{20,4},{24,8},{28,12},{1,17},{... | collective-permute-start | bytes 9224 | tf_op jit(solution)/shard_map/ppermute | solution.py:102
  643.3 8.6 %collective-permute-start.14 = (bf16[192,768]{1,0:T(8,128)(2,1)S(1)}, bf16[192,768]{1,0:T(8,128)(2,1)S(1)}, u32[]{:S(2)}, u32[]{:S(2)}) collective-permute-start(bf16[192,768]{1,0:T(8,128)(2,1)S(1)} %maximum_select_fusion.10), channel_id=1, source_target_pairs={{0,4},{4,0},{8,12},{12,8},{16,20},{20,16},{24,28},{28,24},{1,5},{5... | collective-permute-start | bytes 884744 | tf_op jit(solution)/shard_map/ppermute | solution.py:88
  (131 other events, 712.1 us)
Sparse Core Ops, SparseCore 0:
  10.2 39.7 all-gather.20
  52.1 35.8 all-gather.16
  90.9 34.2 reduce-scatter.12
  127.4 34.2 reduce-scatter.8
  163.7 35.8 all-gather.22
  201.0 35.8 all-gather.18
  239.8 34.2 reduce-scatter.14
  276.5 34.2 reduce-scatter.10
  316.9 35.8 all-gather.24
  354.2 35.8 all-gather.28
  401.5 34.2 reduce-scatter.20
  438.0 34.2 reduce-scatter.16
  483.6 36.5 all-gather.26
  521.7 35.8 all-gather.30
  575.0 34.2 reduce-scatter.18
  612.1 34.2 reduce-scatter.22

commit v5 on v4

--- a/solution.py
+++ b/solution.py
@@ -110,6 +110,7 @@
     seg_kind,
     seg_lens,
     row_kind,
+    out_rows_w,
     w_qkv,
     qv_bias,
     w_out,
@@ -172,8 +173,10 @@
         "schqk,sckhd->scqhd", probs_low, heads(value_rows), preferred_element_type=jnp.float32
     )
     mixed = mixed.reshape(n_seg, seg_rows, -1).astype(jnp.bfloat16)
-    attn_parts = jnp.einsum("sre,sed->srd", mixed, out_sel, preferred_element_type=jnp.float32)
-    attn_rows = scatter_sum(attn_parts)
+    mixed_rows = lax.all_to_all(mixed, "tensor", 0, 0, tiled=True)
+    attn_rows = jnp.einsum(
+        "erc,ecd->rd", mixed_rows, out_rows_w, preferred_element_type=jnp.float32
+    )
 
     hidden_one = inputs.astype(jnp.float32) + attn_rows + pick(resid_bias[:, 0])
     gain_one = pick(norm_gain[:, 0])
@@ -294,6 +297,8 @@
     chains = dev_chains // STREAMS
     seg_rows = chains * CHAIN
     weights = (w_qkv, qv_bias, w_out, resid_bias, norm_gain, norm_shift, w_up, up_bias, w_down)
+    peer_kind = block_kind[(jnp.arange(n_tensor) * tok_dev) // block_rows]
+    out_rows_w = lax.all_to_all(w_out[peer_kind], "tensor", 0, 0, tiled=True)
     outs, ins, grads, smalls = [], [], [], []
     for part in range(STREAMS):
         first_row = jnp.arange(n_tensor) * tok_dev + part * seg_rows
@@ -306,7 +311,7 @@
         row_kind = block_kind[own_rows // block_rows]
         rows = slice(part * seg_rows, (part + 1) * seg_rows)
         out_part, in_part, grad_part, small_part = stream(
-            inputs[rows], cotangent[rows], seg_kind, seg_lens, row_kind, *weights
+            inputs[rows], cotangent[rows], seg_kind, seg_lens, row_kind, out_rows_w, *weights
         )
         outs.append(out_part)
         ins.append(in_part)

time: 691 us -> 673 us (0.974)
  waiting for transfers between devices: 296 us -> 278 us
  starting transfers between devices: 31.6 us -> 44.7 us
    reduce_scatter x8 -> x6, waiting for transfers between devices: 73.2 us -> 55.3 us  [scatter_sum(): lax.psum_scatter(seg_parts.reshape(n_seg * seg_rows, width).astype(jnp.bf...]
    all_to_all x0 -> x3, starting transfers between devices: none -> 13.9 us  [the longest x2 7.57 us: stream(): mixed_rows = lax.all_to_all(mixed, 'tensor', 0, 0, tiled=True)]
    unnamed x295 -> x279, local copies, waits for them, and re-layouts: 23.5 us -> 19.9 us
  transfers between devices with their start and end apart: 51 -> 52, of which waited for: 25 -> 24; matrix products, arithmetic and copies ran while one was open for 44% -> 43% of each run, Pallas kernels for 0% -> 0%
where the time goes in v5:
time: 673 us; the launch traced here: 663 us
  waiting for transfers between devices  278 us (41%)
  matrix products  132 us (20%)
  local copies, waits for them, and re-layouts  108 us (16%)
  other arithmetic  84.3 us (13%)
  starting transfers between devices  44.7 us (7%)
  between operations  16.6 us (2%)
    all_gather x8, waiting for transfers between devices, gather_rows(): return lax.all_gather(local_rows, 'tensor', axis=0, tiled=False)  146 us
    reduce_scatter x6, waiting for transfers between devices, scatter_sum(): lax.psum_scatter(seg_parts.reshape(n_seg * seg_rows, width).astype(jnp.bf...  55.3 us
    ppermute x12, waiting for transfers between devices, dp_sum_low(): gots = lax.ppermute(sends, 'dp', dp_perm(n_dp, 1 << b))  42.3 us
    unnamed x279, local copies, waits for them, and re-layouts  19.9 us
    ppermute x12, waiting for transfers between devices, dp_sum_low(): gots = lax.ppermute(tuple(cur), 'dp', dp_perm(n_dp, 1 << b))  17.4 us
    dot_general x12, matrix products, pick(): return jnp.dot(kind_hot, kind_table.astype(jnp.float32), precision=highest)  15.4 us
    dot_general x12, matrix products, type_sum(): jnp.einsum('rt,rd->td', kind_hot, values, precision=lax.Precision.HIGHEST)  15 us
    convert_element_type x2, other arithmetic, stream(): activ = jax.nn.gelu(pre_act, approximate=False).astype(jnp.bfloat16)  14.6 us
  transfers between devices with their start and end apart: 52, of which 24 were waited for; matrix products, arithmetic and copies ran while one was open for 43% of the time, Pallas kernels for 0%

profile of v5, /device:TPU:0, one launch (start us, length us, event | category | flops | bytes accessed | tf_op | source)
XLA Modules:
  0.0 662.8 jit_solution(2723790231759965272)
XLA Ops:
  13.0 6.3 all-to-all-start.1
  22.7 4.0 gather_fusion.9
  26.7 4.1 gather_fusion.1
  41.1 32.4 %all-gather.21.cloned.1.call-done = bf16[1024,768]{1,0:T(8,128)(2,1)} async-done(((bf16[256,768]{1,0:T(8,128)(2,1)}), bf16[1024,768]{1,0:T(8,128)(2,1)}) %all-gather.21.cloned.1.call-update) | async-done | bytes 1572880 | tf_op jit(solution)/shard_map/all_gather | solution.py:44
  73.5 3.6 convolution_bitcast_fusion
  89.1 22.7 %all-gather.17.cloned.1.call-done = bf16[1024,768]{1,0:T(8,128)(2,1)} async-done(((bf16[256,768]{1,0:T(8,128)(2,1)}), bf16[1024,768]{1,0:T(8,128)(2,1)}) %all-gather.17.cloned.1.call-update) | async-done | bytes 1572880 | tf_op jit(solution)/shard_map/all_gather | solution.py:44
  111.8 5.0 convolution_bitcast_fusion.1
  116.8 4.1 all-to-all-start.2
  121.0 2.6 fusion.213
  142.9 3.5 all-to-all-start
  149.3 3.2 gather_fusion.14
  152.4 3.2 gather_fusion.7
  155.6 5.0 gather_fusion.12
  160.6 3.1 gather_fusion.5
  175.5 6.1 all-gather.23.cloned.1.call-done
  181.6 5.1 fusion.94
  186.7 7.3 %fusion.6 = bf16[4,256,768]{2,1,0:T(8,128)(2,1)S(1)} fusion(f32[4,256,768]{2,1,0:T(8,128)S(1)} %get-tuple-element.88, f32[4,768]{1,0:T(4,128)S(1)} %copy-done.81, u8[256,768]{1,0:T(8,128)(4,1)S(1)} %get-tuple-element.36, u8[256,768]{1,0:T(8,128)(4,1)S(1)} %get-tuple-element.35), kind=kLoop, calls=%fused_computation.29 | loop fusion | flops 55836672 | bytes 5124096 | tf_op jit(solution)/shard_map/convert_element_type | solution.py:190
  194.0 2.6 convolution_convert_fusion.4
  197.1 22.3 %all-gather.19.cloned.1.call-done = bf16[1024,768]{1,0:T(8,128)(2,1)} async-done(((bf16[256,768]{1,0:T(8,128)(2,1)}), bf16[1024,768]{1,0:T(8,128)(2,1)}) %all-gather.19.cloned.1.call-update) | async-done | bytes 1572880 | tf_op jit(solution)/shard_map/all_gather | solution.py:44
  219.5 5.1 fusion.93
  224.5 7.3 %fusion.3 = bf16[4,256,768]{2,1,0:T(8,128)(2,1)S(1)} fusion(f32[4,256,768]{2,1,0:T(8,128)S(1)} %get-tuple-element.97, f32[4,768]{1,0:T(4,128)S(1)} %copy-done.82, u8[256,768]{1,0:T(8,128)(4,1)S(1)} %get-tuple-element.34, u8[256,768]{1,0:T(8,128)(4,1)S(1)} %get-tuple-element.33), kind=kLoop, calls=%fused_computation.26 | loop fusion | flops 55836672 | bytes 5124096 | tf_op jit(solution)/shard_map/convert_element_type | solution.py:190
  231.9 2.6 convolution_convert_fusion.5
  235.8 20.7 %reduce-scatter.9.cloned.1.call-done = bf16[256,768]{1,0:T(8,128)(2,1)} async-done(((bf16[1024,768]{1,0:T(8,128)(2,1)}), bf16[256,768]{1,0:T(8,128)(2,1)}) %reduce-scatter.9.cloned.1.call-update) | async-done | bytes 393232 | tf_op jit(solution)/shard_map/reduce_scatter | solution.py:49
  258.4 34.6 %reduce-scatter.7.cloned.1.call-done = bf16[256,768]{1,0:T(8,128)(2,1)} async-done(((bf16[1024,768]{1,0:T(8,128)(2,1)}), bf16[256,768]{1,0:T(8,128)(2,1)}) %reduce-scatter.7.cloned.1.call-update) | async-done | bytes 393232 | tf_op jit(solution)/shard_map/reduce_scatter | solution.py:49
  299.8 2.8 gather_fusion.15
  306.4 2.7 copy.95
  309.0 2.6 copy.92
  311.7 2.6 copy.101
  314.2 2.6 copy.100
  316.9 2.6 copy.103
  319.5 2.6 copy.102
  329.6 5.1 all-gather.25.cloned.1.call-done
  334.8 6.9 %convert_reduce_fusion.1 = (f32[4,768]{1,0:T(4,128)S(1)}, bf16[4,256,768]{2,1,0:T(8,128)(2,1)}) fusion(f32[4,256,768]{2,1,0:T(8,128)} %copy-done.45, f32[4,768]{1,0:T(4,128)S(1)} %copy-done.82, bf16[4,256,768]{2,1,0:T(8,128)(2,1)} %bitcast.428, bf16[4,768,768]{2,1,0:T(8,128)(2,1)} %gather_fusion.7), kind=kOutput, calls=%fused_computation.60 | convolution fusion | flops 1219752960 | bytes 11034624 | tf_op jit(solution)/shard_map/srd,sfd->srf/dot_general | solution.py:205
  341.7 30.6 %all-gather.29.cloned.1.call-done = bf16[1024,768]{1,0:T(8,128)(2,1)} async-done(((bf16[256,768]{1,0:T(8,128)(2,1)}), bf16[1024,768]{1,0:T(8,128)(2,1)}) %all-gather.29.cloned.1.call-update) | async-done | bytes 1572880 | tf_op jit(solution)/shard_map/all_gather | solution.py:44
  372.3 5.8 convert_reduce_fusion
  378.1 5.5 convolution_convert_fusion
  383.9 4.7 fusion.25
  388.6 2.7 bitcast_add_fusion.1
  395.3 2.7 fusion.21
  398.0 2.8 bitcast_add_fusion
  404.3 2.6 convolution_convert_fusion.2
  407.5 3.3 bitcast_add_fusion.4
  415.2 12.0 %collective-permute-done.21 = bf16[384,768]{1,0:T(8,128)(2,1)S(1)} collective-permute-done((bf16[384,768]{1,0:T(8,128)(2,1)S(1)}, bf16[384,768]{1,0:T(8,128)(2,1)S(1)}, u32[]{:S(2)}, u32[]{:S(2)}) %collective-permute-start.21) | collective-permute-done | bytes 589856 | tf_op jit(solution)/shard_map/ppermute | solution.py:83
  429.0 10.4 %collective-permute-done.30 = bf16[384,768]{1,0:T(8,128)(2,1)S(1)} collective-permute-done((bf16[384,768]{1,0:T(8,128)(2,1)S(1)}, bf16[384,768]{1,0:T(8,128)(2,1)S(1)}, u32[]{:S(2)}, u32[]{:S(2)}) %collective-permute-start.30) | collective-permute-done | bytes 589856 | tf_op jit(solution)/shard_map/ppermute | solution.py:83
  445.0 4.6 collective-permute-done.31
  451.8 4.1 collective-permute-done.23
  476.1 4.2 collective-permute-done.15
  481.9 5.3 collective-permute-done.16
  496.7 2.7 maximum_select_fusion.4
  501.2 3.0 maximum_select_fusion
  504.3 2.6 convolution_convert_fusion.11
  513.2 27.0 %all-gather.31.cloned.1.call-done = bf16[1024,768]{1,0:T(8,128)(2,1)} async-done(((bf16[256,768]{1,0:T(8,128)(2,1)}), bf16[1024,768]{1,0:T(8,128)(2,1)}) %all-gather.31.cloned.1.call-update) | async-done | bytes 1572880 | tf_op jit(solution)/shard_map/all_gather | solution.py:44
  551.6 4.8 bitcast_convert_fusion.1
  562.5 2.9 fusion.17
  577.5 2.7 bitcast_convert_fusion
  585.5 9.8 %collective-permute-done.1 = bf16[1152,192]{0,1:T(8,128)(2,1)S(1)} collective-permute-done((bf16[1152,192]{0,1:T(8,128)(2,1)S(1)}, bf16[1152,192]{0,1:T(8,128)(2,1)S(1)}, u32[]{:S(2)}, u32[]{:S(2)}) %collective-permute-start.1) | collective-permute-done | bytes 442400 | tf_op jit(solution)/shard_map/ppermute | solution.py:83
  598.0 4.6 collective-permute-done.2
  605.2 4.8 collective-permute-done.3
  614.1 5.2 collective-permute-done.4
  622.7 3.2 collective-permute-done.13
  626.1 2.8 maximum_select_fusion.1
  628.9 2.5 convert.14
  638.2 6.6 reshape.739
  644.8 5.4 copy.104
  (594 shorter events, 207.4 us)
Async XLA Ops:
  7.2 142.1 %copy-start = (bf16[2,768,768]{2,1,0:T(8,128)(2,1)S(1)}, bf16[2,768,768]{2,1,0:T(8,128)(2,1)}, u32[]{:S(2)}) copy-start(bf16[2,768,768]{2,1,0:T(8,128)(2,1)} %param.25) | copy-start | bytes 7077892
  7.2 66.3 %all-gather.21.cloned.1.call-start = ((), (), s32[]{:S(2)}) async-start(), calls=%async_computation.17 | async-start | bytes 1966080 | tf_op jit(solution)/shard_map/all_gather | solution.py:44
  13.0 103.8 %all-to-all-start.1 = ((bf16[4,192,768]{2,1,0:T(8,128)(2,1)}), bf16[4,192,768]{2,1,0:T(8,128)(2,1)}, u32[]{:S(2)}, u32[]{:S(2)}) async-start(bf16[4,192,768]{2,1,0:T(8,128)(2,1)} %gather_fusion.4), calls=%async_computation.1 | async-start | bytes 2359296 | tf_op jit(solution)/shard_map/all_to_all | solution.py:301
  19.4 92.5 %all-gather.17.cloned.1.call-start = ((), (), s32[]{:S(2)}) async-start(), calls=%async_computation.15 | async-start | bytes 1966080 | tf_op jit(solution)/shard_map/all_gather | solution.py:44
  32.8 53.4 %copy-start.74 = (f32[4,3,64]{2,1,0:T(4,128)}, f32[4,3,64]{2,1,0:T(4,128)S(1)}, u32[]{:S(2)}) copy-start(f32[4,3,64]{2,1,0:T(4,128)S(1)} %add.515) | copy-start | bytes 9220
  36.1 37.4 %copy-start.103 = (bf16[2,1,768]{2,1,0:T(2,128)(2,1)}, bf16[2,1,768]{2,1,0:T(2,128)(2,1)S(1)}, u32[]{:S(2)}) copy-start(bf16[2,1,768]{2,1,0:T(2,128)(2,1)S(1)} %get-tuple-element.76) | copy-start | bytes 9220
  116.8 15.3 %all-to-all-start.2 = ((bf16[4,256,192]{1,2,0:T(8,128)(2,1)}), bf16[4,256,192]{1,2,0:T(8,128)(2,1)}, u32[]{:S(2)}, u32[]{:S(2)}) async-start(bf16[4,256,192]{1,2,0:T(8,128)(2,1)} %convert_element_type.532), calls=%async_computation.3 | async-start | bytes 786432 | tf_op jit(solution)/shard_map/all_to_all | solution.py:176
  121.0 60.6 %all-gather.23.cloned.1.call-start = ((), (), s32[]{:S(2)}) async-start(), calls=%async_computation.18 | async-start | bytes 1966080 | tf_op jit(solution)/shard_map/all_gather | solution.py:44
  142.9 27.0 %all-to-all-start = ((bf16[4,256,192]{1,2,0:T(8,128)(2,1)}), bf16[4,256,192]{1,2,0:T(8,128)(2,1)S(1)}, u32[]{:S(2)}, u32[]{:S(2)}) async-start(bf16[4,256,192]{1,2,0:T(8,128)(2,1)} %convert_element_type.516), calls=%async_computation | async-start | bytes 786432 | tf_op jit(solution)/shard_map/all_to_all | solution.py:176
  146.4 73.1 %all-gather.19.cloned.1.call-start = ((), (), s32[]{:S(2)}) async-start(), calls=%async_computation.16 | async-start | bytes 1966080 | tf_op jit(solution)/shard_map/all_gather | solution.py:44
  175.4 81.1 %reduce-scatter.9.cloned.1.call-start = ((), (), s32[]{:S(2)}) async-start(), calls=%async_computation.10 | async-start | bytes 1966080 | tf_op jit(solution)/shard_map/reduce_scatter | solution.py:49
  194.0 25.5 %copy-start.82 = (f32[4,768]{1,0:T(4,128)S(1)}, f32[4,768]{1,0:T(4,128)}, u32[]{:S(2)}) copy-start(f32[4,768]{1,0:T(4,128)} %convert_element_type.518) | copy-start | bytes 36868
  196.6 96.4 %reduce-scatter.7.cloned.1.call-start = ((), (), s32[]{:S(2)}) async-start(), calls=%async_computation.9 | async-start | bytes 1966080 | tf_op jit(solution)/shard_map/reduce_scatter | solution.py:49
  234.5 100.2 %all-gather.25.cloned.1.call-start = ((), (), s32[]{:S(2)}) async-start(), calls=%async_computation.19 | async-start | bytes 1966080 | tf_op jit(solution)/shard_map/all_gather | solution.py:44
  294.7 31.7 %copy-start.83 = (f32[256]{0:T(256)}, f32[256]{0:T(256)S(1)}, u32[]{:S(2)}) copy-start(f32[256]{0:T(256)S(1)} %broadcast_multiply_fusion.10) | copy-start | bytes 3076
  295.0 31.4 %copy-start.95 = (f32[256]{0:T(256)}, f32[256]{0:T(256)S(1)}, u32[]{:S(2)}) copy-start(f32[256]{0:T(256)S(1)} %add_rsqrt_fusion.2) | copy-start | bytes 3076
  298.8 73.5 %all-gather.29.cloned.1.call-start = ((), (), s32[]{:S(2)}) async-start(), calls=%async_computation.21 | async-start | bytes 1966080 | tf_op jit(solution)/shard_map/all_gather | solution.py:44
  299.5 158.8 %reduce-scatter.15.cloned.1.call-start = ((), (), s32[]{:S(2)}) async-start(), calls=%async_computation.13 | async-start | bytes 1966080 | tf_op jit(solution)/shard_map/reduce_scatter | solution.py:49
  306.4 91.7 %copy-start.119 = (bf16[4,2]{0,1:T(2,128)(2,1)}, bf16[4,2]{0,1:T(2,128)(2,1)S(1)}, u32[]{:S(2)}) copy-start(bf16[4,2]{0,1:T(2,128)(2,1)S(1)} %convert_convert_fusion.1) | copy-start | bytes 52
  306.4 86.2 %copy-start.124 = (bf16[4,2]{0,1:T(2,128)(2,1)}, bf16[4,2]{0,1:T(2,128)(2,1)S(1)}, u32[]{:S(2)}) copy-start(bf16[4,2]{0,1:T(2,128)(2,1)S(1)} %convert_convert_fusion) | copy-start | bytes 52
  383.6 78.2 %reduce-scatter.11.cloned.1.call-start = ((), (), s32[]{:S(2)}) async-start(), calls=%async_computation.11 | async-start | bytes 1966080 | tf_op jit(solution)/shard_map/reduce_scatter | solution.py:49
  392.6 15.0 %collective-permute-start.20 = (bf16[768,768]{1,0:T(8,128)(2,1)}, bf16[768,768]{1,0:T(8,128)(2,1)}, u32[]{:S(2)}, u32[]{:S(2)}) collective-permute-start(bf16[768,768]{1,0:T(8,128)(2,1)} %fusion.79), channel_id=1, source_target_pairs={{0,4},{4,0},{8,12},{12,8},{16,20},{20,16},{24,28},{28,24},{1,5},{5... | collective-permute-start | bytes 3538952 | tf_op jit(solution)/shard_map/ppermute | solution.py:83
  404.3 8.2 %collective-permute-start.29 = (bf16[768,768]{1,0:T(8,128)(2,1)}, bf16[768,768]{1,0:T(8,128)(2,1)}, u32[]{:S(2)}, u32[]{:S(2)}) collective-permute-start(bf16[768,768]{1,0:T(8,128)(2,1)} %fusion.80), channel_id=1, source_target_pairs={{0,4},{4,0},{8,12},{12,8},{16,20},{20,16},{24,28},{28,24},{1,5},{5... | collective-permute-start | bytes 3538952 | tf_op jit(solution)/shard_map/ppermute | solution.py:83
  406.9 97.3 %all-gather.27.cloned.1.call-start = ((), (), s32[]{:S(2)}) async-start(), calls=%async_computation.20 | async-start | bytes 1966080 | tf_op jit(solution)/shard_map/all_gather | solution.py:44
  410.9 16.3 %collective-permute-start.21 = (bf16[384,768]{1,0:T(8,128)(2,1)S(1)}, bf16[384,768]{1,0:T(8,128)(2,1)S(1)}, u32[]{:S(2)}, u32[]{:S(2)}) collective-permute-start(bf16[384,768]{1,0:T(8,128)(2,1)S(1)} %select_convert_fusion.4), channel_id=1, source_target_pairs={{0,8},{4,12},{8,0},{12,4},{16,24},{20,28},{24,16},{28,20},{1,9},{5... | collective-permute-start | bytes 1769480 | tf_op jit(solution)/shard_map/ppermute | solution.py:83
  414.2 25.1 %collective-permute-start.30 = (bf16[384,768]{1,0:T(8,128)(2,1)S(1)}, bf16[384,768]{1,0:T(8,128)(2,1)S(1)}, u32[]{:S(2)}, u32[]{:S(2)}) collective-permute-start(bf16[384,768]{1,0:T(8,128)(2,1)S(1)} %select_convert_fusion.3), channel_id=1, source_target_pairs={{0,8},{4,12},{8,0},{12,4},{16,24},{20,28},{24,16},{28,20},{1,9},{5... | collective-permute-start | bytes 1769480 | tf_op jit(solution)/shard_map/ppermute | solution.py:83
  415.0 27.9 %collective-permute-start.26 = (f32[2,768]{1,0:T(2,128)S(1)}, f32[2,768]{1,0:T(2,128)S(1)}, u32[]{:S(2)}, u32[]{:S(2)}) collective-permute-start(f32[2,768]{1,0:T(2,128)S(1)} %convolution_add_fusion.8), channel_id=1, source_target_pairs={{0,4},{4,0},{8,12},{12,8},{16,20},{20,16},{24,28},{28,24},{1,5},{5... | collective-permute-start | bytes 18440 | tf_op jit(solution)/shard_map/ppermute | solution.py:102
  427.4 13.7 %collective-permute-start.22 = (bf16[192,768]{1,0:T(8,128)(2,1)S(1)}, bf16[192,768]{1,0:T(8,128)(2,1)S(1)}, u32[]{:S(2)}, u32[]{:S(2)}) collective-permute-start(bf16[192,768]{1,0:T(8,128)(2,1)S(1)} %select_convert_fusion.7), channel_id=1, source_target_pairs={{0,16},{4,20},{8,24},{12,28},{16,0},{20,4},{24,8},{28,12},{1,17},{... | collective-permute-start | bytes 884744 | tf_op jit(solution)/shard_map/ppermute | solution.py:83
  439.6 9.9 %collective-permute-start.31 = (bf16[192,768]{1,0:T(8,128)(2,1)S(1)}, bf16[192,768]{1,0:T(8,128)(2,1)S(1)}, u32[]{:S(2)}, u32[]{:S(2)}) collective-permute-start(bf16[192,768]{1,0:T(8,128)(2,1)S(1)} %select_convert_fusion.6), channel_id=1, source_target_pairs={{0,16},{4,20},{8,24},{12,28},{16,0},{20,4},{24,8},{28,12},{1,17},{... | collective-permute-start | bytes 884744 | tf_op jit(solution)/shard_map/ppermute | solution.py:83
  441.3 14.6 %collective-permute-start.23 = (bf16[192,768]{1,0:T(8,128)(2,1)S(1)}, bf16[192,768]{1,0:T(8,128)(2,1)S(1)}, u32[]{:S(2)}, u32[]{:S(2)}) collective-permute-start(bf16[192,768]{1,0:T(8,128)(2,1)S(1)} %add_convert_fusion.1), channel_id=1, source_target_pairs={{0,16},{4,20},{8,24},{12,28},{16,0},{20,4},{24,8},{28,12},{1,17},{... | collective-permute-start | bytes 884744 | tf_op jit(solution)/shard_map/ppermute | solution.py:88
  443.5 44.2 %collective-permute-start.27 = (f32[2,768]{1,0:T(2,128)}, f32[2,768]{1,0:T(2,128)}, u32[]{:S(2)}, u32[]{:S(2)}) collective-permute-start(f32[2,768]{1,0:T(2,128)} %add.575), channel_id=1, source_target_pairs={{0,8},{4,12},{8,0},{12,4},{16,24},{20,28},{24,16},{28,20},{1,9},{5... | collective-permute-start | bytes 18440 | tf_op jit(solution)/shard_map/ppermute | solution.py:102
  450.4 30.0 %collective-permute-start.32 = (bf16[192,768]{1,0:T(8,128)(2,1)}, bf16[192,768]{1,0:T(8,128)(2,1)}, u32[]{:S(2)}, u32[]{:S(2)}) collective-permute-start(bf16[192,768]{1,0:T(8,128)(2,1)} %add_convert_fusion), channel_id=1, source_target_pairs={{0,16},{4,20},{8,24},{12,28},{16,0},{20,4},{24,8},{28,12},{1,17},{... | collective-permute-start | bytes 884744 | tf_op jit(solution)/shard_map/ppermute | solution.py:88
  456.9 17.0 %collective-permute-start.24 = (bf16[384,768]{1,0:T(8,128)(2,1)}, bf16[384,768]{1,0:T(8,128)(2,1)}, u32[]{:S(2)}, u32[]{:S(2)}) collective-permute-start(bf16[384,768]{1,0:T(8,128)(2,1)} %maximum_select_fusion.7), channel_id=1, source_target_pairs={{0,8},{4,12},{8,0},{12,4},{16,24},{20,28},{24,16},{28,20},{1,9},{5... | collective-permute-start | bytes 1769480 | tf_op jit(solution)/shard_map/ppermute | solution.py:88
  465.7 74.6 %all-gather.31.cloned.1.call-start = ((), (), s32[]{:S(2)}) async-start(), calls=%async_computation.22 | async-start | bytes 1966080 | tf_op jit(solution)/shard_map/all_gather | solution.py:44
  473.3 7.0 %collective-permute-start.15 = (f32[3,2,2,768]{3,1,2,0:T(2,128)S(1)}, f32[3,2,2,768]{3,1,2,0:T(2,128)S(1)}, u32[]{:S(2)}, u32[]{:S(2)}) collective-permute-start(f32[3,2,2,768]{3,1,2,0:T(2,128)S(1)} %maximum_add_fusion), channel_id=1, source_target_pairs={{0,1},{1,0},{2,3},{3,2},{4,5},{5,4},{6,7},{7,6},{8,9},{9,8},{10,11... | collective-permute-start | bytes 110600 | tf_op jit(solution)/shard_map/ppermute | solution.py:102
  476.0 25.2 %collective-permute-start.25 = (bf16[768,768]{1,0:T(8,128)(2,1)S(1)}, bf16[768,768]{1,0:T(8,128)(2,1)}, u32[]{:S(2)}, u32[]{:S(2)}) collective-permute-start(bf16[768,768]{1,0:T(8,128)(2,1)S(1)} %maximum_select_fusion.3), channel_id=1, source_target_pairs={{0,4},{4,0},{8,12},{12,8},{16,20},{20,16},{24,28},{28,24},{1,5},{5... | collective-permute-start | bytes 3538952 | tf_op jit(solution)/shard_map/ppermute | solution.py:88
  480.3 6.9 %collective-permute-start.16 = (f32[3,2,2,768]{3,1,2,0:T(2,128)S(1)}, f32[3,2,2,768]{3,1,2,0:T(2,128)S(1)}, u32[]{:S(2)}, u32[]{:S(2)}) collective-permute-start(f32[3,2,2,768]{3,1,2,0:T(2,128)S(1)} %fusion.276), channel_id=1, source_target_pairs={{0,2},{1,3},{2,0},{3,1},{4,6},{5,7},{6,4},{7,5},{8,10},{9,11},{10,... | collective-permute-start | bytes 110600 | tf_op jit(solution)/shard_map/ppermute | solution.py:102
  481.8 14.9 %collective-permute-start.33 = (bf16[384,768]{1,0:T(8,128)(2,1)S(1)}, bf16[384,768]{1,0:T(8,128)(2,1)}, u32[]{:S(2)}, u32[]{:S(2)}) collective-permute-start(bf16[384,768]{1,0:T(8,128)(2,1)S(1)} %maximum_select_fusion.8), channel_id=1, source_target_pairs={{0,8},{4,12},{8,0},{12,4},{16,24},{20,28},{24,16},{28,20},{1,9},{5... | collective-permute-start | bytes 1769480 | tf_op jit(solution)/shard_map/ppermute | solution.py:88
  487.3 2.6 collective-permute-start.17
  488.4 3.6 collective-permute-start.28
  489.9 5.2 collective-permute-start.18
  492.7 157.5 %reduce-scatter.13.cloned.1.call-start = ((), (), s32[]{:S(2)}) async-start(), calls=%async_computation.12 | async-start | bytes 1966080 | tf_op jit(solution)/shard_map/reduce_scatter | solution.py:49
  495.1 4.2 collective-permute-start.19
  499.4 126.7 %collective-permute-start.34 = (bf16[768,768]{1,0:T(8,128)(2,1)}, bf16[768,768]{1,0:T(8,128)(2,1)}, u32[]{:S(2)}, u32[]{:S(2)}) collective-permute-start(bf16[768,768]{1,0:T(8,128)(2,1)} %maximum_select_fusion.4), channel_id=1, source_target_pairs={{0,4},{4,0},{8,12},{12,8},{16,20},{20,16},{24,28},{28,24},{1,5},{5... | collective-permute-start | bytes 3538952 | tf_op jit(solution)/shard_map/ppermute | solution.py:88
  511.2 31.6 %copy-start.5 = (f32[4,2,3,128,128]{3,4,2,1,0:T(8,128)S(1)}, f32[4,2,3,128,128]{3,4,2,1,0:T(8,128)}, u32[]{:S(2)}) copy-start(f32[4,2,3,128,128]{3,4,2,1,0:T(8,128)} %copy-done.4) | copy-start | bytes 4718596
  511.2 31.6 %copy-start.59 = (f32[4,2,3,128]{3,2,1,0:T(4,128)S(1)}, f32[4,2,3,128]{3,2,1,0:T(4,128)}, u32[]{:S(2)}) copy-start(f32[4,2,3,128]{3,2,1,0:T(4,128)} %copy-done.58) | copy-start | bytes 36868
  556.4 95.7 %reduce-scatter.17.cloned.1.call-start = ((), (), s32[]{:S(2)}) async-start(), calls=%async_computation.14 | async-start | bytes 1966080 | tf_op jit(solution)/shard_map/reduce_scatter | solution.py:49
  562.5 49.4 %collective-permute-start.6 = (f32[2,2,192]{2,0,1:T(2,128)S(1)}, f32[2,2,192]{2,0,1:T(2,128)S(1)}, u32[]{:S(2)}, u32[]{:S(2)}) collective-permute-start(f32[2,2,192]{2,0,1:T(2,128)S(1)} %maximum_add_fusion.1), channel_id=1, source_target_pairs={{0,4},{4,0},{8,12},{12,8},{16,20},{20,16},{24,28},{28,24},{1,5},{5... | collective-permute-start | bytes 9224 | tf_op jit(solution)/shard_map/ppermute | solution.py:102
  569.6 10.6 %collective-permute-start = (bf16[2304,192]{0,1:T(8,128)(2,1)}, bf16[2304,192]{0,1:T(8,128)(2,1)}, u32[]{:S(2)}, u32[]{:S(2)}) collective-permute-start(bf16[2304,192]{0,1:T(8,128)(2,1)} %bitcast.163), channel_id=1, source_target_pairs={{0,4},{4,0},{8,12},{12,8},{16,20},{20,16},{24,28},{28,24},{1,5},{5... | collective-permute-start | bytes 2654216 | tf_op jit(solution)/shard_map/ppermute | solution.py:83
  574.5 9.3 %collective-permute-start.9 = (bf16[192,768]{1,0:T(8,128)(2,1)}, bf16[192,768]{1,0:T(8,128)(2,1)}, u32[]{:S(2)}, u32[]{:S(2)}) collective-permute-start(bf16[192,768]{1,0:T(8,128)(2,1)} %fusion.123), channel_id=1, source_target_pairs={{0,4},{4,0},{8,12},{12,8},{16,20},{20,16},{24,28},{28,24},{1,5},{5... | collective-permute-start | bytes 884744 | tf_op jit(solution)/shard_map/ppermute | solution.py:83
  582.2 13.1 %collective-permute-start.1 = (bf16[1152,192]{0,1:T(8,128)(2,1)S(1)}, bf16[1152,192]{0,1:T(8,128)(2,1)S(1)}, u32[]{:S(2)}, u32[]{:S(2)}) collective-permute-start(bf16[1152,192]{0,1:T(8,128)(2,1)S(1)} %select_convert_fusion.5), channel_id=1, source_target_pairs={{0,8},{4,12},{8,0},{12,4},{16,24},{20,28},{24,16},{28,20},{1,9},{5... | collective-permute-start | bytes 1327112 | tf_op jit(solution)/shard_map/ppermute | solution.py:83
  584.8 27.0 %copy-start.89 = (f32[2,1,192]{2,0,1:T(2,128)S(1)}, f32[2,1,192]{2,0,1:T(2,128)}, u32[]{:S(2)}) copy-start(f32[2,1,192]{2,0,1:T(2,128)} %convolution_bitcast_fusion.20) | copy-start | bytes 4612
  584.8 27.0 %copy-start.90 = (f32[2,1,192]{2,0,1:T(2,128)S(1)}, f32[2,1,192]{2,0,1:T(2,128)}, u32[]{:S(2)}) copy-start(f32[2,1,192]{2,0,1:T(2,128)} %convolution_bitcast_fusion.21) | copy-start | bytes 4612
  584.9 13.1 %collective-permute-start.10 = (bf16[96,768]{1,0:T(8,128)(2,1)S(1)}, bf16[96,768]{1,0:T(8,128)(2,1)S(1)}, u32[]{:S(2)}, u32[]{:S(2)}) collective-permute-start(bf16[96,768]{1,0:T(8,128)(2,1)S(1)} %select_convert_fusion.10), channel_id=1, source_target_pairs={{0,8},{4,12},{8,0},{12,4},{16,24},{20,28},{24,16},{28,20},{1,9},{5... | collective-permute-start | bytes 442376 | tf_op jit(solution)/shard_map/ppermute | solution.py:83
  595.6 7.0 %collective-permute-start.2 = (bf16[576,192]{0,1:T(8,128)(2,1)S(1)}, bf16[576,192]{0,1:T(8,128)(2,1)S(1)}, u32[]{:S(2)}, u32[]{:S(2)}) collective-permute-start(bf16[576,192]{0,1:T(8,128)(2,1)S(1)} %select_convert_fusion.9), channel_id=1, source_target_pairs={{0,16},{4,20},{8,24},{12,28},{16,0},{20,4},{24,8},{28,12},{1,17},{... | collective-permute-start | bytes 663560 | tf_op jit(solution)/shard_map/ppermute | solution.py:83
  603.0 7.0 %collective-permute-start.3 = (bf16[576,192]{0,1:T(8,128)(2,1)S(1)}, bf16[576,192]{0,1:T(8,128)(2,1)S(1)}, u32[]{:S(2)}, u32[]{:S(2)}) collective-permute-start(bf16[576,192]{0,1:T(8,128)(2,1)S(1)} %add_convert_fusion.2), channel_id=1, source_target_pairs={{0,16},{4,20},{8,24},{12,28},{16,0},{20,4},{24,8},{28,12},{1,17},{... | collective-permute-start | bytes 663560 | tf_op jit(solution)/shard_map/ppermute | solution.py:88
  604.6 7.9 %collective-permute-start.11 = (bf16[48,768]{1,0:T(8,128)(2,1)S(1)}, bf16[48,768]{1,0:T(8,128)(2,1)S(1)}, u32[]{:S(2)}, u32[]{:S(2)}) collective-permute-start(bf16[48,768]{1,0:T(8,128)(2,1)S(1)} %select_convert_fusion.11), channel_id=1, source_target_pairs={{0,16},{4,20},{8,24},{12,28},{16,0},{20,4},{24,8},{28,12},{1,17},{... | collective-permute-start | bytes 221192 | tf_op jit(solution)/shard_map/ppermute | solution.py:83
  610.3 9.0 %collective-permute-start.4 = (bf16[1152,192]{0,1:T(8,128)(2,1)S(1)}, bf16[1152,192]{0,1:T(8,128)(2,1)S(1)}, u32[]{:S(2)}, u32[]{:S(2)}) collective-permute-start(bf16[1152,192]{0,1:T(8,128)(2,1)S(1)} %maximum_select_fusion.9), channel_id=1, source_target_pairs={{0,8},{4,12},{8,0},{12,4},{16,24},{20,28},{24,16},{28,20},{1,9},{5... | collective-permute-start | bytes 1327112 | tf_op jit(solution)/shard_map/ppermute | solution.py:88
  611.9 9.3 %collective-permute-start.7 = (f32[2,2,192]{2,0,1:T(2,128)S(1)}, f32[2,2,192]{2,0,1:T(2,128)S(1)}, u32[]{:S(2)}, u32[]{:S(2)}) collective-permute-start(f32[2,2,192]{2,0,1:T(2,128)S(1)} %fusion.277), channel_id=1, source_target_pairs={{0,8},{4,12},{8,0},{12,4},{16,24},{20,28},{24,16},{28,20},{1,9},{5... | collective-permute-start | bytes 9224 | tf_op jit(solution)/shard_map/ppermute | solution.py:102
  612.5 7.1 %collective-permute-start.12 = (bf16[48,768]{1,0:T(8,128)(2,1)S(1)}, bf16[48,768]{1,0:T(8,128)(2,1)S(1)}, u32[]{:S(2)}, u32[]{:S(2)}) collective-permute-start(bf16[48,768]{1,0:T(8,128)(2,1)S(1)} %add_convert_fusion.3), channel_id=1, source_target_pairs={{0,16},{4,20},{8,24},{12,28},{16,0},{20,4},{24,8},{28,12},{1,17},{... | collective-permute-start | bytes 221192 | tf_op jit(solution)/shard_map/ppermute | solution.py:88
  619.5 16.4 %collective-permute-start.5 = (bf16[2304,192]{0,1:T(8,128)(2,1)S(1)}, bf16[2304,192]{0,1:T(8,128)(2,1)S(1)}, u32[]{:S(2)}, u32[]{:S(2)}) collective-permute-start(bf16[2304,192]{0,1:T(8,128)(2,1)S(1)} %maximum_select_fusion.5), channel_id=1, source_target_pairs={{0,4},{4,0},{8,12},{12,8},{16,20},{20,16},{24,28},{28,24},{1,5},{5... | collective-permute-start | bytes 2654216 | tf_op jit(solution)/shard_map/ppermute | solution.py:88
  619.6 6.3 collective-permute-start.13
  621.2 12.8 %collective-permute-start.8 = (f32[2,2,192]{2,0,1:T(2,128)S(1)}, f32[2,2,192]{2,0,1:T(2,128)S(1)}, u32[]{:S(2)}, u32[]{:S(2)}) collective-permute-start(f32[2,2,192]{2,0,1:T(2,128)S(1)} %fusion.279), channel_id=1, source_target_pairs={{0,16},{4,20},{8,24},{12,28},{16,0},{20,4},{24,8},{28,12},{1,17},{... | collective-permute-start | bytes 9224 | tf_op jit(solution)/shard_map/ppermute | solution.py:102
  626.0 8.6 %collective-permute-start.14 = (bf16[192,768]{1,0:T(8,128)(2,1)S(1)}, bf16[192,768]{1,0:T(8,128)(2,1)S(1)}, u32[]{:S(2)}, u32[]{:S(2)}) collective-permute-start(bf16[192,768]{1,0:T(8,128)(2,1)S(1)} %maximum_select_fusion.10), channel_id=1, source_target_pairs={{0,4},{4,0},{8,12},{12,8},{16,20},{20,16},{24,28},{28,24},{1,5},{5... | collective-permute-start | bytes 884744 | tf_op jit(solution)/shard_map/ppermute | solution.py:88
  (124 other events, 702.1 us)
Sparse Core Ops, SparseCore 0:
  10.2 63.3 all-gather.20
  75.7 36.1 all-gather.16
  137.0 44.4 all-gather.22
  183.6 35.8 all-gather.18
  222.2 34.2 reduce-scatter.8
  258.7 34.2 reduce-scatter.6
  298.9 35.8 all-gather.24
  336.3 35.9 all-gather.28
  383.7 34.2 reduce-scatter.14
  420.2 34.2 reduce-scatter.10
  465.8 36.5 all-gather.26
  504.4 35.8 all-gather.30
  556.5 34.3 reduce-scatter.12
  593.6 34.2 reduce-scatter.16

commit v6 on v5

--- a/solution.py
+++ b/solution.py
@@ -111,19 +111,15 @@
     seg_lens,
     row_kind,
     out_rows_w,
-    w_qkv,
-    qv_bias,
-    w_out,
+    selected,
     resid_bias,
     norm_gain,
     norm_shift,
-    w_up,
-    up_bias,
-    w_down,
 ):
+    qkv_sel, qvb_sel, out_sel, up_sel, ubias_sel, down_sel = selected
     n_seg, chains = seg_lens.shape
     seg_rows = chains * CHAIN
-    heads_here = w_qkv.shape[3] // HEAD_DIM
+    heads_here = qkv_sel.shape[3] // HEAD_DIM
     score_scale = HEAD_DIM ** (-0.5)
     highest = lax.Precision.HIGHEST
     seg_hot = (seg_kind[:, None] == jnp.arange(2)[None, :]).astype(jnp.float32)
@@ -137,12 +133,6 @@
 
     key_valid = jnp.arange(CHAIN)[None, None, :] < seg_lens[:, :, None]
 
-    qkv_sel = w_qkv[seg_kind]
-    qvb_sel = qv_bias[seg_kind].astype(jnp.float32)
-    out_sel = w_out[seg_kind]
-    up_sel = w_up[seg_kind]
-    ubias_sel = up_bias[seg_kind].astype(jnp.float32)
-    down_sel = w_down[seg_kind]
 
     input_segs = gather_rows(inputs)
     projected = jnp.einsum(
@@ -253,7 +243,7 @@
     d_key = d_key.reshape(n_seg, seg_rows, -1).astype(jnp.bfloat16)
     d_proj = jnp.stack([d_query, d_key, d_value])
     grad_qkv = jnp.einsum(
-        "strd,jsre->tjde", masked(input_segs, seg_hot), d_proj, preferred_element_type=jnp.float32
+        "strd,jsre->tjed", masked(input_segs, seg_hot), d_proj, preferred_element_type=jnp.float32
     )
     grad_qv = jnp.stack(
         [
@@ -296,13 +286,19 @@
     dev_chains = tok_dev // CHAIN
     chains = dev_chains // STREAMS
     seg_rows = chains * CHAIN
-    weights = (w_qkv, qv_bias, w_out, resid_bias, norm_gain, norm_shift, w_up, up_bias, w_down)
     peer_kind = block_kind[(jnp.arange(n_tensor) * tok_dev) // block_rows]
-    out_rows_w = lax.all_to_all(w_out[peer_kind], "tensor", 0, 0, tiled=True)
+    out_sel = w_out[peer_kind]
+    selected = (
+        w_qkv[peer_kind],
+        qv_bias[peer_kind].astype(jnp.float32),
+        out_sel,
+        w_up[peer_kind],
+        up_bias[peer_kind].astype(jnp.float32),
+        w_down[peer_kind],
+    )
+    out_rows_w = lax.all_to_all(out_sel, "tensor", 0, 0, tiled=True)
     outs, ins, grads, smalls = [], [], [], []
     for part in range(STREAMS):
-        first_row = jnp.arange(n_tensor) * tok_dev + part * seg_rows
-        seg_kind = block_kind[first_row // block_rows]
         chain_ids = (
             jnp.arange(n_tensor)[:, None] * dev_chains + part * chains + jnp.arange(chains)[None, :]
         )
@@ -311,7 +307,16 @@
         row_kind = block_kind[own_rows // block_rows]
         rows = slice(part * seg_rows, (part + 1) * seg_rows)
         out_part, in_part, grad_part, small_part = stream(
-            inputs[rows], cotangent[rows], seg_kind, seg_lens, row_kind, out_rows_w, *weights
+            inputs[rows],
+            cotangent[rows],
+            peer_kind,
+            seg_lens,
+            row_kind,
+            out_rows_w,
+            selected,
+            resid_bias,
+            norm_gain,
+            norm_shift,
         )
         outs.append(out_part)
         ins.append(in_part)
@@ -324,9 +329,18 @@
     )
     small = sum(smalls[1:], smalls[0])
     up_total, down_total = dp_sum_low((grad_up, grad_down))
-    qkv_total, out_total = dp_sum_low((grad_qkv, grad_out_w))
+    qkv_t_total, out_total = dp_sum_low((grad_qkv, grad_out_w))
+    qkv_total = jnp.swapaxes(qkv_t_total, 2, 3)
     (small_grads,) = exact_sum((small,), "tensor")
-    qv_total, ubias_total, small_total = exact_sum((grad_qv, grad_ubias, small_grads), "dp")
+    width = small.shape[-1]
+    packed = jnp.concatenate(
+        [small_grads.reshape(-1, width), grad_ubias.reshape(-1, width), grad_qv.reshape(-1, width)]
+    )
+    (packed,) = exact_sum((packed,), "dp")
+    n_small, n_ubias = small_grads.size // width, grad_ubias.size // width
+    small_total = packed[:n_small].reshape(small_grads.shape)
+    ubias_total = packed[n_small : n_small + n_ubias].reshape(grad_ubias.shape)
+    qv_total = packed[n_small + n_ubias :].reshape(grad_qv.shape)
     return (
         layer_out,
         input_grad,

time: 673 us -> 681 us (1.012)
  waiting for transfers between devices: 278 us -> 318 us
  local copies, waits for them, and re-layouts: 108 us -> 80.3 us
  matrix products: 132 us -> 139 us
    all_gather x8, waiting for transfers between devices: 146 us -> 173 us  [gather_rows(): return lax.all_gather(local_rows, 'tensor', axis=0, tiled=False)]
    all_to_all x2, waiting for transfers between devices: 2.4 us -> 19.9 us  [stream(): mixed_rows = lax.all_to_all(mixed, 'tensor', 0, 0, tiled=True)]
    gather x14 -> x7, local copies, waits for them, and re-layouts: 32.7 us -> 16.2 us  [the longest x1 4.82 us: local(): w_up[peer_kind]]
    reduce_scatter x6, waiting for transfers between devices: 55.3 us -> 63.1 us  [scatter_sum(): lax.psum_scatter(seg_parts.reshape(n_seg * seg_rows, width).astype(jnp.bf...]
    unnamed x279 -> x278, local copies, waits for them, and re-layouts: 19.9 us -> 12.4 us
    convert_element_type x2 -> x0, local copies, waits for them, and re-layouts: 7.38 us -> none  [the longest x1 6.62 us: dp_sum_low(): c.astype(jnp.float32).reshape(shape)]
    select_n x11 -> x12, other arithmetic: 13.6 us -> 16.3 us  [dp_sum_low(): jnp.where(upper, jnp.concatenate([g, c]), jnp.concatenate([c, g]))]
    convert_element_type x2 -> x1, other arithmetic: 14.6 us -> 14.3 us  [stream(): activ = jax.nn.gelu(pre_act, approximate=False).astype(jnp.bfloat16)]
  transfers between devices with their start and end apart: 52 -> 46, of which waited for: 24 -> 24; matrix products, arithmetic and copies ran while one was open for 43% -> 35% of each run, Pallas kernels for 0% -> 0%
where the time goes in v6:
time: 681 us; the launch traced here: 671 us
  waiting for transfers between devices  318 us (47%)
  matrix products  139 us (20%)
  local copies, waits for them, and re-layouts  80.3 us (12%)
  other arithmetic  77.9 us (11%)
  starting transfers between devices  40.4 us (6%)
  between operations  16.5 us (2%)
    all_gather x8, waiting for transfers between devices, gather_rows(): return lax.all_gather(local_rows, 'tensor', axis=0, tiled=False)  173 us
    reduce_scatter x6, waiting for transfers between devices, scatter_sum(): lax.psum_scatter(seg_parts.reshape(n_seg * seg_rows, width).astype(jnp.bf...  63.1 us
    ppermute x12, waiting for transfers between devices, dp_sum_low(): gots = lax.ppermute(sends, 'dp', dp_perm(n_dp, 1 << b))  40.7 us
    all_to_all x2, waiting for transfers between devices, stream(): mixed_rows = lax.all_to_all(mixed, 'tensor', 0, 0, tiled=True)  19.9 us
    select_n x12, other arithmetic, dp_sum_low(): jnp.where(upper, jnp.concatenate([g, c]), jnp.concatenate([c, g]))  16.3 us
    dot_general x12, matrix products, type_sum(): jnp.einsum('rt,rd->td', kind_hot, values, precision=lax.Precision.HIGHEST)  15.6 us
    dot_general x2, matrix products, stream(): jnp.einsum('srd,sfd->srf', two_segs, down_sel, preferred_element_type=jnp...  15.2 us
    dot_general x12, matrix products, pick(): return jnp.dot(kind_hot, kind_table.astype(jnp.float32), precision=highest)  14.4 us
  transfers between devices with their start and end apart: 46, of which 24 were waited for; matrix products, arithmetic and copies ran while one was open for 35% of the time, Pallas kernels for 0%

profile of v6, /device:TPU:0, one launch (start us, length us, event | category | flops | bytes accessed | tf_op | source)
XLA Modules:
  0.0 671.3 jit_solution(3279082882833389378)
XLA Ops:
  13.0 6.3 all-to-all-start.1
  25.3 4.1 gather_fusion.1
  29.3 2.4 compare_select_fusion.4
  34.2 39.4 %all-gather.21.cloned.1.call-done = bf16[1024,768]{1,0:T(8,128)(2,1)} async-done(((bf16[256,768]{1,0:T(8,128)(2,1)}), bf16[1024,768]{1,0:T(8,128)(2,1)}) %all-gather.21.cloned.1.call-update) | async-done | bytes 1572880 | tf_op jit(solution)/shard_map/all_gather | solution.py:44
  73.5 3.6 convolution_bitcast_fusion
  78.7 2.4 fusion.211
  90.7 21.1 %all-gather.17.cloned.1.call-done = bf16[1024,768]{1,0:T(8,128)(2,1)} async-done(((bf16[256,768]{1,0:T(8,128)(2,1)}), bf16[1024,768]{1,0:T(8,128)(2,1)}) %all-gather.17.cloned.1.call-update) | async-done | bytes 1572880 | tf_op jit(solution)/shard_map/all_gather | solution.py:44
  111.8 5.0 convolution_bitcast_fusion.1
  116.8 4.1 all-to-all-start.2
  121.0 2.6 fusion.210
  144.5 4.2 all-to-all-start
  148.8 2.4 compare_select_fusion.7
  152.2 19.1 %all-to-all-done = bf16[4,256,192]{1,2,0:T(8,128)(2,1)} async-done(((bf16[4,256,192]{1,2,0:T(8,128)(2,1)}), bf16[4,256,192]{1,2,0:T(8,128)(2,1)}, u32[]{:S(2)}, u32[]{:S(2)}) %all-to-all-start) | async-done | bytes 393248 | tf_op jit(solution)/shard_map/all_to_all | solution.py:166
  176.8 3.2 gather_fusion.7
  180.0 4.8 gather_fusion.5
  184.8 5.9 fusion.226
  190.7 30.9 %all-gather.19.cloned.1.call-done = bf16[1024,768]{1,0:T(8,128)(2,1)} async-done(((bf16[256,768]{1,0:T(8,128)(2,1)}), bf16[1024,768]{1,0:T(8,128)(2,1)}) %all-gather.19.cloned.1.call-update) | async-done | bytes 1572880 | tf_op jit(solution)/shard_map/all_gather | solution.py:44
  221.6 7.0 %fusion.92 = (u8[256,768]{1,0:T(8,128)(4,1)S(1)}, u8[256,768]{1,0:T(8,128)(4,1)S(1)}, u8[256,768]{1,0:T(8,128)(4,1)S(1)}, u8[256,768]{1,0:T(8,128)(4,1)S(1)}, f32[4,256,768]{2,1,0:T(8,128)S(1)}) fusion(f32[4,768]{1,0:T(4,128)S(1)} %convert_element_type.493, f32[4,256,768]{2,1,0:T(8,128)} %fusion.226, bf16[4,256,768]{2,1,0:T(8,128)(2,1)} %bitcast.359, ...), kind=kOutput, calls=%fused_computation.240 | convolution fusion | flops 1229193216 | bytes 13381632 | tf_op jit(solution)/shard_map/srd,sdf->srf/dot_general | solution.py:177
  228.6 14.3 %fusion.3 = (bf16[4,256,768]{2,1,0:T(8,128)(2,1)S(1)}, bf16[4,256,768]{2,1,0:T(8,128)(2,1)S(1)}) fusion(f32[4,256,768]{2,1,0:T(8,128)S(1)} %get-tuple-element.74, f32[4,768]{1,0:T(4,128)S(1)} %convert_element_type.493, u8[256,768]{1,0:T(8,128)(4,1)S(1)} %get-tuple-element.12, u8[256,768]{1,0:T(8,128)(4,1)S(1)} %get-tuple-element.11, ...), kind=kLoop, calls=%fused_computation.20 | loop fusion | flops 110886912 | bytes 10235904 | tf_op jit(solution)/shard_map/convert_element_type | solution.py:180
  243.0 2.6 convolution_convert_fusion.5
  245.7 4.9 convolution_convert_fusion.4
  251.2 28.9 %reduce-scatter.7.cloned.1.call-done = bf16[256,768]{1,0:T(8,128)(2,1)} async-done(((bf16[1024,768]{1,0:T(8,128)(2,1)}), bf16[256,768]{1,0:T(8,128)(2,1)}) %reduce-scatter.7.cloned.1.call-update) | async-done | bytes 393232 | tf_op jit(solution)/shard_map/reduce_scatter | solution.py:49
  282.4 34.2 %reduce-scatter.9.cloned.1.call-done = bf16[256,768]{1,0:T(8,128)(2,1)} async-done(((bf16[1024,768]{1,0:T(8,128)(2,1)}), bf16[256,768]{1,0:T(8,128)(2,1)}) %reduce-scatter.9.cloned.1.call-update) | async-done | bytes 393232 | tf_op jit(solution)/shard_map/reduce_scatter | solution.py:49
  319.9 2.8 fusion.206
  328.4 2.6 copy.91
  331.0 2.6 copy.88
  333.6 2.6 copy.96
  336.2 2.6 copy.97
  338.8 2.6 copy.98
  341.4 2.6 copy.99
  348.3 10.4 %all-gather.25.cloned.1.call-done = bf16[1024,768]{1,0:T(8,128)(2,1)} async-done(((bf16[256,768]{1,0:T(8,128)(2,1)}), bf16[1024,768]{1,0:T(8,128)(2,1)}) %all-gather.25.cloned.1.call-update) | async-done | bytes 1572880 | tf_op jit(solution)/shard_map/all_gather | solution.py:44
  358.7 7.5 %convert_reduce_fusion.1 = (f32[4,768]{1,0:T(4,128)}, bf16[4,256,768]{2,1,0:T(8,128)(2,1)}) fusion(f32[4,256,768]{2,1,0:T(8,128)} %copy-done.44, f32[4,768]{1,0:T(4,128)} %copy-done.92, bf16[4,256,768]{2,1,0:T(8,128)(2,1)} %bitcast.405, bf16[4,768,768]{2,1,0:T(8,128)(2,1)} %gather_fusion.7), kind=kOutput, calls=%fused_computation.58 | convolution fusion | flops 1219752960 | bytes 11034624 | tf_op jit(solution)/shard_map/srd,sfd->srf/dot_general | solution.py:195
  366.3 29.9 %all-gather.29.cloned.1.call-done = bf16[1024,768]{1,0:T(8,128)(2,1)} async-done(((bf16[256,768]{1,0:T(8,128)(2,1)}), bf16[1024,768]{1,0:T(8,128)(2,1)}) %all-gather.29.cloned.1.call-update) | async-done | bytes 1572880 | tf_op jit(solution)/shard_map/all_gather | solution.py:44
  396.2 7.6 %convert_reduce_fusion = (f32[4,768]{1,0:T(4,128)}, bf16[4,256,768]{2,1,0:T(8,128)(2,1)}) fusion(f32[4,256,768]{2,1,0:T(8,128)} %fusion.226, f32[4,768]{1,0:T(4,128)} %copy-done.92, bf16[4,256,768]{2,1,0:T(8,128)(2,1)} %bitcast.407, bf16[4,768,768]{2,1,0:T(8,128)(2,1)} %gather_fusion.7), kind=kOutput, calls=%fused_computation.57 | convolution fusion | flops 1219752960 | bytes 11034624 | tf_op jit(solution)/shard_map/srd,sfd->srf/dot_general | solution.py:195
  403.8 4.9 convolution_convert_fusion.2
  409.3 4.7 fusion.25
  414.0 2.9 bitcast_add_fusion.1
  418.8 2.7 fusion.21
  421.5 2.8 bitcast_add_fusion
  435.2 2.6 convolution_convert_fusion
  437.8 9.7 %collective-permute-done.18 = bf16[384,768]{1,0:T(8,128)(2,1)S(1)} collective-permute-done((bf16[384,768]{1,0:T(8,128)(2,1)}, bf16[384,768]{1,0:T(8,128)(2,1)S(1)}, u32[]{:S(2)}, u32[]{:S(2)}) %collective-permute-start.18) | collective-permute-done | bytes 589856 | tf_op jit(solution)/shard_map/ppermute | solution.py:83
  451.0 8.0 %collective-permute-done.24 = bf16[384,768]{1,0:T(8,128)(2,1)S(1)} collective-permute-done((bf16[384,768]{1,0:T(8,128)(2,1)}, bf16[384,768]{1,0:T(8,128)(2,1)S(1)}, u32[]{:S(2)}, u32[]{:S(2)}) %collective-permute-start.24) | collective-permute-done | bytes 589856 | tf_op jit(solution)/shard_map/ppermute | solution.py:83
  461.7 7.5 %collective-permute-done.25 = bf16[192,768]{1,0:T(8,128)(2,1)S(1)} collective-permute-done((bf16[192,768]{1,0:T(8,128)(2,1)S(1)}, bf16[192,768]{1,0:T(8,128)(2,1)S(1)}, u32[]{:S(2)}, u32[]{:S(2)}) %collective-permute-start.25) | collective-permute-done | bytes 294944 | tf_op jit(solution)/shard_map/ppermute | solution.py:83
  471.6 3.9 collective-permute-done.20
  499.9 2.9 maximum_select_fusion.3
  503.1 2.7 collective-permute-done.6
  506.1 2.9 maximum_select_fusion.4
  509.1 4.4 collective-permute-done.7
  514.3 12.5 %all-gather.27.cloned.1.call-done = bf16[1024,768]{1,0:T(8,128)(2,1)} async-done(((bf16[256,768]{1,0:T(8,128)(2,1)}), bf16[1024,768]{1,0:T(8,128)(2,1)}) %all-gather.27.cloned.1.call-update) | async-done | bytes 1572880 | tf_op jit(solution)/shard_map/all_gather | solution.py:44
  526.7 2.4 convolution_convert_fusion.11
  536.2 28.5 %all-gather.31.cloned.1.call-done = bf16[1024,768]{1,0:T(8,128)(2,1)} async-done(((bf16[256,768]{1,0:T(8,128)(2,1)}), bf16[1024,768]{1,0:T(8,128)(2,1)}) %all-gather.31.cloned.1.call-update) | async-done | bytes 1572880 | tf_op jit(solution)/shard_map/all_gather | solution.py:44
  564.6 3.2 convolution_convert_fusion.10
  576.8 4.7 bitcast_convert_fusion
  585.0 3.8 fusion.17
  599.0 2.7 bitcast_convert_fusion.1
  608.9 9.9 %collective-permute-done.1 = bf16[288,768]{1,0:T(8,128)(2,1)S(1)} collective-permute-done((bf16[288,768]{1,0:T(8,128)(2,1)S(1)}, bf16[288,768]{1,0:T(8,128)(2,1)S(1)}, u32[]{:S(2)}, u32[]{:S(2)}) %collective-permute-start.1) | collective-permute-done | bytes 442400 | tf_op jit(solution)/shard_map/ppermute | solution.py:83
  620.9 4.6 collective-permute-done.2
  627.7 4.3 collective-permute-done.3
  634.6 2.9 maximum_select_fusion
  639.5 2.4 collective-permute-done.4
  642.4 2.7 maximum_select_fusion.1
  645.0 2.5 convert.15
  647.6 2.5 convert.16
  659.4 2.3 convert_add_fusion.3
  (564 shorter events, 173.2 us)
Async XLA Ops:
  7.2 169.6 %copy-start = (bf16[2,768,768]{2,1,0:T(8,128)(2,1)S(1)}, bf16[2,768,768]{2,1,0:T(8,128)(2,1)}, u32[]{:S(2)}) copy-start(bf16[2,768,768]{2,1,0:T(8,128)(2,1)} %param.25) | copy-start | bytes 7077892
  7.2 66.3 %all-gather.21.cloned.1.call-start = ((), (), s32[]{:S(2)}) async-start(), calls=%async_computation.17 | async-start | bytes 1966080 | tf_op jit(solution)/shard_map/all_gather | solution.py:44
  13.0 103.8 %all-to-all-start.1 = ((bf16[4,192,768]{2,1,0:T(8,128)(2,1)}), bf16[4,192,768]{2,1,0:T(8,128)(2,1)}, u32[]{:S(2)}, u32[]{:S(2)}) async-start(bf16[4,192,768]{2,1,0:T(8,128)(2,1)} %gather_fusion.4), calls=%async_computation.1 | async-start | bytes 2359296 | tf_op jit(solution)/shard_map/all_to_all | solution.py:299
  19.4 92.5 %all-gather.17.cloned.1.call-start = ((), (), s32[]{:S(2)}) async-start(), calls=%async_computation.15 | async-start | bytes 1966080 | tf_op jit(solution)/shard_map/all_gather | solution.py:44
  23.9 62.2 %copy-start.72 = (f32[4,3,64]{2,1,0:T(4,128)}, f32[4,3,64]{2,1,0:T(4,128)S(1)}, u32[]{:S(2)}) copy-start(f32[4,3,64]{2,1,0:T(4,128)S(1)} %add.423) | copy-start | bytes 9220
  24.0 103.2 %copy-start.69 = (f32[4,3,64]{2,1,0:T(4,128)}, f32[4,3,64]{2,1,0:T(4,128)S(1)}, u32[]{:S(2)}) copy-start(f32[4,3,64]{2,1,0:T(4,128)S(1)} %add.430) | copy-start | bytes 9220
  116.8 15.3 %all-to-all-start.2 = ((bf16[4,256,192]{1,2,0:T(8,128)(2,1)}), bf16[4,256,192]{1,2,0:T(8,128)(2,1)}, u32[]{:S(2)}, u32[]{:S(2)}) async-start(bf16[4,256,192]{1,2,0:T(8,128)(2,1)} %convert_element_type.506), calls=%async_computation.3 | async-start | bytes 786432 | tf_op jit(solution)/shard_map/all_to_all | solution.py:166
  121.0 63.8 %all-gather.23.cloned.1.call-start = ((), (), s32[]{:S(2)}) async-start(), calls=%async_computation.18 | async-start | bytes 1966080 | tf_op jit(solution)/shard_map/all_gather | solution.py:44
  144.5 26.8 %all-to-all-start = ((bf16[4,256,192]{1,2,0:T(8,128)(2,1)}), bf16[4,256,192]{1,2,0:T(8,128)(2,1)}, u32[]{:S(2)}, u32[]{:S(2)}) async-start(bf16[4,256,192]{1,2,0:T(8,128)(2,1)} %convert_element_type.491), calls=%async_computation | async-start | bytes 786432 | tf_op jit(solution)/shard_map/all_to_all | solution.py:166
  148.6 72.9 %all-gather.19.cloned.1.call-start = ((), (), s32[]{:S(2)}) async-start(), calls=%async_computation.16 | async-start | bytes 1966080 | tf_op jit(solution)/shard_map/all_gather | solution.py:44
  151.2 331.2 %copy-start.89 = (s32[256,1]{0,1:T(1,128)}, s32[256,1]{0,1:T(1,128)S(1)}, u32[]{:S(2)}) copy-start(s32[256,1]{0,1:T(1,128)S(1)} %compare_select_fusion.7) | copy-start | bytes 3076
  152.2 21.8 %copy-start.32 = (f32[256,768]{1,0:T(8,128)}, f32[256,768]{1,0:T(8,128)S(1)}, u32[]{:S(2)}) copy-start(f32[256,768]{1,0:T(8,128)S(1)} %fusion.134) | copy-start | bytes 2359300
  152.2 22.4 %copy-start.112 = (bf16[2,1,768]{2,1,0:T(2,128)(2,1)S(1)}, bf16[2,1,768]{2,1,0:T(2,128)(2,1)}, u32[]{:S(2)}) copy-start(bf16[2,1,768]{2,1,0:T(2,128)(2,1)} %get-tuple-element.53) | copy-start | bytes 9220
  176.0 104.1 %reduce-scatter.7.cloned.1.call-start = ((), (), s32[]{:S(2)}) async-start(), calls=%async_computation.9 | async-start | bytes 1966080 | tf_op jit(solution)/shard_map/reduce_scatter | solution.py:49
  176.8 51.8 %copy-start.92 = (f32[4,768]{1,0:T(4,128)}, f32[4,768]{1,0:T(4,128)S(1)}, u32[]{:S(2)}) copy-start(f32[4,768]{1,0:T(4,128)S(1)} %convert_element_type.493) | copy-start | bytes 36868
  184.8 58.2 %slice-start = ((s8[4718592]{0:T(1024)(128)(4,1)}), s8[524288]{0:T(1024)(128)(4,1)S(1)}, s32[]{:S(2)}) async-start(s8[4718592]{0:T(1024)(128)(4,1)} %bitcast.339), calls=%async_computation.23 | async-start | bytes 1048576
  221.5 21.4 %slice-start.1 = ((s8[4718592]{0:T(1024)(128)(4,1)}), s8[4194304]{0:T(1024)(128)(4,1)S(1)}, s32[]{:S(2)}) async-start(s8[4718592]{0:T(1024)(128)(4,1)} %bitcast.339), calls=%async_computation.24 | async-start | bytes 8388608
  245.6 70.9 %reduce-scatter.9.cloned.1.call-start = ((), (), s32[]{:S(2)}) async-start(), calls=%async_computation.10 | async-start | bytes 1966080 | tf_op jit(solution)/shard_map/reduce_scatter | solution.py:49
  250.6 29.5 %copy-start.43 = (f32[256,768]{1,0:T(8,128)S(1)}, f32[256,768]{1,0:T(8,128)}, u32[]{:S(2)}) copy-start(f32[256,768]{1,0:T(8,128)} %get-tuple-element.71) | copy-start | bytes 2359300
  250.6 108.1 %all-gather.25.cloned.1.call-start = ((), (), s32[]{:S(2)}) async-start(), calls=%async_computation.19 | async-start | bytes 1966080 | tf_op jit(solution)/shard_map/all_gather | solution.py:44
  251.2 67.3 %copy-start.18 = (f32[256,768]{1,0:T(8,128)}, f32[256,768]{1,0:T(8,128)S(1)}, u32[]{:S(2)}) copy-start(f32[256,768]{1,0:T(8,128)S(1)} %fusion.131) | copy-start | bytes 2359300
  280.1 38.4 %copy-start.38 = (bf16[512,768]{1,0:T(8,128)(2,1)S(1)}, bf16[512,768]{1,0:T(8,128)(2,1)}, u32[]{:S(2)}) copy-start(bf16[512,768]{1,0:T(8,128)(2,1)} %param.14) | copy-start | bytes 2359300
  322.7 73.5 %all-gather.29.cloned.1.call-start = ((), (), s32[]{:S(2)}) async-start(), calls=%async_computation.21 | async-start | bytes 1966080 | tf_op jit(solution)/shard_map/all_gather | solution.py:44
  323.4 158.9 %reduce-scatter.11.cloned.1.call-start = ((), (), s32[]{:S(2)}) async-start(), calls=%async_computation.11 | async-start | bytes 1966080 | tf_op jit(solution)/shard_map/reduce_scatter | solution.py:49
  408.8 84.0 %reduce-scatter.15.cloned.1.call-start = ((), (), s32[]{:S(2)}) async-start(), calls=%async_computation.13 | async-start | bytes 1966080 | tf_op jit(solution)/shard_map/reduce_scatter | solution.py:49
  417.1 12.5 %collective-permute-start.17 = (bf16[768,768]{1,0:T(8,128)(2,1)S(1)}, bf16[768,768]{1,0:T(8,128)(2,1)S(1)}, u32[]{:S(2)}, u32[]{:S(2)}) collective-permute-start(bf16[768,768]{1,0:T(8,128)(2,1)S(1)} %fusion.78), channel_id=1, source_target_pairs={{0,4},{4,0},{8,12},{12,8},{16,20},{20,16},{24,28},{28,24},{1,5},{5... | collective-permute-start | bytes 3538952 | tf_op jit(solution)/shard_map/ppermute | solution.py:83
  424.5 8.1 %collective-permute-start.23 = (bf16[768,768]{1,0:T(8,128)(2,1)S(1)}, bf16[768,768]{1,0:T(8,128)(2,1)S(1)}, u32[]{:S(2)}, u32[]{:S(2)}) collective-permute-start(bf16[768,768]{1,0:T(8,128)(2,1)S(1)} %fusion.79), channel_id=1, source_target_pairs={{0,4},{4,0},{8,12},{12,8},{16,20},{20,16},{24,28},{28,24},{1,5},{5... | collective-permute-start | bytes 3538952 | tf_op jit(solution)/shard_map/ppermute | solution.py:83
  431.0 16.6 %collective-permute-start.18 = (bf16[384,768]{1,0:T(8,128)(2,1)}, bf16[384,768]{1,0:T(8,128)(2,1)S(1)}, u32[]{:S(2)}, u32[]{:S(2)}) collective-permute-start(bf16[384,768]{1,0:T(8,128)(2,1)} %select_convert_fusion.4), channel_id=1, source_target_pairs={{0,8},{4,12},{8,0},{12,4},{16,24},{20,28},{24,16},{28,20},{1,9},{5... | collective-permute-start | bytes 1769480 | tf_op jit(solution)/shard_map/ppermute | solution.py:83
  434.6 24.4 %collective-permute-start.24 = (bf16[384,768]{1,0:T(8,128)(2,1)}, bf16[384,768]{1,0:T(8,128)(2,1)S(1)}, u32[]{:S(2)}, u32[]{:S(2)}) collective-permute-start(bf16[384,768]{1,0:T(8,128)(2,1)} %select_convert_fusion.3), channel_id=1, source_target_pairs={{0,8},{4,12},{8,0},{12,4},{16,24},{20,28},{24,16},{28,20},{1,9},{5... | collective-permute-start | bytes 1769480 | tf_op jit(solution)/shard_map/ppermute | solution.py:83
  437.8 89.0 %all-gather.27.cloned.1.call-start = ((), (), s32[]{:S(2)}) async-start(), calls=%async_computation.20 | async-start | bytes 1966080 | tf_op jit(solution)/shard_map/all_gather | solution.py:44
  437.8 21.1 %copy-start.15 = (f32[768,768]{1,0:T(8,128)S(1)}, f32[768,768]{1,0:T(8,128)}, u32[]{:S(2)}) copy-start(f32[768,768]{1,0:T(8,128)} %copy-done.14) | copy-start | bytes 7077892
  449.5 11.5 %collective-permute-start.19 = (bf16[192,768]{1,0:T(8,128)(2,1)S(1)}, bf16[192,768]{1,0:T(8,128)(2,1)S(1)}, u32[]{:S(2)}, u32[]{:S(2)}) collective-permute-start(bf16[192,768]{1,0:T(8,128)(2,1)S(1)} %select_convert_fusion.7), channel_id=1, source_target_pairs={{0,16},{4,20},{8,24},{12,28},{16,0},{20,4},{24,8},{28,12},{1,17},{... | collective-permute-start | bytes 884744 | tf_op jit(solution)/shard_map/ppermute | solution.py:83
  459.3 9.9 %collective-permute-start.25 = (bf16[192,768]{1,0:T(8,128)(2,1)S(1)}, bf16[192,768]{1,0:T(8,128)(2,1)S(1)}, u32[]{:S(2)}, u32[]{:S(2)}) collective-permute-start(bf16[192,768]{1,0:T(8,128)(2,1)S(1)} %select_convert_fusion.6), channel_id=1, source_target_pairs={{0,16},{4,20},{8,24},{12,28},{16,0},{20,4},{24,8},{28,12},{1,17},{... | collective-permute-start | bytes 884744 | tf_op jit(solution)/shard_map/ppermute | solution.py:83
  461.1 23.5 %copy-start.12 = (f32[256,768]{1,0:T(8,128)S(1)}, f32[256,768]{1,0:T(8,128)}, u32[]{:S(2)}) copy-start(f32[256,768]{1,0:T(8,128)} %copy-done.11) | copy-start | bytes 2359300
  461.1 23.5 %copy-start.33 = (f32[256,768]{1,0:T(8,128)S(1)}, f32[256,768]{1,0:T(8,128)}, u32[]{:S(2)}) copy-start(f32[256,768]{1,0:T(8,128)} %copy-done.32) | copy-start | bytes 2359300
  461.1 14.4 %collective-permute-start.20 = (bf16[192,768]{1,0:T(8,128)(2,1)S(1)}, bf16[192,768]{1,0:T(8,128)(2,1)S(1)}, u32[]{:S(2)}, u32[]{:S(2)}) collective-permute-start(bf16[192,768]{1,0:T(8,128)(2,1)S(1)} %add_convert_fusion.1), channel_id=1, source_target_pairs={{0,16},{4,20},{8,24},{12,28},{16,0},{20,4},{24,8},{28,12},{1,17},{... | collective-permute-start | bytes 884744 | tf_op jit(solution)/shard_map/ppermute | solution.py:88
  469.3 10.5 %collective-permute-start.26 = (bf16[192,768]{1,0:T(8,128)(2,1)S(1)}, bf16[192,768]{1,0:T(8,128)(2,1)S(1)}, u32[]{:S(2)}, u32[]{:S(2)}) collective-permute-start(bf16[192,768]{1,0:T(8,128)(2,1)S(1)} %add_convert_fusion), channel_id=1, source_target_pairs={{0,16},{4,20},{8,24},{12,28},{16,0},{20,4},{24,8},{28,12},{1,17},{... | collective-permute-start | bytes 884744 | tf_op jit(solution)/shard_map/ppermute | solution.py:88
  476.6 23.3 %collective-permute-start.21 = (bf16[384,768]{1,0:T(8,128)(2,1)}, bf16[384,768]{1,0:T(8,128)(2,1)}, u32[]{:S(2)}, u32[]{:S(2)}) collective-permute-start(bf16[384,768]{1,0:T(8,128)(2,1)} %maximum_select_fusion.7), channel_id=1, source_target_pairs={{0,8},{4,12},{8,0},{12,4},{16,24},{20,28},{24,16},{28,20},{1,9},{5... | collective-permute-start | bytes 1769480 | tf_op jit(solution)/shard_map/ppermute | solution.py:88
  480.9 25.2 %collective-permute-start.27 = (bf16[384,768]{1,0:T(8,128)(2,1)}, bf16[384,768]{1,0:T(8,128)(2,1)}, u32[]{:S(2)}, u32[]{:S(2)}) collective-permute-start(bf16[384,768]{1,0:T(8,128)(2,1)} %maximum_select_fusion.8), channel_id=1, source_target_pairs={{0,8},{4,12},{8,0},{12,4},{16,24},{20,28},{24,16},{28,20},{1,9},{5... | collective-permute-start | bytes 1769480 | tf_op jit(solution)/shard_map/ppermute | solution.py:88
  484.5 21.3 %copy-start.74 = (f32[1,2,2,768]{3,1,2,0:T(2,128)}, f32[1,2,2,768]{3,1,2,0:T(2,128)S(1)}, u32[]{:S(2)}) copy-start(f32[1,2,2,768]{3,1,2,0:T(2,128)S(1)} %maximum_bitcast_fusion.2) | copy-start | bytes 36868
  489.6 75.0 %all-gather.31.cloned.1.call-start = ((), (), s32[]{:S(2)}) async-start(), calls=%async_computation.22 | async-start | bytes 1966080 | tf_op jit(solution)/shard_map/all_gather | solution.py:44
  499.3 6.5 collective-permute-start.6
  502.8 131.8 %collective-permute-start.22 = (bf16[768,768]{1,0:T(8,128)(2,1)}, bf16[768,768]{1,0:T(8,128)(2,1)}, u32[]{:S(2)}, u32[]{:S(2)}) collective-permute-start(bf16[768,768]{1,0:T(8,128)(2,1)} %maximum_select_fusion.3), channel_id=1, source_target_pairs={{0,4},{4,0},{8,12},{12,8},{16,20},{20,16},{24,28},{28,24},{1,5},{5... | collective-permute-start | bytes 3538952 | tf_op jit(solution)/shard_map/ppermute | solution.py:88
  502.8 156.6 %reduce-scatter.17.cloned.1.call-start = ((), (), s32[]{:S(2)}) async-start(), calls=%async_computation.14 | async-start | bytes 1966080 | tf_op jit(solution)/shard_map/reduce_scatter | solution.py:49
  505.9 7.6 %collective-permute-start.7 = (f32[3,2,2,768]{3,1,2,0:T(2,128)S(1)}, f32[3,2,2,768]{3,1,2,0:T(2,128)S(1)}, u32[]{:S(2)}, u32[]{:S(2)}) collective-permute-start(f32[3,2,2,768]{3,1,2,0:T(2,128)S(1)} %fusion.276), channel_id=1, source_target_pairs={{0,2},{1,3},{2,0},{3,1},{4,6},{5,7},{6,4},{7,5},{8,10},{9,11},{10,... | collective-permute-start | bytes 110600 | tf_op jit(solution)/shard_map/ppermute | solution.py:102
  509.0 133.3 %collective-permute-start.28 = (bf16[768,768]{1,0:T(8,128)(2,1)}, bf16[768,768]{1,0:T(8,128)(2,1)}, u32[]{:S(2)}, u32[]{:S(2)}) collective-permute-start(bf16[768,768]{1,0:T(8,128)(2,1)} %maximum_select_fusion.4), channel_id=1, source_target_pairs={{0,4},{4,0},{8,12},{12,8},{16,20},{20,16},{24,28},{28,24},{1,5},{5... | collective-permute-start | bytes 3538952 | tf_op jit(solution)/shard_map/ppermute | solution.py:88
  536.2 32.8 %copy-start.5 = (f32[4,2,3,128,128]{3,4,2,1,0:T(8,128)S(1)}, f32[4,2,3,128,128]{3,4,2,1,0:T(8,128)}, u32[]{:S(2)}) copy-start(f32[4,2,3,128,128]{3,4,2,1,0:T(8,128)} %copy-done.4) | copy-start | bytes 4718596
  536.2 32.8 %copy-start.60 = (f32[4,2,3,128]{3,2,1,0:T(4,128)S(1)}, f32[4,2,3,128]{3,2,1,0:T(4,128)}, u32[]{:S(2)}) copy-start(f32[4,2,3,128]{3,2,1,0:T(4,128)} %copy-done.59) | copy-start | bytes 36868
  581.5 80.2 %reduce-scatter.13.cloned.1.call-start = ((), (), s32[]{:S(2)}) async-start(), calls=%async_computation.12 | async-start | bytes 1966080 | tf_op jit(solution)/shard_map/reduce_scatter | solution.py:49
  584.9 17.3 %collective-permute-start.8 = (f32[15,768]{1,0:T(8,128)S(1)}, f32[15,768]{1,0:T(8,128)S(1)}, u32[]{:S(2)}, u32[]{:S(2)}) collective-permute-start(f32[15,768]{1,0:T(8,128)S(1)} %pad_maximum_fusion.6), channel_id=1, source_target_pairs={{0,4},{4,0},{8,12},{12,8},{16,20},{20,16},{24,28},{28,24},{1,5},{5... | collective-permute-start | bytes 138248 | tf_op jit(solution)/shard_map/ppermute | solution.py:102
  592.1 11.6 %collective-permute-start = (bf16[576,768]{1,0:T(8,128)(2,1)}, bf16[576,768]{1,0:T(8,128)(2,1)}, u32[]{:S(2)}, u32[]{:S(2)}) collective-permute-start(bf16[576,768]{1,0:T(8,128)(2,1)} %bitcast.59), channel_id=1, source_target_pairs={{0,4},{4,0},{8,12},{12,8},{16,20},{20,16},{24,28},{28,24},{1,5},{5... | collective-permute-start | bytes 2654216 | tf_op jit(solution)/shard_map/ppermute | solution.py:83
  601.7 4.6 collective-permute-start.11
  602.2 35.4 %collective-permute-start.9 = (f32[15,768]{1,0:T(8,128)S(1)}, f32[15,768]{1,0:T(8,128)S(1)}, u32[]{:S(2)}, u32[]{:S(2)}) collective-permute-start(f32[15,768]{1,0:T(8,128)S(1)} %fusion.275), channel_id=1, source_target_pairs={{0,8},{4,12},{8,0},{12,4},{16,24},{20,28},{24,16},{28,20},{1,9},{5... | collective-permute-start | bytes 138248 | tf_op jit(solution)/shard_map/ppermute | solution.py:102
  605.6 13.1 %collective-permute-start.1 = (bf16[288,768]{1,0:T(8,128)(2,1)S(1)}, bf16[288,768]{1,0:T(8,128)(2,1)S(1)}, u32[]{:S(2)}, u32[]{:S(2)}) collective-permute-start(bf16[288,768]{1,0:T(8,128)(2,1)S(1)} %select_convert_fusion.5), channel_id=1, source_target_pairs={{0,8},{4,12},{8,0},{12,4},{16,24},{20,28},{24,16},{28,20},{1,9},{5... | collective-permute-start | bytes 1327112 | tf_op jit(solution)/shard_map/ppermute | solution.py:83
  607.5 13.4 %collective-permute-start.12 = (bf16[96,768]{1,0:T(8,128)(2,1)S(1)}, bf16[96,768]{1,0:T(8,128)(2,1)S(1)}, u32[]{:S(2)}, u32[]{:S(2)}) collective-permute-start(bf16[96,768]{1,0:T(8,128)(2,1)S(1)} %select_convert_fusion.10), channel_id=1, source_target_pairs={{0,8},{4,12},{8,0},{12,4},{16,24},{20,28},{24,16},{28,20},{1,9},{5... | collective-permute-start | bytes 442376 | tf_op jit(solution)/shard_map/ppermute | solution.py:83
  618.9 6.5 collective-permute-start.2
  625.5 6.5 collective-permute-start.3
  627.0 6.1 collective-permute-start.13
  632.2 9.8 %collective-permute-start.4 = (bf16[288,768]{1,0:T(8,128)(2,1)S(1)}, bf16[288,768]{1,0:T(8,128)(2,1)S(1)}, u32[]{:S(2)}, u32[]{:S(2)}) collective-permute-start(bf16[288,768]{1,0:T(8,128)(2,1)S(1)} %maximum_select_fusion.9), channel_id=1, source_target_pairs={{0,8},{4,12},{8,0},{12,4},{16,24},{20,28},{24,16},{28,20},{1,9},{5... | collective-permute-start | bytes 1327112 | tf_op jit(solution)/shard_map/ppermute | solution.py:88
  633.1 5.1 collective-permute-start.14
  637.6 12.5 %collective-permute-start.10 = (f32[15,768]{1,0:T(8,128)S(1)}, f32[15,768]{1,0:T(8,128)S(1)}, u32[]{:S(2)}, u32[]{:S(2)}) collective-permute-start(f32[15,768]{1,0:T(8,128)S(1)} %add.489), channel_id=1, source_target_pairs={{0,16},{4,20},{8,24},{12,28},{16,0},{20,4},{24,8},{28,12},{1,17},{... | collective-permute-start | bytes 138248 | tf_op jit(solution)/shard_map/ppermute | solution.py:102
  638.3 12.4 %collective-permute-start.15 = (bf16[96,768]{1,0:T(8,128)(2,1)S(1)}, bf16[96,768]{1,0:T(8,128)(2,1)S(1)}, u32[]{:S(2)}, u32[]{:S(2)}) collective-permute-start(bf16[96,768]{1,0:T(8,128)(2,1)S(1)} %maximum_select_fusion.11), channel_id=1, source_target_pairs={{0,8},{4,12},{8,0},{12,4},{16,24},{20,28},{24,16},{28,20},{1,9},{5... | collective-permute-start | bytes 442376 | tf_op jit(solution)/shard_map/ppermute | solution.py:88
  642.3 12.9 %collective-permute-start.5 = (bf16[576,768]{1,0:T(8,128)(2,1)S(1)}, bf16[576,768]{1,0:T(8,128)(2,1)}, u32[]{:S(2)}, u32[]{:S(2)}) collective-permute-start(bf16[576,768]{1,0:T(8,128)(2,1)S(1)} %maximum_select_fusion.5), channel_id=1, source_target_pairs={{0,4},{4,0},{8,12},{12,8},{16,20},{20,16},{24,28},{28,24},{1,5},{5... | collective-permute-start | bytes 2654216 | tf_op jit(solution)/shard_map/ppermute | solution.py:88
  650.8 3.1 collective-permute-start.16
  (121 other events, 551.5 us)
Sparse Core Ops, SparseCore 0:
  10.2 63.3 all-gather.20
  75.7 36.1 all-gather.16
  137.7 45.9 all-gather.22
  185.7 35.8 all-gather.18
  245.7 34.2 reduce-scatter.6
  282.2 34.2 reduce-scatter.8
  322.8 35.8 all-gather.24
  360.3 35.8 all-gather.28
  408.9 34.2 reduce-scatter.10
  446.0 34.2 reduce-scatter.14
  489.7 36.9 all-gather.26
  528.7 35.8 all-gather.30
  581.7 34.2 reduce-scatter.16
  618.2 34.2 reduce-scatter.12

commit v7 on v6

--- a/solution.py
+++ b/solution.py
@@ -106,6 +106,7 @@
 
 def stream(
     inputs,
+    input_segs,
     cotangent,
     seg_kind,
     seg_lens,
@@ -134,7 +135,6 @@
     key_valid = jnp.arange(CHAIN)[None, None, :] < seg_lens[:, :, None]
 
 
-    input_segs = gather_rows(inputs)
     projected = jnp.einsum(
         "srd,sjde->jsre", input_segs, qkv_sel, preferred_element_type=jnp.float32
     )
@@ -296,6 +296,9 @@
         up_bias[peer_kind].astype(jnp.float32),
         w_down[peer_kind],
     )
+    row_parts = [slice(part * seg_rows, (part + 1) * seg_rows) for part in range(STREAMS)]
+    gathered = [gather_rows(inputs[rows]) for rows in row_parts]
+    out_sel, gathered[0] = lax.optimization_barrier((out_sel, gathered[0]))
     out_rows_w = lax.all_to_all(out_sel, "tensor", 0, 0, tiled=True)
     outs, ins, grads, smalls = [], [], [], []
     for part in range(STREAMS):
@@ -305,9 +308,10 @@
         seg_lens = lengths[chain_ids]
         own_rows = rank * tok_dev + part * seg_rows + jnp.arange(seg_rows)
         row_kind = block_kind[own_rows // block_rows]
-        rows = slice(part * seg_rows, (part + 1) * seg_rows)
+        rows = row_parts[part]
         out_part, in_part, grad_part, small_part = stream(
             inputs[rows],
+            gathered[part],
             cotangent[rows],
             peer_kind,
             seg_lens,

time: 681 us -> 675 us (level)
    all_to_all x1, waiting for transfers between devices: 0.01 us -> 11.6 us  [local(): out_rows_w = lax.all_to_all(out_sel, 'tensor', 0, 0, tiled=True)]
    all_gather x8, waiting for transfers between devices: 173 us -> 162 us  [gather_rows(): return lax.all_gather(local_rows, 'tensor', axis=0, tiled=False)]
    unnamed x278 -> x304, local copies, waits for them, and re-layouts: 12.4 us -> 14.6 us
  transfers between devices with their start and end apart: 46 -> 46, of which waited for: 24 -> 24; matrix products, arithmetic and copies ran while one was open for 35% -> 34% of each run, Pallas kernels for 0% -> 0%
where the time goes in v7:
time: 675 us; the launch traced here: 664 us
  waiting for transfers between devices  319 us (47%)
  matrix products  133 us (20%)
  local copies, waits for them, and re-layouts  83.4 us (12%)
  other arithmetic  75.9 us (11%)
  starting transfers between devices  36.9 us (5%)
  between operations  16.4 us (2%)
    all_gather x8, waiting for transfers between devices, gather_rows(): return lax.all_gather(local_rows, 'tensor', axis=0, tiled=False)  162 us
    reduce_scatter x6, waiting for transfers between devices, scatter_sum(): lax.psum_scatter(seg_parts.reshape(n_seg * seg_rows, width).astype(jnp.bf...  63.8 us
    ppermute x12, waiting for transfers between devices, dp_sum_low(): gots = lax.ppermute(sends, 'dp', dp_perm(n_dp, 1 << b))  40.5 us
    all_to_all x2, waiting for transfers between devices, stream(): mixed_rows = lax.all_to_all(mixed, 'tensor', 0, 0, tiled=True)  18.7 us
    select_n x12, other arithmetic, dp_sum_low(): jnp.where(upper, jnp.concatenate([g, c]), jnp.concatenate([c, g]))  16.3 us
    dot_general x12, matrix products, type_sum(): jnp.einsum('rt,rd->td', kind_hot, values, precision=lax.Precision.HIGHEST)  15.4 us
    dot_general x2, matrix products, stream(): jnp.einsum('srd,sfd->srf', two_segs, down_sel, preferred_element_type=jnp...  15.1 us
    unnamed x304, local copies, waits for them, and re-layouts  14.6 us
  transfers between devices with their start and end apart: 46, of which 24 were waited for; matrix products, arithmetic and copies ran while one was open for 34% of the time, Pallas kernels for 0%

profile of v7, /device:TPU:0, one launch (start us, length us, event | category | flops | bytes accessed | tf_op | source)
XLA Modules:
  0.0 664.0 jit_solution(8168065837308891320)
XLA Ops:
  16.5 4.0 gather_fusion.1
  20.5 29.4 %all-gather.21.cloned.1.call-done = bf16[1024,768]{1,0:T(8,128)(2,1)} async-done(((bf16[256,768]{1,0:T(8,128)(2,1)}), bf16[1024,768]{1,0:T(8,128)(2,1)}) %all-gather.21.cloned.1.call-update) | async-done | bytes 1572880 | tf_op jit(solution)/shard_map/all_gather | solution.py:44
  49.9 3.6 convolution_bitcast_fusion
  55.1 2.5 fusion.212
  64.8 3.5 all-to-all-start.2
  71.7 24.7 %all-gather.17.cloned.1.call-done = bf16[1024,768]{1,0:T(8,128)(2,1)} async-done(((bf16[256,768]{1,0:T(8,128)(2,1)}), bf16[1024,768]{1,0:T(8,128)(2,1)}) %all-gather.17.cloned.1.call-update) | async-done | bytes 1572880 | tf_op jit(solution)/shard_map/all_gather | solution.py:44
  96.4 4.3 all-to-all-start.1
  101.4 2.6 compare_select_fusion.4
  105.9 3.6 convolution_bitcast_fusion.1
  111.1 2.8 fusion.211
  117.8 11.6 %all-to-all-done.1 = bf16[4,192,768]{2,1,0:T(8,128)(2,1)} async-done(((bf16[4,192,768]{2,1,0:T(8,128)(2,1)}), bf16[4,192,768]{2,1,0:T(8,128)(2,1)}, u32[]{:S(2)}, u32[]{:S(2)}) %all-to-all-start.1) | async-done | bytes 1179680 | tf_op jit(solution)/shard_map/all_to_all | solution.py:302
  139.3 3.5 all-to-all-start
  142.9 2.6 compare_select_fusion.7
  147.1 18.7 %all-to-all-done = bf16[4,256,192]{1,2,0:T(8,128)(2,1)S(1)} async-done(((bf16[4,256,192]{1,2,0:T(8,128)(2,1)}), bf16[4,256,192]{1,2,0:T(8,128)(2,1)S(1)}, u32[]{:S(2)}, u32[]{:S(2)}) %all-to-all-start) | async-done | bytes 393248 | tf_op jit(solution)/shard_map/all_to_all | solution.py:166
  171.3 3.2 gather_fusion.7
  174.5 4.8 gather_fusion.5
  179.3 5.9 fusion.227
  185.2 31.5 %all-gather.19.cloned.1.call-done = bf16[1024,768]{1,0:T(8,128)(2,1)} async-done(((bf16[256,768]{1,0:T(8,128)(2,1)}), bf16[1024,768]{1,0:T(8,128)(2,1)}) %all-gather.19.cloned.1.call-update) | async-done | bytes 1572880 | tf_op jit(solution)/shard_map/all_gather | solution.py:44
  216.8 7.0 %fusion.93 = (u8[256,768]{1,0:T(8,128)(4,1)S(1)}, u8[256,768]{1,0:T(8,128)(4,1)S(1)}, u8[256,768]{1,0:T(8,128)(4,1)S(1)}, u8[256,768]{1,0:T(8,128)(4,1)S(1)}, f32[4,256,768]{2,1,0:T(8,128)S(1)}) fusion(f32[4,768]{1,0:T(4,128)S(1)} %convert_element_type.493, f32[4,256,768]{2,1,0:T(8,128)} %fusion.227, bf16[4,256,768]{2,1,0:T(8,128)(2,1)} %bitcast.359, ...), kind=kOutput, calls=%fused_computation.241 | convolution fusion | flops 1229193216 | bytes 13381632 | tf_op jit(solution)/shard_map/srd,sdf->srf/dot_general | solution.py:177
  223.8 14.3 %fusion.3 = (bf16[4,256,768]{2,1,0:T(8,128)(2,1)S(1)}, bf16[4,256,768]{2,1,0:T(8,128)(2,1)S(1)}) fusion(f32[4,256,768]{2,1,0:T(8,128)S(1)} %get-tuple-element.78, f32[4,768]{1,0:T(4,128)S(1)} %convert_element_type.493, u8[256,768]{1,0:T(8,128)(4,1)S(1)} %get-tuple-element.16, u8[256,768]{1,0:T(8,128)(4,1)S(1)} %get-tuple-element.15, ...), kind=kLoop, calls=%fused_computation.20 | loop fusion | flops 110886912 | bytes 10235904 | tf_op jit(solution)/shard_map/convert_element_type | solution.py:180
  238.2 2.6 convolution_convert_fusion.5
  240.9 4.9 convolution_convert_fusion.4
  246.2 29.1 %reduce-scatter.7.cloned.1.call-done = bf16[256,768]{1,0:T(8,128)(2,1)} async-done(((bf16[1024,768]{1,0:T(8,128)(2,1)}), bf16[256,768]{1,0:T(8,128)(2,1)}) %reduce-scatter.7.cloned.1.call-update) | async-done | bytes 393232 | tf_op jit(solution)/shard_map/reduce_scatter | solution.py:49
  277.0 34.7 %reduce-scatter.9.cloned.1.call-done = bf16[256,768]{1,0:T(8,128)(2,1)} async-done(((bf16[1024,768]{1,0:T(8,128)(2,1)}), bf16[256,768]{1,0:T(8,128)(2,1)}) %reduce-scatter.9.cloned.1.call-update) | async-done | bytes 393232 | tf_op jit(solution)/shard_map/reduce_scatter | solution.py:49
  314.5 2.6 fusion.207
  322.7 2.6 copy.88
  325.4 2.6 copy.91
  328.0 2.6 copy.96
  330.7 2.6 copy.97
  333.2 2.6 copy.98
  335.9 2.6 copy.99
  342.1 11.1 %all-gather.25.cloned.1.call-done = bf16[1024,768]{1,0:T(8,128)(2,1)} async-done(((bf16[256,768]{1,0:T(8,128)(2,1)}), bf16[1024,768]{1,0:T(8,128)(2,1)}) %all-gather.25.cloned.1.call-update) | async-done | bytes 1572880 | tf_op jit(solution)/shard_map/all_gather | solution.py:44
  353.2 7.5 %convert_reduce_fusion.1 = (f32[4,768]{1,0:T(4,128)}, bf16[4,256,768]{2,1,0:T(8,128)(2,1)}) fusion(f32[4,256,768]{2,1,0:T(8,128)} %copy-done.51, f32[4,768]{1,0:T(4,128)} %copy-done.101, bf16[4,256,768]{2,1,0:T(8,128)(2,1)} %bitcast.405, bf16[4,768,768]{2,1,0:T(8,128)(2,1)} %gather_fusion.7), kind=kOutput, calls=%fused_computation.58 | convolution fusion | flops 1219752960 | bytes 11034624 | tf_op jit(solution)/shard_map/srd,sfd->srf/dot_general | solution.py:195
  360.7 30.0 %all-gather.29.cloned.1.call-done = bf16[1024,768]{1,0:T(8,128)(2,1)} async-done(((bf16[256,768]{1,0:T(8,128)(2,1)}), bf16[1024,768]{1,0:T(8,128)(2,1)}) %all-gather.29.cloned.1.call-update) | async-done | bytes 1572880 | tf_op jit(solution)/shard_map/all_gather | solution.py:44
  390.7 7.6 %convert_reduce_fusion = (f32[4,768]{1,0:T(4,128)}, bf16[4,256,768]{2,1,0:T(8,128)(2,1)}) fusion(f32[4,256,768]{2,1,0:T(8,128)} %fusion.227, f32[4,768]{1,0:T(4,128)} %copy-done.101, bf16[4,256,768]{2,1,0:T(8,128)(2,1)} %bitcast.407, bf16[4,768,768]{2,1,0:T(8,128)(2,1)} %gather_fusion.7), kind=kOutput, calls=%fused_computation.57 | convolution fusion | flops 1219752960 | bytes 11034624 | tf_op jit(solution)/shard_map/srd,sfd->srf/dot_general | solution.py:195
  398.3 4.9 convolution_convert_fusion.2
  403.5 4.7 fusion.25
  408.2 2.9 bitcast_add_fusion.1
  413.0 2.7 fusion.21
  415.7 2.8 bitcast_add_fusion
  428.9 2.6 convolution_convert_fusion
  431.6 9.2 %collective-permute-done.18 = bf16[384,768]{1,0:T(8,128)(2,1)S(1)} collective-permute-done((bf16[384,768]{1,0:T(8,128)(2,1)S(1)}, bf16[384,768]{1,0:T(8,128)(2,1)S(1)}, u32[]{:S(2)}, u32[]{:S(2)}) %collective-permute-start.18) | collective-permute-done | bytes 589856 | tf_op jit(solution)/shard_map/ppermute | solution.py:83
  444.2 8.1 %collective-permute-done.24 = bf16[384,768]{1,0:T(8,128)(2,1)S(1)} collective-permute-done((bf16[384,768]{1,0:T(8,128)(2,1)}, bf16[384,768]{1,0:T(8,128)(2,1)S(1)}, u32[]{:S(2)}, u32[]{:S(2)}) %collective-permute-start.24) | collective-permute-done | bytes 589856 | tf_op jit(solution)/shard_map/ppermute | solution.py:83
  455.1 7.5 %collective-permute-done.25 = bf16[192,768]{1,0:T(8,128)(2,1)S(1)} collective-permute-done((bf16[192,768]{1,0:T(8,128)(2,1)S(1)}, bf16[192,768]{1,0:T(8,128)(2,1)S(1)}, u32[]{:S(2)}, u32[]{:S(2)}) %collective-permute-start.25) | collective-permute-done | bytes 294944 | tf_op jit(solution)/shard_map/ppermute | solution.py:83
  465.0 4.0 collective-permute-done.20
  493.2 2.9 maximum_select_fusion.3
  496.6 2.9 collective-permute-done.6
  500.1 2.9 maximum_select_fusion.4
  503.0 4.5 collective-permute-done.7
  510.4 10.3 %all-gather.27.cloned.1.call-done = bf16[1024,768]{1,0:T(8,128)(2,1)} async-done(((bf16[256,768]{1,0:T(8,128)(2,1)}), bf16[1024,768]{1,0:T(8,128)(2,1)}) %all-gather.27.cloned.1.call-update) | async-done | bytes 1572880 | tf_op jit(solution)/shard_map/all_gather | solution.py:44
  520.7 2.8 convolution_convert_fusion.11
  533.2 25.4 %all-gather.31.cloned.1.call-done = bf16[1024,768]{1,0:T(8,128)(2,1)} async-done(((bf16[256,768]{1,0:T(8,128)(2,1)}), bf16[1024,768]{1,0:T(8,128)(2,1)}) %all-gather.31.cloned.1.call-update) | async-done | bytes 1572880 | tf_op jit(solution)/shard_map/all_gather | solution.py:44
  558.6 2.8 convolution_convert_fusion.10
  569.1 4.7 bitcast_convert_fusion
  577.9 3.8 fusion.17
  591.7 2.7 bitcast_convert_fusion.1
  601.8 9.9 %collective-permute-done.1 = bf16[288,768]{1,0:T(8,128)(2,1)S(1)} collective-permute-done((bf16[288,768]{1,0:T(8,128)(2,1)S(1)}, bf16[288,768]{1,0:T(8,128)(2,1)S(1)}, u32[]{:S(2)}, u32[]{:S(2)}) %collective-permute-start.1) | collective-permute-done | bytes 442400 | tf_op jit(solution)/shard_map/ppermute | solution.py:83
  613.7 4.8 collective-permute-done.2
  620.7 4.4 collective-permute-done.3
  627.8 2.9 maximum_select_fusion
  635.3 2.8 maximum_select_fusion.1
  638.1 2.5 convert.15
  640.6 2.5 convert.16
  652.4 2.3 convert_add_fusion.3
  (590 shorter events, 170.6 us)
Async XLA Ops:
  7.2 164.1 %copy-start = (bf16[2,768,768]{2,1,0:T(8,128)(2,1)S(1)}, bf16[2,768,768]{2,1,0:T(8,128)(2,1)}, u32[]{:S(2)}) copy-start(bf16[2,768,768]{2,1,0:T(8,128)(2,1)} %param.25) | copy-start | bytes 7077892
  7.2 42.7 %all-gather.21.cloned.1.call-start = ((), (), s32[]{:S(2)}) async-start(), calls=%async_computation.17 | async-start | bytes 1966080 | tf_op jit(solution)/shard_map/all_gather | solution.py:44
  9.5 87.0 %all-gather.17.cloned.1.call-start = ((), (), s32[]{:S(2)}) async-start(), calls=%async_computation.15 | async-start | bytes 1966080 | tf_op jit(solution)/shard_map/all_gather | solution.py:44
  14.8 100.5 %copy-start.72 = (f32[4,3,64]{2,1,0:T(4,128)}, f32[4,3,64]{2,1,0:T(4,128)S(1)}, u32[]{:S(2)}) copy-start(f32[4,3,64]{2,1,0:T(4,128)S(1)} %add.430) | copy-start | bytes 9220
  63.8 40.3 %copy-start.129 = (bf16[2,2,768]{2,1,0:T(2,128)(2,1)S(1)}, bf16[2,2,768]{2,1,0:T(2,128)(2,1)}, u32[]{:S(2)}) copy-start(bf16[2,2,768]{2,1,0:T(2,128)(2,1)} %param.22) | copy-start | bytes 18436
  64.8 31.7 %all-to-all-start.2 = ((bf16[4,256,192]{1,2,0:T(8,128)(2,1)}), bf16[4,256,192]{1,2,0:T(8,128)(2,1)S(1)}, u32[]{:S(2)}, u32[]{:S(2)}) async-start(bf16[4,256,192]{1,2,0:T(8,128)(2,1)} %convert_element_type.506), calls=%async_computation.3 | async-start | bytes 786432 | tf_op jit(solution)/shard_map/all_to_all | solution.py:166
  71.7 37.8 %copy-start.125 = (bf16[2,1,768]{2,1,0:T(2,128)(2,1)}, bf16[2,1,768]{2,1,0:T(2,128)(2,1)S(1)}, u32[]{:S(2)}) copy-start(bf16[2,1,768]{2,1,0:T(2,128)(2,1)S(1)} %get-tuple-element.60) | copy-start | bytes 9220
  96.4 33.0 %all-to-all-start.1 = ((bf16[4,192,768]{2,1,0:T(8,128)(2,1)}), bf16[4,192,768]{2,1,0:T(8,128)(2,1)}, u32[]{:S(2)}, u32[]{:S(2)}) async-start(bf16[4,192,768]{2,1,0:T(8,128)(2,1)} %gather_fusion.2), calls=%async_computation.1 | async-start | bytes 2359296 | tf_op jit(solution)/shard_map/all_to_all | solution.py:302
  100.7 78.6 %all-gather.23.cloned.1.call-start = ((), (), s32[]{:S(2)}) async-start(), calls=%async_computation.18 | async-start | bytes 1966080 | tf_op jit(solution)/shard_map/all_gather | solution.py:44
  104.1 28.1 %copy-start.88 = (s32[256,1]{0,1:T(1,128)}, s32[256,1]{0,1:T(1,128)S(1)}, u32[]{:S(2)}) copy-start(s32[256,1]{0,1:T(1,128)S(1)} %compare_select_fusion.4) | copy-start | bytes 3076
  139.3 26.4 %all-to-all-start = ((bf16[4,256,192]{1,2,0:T(8,128)(2,1)}), bf16[4,256,192]{1,2,0:T(8,128)(2,1)S(1)}, u32[]{:S(2)}, u32[]{:S(2)}) async-start(bf16[4,256,192]{1,2,0:T(8,128)(2,1)} %convert_element_type.491), calls=%async_computation | async-start | bytes 786432 | tf_op jit(solution)/shard_map/all_to_all | solution.py:166
  142.8 73.9 %all-gather.19.cloned.1.call-start = ((), (), s32[]{:S(2)}) async-start(), calls=%async_computation.16 | async-start | bytes 1966080 | tf_op jit(solution)/shard_map/all_gather | solution.py:44
  170.3 104.9 %reduce-scatter.7.cloned.1.call-start = ((), (), s32[]{:S(2)}) async-start(), calls=%async_computation.9 | async-start | bytes 1966080 | tf_op jit(solution)/shard_map/reduce_scatter | solution.py:49
  171.3 52.5 %copy-start.101 = (f32[4,768]{1,0:T(4,128)}, f32[4,768]{1,0:T(4,128)S(1)}, u32[]{:S(2)}) copy-start(f32[4,768]{1,0:T(4,128)S(1)} %convert_element_type.493) | copy-start | bytes 36868
  179.3 58.9 %slice-start = ((s8[4718592]{0:T(1024)(128)(4,1)}), s8[524288]{0:T(1024)(128)(4,1)S(1)}, s32[]{:S(2)}) async-start(s8[4718592]{0:T(1024)(128)(4,1)} %bitcast.339), calls=%async_computation.23 | async-start | bytes 1048576
  240.8 70.9 %reduce-scatter.9.cloned.1.call-start = ((), (), s32[]{:S(2)}) async-start(), calls=%async_computation.10 | async-start | bytes 1966080 | tf_op jit(solution)/shard_map/reduce_scatter | solution.py:49
  245.8 29.5 %copy-start.50 = (f32[256,768]{1,0:T(8,128)S(1)}, f32[256,768]{1,0:T(8,128)}, u32[]{:S(2)}) copy-start(f32[256,768]{1,0:T(8,128)} %get-tuple-element.75) | copy-start | bytes 2359300
  245.8 29.5 %copy-start.97 = (s32[256,1]{0,1:T(1,128)S(1)}, s32[256,1]{0,1:T(1,128)}, u32[]{:S(2)}) copy-start(s32[256,1]{0,1:T(1,128)} %copy-done.95) | copy-start | bytes 3076
  245.8 29.5 %copy-start.122 = (bf16[2,1,768]{2,1,0:T(2,128)(2,1)S(1)}, bf16[2,1,768]{2,1,0:T(2,128)(2,1)}, u32[]{:S(2)}) copy-start(bf16[2,1,768]{2,1,0:T(2,128)(2,1)} %get-tuple-element.58) | copy-start | bytes 9220
  245.8 107.4 %all-gather.25.cloned.1.call-start = ((), (), s32[]{:S(2)}) async-start(), calls=%async_computation.19 | async-start | bytes 1966080 | tf_op jit(solution)/shard_map/all_gather | solution.py:44
  246.2 67.4 %copy-start.18 = (f32[256,768]{1,0:T(8,128)}, f32[256,768]{1,0:T(8,128)S(1)}, u32[]{:S(2)}) copy-start(f32[256,768]{1,0:T(8,128)S(1)} %fusion.132) | copy-start | bytes 2359300
  275.3 38.4 %copy-start.39 = (bf16[512,768]{1,0:T(8,128)(2,1)S(1)}, bf16[512,768]{1,0:T(8,128)(2,1)}, u32[]{:S(2)}) copy-start(bf16[512,768]{1,0:T(8,128)(2,1)} %param.14) | copy-start | bytes 2359300
  276.7 37.6 %copy-start.105 = (f32[256]{0:T(256)}, f32[256]{0:T(256)S(1)}, u32[]{:S(2)}) copy-start(f32[256]{0:T(256)S(1)} %broadcast_multiply_fusion.10) | copy-start | bytes 3076
  277.0 37.4 %copy-start.115 = (f32[256]{0:T(256)}, f32[256]{0:T(256)S(1)}, u32[]{:S(2)}) copy-start(f32[256]{0:T(256)S(1)} %add_rsqrt_fusion.2) | copy-start | bytes 3076
  317.1 73.5 %all-gather.29.cloned.1.call-start = ((), (), s32[]{:S(2)}) async-start(), calls=%async_computation.21 | async-start | bytes 1966080 | tf_op jit(solution)/shard_map/all_gather | solution.py:44
  317.9 158.0 %reduce-scatter.11.cloned.1.call-start = ((), (), s32[]{:S(2)}) async-start(), calls=%async_computation.11 | async-start | bytes 1966080 | tf_op jit(solution)/shard_map/reduce_scatter | solution.py:49
  403.2 83.4 %reduce-scatter.15.cloned.1.call-start = ((), (), s32[]{:S(2)}) async-start(), calls=%async_computation.13 | async-start | bytes 1966080 | tf_op jit(solution)/shard_map/reduce_scatter | solution.py:49
  411.3 12.5 %collective-permute-start.17 = (bf16[768,768]{1,0:T(8,128)(2,1)S(1)}, bf16[768,768]{1,0:T(8,128)(2,1)S(1)}, u32[]{:S(2)}, u32[]{:S(2)}) collective-permute-start(bf16[768,768]{1,0:T(8,128)(2,1)S(1)} %fusion.79), channel_id=1, source_target_pairs={{0,4},{4,0},{8,12},{12,8},{16,20},{20,16},{24,28},{28,24},{1,5},{5... | collective-permute-start | bytes 3538952 | tf_op jit(solution)/shard_map/ppermute | solution.py:83
  418.8 7.3 %collective-permute-start.23 = (bf16[768,768]{1,0:T(8,128)(2,1)S(1)}, bf16[768,768]{1,0:T(8,128)(2,1)S(1)}, u32[]{:S(2)}, u32[]{:S(2)}) collective-permute-start(bf16[768,768]{1,0:T(8,128)(2,1)S(1)} %fusion.80), channel_id=1, source_target_pairs={{0,4},{4,0},{8,12},{12,8},{16,20},{20,16},{24,28},{28,24},{1,5},{5... | collective-permute-start | bytes 3538952 | tf_op jit(solution)/shard_map/ppermute | solution.py:83
  424.3 16.5 %collective-permute-start.18 = (bf16[384,768]{1,0:T(8,128)(2,1)S(1)}, bf16[384,768]{1,0:T(8,128)(2,1)S(1)}, u32[]{:S(2)}, u32[]{:S(2)}) collective-permute-start(bf16[384,768]{1,0:T(8,128)(2,1)S(1)} %select_convert_fusion.4), channel_id=1, source_target_pairs={{0,8},{4,12},{8,0},{12,4},{16,24},{20,28},{24,16},{28,20},{1,9},{5... | collective-permute-start | bytes 1769480 | tf_op jit(solution)/shard_map/ppermute | solution.py:83
  428.1 24.3 %collective-permute-start.24 = (bf16[384,768]{1,0:T(8,128)(2,1)}, bf16[384,768]{1,0:T(8,128)(2,1)S(1)}, u32[]{:S(2)}, u32[]{:S(2)}) collective-permute-start(bf16[384,768]{1,0:T(8,128)(2,1)} %select_convert_fusion.3), channel_id=1, source_target_pairs={{0,8},{4,12},{8,0},{12,4},{16,24},{20,28},{24,16},{28,20},{1,9},{5... | collective-permute-start | bytes 1769480 | tf_op jit(solution)/shard_map/ppermute | solution.py:83
  431.5 89.1 %all-gather.27.cloned.1.call-start = ((), (), s32[]{:S(2)}) async-start(), calls=%async_computation.20 | async-start | bytes 1966080 | tf_op jit(solution)/shard_map/all_gather | solution.py:44
  442.7 11.6 %collective-permute-start.19 = (bf16[192,768]{1,0:T(8,128)(2,1)S(1)}, bf16[192,768]{1,0:T(8,128)(2,1)S(1)}, u32[]{:S(2)}, u32[]{:S(2)}) collective-permute-start(bf16[192,768]{1,0:T(8,128)(2,1)S(1)} %select_convert_fusion.7), channel_id=1, source_target_pairs={{0,16},{4,20},{8,24},{12,28},{16,0},{20,4},{24,8},{28,12},{1,17},{... | collective-permute-start | bytes 884744 | tf_op jit(solution)/shard_map/ppermute | solution.py:83
  452.7 9.9 %collective-permute-start.25 = (bf16[192,768]{1,0:T(8,128)(2,1)S(1)}, bf16[192,768]{1,0:T(8,128)(2,1)S(1)}, u32[]{:S(2)}, u32[]{:S(2)}) collective-permute-start(bf16[192,768]{1,0:T(8,128)(2,1)S(1)} %select_convert_fusion.6), channel_id=1, source_target_pairs={{0,16},{4,20},{8,24},{12,28},{16,0},{20,4},{24,8},{28,12},{1,17},{... | collective-permute-start | bytes 884744 | tf_op jit(solution)/shard_map/ppermute | solution.py:83
  454.4 24.2 %copy-start.12 = (f32[256,768]{1,0:T(8,128)S(1)}, f32[256,768]{1,0:T(8,128)}, u32[]{:S(2)}) copy-start(f32[256,768]{1,0:T(8,128)} %copy-done.11) | copy-start | bytes 2359300
  454.4 14.5 %collective-permute-start.20 = (bf16[192,768]{1,0:T(8,128)(2,1)S(1)}, bf16[192,768]{1,0:T(8,128)(2,1)S(1)}, u32[]{:S(2)}, u32[]{:S(2)}) collective-permute-start(bf16[192,768]{1,0:T(8,128)(2,1)S(1)} %add_convert_fusion.1), channel_id=1, source_target_pairs={{0,16},{4,20},{8,24},{12,28},{16,0},{20,4},{24,8},{28,12},{1,17},{... | collective-permute-start | bytes 884744 | tf_op jit(solution)/shard_map/ppermute | solution.py:88
  462.7 10.7 %collective-permute-start.26 = (bf16[192,768]{1,0:T(8,128)(2,1)S(1)}, bf16[192,768]{1,0:T(8,128)(2,1)S(1)}, u32[]{:S(2)}, u32[]{:S(2)}) collective-permute-start(bf16[192,768]{1,0:T(8,128)(2,1)S(1)} %add_convert_fusion), channel_id=1, source_target_pairs={{0,16},{4,20},{8,24},{12,28},{16,0},{20,4},{24,8},{28,12},{1,17},{... | collective-permute-start | bytes 884744 | tf_op jit(solution)/shard_map/ppermute | solution.py:88
  469.9 23.3 %collective-permute-start.21 = (bf16[384,768]{1,0:T(8,128)(2,1)}, bf16[384,768]{1,0:T(8,128)(2,1)}, u32[]{:S(2)}, u32[]{:S(2)}) collective-permute-start(bf16[384,768]{1,0:T(8,128)(2,1)} %maximum_select_fusion.7), channel_id=1, source_target_pairs={{0,8},{4,12},{8,0},{12,4},{16,24},{20,28},{24,16},{28,20},{1,9},{5... | collective-permute-start | bytes 1769480 | tf_op jit(solution)/shard_map/ppermute | solution.py:88
  474.4 25.2 %collective-permute-start.27 = (bf16[384,768]{1,0:T(8,128)(2,1)}, bf16[384,768]{1,0:T(8,128)(2,1)}, u32[]{:S(2)}, u32[]{:S(2)}) collective-permute-start(bf16[384,768]{1,0:T(8,128)(2,1)} %maximum_select_fusion.8), channel_id=1, source_target_pairs={{0,8},{4,12},{8,0},{12,4},{16,24},{20,28},{24,16},{28,20},{1,9},{5... | collective-permute-start | bytes 1769480 | tf_op jit(solution)/shard_map/ppermute | solution.py:88
  483.8 74.8 %all-gather.31.cloned.1.call-start = ((), (), s32[]{:S(2)}) async-start(), calls=%async_computation.22 | async-start | bytes 1966080 | tf_op jit(solution)/shard_map/all_gather | solution.py:44
  492.5 28.1 %copy-start.42 = (bf16[4,192,768]{2,1,0:T(8,128)(2,1)S(1)}, bf16[4,192,768]{2,1,0:T(8,128)(2,1)}, u32[]{:S(2)}) copy-start(bf16[4,192,768]{2,1,0:T(8,128)(2,1)} %gather_fusion.2) | copy-start | bytes 3538948
  492.5 6.9 %collective-permute-start.6 = (f32[3,2,2,768]{3,1,2,0:T(2,128)S(1)}, f32[3,2,2,768]{3,1,2,0:T(2,128)S(1)}, u32[]{:S(2)}, u32[]{:S(2)}) collective-permute-start(f32[3,2,2,768]{3,1,2,0:T(2,128)S(1)} %maximum_add_fusion), channel_id=1, source_target_pairs={{0,1},{1,0},{2,3},{3,2},{4,5},{5,4},{6,7},{7,6},{8,9},{9,8},{10,11... | collective-permute-start | bytes 110600 | tf_op jit(solution)/shard_map/ppermute | solution.py:102
  496.1 131.7 %collective-permute-start.22 = (bf16[768,768]{1,0:T(8,128)(2,1)}, bf16[768,768]{1,0:T(8,128)(2,1)}, u32[]{:S(2)}, u32[]{:S(2)}) collective-permute-start(bf16[768,768]{1,0:T(8,128)(2,1)} %maximum_select_fusion.3), channel_id=1, source_target_pairs={{0,4},{4,0},{8,12},{12,8},{16,20},{20,16},{24,28},{28,24},{1,5},{5... | collective-permute-start | bytes 3538952 | tf_op jit(solution)/shard_map/ppermute | solution.py:88
  496.1 156.3 %reduce-scatter.17.cloned.1.call-start = ((), (), s32[]{:S(2)}) async-start(), calls=%async_computation.14 | async-start | bytes 1966080 | tf_op jit(solution)/shard_map/reduce_scatter | solution.py:49
  499.6 7.9 %collective-permute-start.7 = (f32[3,2,2,768]{3,1,2,0:T(2,128)S(1)}, f32[3,2,2,768]{3,1,2,0:T(2,128)S(1)}, u32[]{:S(2)}, u32[]{:S(2)}) collective-permute-start(f32[3,2,2,768]{3,1,2,0:T(2,128)S(1)} %fusion.276), channel_id=1, source_target_pairs={{0,2},{1,3},{2,0},{3,1},{4,6},{5,7},{6,4},{7,5},{8,10},{9,11},{10,... | collective-permute-start | bytes 110600 | tf_op jit(solution)/shard_map/ppermute | solution.py:102
  503.0 132.3 %collective-permute-start.28 = (bf16[768,768]{1,0:T(8,128)(2,1)}, bf16[768,768]{1,0:T(8,128)(2,1)}, u32[]{:S(2)}, u32[]{:S(2)}) collective-permute-start(bf16[768,768]{1,0:T(8,128)(2,1)} %maximum_select_fusion.4), channel_id=1, source_target_pairs={{0,4},{4,0},{8,12},{12,8},{16,20},{20,16},{24,28},{28,24},{1,5},{5... | collective-permute-start | bytes 3538952 | tf_op jit(solution)/shard_map/ppermute | solution.py:88
  533.2 29.4 %copy-start.5 = (f32[4,2,3,128,128]{3,4,2,1,0:T(8,128)S(1)}, f32[4,2,3,128,128]{3,4,2,1,0:T(8,128)}, u32[]{:S(2)}) copy-start(f32[4,2,3,128,128]{3,4,2,1,0:T(8,128)} %copy-done.4) | copy-start | bytes 4718596
  533.2 29.4 %copy-start.66 = (f32[4,2,3,128]{3,2,1,0:T(4,128)S(1)}, f32[4,2,3,128]{3,2,1,0:T(4,128)}, u32[]{:S(2)}) copy-start(f32[4,2,3,128]{3,2,1,0:T(4,128)} %copy-done.65) | copy-start | bytes 36868
  573.8 80.9 %reduce-scatter.13.cloned.1.call-start = ((), (), s32[]{:S(2)}) async-start(), calls=%async_computation.12 | async-start | bytes 1966080 | tf_op jit(solution)/shard_map/reduce_scatter | solution.py:49
  577.9 17.1 %collective-permute-start.8 = (f32[15,768]{1,0:T(8,128)S(1)}, f32[15,768]{1,0:T(8,128)S(1)}, u32[]{:S(2)}, u32[]{:S(2)}) collective-permute-start(f32[15,768]{1,0:T(8,128)S(1)} %pad_maximum_fusion.6), channel_id=1, source_target_pairs={{0,4},{4,0},{8,12},{12,8},{16,20},{20,16},{24,28},{28,24},{1,5},{5... | collective-permute-start | bytes 138248 | tf_op jit(solution)/shard_map/ppermute | solution.py:102
  585.1 11.5 %collective-permute-start = (bf16[576,768]{1,0:T(8,128)(2,1)}, bf16[576,768]{1,0:T(8,128)(2,1)}, u32[]{:S(2)}, u32[]{:S(2)}) collective-permute-start(bf16[576,768]{1,0:T(8,128)(2,1)} %bitcast.59), channel_id=1, source_target_pairs={{0,4},{4,0},{8,12},{12,8},{16,20},{20,16},{24,28},{28,24},{1,5},{5... | collective-permute-start | bytes 2654216 | tf_op jit(solution)/shard_map/ppermute | solution.py:83
  594.5 4.7 collective-permute-start.11
  595.0 35.7 %collective-permute-start.9 = (f32[15,768]{1,0:T(8,128)S(1)}, f32[15,768]{1,0:T(8,128)S(1)}, u32[]{:S(2)}, u32[]{:S(2)}) collective-permute-start(f32[15,768]{1,0:T(8,128)S(1)} %fusion.275), channel_id=1, source_target_pairs={{0,8},{4,12},{8,0},{12,4},{16,24},{20,28},{24,16},{28,20},{1,9},{5... | collective-permute-start | bytes 138248 | tf_op jit(solution)/shard_map/ppermute | solution.py:102
  598.6 13.1 %collective-permute-start.1 = (bf16[288,768]{1,0:T(8,128)(2,1)S(1)}, bf16[288,768]{1,0:T(8,128)(2,1)S(1)}, u32[]{:S(2)}, u32[]{:S(2)}) collective-permute-start(bf16[288,768]{1,0:T(8,128)(2,1)S(1)} %select_convert_fusion.5), channel_id=1, source_target_pairs={{0,8},{4,12},{8,0},{12,4},{16,24},{20,28},{24,16},{28,20},{1,9},{5... | collective-permute-start | bytes 1327112 | tf_op jit(solution)/shard_map/ppermute | solution.py:83
  600.2 13.5 %collective-permute-start.12 = (bf16[96,768]{1,0:T(8,128)(2,1)S(1)}, bf16[96,768]{1,0:T(8,128)(2,1)S(1)}, u32[]{:S(2)}, u32[]{:S(2)}) collective-permute-start(bf16[96,768]{1,0:T(8,128)(2,1)S(1)} %select_convert_fusion.10), channel_id=1, source_target_pairs={{0,8},{4,12},{8,0},{12,4},{16,24},{20,28},{24,16},{28,20},{1,9},{5... | collective-permute-start | bytes 442376 | tf_op jit(solution)/shard_map/ppermute | solution.py:83
  611.9 6.6 collective-permute-start.2
  618.6 6.6 collective-permute-start.3
  620.2 5.9 collective-permute-start.13
  625.3 9.6 %collective-permute-start.4 = (bf16[288,768]{1,0:T(8,128)(2,1)S(1)}, bf16[288,768]{1,0:T(8,128)(2,1)S(1)}, u32[]{:S(2)}, u32[]{:S(2)}) collective-permute-start(bf16[288,768]{1,0:T(8,128)(2,1)S(1)} %maximum_select_fusion.9), channel_id=1, source_target_pairs={{0,8},{4,12},{8,0},{12,4},{16,24},{20,28},{24,16},{28,20},{1,9},{5... | collective-permute-start | bytes 1327112 | tf_op jit(solution)/shard_map/ppermute | solution.py:88
  626.2 5.1 collective-permute-start.14
  630.8 12.4 %collective-permute-start.10 = (f32[15,768]{1,0:T(8,128)S(1)}, f32[15,768]{1,0:T(8,128)S(1)}, u32[]{:S(2)}, u32[]{:S(2)}) collective-permute-start(f32[15,768]{1,0:T(8,128)S(1)} %add.489), channel_id=1, source_target_pairs={{0,16},{4,20},{8,24},{12,28},{16,0},{20,4},{24,8},{28,12},{1,17},{... | collective-permute-start | bytes 138248 | tf_op jit(solution)/shard_map/ppermute | solution.py:102
  631.3 12.4 %collective-permute-start.15 = (bf16[96,768]{1,0:T(8,128)(2,1)S(1)}, bf16[96,768]{1,0:T(8,128)(2,1)S(1)}, u32[]{:S(2)}, u32[]{:S(2)}) collective-permute-start(bf16[96,768]{1,0:T(8,128)(2,1)S(1)} %maximum_select_fusion.11), channel_id=1, source_target_pairs={{0,8},{4,12},{8,0},{12,4},{16,24},{20,28},{24,16},{28,20},{1,9},{5... | collective-permute-start | bytes 442376 | tf_op jit(solution)/shard_map/ppermute | solution.py:88
  635.2 13.0 %collective-permute-start.5 = (bf16[576,768]{1,0:T(8,128)(2,1)S(1)}, bf16[576,768]{1,0:T(8,128)(2,1)}, u32[]{:S(2)}, u32[]{:S(2)}) collective-permute-start(bf16[576,768]{1,0:T(8,128)(2,1)S(1)} %maximum_select_fusion.5), channel_id=1, source_target_pairs={{0,4},{4,0},{8,12},{12,8},{16,20},{20,16},{24,28},{28,24},{1,5},{5... | collective-permute-start | bytes 2654216 | tf_op jit(solution)/shard_map/ppermute | solution.py:88
  643.8 3.1 collective-permute-start.16
  (134 other events, 675.5 us)
Sparse Core Ops, SparseCore 0:
  10.2 39.7 all-gather.20
  52.1 44.3 all-gather.16
  134.3 44.4 all-gather.22
  180.9 35.8 all-gather.18
  240.9 34.2 reduce-scatter.6
  277.4 34.2 reduce-scatter.8
  317.3 35.8 all-gather.24
  354.7 35.8 all-gather.28
  403.4 34.2 reduce-scatter.10
  440.4 34.2 reduce-scatter.14
  483.9 36.7 all-gather.26
  522.7 35.9 all-gather.30
  573.9 34.3 reduce-scatter.16
  610.5 34.2 reduce-scatter.12

commit v8 on v7

--- a/solution.py
+++ b/solution.py
@@ -163,10 +163,15 @@
         "schqk,sckhd->scqhd", probs_low, heads(value_rows), preferred_element_type=jnp.float32
     )
     mixed = mixed.reshape(n_seg, seg_rows, -1).astype(jnp.bfloat16)
-    mixed_rows = lax.all_to_all(mixed, "tensor", 0, 0, tiled=True)
-    attn_rows = jnp.einsum(
-        "erc,ecd->rd", mixed_rows, out_rows_w, preferred_element_type=jnp.float32
-    )
+    if out_rows_w is None:
+        attn_rows = scatter_sum(
+            jnp.einsum("sre,sed->srd", mixed, out_sel, preferred_element_type=jnp.float32)
+        )
+    else:
+        mixed_rows = lax.all_to_all(mixed, "tensor", 0, 0, tiled=True)
+        attn_rows = jnp.einsum(
+            "erc,ecd->rd", mixed_rows, out_rows_w, preferred_element_type=jnp.float32
+        )
 
     hidden_one = inputs.astype(jnp.float32) + attn_rows + pick(resid_bias[:, 0])
     gain_one = pick(norm_gain[:, 0])
@@ -316,7 +321,7 @@
             peer_kind,
             seg_lens,
             row_kind,
-            out_rows_w,
+            out_rows_w if part > 0 else None,
             selected,
             resid_bias,
             norm_gain,

time: 675 us -> 713 us (1.056)
  waiting for transfers between devices: 319 us -> 367 us
    all_gather x8, waiting for transfers between devices: 162 us -> 198 us  [gather_rows(): return lax.all_gather(local_rows, 'tensor', axis=0, tiled=False)]
    all_to_all x1, waiting for transfers between devices: 11.6 us -> 42.1 us  [local(): out_rows_w = lax.all_to_all(out_sel, 'tensor', 0, 0, tiled=True)]
    all_to_all x2 -> x1, waiting for transfers between devices: 18.7 us -> 2.09 us  [stream(): mixed_rows = lax.all_to_all(mixed, 'tensor', 0, 0, tiled=True)]
    unnamed x304 -> x260, local copies, waits for them, and re-layouts: 14.6 us -> 12.2 us
    reduce_scatter x6 -> x7, waiting for transfers between devices: 63.8 us -> 64.1 us  [scatter_sum(): lax.psum_scatter(seg_parts.reshape(n_seg * seg_rows, width).astype(jnp.bf...]
  transfers between devices with their start and end apart: 46 -> 46, of which waited for: 24 -> 25; matrix products, arithmetic and copies ran while one was open for 34% -> 29% of each run, Pallas kernels for 0% -> 0%
where the time goes in v8:
time: 713 us; the launch traced here: 703 us
  waiting for transfers between devices  367 us (51%)
  matrix products  130 us (18%)
  local copies, waits for them, and re-layouts  77.7 us (11%)
  other arithmetic  77 us (11%)
  starting transfers between devices  34.2 us (5%)
  between operations  16.2 us (2%)
    all_gather x8, waiting for transfers between devices, gather_rows(): return lax.all_gather(local_rows, 'tensor', axis=0, tiled=False)  198 us
    reduce_scatter x7, waiting for transfers between devices, scatter_sum(): lax.psum_scatter(seg_parts.reshape(n_seg * seg_rows, width).astype(jnp.bf...  64.1 us
    all_to_all x1, waiting for transfers between devices, local(): out_rows_w = lax.all_to_all(out_sel, 'tensor', 0, 0, tiled=True)  42.1 us
    ppermute x12, waiting for transfers between devices, dp_sum_low(): gots = lax.ppermute(sends, 'dp', dp_perm(n_dp, 1 << b))  40.4 us
    select_n x12, other arithmetic, dp_sum_low(): jnp.where(upper, jnp.concatenate([g, c]), jnp.concatenate([c, g]))  16.3 us
    dot_general x12, matrix products, type_sum(): jnp.einsum('rt,rd->td', kind_hot, values, precision=lax.Precision.HIGHEST)  15.3 us
    dot_general x2, matrix products, stream(): jnp.einsum('srd,sfd->srf', two_segs, down_sel, preferred_element_type=jnp...  15.2 us
    convert_element_type x1, other arithmetic, stream(): activ = jax.nn.gelu(pre_act, approximate=False).astype(jnp.bfloat16)  14.3 us
  transfers between devices with their start and end apart: 46, of which 25 were waited for; matrix products, arithmetic and copies ran while one was open for 29% of the time, Pallas kernels for 0%

profile of v8, /device:TPU:0, one launch (start us, length us, event | category | flops | bytes accessed | tf_op | source)
XLA Modules:
  0.0 702.6 jit_solution(11796982969936717116)
XLA Ops:
  7.3 2.2 fusion.212
  15.8 4.0 gather_fusion.1
  20.6 29.4 %all-gather.21.cloned.1.call-done = bf16[1024,768]{1,0:T(8,128)(2,1)} async-done(((bf16[256,768]{1,0:T(8,128)(2,1)}), bf16[1024,768]{1,0:T(8,128)(2,1)}) %all-gather.21.cloned.1.call-update) | async-done | bytes 1572880 | tf_op jit(solution)/shard_map/all_gather | solution.py:44
  49.9 3.6 convolution_bitcast_fusion
  55.3 32.7 %all-gather.17.cloned.1.call-done = bf16[1024,768]{1,0:T(8,128)(2,1)} async-done(((bf16[256,768]{1,0:T(8,128)(2,1)}), bf16[1024,768]{1,0:T(8,128)(2,1)}) %all-gather.17.cloned.1.call-update) | async-done | bytes 1572880 | tf_op jit(solution)/shard_map/all_gather | solution.py:44
  88.0 3.6 convolution_bitcast_fusion.1
  99.7 2.4 squeeze.48
  108.9 4.1 all-to-all-start
  124.2 4.3 all-to-all-start.1
  128.5 3.0 convolution_convert_fusion.6
  132.3 2.6 compare_select_fusion.4
  135.9 42.1 %all-to-all-done.1 = bf16[4,192,768]{2,1,0:T(8,128)(2,1)} async-done(((bf16[4,192,768]{2,1,0:T(8,128)(2,1)}), bf16[4,192,768]{2,1,0:T(8,128)(2,1)}, u32[]{:S(2)}, u32[]{:S(2)}) %all-to-all-start.1) | async-done | bytes 1179680 | tf_op jit(solution)/shard_map/all_to_all | solution.py:307
  182.6 2.6 compare_select_fusion.7
  190.7 3.2 gather_fusion.7
  193.8 4.8 gather_fusion.5
  198.7 21.4 %all-gather.23.cloned.1.call-done = bf16[1024,768]{1,0:T(8,128)(2,1)} async-done(((bf16[256,768]{1,0:T(8,128)(2,1)}), bf16[1024,768]{1,0:T(8,128)(2,1)}) %all-gather.23.cloned.1.call-update) | async-done | bytes 1572880 | tf_op jit(solution)/shard_map/all_gather | solution.py:44
  220.0 5.9 fusion.226
  226.0 31.4 %all-gather.19.cloned.1.call-done = bf16[1024,768]{1,0:T(8,128)(2,1)} async-done(((bf16[256,768]{1,0:T(8,128)(2,1)}), bf16[1024,768]{1,0:T(8,128)(2,1)}) %all-gather.19.cloned.1.call-update) | async-done | bytes 1572880 | tf_op jit(solution)/shard_map/all_gather | solution.py:44
  257.4 7.0 fusion.92
  264.4 14.3 %fusion.3 = (bf16[4,256,768]{2,1,0:T(8,128)(2,1)S(1)}, bf16[4,256,768]{2,1,0:T(8,128)(2,1)S(1)}) fusion(f32[4,256,768]{2,1,0:T(8,128)S(1)} %get-tuple-element.78, f32[4,768]{1,0:T(4,128)S(1)} %convert_element_type.505, u8[256,768]{1,0:T(8,128)(4,1)S(1)} %get-tuple-element.16, u8[256,768]{1,0:T(8,128)(4,1)S(1)} %get-tuple-element.15, ...), kind=kLoop, calls=%fused_computation.20 | loop fusion | flops 110886912 | bytes 10235904 | tf_op jit(solution)/shard_map/convert_element_type | solution.py:185
  278.8 2.6 convolution_convert_fusion.5
  281.5 4.9 convolution_convert_fusion.4
  286.8 29.1 %reduce-scatter.10.cloned.1.call-done = bf16[256,768]{1,0:T(8,128)(2,1)} async-done(((bf16[1024,768]{1,0:T(8,128)(2,1)}), bf16[256,768]{1,0:T(8,128)(2,1)}) %reduce-scatter.10.cloned.1.call-update) | async-done | bytes 393232 | tf_op jit(solution)/shard_map/reduce_scatter | solution.py:49
  317.6 34.9 %reduce-scatter.12.cloned.1.call-done = bf16[256,768]{1,0:T(8,128)(2,1)} async-done(((bf16[1024,768]{1,0:T(8,128)(2,1)}), bf16[256,768]{1,0:T(8,128)(2,1)}) %reduce-scatter.12.cloned.1.call-update) | async-done | bytes 393232 | tf_op jit(solution)/shard_map/reduce_scatter | solution.py:49
  355.3 2.6 fusion.206
  363.5 2.6 copy.88
  366.2 2.6 copy.91
  368.8 2.7 copy.97
  371.4 2.6 copy.96
  374.0 2.6 copy.98
  376.6 2.6 copy.99
  382.8 11.2 %all-gather.25.cloned.1.call-done = bf16[1024,768]{1,0:T(8,128)(2,1)} async-done(((bf16[256,768]{1,0:T(8,128)(2,1)}), bf16[1024,768]{1,0:T(8,128)(2,1)}) %all-gather.25.cloned.1.call-update) | async-done | bytes 1572880 | tf_op jit(solution)/shard_map/all_gather | solution.py:44
  394.0 7.5 %convert_reduce_fusion.1 = (f32[4,768]{1,0:T(4,128)}, bf16[4,256,768]{2,1,0:T(8,128)(2,1)}) fusion(f32[4,256,768]{2,1,0:T(8,128)} %copy-done.49, f32[4,768]{1,0:T(4,128)} %copy-done.81, bf16[4,256,768]{2,1,0:T(8,128)(2,1)} %bitcast.403, bf16[4,768,768]{2,1,0:T(8,128)(2,1)} %gather_fusion.7), kind=kOutput, calls=%fused_computation.58 | convolution fusion | flops 1219752960 | bytes 11034624 | tf_op jit(solution)/shard_map/srd,sfd->srf/dot_general | solution.py:200
  401.6 30.0 %all-gather.29.cloned.1.call-done = bf16[1024,768]{1,0:T(8,128)(2,1)} async-done(((bf16[256,768]{1,0:T(8,128)(2,1)}), bf16[1024,768]{1,0:T(8,128)(2,1)}) %all-gather.29.cloned.1.call-update) | async-done | bytes 1572880 | tf_op jit(solution)/shard_map/all_gather | solution.py:44
  431.5 7.6 %convert_reduce_fusion = (f32[4,768]{1,0:T(4,128)}, bf16[4,256,768]{2,1,0:T(8,128)(2,1)}) fusion(f32[4,256,768]{2,1,0:T(8,128)} %fusion.226, f32[4,768]{1,0:T(4,128)} %copy-done.81, bf16[4,256,768]{2,1,0:T(8,128)(2,1)} %bitcast.405, bf16[4,768,768]{2,1,0:T(8,128)(2,1)} %gather_fusion.7), kind=kOutput, calls=%fused_computation.57 | convolution fusion | flops 1219752960 | bytes 11034624 | tf_op jit(solution)/shard_map/srd,sfd->srf/dot_general | solution.py:200
  439.2 4.9 convolution_convert_fusion.2
  444.4 4.7 fusion.25
  449.1 2.9 bitcast_add_fusion.1
  453.9 2.7 fusion.21
  456.6 2.8 bitcast_add_fusion
  469.8 2.6 convolution_convert_fusion
  472.4 9.2 %collective-permute-done.18 = bf16[384,768]{1,0:T(8,128)(2,1)S(1)} collective-permute-done((bf16[384,768]{1,0:T(8,128)(2,1)S(1)}, bf16[384,768]{1,0:T(8,128)(2,1)S(1)}, u32[]{:S(2)}, u32[]{:S(2)}) %collective-permute-start.18) | collective-permute-done | bytes 589856 | tf_op jit(solution)/shard_map/ppermute | solution.py:83
  485.1 8.1 %collective-permute-done.24 = bf16[384,768]{1,0:T(8,128)(2,1)S(1)} collective-permute-done((bf16[384,768]{1,0:T(8,128)(2,1)}, bf16[384,768]{1,0:T(8,128)(2,1)S(1)}, u32[]{:S(2)}, u32[]{:S(2)}) %collective-permute-start.24) | collective-permute-done | bytes 589856 | tf_op jit(solution)/shard_map/ppermute | solution.py:83
  495.9 7.5 %collective-permute-done.25 = bf16[192,768]{1,0:T(8,128)(2,1)S(1)} collective-permute-done((bf16[192,768]{1,0:T(8,128)(2,1)S(1)}, bf16[192,768]{1,0:T(8,128)(2,1)S(1)}, u32[]{:S(2)}, u32[]{:S(2)}) %collective-permute-start.25) | collective-permute-done | bytes 294944 | tf_op jit(solution)/shard_map/ppermute | solution.py:83
  505.8 4.0 collective-permute-done.20
  534.5 2.9 maximum_select_fusion.3
  537.9 2.4 collective-permute-done.6
  540.4 3.0 maximum_select_fusion.4
  543.5 4.0 collective-permute-done.7
  548.2 12.5 %all-gather.27.cloned.1.call-done = bf16[1024,768]{1,0:T(8,128)(2,1)} async-done(((bf16[256,768]{1,0:T(8,128)(2,1)}), bf16[1024,768]{1,0:T(8,128)(2,1)}) %all-gather.27.cloned.1.call-update) | async-done | bytes 1572880 | tf_op jit(solution)/shard_map/all_gather | solution.py:44
  560.7 2.4 convolution_convert_fusion.12
  569.4 29.4 %all-gather.31.cloned.1.call-done = bf16[1024,768]{1,0:T(8,128)(2,1)} async-done(((bf16[256,768]{1,0:T(8,128)(2,1)}), bf16[1024,768]{1,0:T(8,128)(2,1)}) %all-gather.31.cloned.1.call-update) | async-done | bytes 1572880 | tf_op jit(solution)/shard_map/all_gather | solution.py:44
  598.8 2.4 convolution_convert_fusion.11
  608.5 4.7 bitcast_convert_fusion
  617.1 4.0 fusion.17
  630.5 2.7 bitcast_convert_fusion.1
  640.4 9.9 %collective-permute-done.1 = bf16[288,768]{1,0:T(8,128)(2,1)S(1)} collective-permute-done((bf16[288,768]{1,0:T(8,128)(2,1)S(1)}, bf16[288,768]{1,0:T(8,128)(2,1)S(1)}, u32[]{:S(2)}, u32[]{:S(2)}) %collective-permute-start.1) | collective-permute-done | bytes 442400 | tf_op jit(solution)/shard_map/ppermute | solution.py:83
  652.3 4.9 collective-permute-done.2
  659.4 4.5 collective-permute-done.3
  666.4 2.9 maximum_select_fusion
  673.8 2.8 maximum_select_fusion.1
  676.6 2.5 convert.15
  679.2 2.5 convert.16
  691.0 2.3 convert_add_fusion.3
  (547 shorter events, 163.5 us)
Async XLA Ops:
  7.2 183.5 %copy-start = (bf16[2,768,768]{2,1,0:T(8,128)(2,1)S(1)}, bf16[2,768,768]{2,1,0:T(8,128)(2,1)}, u32[]{:S(2)}) copy-start(bf16[2,768,768]{2,1,0:T(8,128)(2,1)} %param.25) | copy-start | bytes 7077892
  7.2 42.7 %all-gather.21.cloned.1.call-start = ((), (), s32[]{:S(2)}) async-start(), calls=%async_computation.18 | async-start | bytes 1966080 | tf_op jit(solution)/shard_map/all_gather | solution.py:44
  9.5 78.5 %all-gather.17.cloned.1.call-start = ((), (), s32[]{:S(2)}) async-start(), calls=%async_computation.16 | async-start | bytes 1966080 | tf_op jit(solution)/shard_map/all_gather | solution.py:44
  14.2 552.5 %copy-start.73 = (f32[4,3,64]{2,1,0:T(4,128)}, f32[4,3,64]{2,1,0:T(4,128)S(1)}, u32[]{:S(2)}) copy-start(f32[4,3,64]{2,1,0:T(4,128)S(1)} %add.432) | copy-start | bytes 9220
  108.9 15.2 %all-to-all-start = ((bf16[4,256,192]{1,2,0:T(8,128)(2,1)}), bf16[4,256,192]{1,2,0:T(8,128)(2,1)}, u32[]{:S(2)}, u32[]{:S(2)}) async-start(bf16[4,256,192]{1,2,0:T(8,128)(2,1)} %convert_element_type.518), calls=%async_computation.2 | async-start | bytes 786432 | tf_op jit(solution)/shard_map/all_to_all | solution.py:171
  124.2 53.8 %all-to-all-start.1 = ((bf16[4,192,768]{2,1,0:T(8,128)(2,1)}), bf16[4,192,768]{2,1,0:T(8,128)(2,1)}, u32[]{:S(2)}, u32[]{:S(2)}) async-start(bf16[4,192,768]{2,1,0:T(8,128)(2,1)} %gather_fusion.2), calls=%async_computation.3 | async-start | bytes 2359296 | tf_op jit(solution)/shard_map/all_to_all | solution.py:307
  128.5 57.1 %reduce-scatter.8.cloned.1.call-start = ((), (), s32[]{:S(2)}) async-start(), calls=%async_computation.9 | async-start | bytes 1966080 | tf_op jit(solution)/shard_map/reduce_scatter | solution.py:49
  131.6 88.4 %all-gather.23.cloned.1.call-start = ((), (), s32[]{:S(2)}) async-start(), calls=%async_computation.19 | async-start | bytes 1966080 | tf_op jit(solution)/shard_map/all_gather | solution.py:44
  135.9 44.7 %copy-start.28 = (f32[256,768]{1,0:T(8,128)}, f32[256,768]{1,0:T(8,128)S(1)}, u32[]{:S(2)}) copy-start(f32[256,768]{1,0:T(8,128)S(1)} %fusion.132) | copy-start | bytes 2359300
  182.6 74.8 %all-gather.19.cloned.1.call-start = ((), (), s32[]{:S(2)}) async-start(), calls=%async_computation.17 | async-start | bytes 1966080 | tf_op jit(solution)/shard_map/all_gather | solution.py:44
  189.7 126.2 %reduce-scatter.10.cloned.1.call-start = ((), (), s32[]{:S(2)}) async-start(), calls=%async_computation.10 | async-start | bytes 1966080 | tf_op jit(solution)/shard_map/reduce_scatter | solution.py:49
  190.7 73.7 %copy-start.81 = (f32[4,768]{1,0:T(4,128)}, f32[4,768]{1,0:T(4,128)S(1)}, u32[]{:S(2)}) copy-start(f32[4,768]{1,0:T(4,128)S(1)} %convert_element_type.505) | copy-start | bytes 36868
  220.0 58.8 %slice-start = ((s8[4718592]{0:T(1024)(128)(4,1)}), s8[524288]{0:T(1024)(128)(4,1)S(1)}, s32[]{:S(2)}) async-start(s8[4718592]{0:T(1024)(128)(4,1)} %bitcast.336), calls=%async_computation.24 | async-start | bytes 1048576
  257.4 21.4 %slice-start.1 = ((s8[4718592]{0:T(1024)(128)(4,1)}), s8[4194304]{0:T(1024)(128)(4,1)S(1)}, s32[]{:S(2)}) async-start(s8[4718592]{0:T(1024)(128)(4,1)} %bitcast.336), calls=%async_computation.25 | async-start | bytes 8388608
  281.4 71.1 %reduce-scatter.12.cloned.1.call-start = ((), (), s32[]{:S(2)}) async-start(), calls=%async_computation.11 | async-start | bytes 1966080 | tf_op jit(solution)/shard_map/reduce_scatter | solution.py:49
  286.4 29.5 %copy-start.48 = (f32[256,768]{1,0:T(8,128)S(1)}, f32[256,768]{1,0:T(8,128)}, u32[]{:S(2)}) copy-start(f32[256,768]{1,0:T(8,128)} %get-tuple-element.75) | copy-start | bytes 2359300
  286.4 107.6 %all-gather.25.cloned.1.call-start = ((), (), s32[]{:S(2)}) async-start(), calls=%async_computation.20 | async-start | bytes 1966080 | tf_op jit(solution)/shard_map/all_gather | solution.py:44
  286.8 67.7 %copy-start.18 = (f32[256,768]{1,0:T(8,128)}, f32[256,768]{1,0:T(8,128)S(1)}, u32[]{:S(2)}) copy-start(f32[256,768]{1,0:T(8,128)S(1)} %fusion.131) | copy-start | bytes 2359300
  315.9 38.5 %copy-start.39 = (bf16[512,768]{1,0:T(8,128)(2,1)S(1)}, bf16[512,768]{1,0:T(8,128)(2,1)}, u32[]{:S(2)}) copy-start(bf16[512,768]{1,0:T(8,128)(2,1)} %param.14) | copy-start | bytes 2359300
  317.4 37.8 %copy-start.86 = (f32[256]{0:T(256)}, f32[256]{0:T(256)S(1)}, u32[]{:S(2)}) copy-start(f32[256]{0:T(256)S(1)} %broadcast_multiply_fusion.10) | copy-start | bytes 3076
  317.6 37.5 %copy-start.98 = (f32[256]{0:T(256)}, f32[256]{0:T(256)S(1)}, u32[]{:S(2)}) copy-start(f32[256]{0:T(256)S(1)} %add_rsqrt_fusion.2) | copy-start | bytes 3076
  358.0 73.5 %all-gather.29.cloned.1.call-start = ((), (), s32[]{:S(2)}) async-start(), calls=%async_computation.22 | async-start | bytes 1966080 | tf_op jit(solution)/shard_map/all_gather | solution.py:44
  358.7 157.9 %reduce-scatter.14.cloned.1.call-start = ((), (), s32[]{:S(2)}) async-start(), calls=%async_computation.12 | async-start | bytes 1966080 | tf_op jit(solution)/shard_map/reduce_scatter | solution.py:49
  444.1 82.5 %reduce-scatter.18.cloned.1.call-start = ((), (), s32[]{:S(2)}) async-start(), calls=%async_computation.14 | async-start | bytes 1966080 | tf_op jit(solution)/shard_map/reduce_scatter | solution.py:49
  452.2 12.4 %collective-permute-start.17 = (bf16[768,768]{1,0:T(8,128)(2,1)S(1)}, bf16[768,768]{1,0:T(8,128)(2,1)S(1)}, u32[]{:S(2)}, u32[]{:S(2)}) collective-permute-start(bf16[768,768]{1,0:T(8,128)(2,1)S(1)} %fusion.78), channel_id=1, source_target_pairs={{0,4},{4,0},{8,12},{12,8},{16,20},{20,16},{24,28},{28,24},{1,5},{5... | collective-permute-start | bytes 3538952 | tf_op jit(solution)/shard_map/ppermute | solution.py:83
  459.6 7.3 %collective-permute-start.23 = (bf16[768,768]{1,0:T(8,128)(2,1)S(1)}, bf16[768,768]{1,0:T(8,128)(2,1)S(1)}, u32[]{:S(2)}, u32[]{:S(2)}) collective-permute-start(bf16[768,768]{1,0:T(8,128)(2,1)S(1)} %fusion.79), channel_id=1, source_target_pairs={{0,4},{4,0},{8,12},{12,8},{16,20},{20,16},{24,28},{28,24},{1,5},{5... | collective-permute-start | bytes 3538952 | tf_op jit(solution)/shard_map/ppermute | solution.py:83
  465.2 16.5 %collective-permute-start.18 = (bf16[384,768]{1,0:T(8,128)(2,1)S(1)}, bf16[384,768]{1,0:T(8,128)(2,1)S(1)}, u32[]{:S(2)}, u32[]{:S(2)}) collective-permute-start(bf16[384,768]{1,0:T(8,128)(2,1)S(1)} %select_convert_fusion.4), channel_id=1, source_target_pairs={{0,8},{4,12},{8,0},{12,4},{16,24},{20,28},{24,16},{28,20},{1,9},{5... | collective-permute-start | bytes 1769480 | tf_op jit(solution)/shard_map/ppermute | solution.py:83
  468.9 24.3 %collective-permute-start.24 = (bf16[384,768]{1,0:T(8,128)(2,1)}, bf16[384,768]{1,0:T(8,128)(2,1)S(1)}, u32[]{:S(2)}, u32[]{:S(2)}) collective-permute-start(bf16[384,768]{1,0:T(8,128)(2,1)} %select_convert_fusion.3), channel_id=1, source_target_pairs={{0,8},{4,12},{8,0},{12,4},{16,24},{20,28},{24,16},{28,20},{1,9},{5... | collective-permute-start | bytes 1769480 | tf_op jit(solution)/shard_map/ppermute | solution.py:83
  472.4 88.4 %all-gather.27.cloned.1.call-start = ((), (), s32[]{:S(2)}) async-start(), calls=%async_computation.21 | async-start | bytes 1966080 | tf_op jit(solution)/shard_map/all_gather | solution.py:44
  483.5 11.6 %collective-permute-start.19 = (bf16[192,768]{1,0:T(8,128)(2,1)S(1)}, bf16[192,768]{1,0:T(8,128)(2,1)S(1)}, u32[]{:S(2)}, u32[]{:S(2)}) collective-permute-start(bf16[192,768]{1,0:T(8,128)(2,1)S(1)} %select_convert_fusion.7), channel_id=1, source_target_pairs={{0,16},{4,20},{8,24},{12,28},{16,0},{20,4},{24,8},{28,12},{1,17},{... | collective-permute-start | bytes 884744 | tf_op jit(solution)/shard_map/ppermute | solution.py:83
  493.5 9.9 %collective-permute-start.25 = (bf16[192,768]{1,0:T(8,128)(2,1)S(1)}, bf16[192,768]{1,0:T(8,128)(2,1)S(1)}, u32[]{:S(2)}, u32[]{:S(2)}) collective-permute-start(bf16[192,768]{1,0:T(8,128)(2,1)S(1)} %select_convert_fusion.6), channel_id=1, source_target_pairs={{0,16},{4,20},{8,24},{12,28},{16,0},{20,4},{24,8},{28,12},{1,17},{... | collective-permute-start | bytes 884744 | tf_op jit(solution)/shard_map/ppermute | solution.py:83
  495.3 22.8 %copy-start.116 = (f32[2,1,768]{2,0,1:T(2,128)S(1)}, f32[2,1,768]{2,0,1:T(2,128)}, u32[]{:S(2)}) copy-start(f32[2,1,768]{2,0,1:T(2,128)} %convolution_bitcast_fusion.6) | copy-start | bytes 18436
  495.3 23.5 %copy-start.12 = (f32[256,768]{1,0:T(8,128)S(1)}, f32[256,768]{1,0:T(8,128)}, u32[]{:S(2)}) copy-start(f32[256,768]{1,0:T(8,128)} %copy-done.11) | copy-start | bytes 2359300
  495.3 23.5 %copy-start.32 = (f32[256,768]{1,0:T(8,128)S(1)}, f32[256,768]{1,0:T(8,128)}, u32[]{:S(2)}) copy-start(f32[256,768]{1,0:T(8,128)} %copy-done.31) | copy-start | bytes 2359300
  495.3 23.4 %copy-start.85 = (f32[256]{0:T(256)S(1)}, f32[256]{0:T(256)}, u32[]{:S(2)}) copy-start(f32[256]{0:T(256)} %copy-done.84) | copy-start | bytes 3076
  495.3 23.4 %copy-start.97 = (f32[256]{0:T(256)S(1)}, f32[256]{0:T(256)}, u32[]{:S(2)}) copy-start(f32[256]{0:T(256)} %copy-done.96) | copy-start | bytes 3076
  495.3 14.4 %collective-permute-start.20 = (bf16[192,768]{1,0:T(8,128)(2,1)S(1)}, bf16[192,768]{1,0:T(8,128)(2,1)S(1)}, u32[]{:S(2)}, u32[]{:S(2)}) collective-permute-start(bf16[192,768]{1,0:T(8,128)(2,1)S(1)} %add_convert_fusion.1), channel_id=1, source_target_pairs={{0,16},{4,20},{8,24},{12,28},{16,0},{20,4},{24,8},{28,12},{1,17},{... | collective-permute-start | bytes 884744 | tf_op jit(solution)/shard_map/ppermute | solution.py:88
  503.5 10.7 %collective-permute-start.26 = (bf16[192,768]{1,0:T(8,128)(2,1)S(1)}, bf16[192,768]{1,0:T(8,128)(2,1)S(1)}, u32[]{:S(2)}, u32[]{:S(2)}) collective-permute-start(bf16[192,768]{1,0:T(8,128)(2,1)S(1)} %add_convert_fusion), channel_id=1, source_target_pairs={{0,16},{4,20},{8,24},{12,28},{16,0},{20,4},{24,8},{28,12},{1,17},{... | collective-permute-start | bytes 884744 | tf_op jit(solution)/shard_map/ppermute | solution.py:88
  510.7 23.8 %collective-permute-start.21 = (bf16[384,768]{1,0:T(8,128)(2,1)}, bf16[384,768]{1,0:T(8,128)(2,1)}, u32[]{:S(2)}, u32[]{:S(2)}) collective-permute-start(bf16[384,768]{1,0:T(8,128)(2,1)} %maximum_select_fusion.7), channel_id=1, source_target_pairs={{0,8},{4,12},{8,0},{12,4},{16,24},{20,28},{24,16},{28,20},{1,9},{5... | collective-permute-start | bytes 1769480 | tf_op jit(solution)/shard_map/ppermute | solution.py:88
  515.2 25.2 %collective-permute-start.27 = (bf16[384,768]{1,0:T(8,128)(2,1)}, bf16[384,768]{1,0:T(8,128)(2,1)}, u32[]{:S(2)}, u32[]{:S(2)}) collective-permute-start(bf16[384,768]{1,0:T(8,128)(2,1)} %maximum_select_fusion.8), channel_id=1, source_target_pairs={{0,8},{4,12},{8,0},{12,4},{16,24},{20,28},{24,16},{28,20},{1,9},{5... | collective-permute-start | bytes 1769480 | tf_op jit(solution)/shard_map/ppermute | solution.py:88
  523.8 75.0 %all-gather.31.cloned.1.call-start = ((), (), s32[]{:S(2)}) async-start(), calls=%async_computation.23 | async-start | bytes 1966080 | tf_op jit(solution)/shard_map/all_gather | solution.py:44
  533.8 6.4 collective-permute-start.6
  537.4 129.0 %collective-permute-start.22 = (bf16[768,768]{1,0:T(8,128)(2,1)}, bf16[768,768]{1,0:T(8,128)(2,1)}, u32[]{:S(2)}, u32[]{:S(2)}) collective-permute-start(bf16[768,768]{1,0:T(8,128)(2,1)} %maximum_select_fusion.3), channel_id=1, source_target_pairs={{0,4},{4,0},{8,12},{12,8},{16,20},{20,16},{24,28},{28,24},{1,5},{5... | collective-permute-start | bytes 3538952 | tf_op jit(solution)/shard_map/ppermute | solution.py:88
  537.4 153.6 %reduce-scatter.20.cloned.1.call-start = ((), (), s32[]{:S(2)}) async-start(), calls=%async_computation.15 | async-start | bytes 1966080 | tf_op jit(solution)/shard_map/reduce_scatter | solution.py:49
  540.3 7.2 %collective-permute-start.7 = (f32[3,2,2,768]{3,1,2,0:T(2,128)S(1)}, f32[3,2,2,768]{3,1,2,0:T(2,128)S(1)}, u32[]{:S(2)}, u32[]{:S(2)}) collective-permute-start(f32[3,2,2,768]{3,1,2,0:T(2,128)S(1)} %fusion.275), channel_id=1, source_target_pairs={{0,2},{1,3},{2,0},{3,1},{4,6},{5,7},{6,4},{7,5},{8,10},{9,11},{10,... | collective-permute-start | bytes 110600 | tf_op jit(solution)/shard_map/ppermute | solution.py:102
  543.4 130.4 %collective-permute-start.28 = (bf16[768,768]{1,0:T(8,128)(2,1)}, bf16[768,768]{1,0:T(8,128)(2,1)}, u32[]{:S(2)}, u32[]{:S(2)}) collective-permute-start(bf16[768,768]{1,0:T(8,128)(2,1)} %maximum_select_fusion.4), channel_id=1, source_target_pairs={{0,4},{4,0},{8,12},{12,8},{16,20},{20,16},{24,28},{28,24},{1,5},{5... | collective-permute-start | bytes 3538952 | tf_op jit(solution)/shard_map/ppermute | solution.py:88
  569.4 31.9 %copy-start.5 = (f32[4,2,3,128,128]{3,4,2,1,0:T(8,128)S(1)}, f32[4,2,3,128,128]{3,4,2,1,0:T(8,128)}, u32[]{:S(2)}) copy-start(f32[4,2,3,128,128]{3,4,2,1,0:T(8,128)} %copy-done.4) | copy-start | bytes 4718596
  569.4 31.9 %copy-start.64 = (f32[4,2,3,128]{3,2,1,0:T(4,128)S(1)}, f32[4,2,3,128]{3,2,1,0:T(4,128)}, u32[]{:S(2)}) copy-start(f32[4,2,3,128]{3,2,1,0:T(4,128)} %copy-done.63) | copy-start | bytes 36868
  613.2 80.1 %reduce-scatter.16.cloned.1.call-start = ((), (), s32[]{:S(2)}) async-start(), calls=%async_computation.13 | async-start | bytes 1966080 | tf_op jit(solution)/shard_map/reduce_scatter | solution.py:49
  617.1 16.5 %collective-permute-start.8 = (f32[15,768]{1,0:T(8,128)}, f32[15,768]{1,0:T(8,128)S(1)}, u32[]{:S(2)}, u32[]{:S(2)}) collective-permute-start(f32[15,768]{1,0:T(8,128)} %pad_maximum_fusion.6), channel_id=1, source_target_pairs={{0,4},{4,0},{8,12},{12,8},{16,20},{20,16},{24,28},{28,24},{1,5},{5... | collective-permute-start | bytes 138248 | tf_op jit(solution)/shard_map/ppermute | solution.py:102
  624.5 10.8 %collective-permute-start = (bf16[576,768]{1,0:T(8,128)(2,1)}, bf16[576,768]{1,0:T(8,128)(2,1)}, u32[]{:S(2)}, u32[]{:S(2)}) collective-permute-start(bf16[576,768]{1,0:T(8,128)(2,1)} %bitcast.59), channel_id=1, source_target_pairs={{0,4},{4,0},{8,12},{12,8},{16,20},{20,16},{24,28},{28,24},{1,5},{5... | collective-permute-start | bytes 2654216 | tf_op jit(solution)/shard_map/ppermute | solution.py:83
  633.2 4.6 collective-permute-start.11
  633.7 35.6 %collective-permute-start.9 = (f32[15,768]{1,0:T(8,128)S(1)}, f32[15,768]{1,0:T(8,128)S(1)}, u32[]{:S(2)}, u32[]{:S(2)}) collective-permute-start(f32[15,768]{1,0:T(8,128)S(1)} %fusion.274), channel_id=1, source_target_pairs={{0,8},{4,12},{8,0},{12,4},{16,24},{20,28},{24,16},{28,20},{1,9},{5... | collective-permute-start | bytes 138248 | tf_op jit(solution)/shard_map/ppermute | solution.py:102
  637.2 13.1 %collective-permute-start.1 = (bf16[288,768]{1,0:T(8,128)(2,1)S(1)}, bf16[288,768]{1,0:T(8,128)(2,1)S(1)}, u32[]{:S(2)}, u32[]{:S(2)}) collective-permute-start(bf16[288,768]{1,0:T(8,128)(2,1)S(1)} %select_convert_fusion.5), channel_id=1, source_target_pairs={{0,8},{4,12},{8,0},{12,4},{16,24},{20,28},{24,16},{28,20},{1,9},{5... | collective-permute-start | bytes 1327112 | tf_op jit(solution)/shard_map/ppermute | solution.py:83
  638.9 13.3 %collective-permute-start.12 = (bf16[96,768]{1,0:T(8,128)(2,1)S(1)}, bf16[96,768]{1,0:T(8,128)(2,1)S(1)}, u32[]{:S(2)}, u32[]{:S(2)}) collective-permute-start(bf16[96,768]{1,0:T(8,128)(2,1)S(1)} %select_convert_fusion.10), channel_id=1, source_target_pairs={{0,8},{4,12},{8,0},{12,4},{16,24},{20,28},{24,16},{28,20},{1,9},{5... | collective-permute-start | bytes 442376 | tf_op jit(solution)/shard_map/ppermute | solution.py:83
  650.5 6.7 collective-permute-start.2
  657.2 6.7 collective-permute-start.3
  658.8 6.0 collective-permute-start.13
  664.0 9.4 %collective-permute-start.4 = (bf16[288,768]{1,0:T(8,128)(2,1)S(1)}, bf16[288,768]{1,0:T(8,128)(2,1)S(1)}, u32[]{:S(2)}, u32[]{:S(2)}) collective-permute-start(bf16[288,768]{1,0:T(8,128)(2,1)S(1)} %maximum_select_fusion.9), channel_id=1, source_target_pairs={{0,8},{4,12},{8,0},{12,4},{16,24},{20,28},{24,16},{28,20},{1,9},{5... | collective-permute-start | bytes 1327112 | tf_op jit(solution)/shard_map/ppermute | solution.py:88
  664.8 5.1 collective-permute-start.14
  669.3 12.4 %collective-permute-start.10 = (f32[15,768]{1,0:T(8,128)S(1)}, f32[15,768]{1,0:T(8,128)S(1)}, u32[]{:S(2)}, u32[]{:S(2)}) collective-permute-start(f32[15,768]{1,0:T(8,128)S(1)} %add.491), channel_id=1, source_target_pairs={{0,16},{4,20},{8,24},{12,28},{16,0},{20,4},{24,8},{28,12},{1,17},{... | collective-permute-start | bytes 138248 | tf_op jit(solution)/shard_map/ppermute | solution.py:102
  669.9 12.4 %collective-permute-start.15 = (bf16[96,768]{1,0:T(8,128)(2,1)S(1)}, bf16[96,768]{1,0:T(8,128)(2,1)S(1)}, u32[]{:S(2)}, u32[]{:S(2)}) collective-permute-start(bf16[96,768]{1,0:T(8,128)(2,1)S(1)} %maximum_select_fusion.11), channel_id=1, source_target_pairs={{0,8},{4,12},{8,0},{12,4},{16,24},{20,28},{24,16},{28,20},{1,9},{5... | collective-permute-start | bytes 442376 | tf_op jit(solution)/shard_map/ppermute | solution.py:88
  673.7 13.0 %collective-permute-start.5 = (bf16[576,768]{1,0:T(8,128)(2,1)S(1)}, bf16[576,768]{1,0:T(8,128)(2,1)}, u32[]{:S(2)}, u32[]{:S(2)}) collective-permute-start(bf16[576,768]{1,0:T(8,128)(2,1)S(1)} %maximum_select_fusion.5), channel_id=1, source_target_pairs={{0,4},{4,0},{8,12},{12,8},{16,20},{20,16},{24,28},{28,24},{1,5},{5... | collective-permute-start | bytes 2654216 | tf_op jit(solution)/shard_map/ppermute | solution.py:88
  682.4 3.1 collective-permute-start.16
  (112 other events, 514.5 us)
Sparse Core Ops, SparseCore 0:
  10.2 39.7 all-gather.20
  52.1 35.8 all-gather.16
  132.2 49.2 reduce-scatter.7
  183.5 36.5 all-gather.22
  221.5 35.8 all-gather.18
  281.6 34.2 reduce-scatter.9
  318.2 34.2 reduce-scatter.11
  358.1 35.8 all-gather.24
  395.6 35.8 all-gather.28
  444.2 34.2 reduce-scatter.13
  481.4 34.2 reduce-scatter.17
  523.9 36.7 all-gather.26
  562.9 35.8 all-gather.30
  613.4 34.3 reduce-scatter.19
  649.9 34.2 reduce-scatter.15

commit v9 on v5

--- a/solution.py
+++ b/solution.py
@@ -253,7 +253,7 @@
     d_key = d_key.reshape(n_seg, seg_rows, -1).astype(jnp.bfloat16)
     d_proj = jnp.stack([d_query, d_key, d_value])
     grad_qkv = jnp.einsum(
-        "strd,jsre->tjde", masked(input_segs, seg_hot), d_proj, preferred_element_type=jnp.float32
+        "strd,jsre->tjed", masked(input_segs, seg_hot), d_proj, preferred_element_type=jnp.float32
     )
     grad_qv = jnp.stack(
         [
@@ -324,9 +324,18 @@
     )
     small = sum(smalls[1:], smalls[0])
     up_total, down_total = dp_sum_low((grad_up, grad_down))
-    qkv_total, out_total = dp_sum_low((grad_qkv, grad_out_w))
+    qkv_t_total, out_total = dp_sum_low((grad_qkv, grad_out_w))
+    qkv_total = jnp.swapaxes(qkv_t_total, 2, 3)
     (small_grads,) = exact_sum((small,), "tensor")
-    qv_total, ubias_total, small_total = exact_sum((grad_qv, grad_ubias, small_grads), "dp")
+    width = small.shape[-1]
+    packed = jnp.concatenate(
+        [small_grads.reshape(-1, width), grad_ubias.reshape(-1, width), grad_qv.reshape(-1, width)]
+    )
+    (packed,) = exact_sum((packed,), "dp")
+    n_small, n_ubias = small_grads.size // width, grad_ubias.size // width
+    small_total = packed[:n_small].reshape(small_grads.shape)
+    ubias_total = packed[n_small : n_small + n_ubias].reshape(grad_ubias.shape)
+    qv_total = packed[n_small + n_ubias :].reshape(grad_qv.shape)
     return (
         layer_out,
         input_grad,

time: 673 us -> 643 us (0.955)
  local copies, waits for them, and re-layouts: 108 us -> 92.8 us
    unnamed x279 -> x310, local copies, waits for them, and re-layouts: 19.9 us -> 8.75 us
    all_gather x8, waiting for transfers between devices: 146 us -> 156 us  [gather_rows(): return lax.all_gather(local_rows, 'tensor', axis=0, tiled=False)]
    convert_element_type x2 -> x0, local copies, waits for them, and re-layouts: 7.38 us -> none  [the longest x1 6.62 us: dp_sum_low(): c.astype(jnp.float32).reshape(shape)]
    ppermute x11 -> x5, waiting for transfers between devices: 12.3 us -> 5.52 us  [exact_sum(): lax.ppermute(values, axis, dp_perm(n_ax, 1 << b))]
    select_n x11 -> x12, other arithmetic: 13.6 us -> 16.3 us  [dp_sum_low(): jnp.where(upper, jnp.concatenate([g, c]), jnp.concatenate([c, g]))]
  transfers between devices with their start and end apart: 52 -> 46, of which waited for: 24 -> 26; matrix products, arithmetic and copies ran while one was open for 43% -> 44% of each run, Pallas kernels for 0% -> 0%
where the time goes in v9:
time: 643 us; the launch traced here: 633 us
  waiting for transfers between devices  274 us (43%)
  matrix products  131 us (20%)
  local copies, waits for them, and re-layouts  92.8 us (14%)
  other arithmetic  79.3 us (12%)
  starting transfers between devices  39.3 us (6%)
  between operations  16.8 us (3%)
    all_gather x8, waiting for transfers between devices, gather_rows(): return lax.all_gather(local_rows, 'tensor', axis=0, tiled=False)  156 us
    reduce_scatter x6, waiting for transfers between devices, scatter_sum(): lax.psum_scatter(seg_parts.reshape(n_seg * seg_rows, width).astype(jnp.bf...  55.3 us
    ppermute x12, waiting for transfers between devices, dp_sum_low(): gots = lax.ppermute(sends, 'dp', dp_perm(n_dp, 1 << b))  40.1 us
    dot_general x12, matrix products, pick(): return jnp.dot(kind_hot, kind_table.astype(jnp.float32), precision=highest)  17.3 us
    select_n x12, other arithmetic, dp_sum_low(): jnp.where(upper, jnp.concatenate([g, c]), jnp.concatenate([c, g]))  16.3 us
    convert_element_type x2, other arithmetic, stream(): activ = jax.nn.gelu(pre_act, approximate=False).astype(jnp.bfloat16)  14.6 us
    ppermute x12, waiting for transfers between devices, dp_sum_low(): gots = lax.ppermute(tuple(cur), 'dp', dp_perm(n_dp, 1 << b))  14.1 us
    dot_general x12, matrix products, type_sum(): jnp.einsum('rt,rd->td', kind_hot, values, precision=lax.Precision.HIGHEST)  13 us
  transfers between devices with their start and end apart: 46, of which 26 were waited for; matrix products, arithmetic and copies ran while one was open for 44% of the time, Pallas kernels for 0%

profile of v9, /device:TPU:0, one launch (start us, length us, event | category | flops | bytes accessed | tf_op | source)
XLA Modules:
  0.0 633.4 jit_solution(5949901925949443304)
XLA Ops:
  13.0 6.3 %all-to-all-start.1 = ((bf16[4,192,768]{2,1,0:T(8,128)(2,1)}), bf16[4,192,768]{2,1,0:T(8,128)(2,1)}, u32[]{:S(2)}, u32[]{:S(2)}) async-start(bf16[4,192,768]{2,1,0:T(8,128)(2,1)} %gather_fusion.4), calls=%async_computation.1 | async-start | bytes 2359296 | tf_op jit(solution)/shard_map/all_to_all | solution.py:301
  22.7 4.0 gather_fusion.9
  26.7 4.1 gather_fusion.1
  36.7 2.6 compare_select_fusion.4
  41.8 31.7 %all-gather.21.cloned.1.call-done = bf16[1024,768]{1,0:T(8,128)(2,1)} async-done(((bf16[256,768]{1,0:T(8,128)(2,1)}), bf16[1024,768]{1,0:T(8,128)(2,1)}) %all-gather.21.cloned.1.call-update) | async-done | bytes 1572880 | tf_op jit(solution)/shard_map/all_gather | solution.py:44
  73.5 3.6 convolution_bitcast_fusion
  89.2 22.6 %all-gather.17.cloned.1.call-done = bf16[1024,768]{1,0:T(8,128)(2,1)} async-done(((bf16[256,768]{1,0:T(8,128)(2,1)}), bf16[1024,768]{1,0:T(8,128)(2,1)}) %all-gather.17.cloned.1.call-update) | async-done | bytes 1572880 | tf_op jit(solution)/shard_map/all_gather | solution.py:44
  111.8 5.0 convolution_bitcast_fusion.1
  116.9 4.1 all-to-all-start.2
  121.1 2.6 fusion.212
  143.0 3.5 all-to-all-start
  148.6 3.2 gather_fusion.14
  151.7 3.2 gather_fusion.7
  154.9 5.0 gather_fusion.12
  159.9 3.2 gather_fusion.5
  165.0 2.6 compare_select_fusion.7
  174.7 7.5 %all-gather.23.cloned.1.call-done = bf16[1024,768]{1,0:T(8,128)(2,1)} async-done(((bf16[256,768]{1,0:T(8,128)(2,1)}), bf16[1024,768]{1,0:T(8,128)(2,1)}) %all-gather.23.cloned.1.call-update) | async-done | bytes 1572880 | tf_op jit(solution)/shard_map/all_gather | solution.py:44
  182.3 5.1 fusion.93
  187.3 7.3 %fusion.6 = bf16[4,256,768]{2,1,0:T(8,128)(2,1)S(1)} fusion(f32[4,256,768]{2,1,0:T(8,128)S(1)} %get-tuple-element.66, f32[4,768]{1,0:T(4,128)S(1)} %copy-done.96, u8[256,768]{1,0:T(8,128)(4,1)S(1)} %get-tuple-element.14, u8[256,768]{1,0:T(8,128)(4,1)S(1)} %get-tuple-element.13), kind=kLoop, calls=%fused_computation.30 | loop fusion | flops 55836672 | bytes 5124096 | tf_op jit(solution)/shard_map/convert_element_type | solution.py:190
  194.7 2.6 convolution_convert_fusion.4
  197.5 22.6 %all-gather.19.cloned.1.call-done = bf16[1024,768]{1,0:T(8,128)(2,1)} async-done(((bf16[256,768]{1,0:T(8,128)(2,1)}), bf16[1024,768]{1,0:T(8,128)(2,1)}) %all-gather.19.cloned.1.call-update) | async-done | bytes 1572880 | tf_op jit(solution)/shard_map/all_gather | solution.py:44
  220.2 5.1 fusion.92
  225.2 7.3 %fusion.3 = bf16[4,256,768]{2,1,0:T(8,128)(2,1)S(1)} fusion(f32[4,256,768]{2,1,0:T(8,128)S(1)} %get-tuple-element.75, f32[4,768]{1,0:T(4,128)S(1)} %copy-done.97, u8[256,768]{1,0:T(8,128)(4,1)S(1)} %get-tuple-element.12, u8[256,768]{1,0:T(8,128)(4,1)S(1)} %get-tuple-element.11), kind=kLoop, calls=%fused_computation.27 | loop fusion | flops 55836672 | bytes 5124096 | tf_op jit(solution)/shard_map/convert_element_type | solution.py:190
  232.6 2.6 convolution_convert_fusion.5
  236.5 20.7 %reduce-scatter.9.cloned.1.call-done = bf16[256,768]{1,0:T(8,128)(2,1)} async-done(((bf16[1024,768]{1,0:T(8,128)(2,1)}), bf16[256,768]{1,0:T(8,128)(2,1)}) %reduce-scatter.9.cloned.1.call-update) | async-done | bytes 393232 | tf_op jit(solution)/shard_map/reduce_scatter | solution.py:49
  259.1 34.6 %reduce-scatter.7.cloned.1.call-done = bf16[256,768]{1,0:T(8,128)(2,1)} async-done(((bf16[1024,768]{1,0:T(8,128)(2,1)}), bf16[256,768]{1,0:T(8,128)(2,1)}) %reduce-scatter.7.cloned.1.call-update) | async-done | bytes 393232 | tf_op jit(solution)/shard_map/reduce_scatter | solution.py:49
  299.5 2.8 gather_fusion.15
  307.2 2.7 copy.91
  309.8 2.6 copy.88
  312.4 2.6 copy.97
  315.0 2.6 copy.96
  317.6 2.6 copy.99
  320.2 2.6 copy.98
  328.2 7.2 %all-gather.25.cloned.1.call-done = bf16[1024,768]{1,0:T(8,128)(2,1)} async-done(((bf16[256,768]{1,0:T(8,128)(2,1)}), bf16[1024,768]{1,0:T(8,128)(2,1)}) %all-gather.25.cloned.1.call-update) | async-done | bytes 1572880 | tf_op jit(solution)/shard_map/all_gather | solution.py:44
  335.5 6.4 %convert_reduce_fusion.1 = (f32[4,768]{1,0:T(4,128)}, bf16[4,256,768]{2,1,0:T(8,128)(2,1)S(1)}) fusion(f32[4,256,768]{2,1,0:T(8,128)} %copy-done.47, f32[4,768]{1,0:T(4,128)} %convert_element_type.516, bf16[4,256,768]{2,1,0:T(8,128)(2,1)} %bitcast.413, bf16[4,768,768]{2,1,0:T(8,128)(2,1)} %gather_fusion.7), kind=kOutput, calls=%fused_computation.65 | convolution fusion | flops 1219752960 | bytes 11034624 | tf_op jit(solution)/shard_map/srd,sfd->srf/dot_general | solution.py:205
  341.8 5.7 convolution_convert_fusion.2
  348.0 24.9 %all-gather.29.cloned.1.call-done = bf16[1024,768]{1,0:T(8,128)(2,1)} async-done(((bf16[256,768]{1,0:T(8,128)(2,1)}), bf16[1024,768]{1,0:T(8,128)(2,1)}) %all-gather.29.cloned.1.call-update) | async-done | bytes 1572880 | tf_op jit(solution)/shard_map/all_gather | solution.py:44
  373.0 6.5 %convert_reduce_fusion = (f32[4,768]{1,0:T(4,128)}, bf16[4,256,768]{2,1,0:T(8,128)(2,1)S(1)}) fusion(f32[4,256,768]{2,1,0:T(8,128)} %copy-done.46, f32[4,768]{1,0:T(4,128)} %convert_element_type.532, bf16[4,256,768]{2,1,0:T(8,128)(2,1)} %bitcast.415, bf16[4,768,768]{2,1,0:T(8,128)(2,1)} %gather_fusion.14), kind=kOutput, calls=%fused_computation.64 | convolution fusion | flops 1219752960 | bytes 11034624 | tf_op jit(solution)/shard_map/srd,sfd->srf/dot_general | solution.py:205
  379.5 2.7 fusion.25
  382.2 2.8 bitcast_add_fusion.1
  386.9 2.7 fusion.21
  389.6 2.7 bitcast_add_fusion
  401.9 2.6 convolution_convert_fusion
  404.5 9.7 %collective-permute-done.18 = bf16[384,768]{1,0:T(8,128)(2,1)S(1)} collective-permute-done((bf16[384,768]{1,0:T(8,128)(2,1)}, bf16[384,768]{1,0:T(8,128)(2,1)S(1)}, u32[]{:S(2)}, u32[]{:S(2)}) %collective-permute-start.18) | collective-permute-done | bytes 589856 | tf_op jit(solution)/shard_map/ppermute | solution.py:83
  417.7 8.1 %collective-permute-done.24 = bf16[384,768]{1,0:T(8,128)(2,1)S(1)} collective-permute-done((bf16[384,768]{1,0:T(8,128)(2,1)}, bf16[384,768]{1,0:T(8,128)(2,1)S(1)}, u32[]{:S(2)}, u32[]{:S(2)}) %collective-permute-start.24) | collective-permute-done | bytes 589856 | tf_op jit(solution)/shard_map/ppermute | solution.py:83
  428.5 7.5 %collective-permute-done.25 = bf16[192,768]{1,0:T(8,128)(2,1)S(1)} collective-permute-done((bf16[192,768]{1,0:T(8,128)(2,1)S(1)}, bf16[192,768]{1,0:T(8,128)(2,1)S(1)}, u32[]{:S(2)}, u32[]{:S(2)}) %collective-permute-start.25) | collective-permute-done | bytes 294944 | tf_op jit(solution)/shard_map/ppermute | solution.py:83
  438.4 3.9 collective-permute-done.20
  459.9 2.9 maximum_select_fusion.3
  468.1 2.9 maximum_select_fusion.4
  471.0 3.0 collective-permute-done.7
  476.9 12.3 %all-gather.27.cloned.1.call-done = bf16[1024,768]{1,0:T(8,128)(2,1)} async-done(((bf16[256,768]{1,0:T(8,128)(2,1)}), bf16[1024,768]{1,0:T(8,128)(2,1)}) %all-gather.27.cloned.1.call-update) | async-done | bytes 1572880 | tf_op jit(solution)/shard_map/all_gather | solution.py:44
  489.2 2.8 convolution_convert_fusion.11
  500.2 26.9 %all-gather.31.cloned.1.call-done = bf16[1024,768]{1,0:T(8,128)(2,1)} async-done(((bf16[256,768]{1,0:T(8,128)(2,1)}), bf16[1024,768]{1,0:T(8,128)(2,1)}) %all-gather.31.cloned.1.call-update) | async-done | bytes 1572880 | tf_op jit(solution)/shard_map/all_gather | solution.py:44
  537.3 4.8 bitcast_convert_fusion.1
  546.5 3.3 fusion.17
  559.7 2.7 bitcast_convert_fusion
  570.2 9.9 %collective-permute-done.1 = bf16[288,768]{1,0:T(8,128)(2,1)S(1)} collective-permute-done((bf16[288,768]{1,0:T(8,128)(2,1)S(1)}, bf16[288,768]{1,0:T(8,128)(2,1)S(1)}, u32[]{:S(2)}, u32[]{:S(2)}) %collective-permute-start.1) | collective-permute-done | bytes 442400 | tf_op jit(solution)/shard_map/ppermute | solution.py:83
  582.5 3.7 collective-permute-done.2
  588.5 3.8 collective-permute-done.3
  594.9 2.9 maximum_select_fusion
  599.7 3.4 collective-permute-done.4
  603.5 2.7 maximum_select_fusion.1
  606.2 2.5 convert.16
  608.8 2.5 convert.15
  (615 shorter events, 188.9 us)
Async XLA Ops:
  7.2 141.4 %copy-start = (bf16[2,768,768]{2,1,0:T(8,128)(2,1)S(1)}, bf16[2,768,768]{2,1,0:T(8,128)(2,1)}, u32[]{:S(2)}) copy-start(bf16[2,768,768]{2,1,0:T(8,128)(2,1)} %param.25) | copy-start | bytes 7077892
  7.2 66.3 %all-gather.21.cloned.1.call-start = ((), (), s32[]{:S(2)}) async-start(), calls=%async_computation.17 | async-start | bytes 1966080 | tf_op jit(solution)/shard_map/all_gather | solution.py:44
  13.0 103.8 %all-to-all-start.1 = ((bf16[4,192,768]{2,1,0:T(8,128)(2,1)}), bf16[4,192,768]{2,1,0:T(8,128)(2,1)}, u32[]{:S(2)}, u32[]{:S(2)}) async-start(bf16[4,192,768]{2,1,0:T(8,128)(2,1)} %gather_fusion.4), calls=%async_computation.1 | async-start | bytes 2359296 | tf_op jit(solution)/shard_map/all_to_all | solution.py:301
  19.4 92.5 %all-gather.17.cloned.1.call-start = ((), (), s32[]{:S(2)}) async-start(), calls=%async_computation.15 | async-start | bytes 1966080 | tf_op jit(solution)/shard_map/all_gather | solution.py:44
  21.5 125.2 %copy-start.126 = (s32[1024]{0:T(1024)}, s32[1024]{0:T(1024)S(1)}, u32[]{:S(2)}) copy-start(s32[1024]{0:T(1024)S(1)} %pad_clamp_fusion.1) | copy-start | bytes 12292
  33.4 52.9 %copy-start.90 = (f32[4,3,64]{2,1,0:T(4,128)}, f32[4,3,64]{2,1,0:T(4,128)S(1)}, u32[]{:S(2)}) copy-start(f32[4,3,64]{2,1,0:T(4,128)S(1)} %add.507) | copy-start | bytes 9220
  36.7 36.8 %copy-start.121 = (bf16[2,1,768]{2,1,0:T(2,128)(2,1)}, bf16[2,1,768]{2,1,0:T(2,128)(2,1)S(1)}, u32[]{:S(2)}) copy-start(bf16[2,1,768]{2,1,0:T(2,128)(2,1)S(1)} %get-tuple-element.54) | copy-start | bytes 9220
  116.9 15.3 %all-to-all-start.2 = ((bf16[4,256,192]{1,2,0:T(8,128)(2,1)}), bf16[4,256,192]{1,2,0:T(8,128)(2,1)}, u32[]{:S(2)}, u32[]{:S(2)}) async-start(bf16[4,256,192]{1,2,0:T(8,128)(2,1)} %convert_element_type.530), calls=%async_computation.3 | async-start | bytes 786432 | tf_op jit(solution)/shard_map/all_to_all | solution.py:176
  121.0 61.2 %all-gather.23.cloned.1.call-start = ((), (), s32[]{:S(2)}) async-start(), calls=%async_computation.18 | async-start | bytes 1966080 | tf_op jit(solution)/shard_map/all_gather | solution.py:44
  143.0 26.4 %all-to-all-start = ((bf16[4,256,192]{1,2,0:T(8,128)(2,1)}), bf16[4,256,192]{1,2,0:T(8,128)(2,1)S(1)}, u32[]{:S(2)}, u32[]{:S(2)}) async-start(bf16[4,256,192]{1,2,0:T(8,128)(2,1)} %convert_element_type.514), calls=%async_computation | async-start | bytes 786432 | tf_op jit(solution)/shard_map/all_to_all | solution.py:176
  146.5 73.7 %all-gather.19.cloned.1.call-start = ((), (), s32[]{:S(2)}) async-start(), calls=%async_computation.16 | async-start | bytes 1966080 | tf_op jit(solution)/shard_map/all_gather | solution.py:44
  167.6 228.3 %copy-start.88 = (s32[256,1]{0,1:T(1,128)}, s32[256,1]{0,1:T(1,128)S(1)}, u32[]{:S(2)}) copy-start(s32[256,1]{0,1:T(1,128)S(1)} %compare_select_fusion.7) | copy-start | bytes 3076
  172.4 278.6 %copy-start.100 = (f32[256]{0:T(256)}, f32[256]{0:T(256)S(1)}, u32[]{:S(2)}) copy-start(f32[256]{0:T(256)S(1)} %broadcast_multiply_fusion.11) | copy-start | bytes 3076
  174.7 82.5 %reduce-scatter.9.cloned.1.call-start = ((), (), s32[]{:S(2)}) async-start(), calls=%async_computation.10 | async-start | bytes 1966080 | tf_op jit(solution)/shard_map/reduce_scatter | solution.py:49
  194.7 25.5 %copy-start.97 = (f32[4,768]{1,0:T(4,128)S(1)}, f32[4,768]{1,0:T(4,128)}, u32[]{:S(2)}) copy-start(f32[4,768]{1,0:T(4,128)} %convert_element_type.516) | copy-start | bytes 36868
  197.3 96.4 %reduce-scatter.7.cloned.1.call-start = ((), (), s32[]{:S(2)}) async-start(), calls=%async_computation.9 | async-start | bytes 1966080 | tf_op jit(solution)/shard_map/reduce_scatter | solution.py:49
  232.6 24.6 %copy-start.118 = (bf16[2,1,768]{2,1,0:T(2,128)(2,1)S(1)}, bf16[2,1,768]{2,1,0:T(2,128)(2,1)}, u32[]{:S(2)}) copy-start(bf16[2,1,768]{2,1,0:T(2,128)(2,1)} %get-tuple-element.52) | copy-start | bytes 9220
  235.3 100.2 %all-gather.25.cloned.1.call-start = ((), (), s32[]{:S(2)}) async-start(), calls=%async_computation.19 | async-start | bytes 1966080 | tf_op jit(solution)/shard_map/all_gather | solution.py:44
  259.1 38.4 %copy-start.112 = (f32[256]{0:T(256)}, f32[256]{0:T(256)S(1)}, u32[]{:S(2)}) copy-start(f32[256]{0:T(256)S(1)} %add_rsqrt_fusion) | copy-start | bytes 3076
  299.5 73.5 %all-gather.29.cloned.1.call-start = ((), (), s32[]{:S(2)}) async-start(), calls=%async_computation.21 | async-start | bytes 1966080 | tf_op jit(solution)/shard_map/all_gather | solution.py:44
  306.1 143.3 %reduce-scatter.11.cloned.1.call-start = ((), (), s32[]{:S(2)}) async-start(), calls=%async_computation.11 | async-start | bytes 1966080 | tf_op jit(solution)/shard_map/reduce_scatter | solution.py:49
  347.6 104.8 %reduce-scatter.15.cloned.1.call-start = ((), (), s32[]{:S(2)}) async-start(), calls=%async_computation.13 | async-start | bytes 1966080 | tf_op jit(solution)/shard_map/reduce_scatter | solution.py:49
  385.2 11.3 %collective-permute-start.17 = (bf16[768,768]{1,0:T(8,128)(2,1)S(1)}, bf16[768,768]{1,0:T(8,128)(2,1)S(1)}, u32[]{:S(2)}, u32[]{:S(2)}) collective-permute-start(bf16[768,768]{1,0:T(8,128)(2,1)S(1)} %fusion.78), channel_id=1, source_target_pairs={{0,4},{4,0},{8,12},{12,8},{16,20},{20,16},{24,28},{28,24},{1,5},{5... | collective-permute-start | bytes 3538952 | tf_op jit(solution)/shard_map/ppermute | solution.py:83
  392.5 6.8 %collective-permute-start.23 = (bf16[768,768]{1,0:T(8,128)(2,1)S(1)}, bf16[768,768]{1,0:T(8,128)(2,1)S(1)}, u32[]{:S(2)}, u32[]{:S(2)}) collective-permute-start(bf16[768,768]{1,0:T(8,128)(2,1)S(1)} %fusion.79), channel_id=1, source_target_pairs={{0,4},{4,0},{8,12},{12,8},{16,20},{20,16},{24,28},{28,24},{1,5},{5... | collective-permute-start | bytes 3538952 | tf_op jit(solution)/shard_map/ppermute | solution.py:83
  397.9 16.4 %collective-permute-start.18 = (bf16[384,768]{1,0:T(8,128)(2,1)}, bf16[384,768]{1,0:T(8,128)(2,1)S(1)}, u32[]{:S(2)}, u32[]{:S(2)}) collective-permute-start(bf16[384,768]{1,0:T(8,128)(2,1)} %select_convert_fusion.4), channel_id=1, source_target_pairs={{0,8},{4,12},{8,0},{12,4},{16,24},{20,28},{24,16},{28,20},{1,9},{5... | collective-permute-start | bytes 1769480 | tf_op jit(solution)/shard_map/ppermute | solution.py:83
  401.3 24.5 %collective-permute-start.24 = (bf16[384,768]{1,0:T(8,128)(2,1)}, bf16[384,768]{1,0:T(8,128)(2,1)S(1)}, u32[]{:S(2)}, u32[]{:S(2)}) collective-permute-start(bf16[384,768]{1,0:T(8,128)(2,1)} %select_convert_fusion.3), channel_id=1, source_target_pairs={{0,8},{4,12},{8,0},{12,4},{16,24},{20,28},{24,16},{28,20},{1,9},{5... | collective-permute-start | bytes 1769480 | tf_op jit(solution)/shard_map/ppermute | solution.py:83
  404.5 84.8 %all-gather.27.cloned.1.call-start = ((), (), s32[]{:S(2)}) async-start(), calls=%async_computation.20 | async-start | bytes 1966080 | tf_op jit(solution)/shard_map/all_gather | solution.py:44
  404.5 21.3 %copy-start.16 = (f32[768,768]{1,0:T(8,128)S(1)}, f32[768,768]{1,0:T(8,128)}, u32[]{:S(2)}) copy-start(f32[768,768]{1,0:T(8,128)} %copy-done.15) | copy-start | bytes 7077892
  416.2 11.6 %collective-permute-start.19 = (bf16[192,768]{1,0:T(8,128)(2,1)S(1)}, bf16[192,768]{1,0:T(8,128)(2,1)S(1)}, u32[]{:S(2)}, u32[]{:S(2)}) collective-permute-start(bf16[192,768]{1,0:T(8,128)(2,1)S(1)} %select_convert_fusion.7), channel_id=1, source_target_pairs={{0,16},{4,20},{8,24},{12,28},{16,0},{20,4},{24,8},{28,12},{1,17},{... | collective-permute-start | bytes 884744 | tf_op jit(solution)/shard_map/ppermute | solution.py:83
  426.1 23.3 %copy-start.12 = (f32[256,768]{1,0:T(8,128)S(1)}, f32[256,768]{1,0:T(8,128)}, u32[]{:S(2)}) copy-start(f32[256,768]{1,0:T(8,128)} %get-tuple-element.33) | copy-start | bytes 2359300
  426.1 23.3 %copy-start.111 = (f32[256]{0:T(256)S(1)}, f32[256]{0:T(256)}, u32[]{:S(2)}) copy-start(f32[256]{0:T(256)} %copy-done.110) | copy-start | bytes 3076
  426.1 9.9 %collective-permute-start.25 = (bf16[192,768]{1,0:T(8,128)(2,1)S(1)}, bf16[192,768]{1,0:T(8,128)(2,1)S(1)}, u32[]{:S(2)}, u32[]{:S(2)}) collective-permute-start(bf16[192,768]{1,0:T(8,128)(2,1)S(1)} %select_convert_fusion.6), channel_id=1, source_target_pairs={{0,16},{4,20},{8,24},{12,28},{16,0},{20,4},{24,8},{28,12},{1,17},{... | collective-permute-start | bytes 884744 | tf_op jit(solution)/shard_map/ppermute | solution.py:83
  427.9 14.5 %collective-permute-start.20 = (bf16[192,768]{1,0:T(8,128)(2,1)S(1)}, bf16[192,768]{1,0:T(8,128)(2,1)S(1)}, u32[]{:S(2)}, u32[]{:S(2)}) collective-permute-start(bf16[192,768]{1,0:T(8,128)(2,1)S(1)} %add_convert_fusion.1), channel_id=1, source_target_pairs={{0,16},{4,20},{8,24},{12,28},{16,0},{20,4},{24,8},{28,12},{1,17},{... | collective-permute-start | bytes 884744 | tf_op jit(solution)/shard_map/ppermute | solution.py:88
  436.2 10.7 %collective-permute-start.26 = (bf16[192,768]{1,0:T(8,128)(2,1)S(1)}, bf16[192,768]{1,0:T(8,128)(2,1)S(1)}, u32[]{:S(2)}, u32[]{:S(2)}) collective-permute-start(bf16[192,768]{1,0:T(8,128)(2,1)S(1)} %add_convert_fusion), channel_id=1, source_target_pairs={{0,16},{4,20},{8,24},{12,28},{16,0},{20,4},{24,8},{28,12},{1,17},{... | collective-permute-start | bytes 884744 | tf_op jit(solution)/shard_map/ppermute | solution.py:88
  443.4 16.5 %collective-permute-start.21 = (bf16[384,768]{1,0:T(8,128)(2,1)}, bf16[384,768]{1,0:T(8,128)(2,1)}, u32[]{:S(2)}, u32[]{:S(2)}) collective-permute-start(bf16[384,768]{1,0:T(8,128)(2,1)} %maximum_select_fusion.7), channel_id=1, source_target_pairs={{0,8},{4,12},{8,0},{12,4},{16,24},{20,28},{24,16},{28,20},{1,9},{5... | collective-permute-start | bytes 1769480 | tf_op jit(solution)/shard_map/ppermute | solution.py:88
  447.9 20.2 %collective-permute-start.27 = (bf16[384,768]{1,0:T(8,128)(2,1)}, bf16[384,768]{1,0:T(8,128)(2,1)}, u32[]{:S(2)}, u32[]{:S(2)}) collective-permute-start(bf16[384,768]{1,0:T(8,128)(2,1)} %maximum_select_fusion.8), channel_id=1, source_target_pairs={{0,8},{4,12},{8,0},{12,4},{16,24},{20,28},{24,16},{28,20},{1,9},{5... | collective-permute-start | bytes 1769480 | tf_op jit(solution)/shard_map/ppermute | solution.py:88
  452.3 74.8 %all-gather.31.cloned.1.call-start = ((), (), s32[]{:S(2)}) async-start(), calls=%async_computation.22 | async-start | bytes 1966080 | tf_op jit(solution)/shard_map/all_gather | solution.py:44
  458.7 30.5 %copy-start.39 = (bf16[4,192,768]{2,1,0:T(8,128)(2,1)S(1)}, bf16[4,192,768]{2,1,0:T(8,128)(2,1)}, u32[]{:S(2)}) copy-start(bf16[4,192,768]{2,1,0:T(8,128)(2,1)} %gather_fusion.4) | copy-start | bytes 3538948
  459.2 6.4 %collective-permute-start.6 = (f32[3,2,2,768]{3,1,2,0:T(2,128)S(1)}, f32[3,2,2,768]{3,1,2,0:T(2,128)S(1)}, u32[]{:S(2)}, u32[]{:S(2)}) collective-permute-start(f32[3,2,2,768]{3,1,2,0:T(2,128)S(1)} %maximum_add_fusion), channel_id=1, source_target_pairs={{0,1},{1,0},{2,3},{3,2},{4,5},{5,4},{6,7},{7,6},{8,9},{9,8},{10,11... | collective-permute-start | bytes 110600 | tf_op jit(solution)/shard_map/ppermute | solution.py:102
  462.8 132.1 %collective-permute-start.22 = (bf16[768,768]{1,0:T(8,128)(2,1)}, bf16[768,768]{1,0:T(8,128)(2,1)}, u32[]{:S(2)}, u32[]{:S(2)}) collective-permute-start(bf16[768,768]{1,0:T(8,128)(2,1)} %maximum_select_fusion.3), channel_id=1, source_target_pairs={{0,4},{4,0},{8,12},{12,8},{16,20},{20,16},{24,28},{28,24},{1,5},{5... | collective-permute-start | bytes 3538952 | tf_op jit(solution)/shard_map/ppermute | solution.py:88
  462.9 157.8 %reduce-scatter.13.cloned.1.call-start = ((), (), s32[]{:S(2)}) async-start(), calls=%async_computation.12 | async-start | bytes 1966080 | tf_op jit(solution)/shard_map/reduce_scatter | solution.py:49
  467.0 26.1 %copy-start.7 = (f32[4,2,3,128,128]{3,4,2,1,0:T(8,128)S(1)}, f32[4,2,3,128,128]{3,4,2,1,0:T(8,128)}, u32[]{:S(2)}) copy-start(f32[4,2,3,128,128]{3,4,2,1,0:T(8,128)} %copy-done.6) | copy-start | bytes 4718596
  467.0 26.1 %copy-start.36 = (f32[4,2,128,3,64]{2,1,4,3,0:T(2,128)S(1)}, f32[4,2,128,3,64]{2,1,4,3,0:T(2,128)}, u32[]{:S(2)}) copy-start(f32[4,2,128,3,64]{2,1,4,3,0:T(2,128)} %squeeze.47) | copy-start | bytes 2359300
  467.0 26.1 %copy-start.66 = (f32[4,2,3,128]{3,2,1,0:T(4,128)S(1)}, f32[4,2,3,128]{3,2,1,0:T(4,128)}, u32[]{:S(2)}) copy-start(f32[4,2,3,128]{3,2,1,0:T(4,128)} %copy-done.65) | copy-start | bytes 36868
  467.1 6.9 %collective-permute-start.7 = (f32[3,2,2,768]{3,1,2,0:T(2,128)S(1)}, f32[3,2,2,768]{3,1,2,0:T(2,128)S(1)}, u32[]{:S(2)}, u32[]{:S(2)}) collective-permute-start(f32[3,2,2,768]{3,1,2,0:T(2,128)S(1)} %fusion.277), channel_id=1, source_target_pairs={{0,2},{1,3},{2,0},{3,1},{4,6},{5,7},{6,4},{7,5},{8,10},{9,11},{10,... | collective-permute-start | bytes 110600 | tf_op jit(solution)/shard_map/ppermute | solution.py:102
  471.0 132.6 %collective-permute-start.28 = (bf16[768,768]{1,0:T(8,128)(2,1)}, bf16[768,768]{1,0:T(8,128)(2,1)}, u32[]{:S(2)}, u32[]{:S(2)}) collective-permute-start(bf16[768,768]{1,0:T(8,128)(2,1)} %maximum_select_fusion.4), channel_id=1, source_target_pairs={{0,4},{4,0},{8,12},{12,8},{16,20},{20,16},{24,28},{28,24},{1,5},{5... | collective-permute-start | bytes 3538952 | tf_op jit(solution)/shard_map/ppermute | solution.py:88
  498.2 31.5 %copy-start.5 = (f32[4,2,3,128,128]{3,4,2,1,0:T(8,128)S(1)}, f32[4,2,3,128,128]{3,4,2,1,0:T(8,128)}, u32[]{:S(2)}) copy-start(f32[4,2,3,128,128]{3,4,2,1,0:T(8,128)} %copy-done.4) | copy-start | bytes 4718596
  498.2 31.5 %copy-start.64 = (f32[4,2,3,128]{3,2,1,0:T(4,128)S(1)}, f32[4,2,3,128]{3,2,1,0:T(4,128)}, u32[]{:S(2)}) copy-start(f32[4,2,3,128]{3,2,1,0:T(4,128)} %copy-done.63) | copy-start | bytes 36868
  542.1 80.5 %reduce-scatter.17.cloned.1.call-start = ((), (), s32[]{:S(2)}) async-start(), calls=%async_computation.14 | async-start | bytes 1966080 | tf_op jit(solution)/shard_map/reduce_scatter | solution.py:49
  546.5 16.0 %collective-permute-start.8 = (f32[15,768]{1,0:T(8,128)}, f32[15,768]{1,0:T(8,128)}, u32[]{:S(2)}, u32[]{:S(2)}) collective-permute-start(f32[15,768]{1,0:T(8,128)} %pad_maximum_fusion.6), channel_id=1, source_target_pairs={{0,4},{4,0},{8,12},{12,8},{16,20},{20,16},{24,28},{28,24},{1,5},{5... | collective-permute-start | bytes 138248 | tf_op jit(solution)/shard_map/ppermute | solution.py:102
  553.1 11.8 %collective-permute-start = (bf16[576,768]{1,0:T(8,128)(2,1)}, bf16[576,768]{1,0:T(8,128)(2,1)}, u32[]{:S(2)}, u32[]{:S(2)}) collective-permute-start(bf16[576,768]{1,0:T(8,128)(2,1)} %bitcast.62), channel_id=1, source_target_pairs={{0,4},{4,0},{8,12},{12,8},{16,20},{20,16},{24,28},{28,24},{1,5},{5... | collective-permute-start | bytes 2654216 | tf_op jit(solution)/shard_map/ppermute | solution.py:83
  562.4 5.1 collective-permute-start.11
  563.3 34.6 %collective-permute-start.9 = (f32[15,768]{1,0:T(8,128)S(1)}, f32[15,768]{1,0:T(8,128)S(1)}, u32[]{:S(2)}, u32[]{:S(2)}) collective-permute-start(f32[15,768]{1,0:T(8,128)S(1)} %fusion.276), channel_id=1, source_target_pairs={{0,8},{4,12},{8,0},{12,4},{16,24},{20,28},{24,16},{28,20},{1,9},{5... | collective-permute-start | bytes 138248 | tf_op jit(solution)/shard_map/ppermute | solution.py:102
  566.9 13.1 %collective-permute-start.1 = (bf16[288,768]{1,0:T(8,128)(2,1)S(1)}, bf16[288,768]{1,0:T(8,128)(2,1)S(1)}, u32[]{:S(2)}, u32[]{:S(2)}) collective-permute-start(bf16[288,768]{1,0:T(8,128)(2,1)S(1)} %select_convert_fusion.5), channel_id=1, source_target_pairs={{0,8},{4,12},{8,0},{12,4},{16,24},{20,28},{24,16},{28,20},{1,9},{5... | collective-permute-start | bytes 1327112 | tf_op jit(solution)/shard_map/ppermute | solution.py:83
  568.6 13.9 %collective-permute-start.12 = (bf16[96,768]{1,0:T(8,128)(2,1)S(1)}, bf16[96,768]{1,0:T(8,128)(2,1)S(1)}, u32[]{:S(2)}, u32[]{:S(2)}) collective-permute-start(bf16[96,768]{1,0:T(8,128)(2,1)S(1)} %select_convert_fusion.10), channel_id=1, source_target_pairs={{0,8},{4,12},{8,0},{12,4},{16,24},{20,28},{24,16},{28,20},{1,9},{5... | collective-permute-start | bytes 442376 | tf_op jit(solution)/shard_map/ppermute | solution.py:83
  580.2 6.0 collective-permute-start.2
  586.3 6.0 collective-permute-start.3
  587.8 5.5 collective-permute-start.13
  592.4 10.7 %collective-permute-start.4 = (bf16[288,768]{1,0:T(8,128)(2,1)S(1)}, bf16[288,768]{1,0:T(8,128)(2,1)S(1)}, u32[]{:S(2)}, u32[]{:S(2)}) collective-permute-start(bf16[288,768]{1,0:T(8,128)(2,1)S(1)} %maximum_select_fusion.9), channel_id=1, source_target_pairs={{0,8},{4,12},{8,0},{12,4},{16,24},{20,28},{24,16},{28,20},{1,9},{5... | collective-permute-start | bytes 1327112 | tf_op jit(solution)/shard_map/ppermute | solution.py:88
  593.4 5.1 collective-permute-start.14
  597.9 13.4 %collective-permute-start.10 = (f32[15,768]{1,0:T(8,128)S(1)}, f32[15,768]{1,0:T(8,128)S(1)}, u32[]{:S(2)}, u32[]{:S(2)}) collective-permute-start(f32[15,768]{1,0:T(8,128)S(1)} %add.555), channel_id=1, source_target_pairs={{0,16},{4,20},{8,24},{12,28},{16,0},{20,4},{24,8},{28,12},{1,17},{... | collective-permute-start | bytes 138248 | tf_op jit(solution)/shard_map/ppermute | solution.py:102
  598.6 13.4 %collective-permute-start.15 = (bf16[96,768]{1,0:T(8,128)(2,1)S(1)}, bf16[96,768]{1,0:T(8,128)(2,1)S(1)}, u32[]{:S(2)}, u32[]{:S(2)}) collective-permute-start(bf16[96,768]{1,0:T(8,128)(2,1)S(1)} %maximum_select_fusion.11), channel_id=1, source_target_pairs={{0,8},{4,12},{8,0},{12,4},{16,24},{20,28},{24,16},{28,20},{1,9},{5... | collective-permute-start | bytes 442376 | tf_op jit(solution)/shard_map/ppermute | solution.py:88
  603.5 12.9 %collective-permute-start.5 = (bf16[576,768]{1,0:T(8,128)(2,1)S(1)}, bf16[576,768]{1,0:T(8,128)(2,1)}, u32[]{:S(2)}, u32[]{:S(2)}) collective-permute-start(bf16[576,768]{1,0:T(8,128)(2,1)S(1)} %maximum_select_fusion.5), channel_id=1, source_target_pairs={{0,4},{4,0},{8,12},{12,8},{16,20},{20,16},{24,28},{28,24},{1,5},{5... | collective-permute-start | bytes 2654216 | tf_op jit(solution)/shard_map/ppermute | solution.py:88
  612.0 3.1 collective-permute-start.16
  (137 other events, 628.0 us)
Sparse Core Ops, SparseCore 0:
  10.2 63.3 all-gather.20
  75.7 36.1 all-gather.16
  137.1 45.0 all-gather.22
  184.2 35.8 all-gather.18
  222.9 34.2 reduce-scatter.8
  259.4 34.2 reduce-scatter.6
  299.6 35.8 all-gather.24
  337.0 35.8 all-gather.28
  375.3 34.2 reduce-scatter.10
  412.3 34.2 reduce-scatter.14
  452.4 36.7 all-gather.26
  491.2 35.8 all-gather.30
  542.3 34.2 reduce-scatter.12
  579.3 34.2 reduce-scatter.16

commit v10 on v9

--- a/solution.py
+++ b/solution.py
@@ -106,6 +106,8 @@
 
 def stream(
     inputs,
+    input_segs,
+    after,
     cotangent,
     seg_kind,
     seg_lens,
@@ -144,7 +146,8 @@
     ubias_sel = up_bias[seg_kind].astype(jnp.float32)
     down_sel = w_down[seg_kind]
 
-    input_segs = gather_rows(inputs)
+    if after is not None:
+        input_segs, _ = lax.optimization_barrier((input_segs, after["normed"]))
     projected = jnp.einsum(
         "srd,sjde->jsre", input_segs, qkv_sel, preferred_element_type=jnp.float32
     )
@@ -220,6 +223,8 @@
     shift_grads = jnp.stack([type_sum(kind_hot, d_normed), type_sum(kind_hot, grad_out)], axis=1)
     rbias_grads = jnp.stack([type_sum(kind_hot, d_one), type_sum(kind_hot, d_two)], axis=1)
     one_segs = gather_rows(d_one.astype(jnp.bfloat16))
+    if after is not None:
+        one_segs, _ = lax.optimization_barrier((one_segs, after["qkv_back"]))
 
     grad_out_w = jnp.einsum(
         "stre,srd->ted", masked(mixed, seg_hot), one_segs, preferred_element_type=jnp.float32
@@ -264,12 +269,14 @@
     )
     qkv_back = jnp.einsum("jsre,sjde->srd", d_proj, qkv_sel, preferred_element_type=jnp.float32)
     input_grad = scatter_sum(qkv_back) + d_one
+    marks = {"normed": normed_low, "qkv_back": qkv_back}
     small = jnp.stack([rbias_grads, gain_grads, shift_grads])
     return (
         layer_out,
         input_grad,
         (grad_qkv, grad_qv, grad_out_w, grad_up, grad_ubias, grad_down),
         small,
+        marks,
     )
 
 
@@ -298,7 +305,11 @@
     seg_rows = chains * CHAIN
     weights = (w_qkv, qv_bias, w_out, resid_bias, norm_gain, norm_shift, w_up, up_bias, w_down)
     peer_kind = block_kind[(jnp.arange(n_tensor) * tok_dev) // block_rows]
-    out_rows_w = lax.all_to_all(w_out[peer_kind], "tensor", 0, 0, tiled=True)
+    row_parts = [slice(part * seg_rows, (part + 1) * seg_rows) for part in range(STREAMS)]
+    gathered = [gather_rows(inputs[rows]) for rows in row_parts]
+    out_sel, gathered[0] = lax.optimization_barrier((w_out[peer_kind], gathered[0]))
+    out_rows_w = lax.all_to_all(out_sel, "tensor", 0, 0, tiled=True)
+    marks = None
     outs, ins, grads, smalls = [], [], [], []
     for part in range(STREAMS):
         first_row = jnp.arange(n_tensor) * tok_dev + part * seg_rows
@@ -309,9 +320,17 @@
         seg_lens = lengths[chain_ids]
         own_rows = rank * tok_dev + part * seg_rows + jnp.arange(seg_rows)
         row_kind = block_kind[own_rows // block_rows]
-        rows = slice(part * seg_rows, (part + 1) * seg_rows)
-        out_part, in_part, grad_part, small_part = stream(
-            inputs[rows], cotangent[rows], seg_kind, seg_lens, row_kind, out_rows_w, *weights
+        rows = row_parts[part]
+        out_part, in_part, grad_part, small_part, marks = stream(
+            inputs[rows],
+            gathered[part],
+            marks,
+            cotangent[rows],
+            seg_kind,
+            seg_lens,
+            row_kind,
+            out_rows_w,
+            *weights,
         )
         outs.append(out_part)
         ins.append(in_part)

time: 643 us -> 659 us (1.025)
  other arithmetic: 79.3 us -> 91 us
    all_gather x8, waiting for transfers between devices: 156 us -> 119 us  [gather_rows(): return lax.all_gather(local_rows, 'tensor', axis=0, tiled=False)]
    all_to_all x1, waiting for transfers between devices: 0.01 us -> 19.1 us  [local(): out_rows_w = lax.all_to_all(out_sel, 'tensor', 0, 0, tiled=True)]
    all_to_all x2, waiting for transfers between devices: 2.52 us -> 17.2 us  [stream(): mixed_rows = lax.all_to_all(mixed, 'tensor', 0, 0, tiled=True)]
  transfers between devices with their start and end apart: 46 -> 46, of which waited for: 26 -> 23; matrix products, arithmetic and copies ran while one was open for 44% -> 44% of each run, Pallas kernels for 0% -> 0%
where the time goes in v10:
time: 659 us; the launch traced here: 648 us
  waiting for transfers between devices  274 us (42%)
  matrix products  131 us (20%)
  local copies, waits for them, and re-layouts  98.2 us (15%)
  other arithmetic  91 us (14%)
  starting transfers between devices  37.4 us (6%)
  between operations  16.3 us (2%)
    all_gather x8, waiting for transfers between devices, gather_rows(): return lax.all_gather(local_rows, 'tensor', axis=0, tiled=False)  119 us
    reduce_scatter x6, waiting for transfers between devices, scatter_sum(): lax.psum_scatter(seg_parts.reshape(n_seg * seg_rows, width).astype(jnp.bf...  53.5 us
    ppermute x12, waiting for transfers between devices, dp_sum_low(): gots = lax.ppermute(sends, 'dp', dp_perm(n_dp, 1 << b))  43.8 us
    all_to_all x1, waiting for transfers between devices, local(): out_rows_w = lax.all_to_all(out_sel, 'tensor', 0, 0, tiled=True)  19.1 us
    select_n x12, other arithmetic, dp_sum_low(): jnp.where(upper, jnp.concatenate([g, c]), jnp.concatenate([c, g]))  17.5 us
    all_to_all x2, waiting for transfers between devices, stream(): mixed_rows = lax.all_to_all(mixed, 'tensor', 0, 0, tiled=True)  17.2 us
    dot_general x12, matrix products, type_sum(): jnp.einsum('rt,rd->td', kind_hot, values, precision=lax.Precision.HIGHEST)  16.3 us
    dot_general x12, matrix products, pick(): return jnp.dot(kind_hot, kind_table.astype(jnp.float32), precision=highest)  16.2 us
  transfers between devices with their start and end apart: 46, of which 23 were waited for; matrix products, arithmetic and copies ran while one was open for 44% of the time, Pallas kernels for 0%

profile of v10, /device:TPU:0, one launch (start us, length us, event | category | flops | bytes accessed | tf_op | source)
XLA Modules:
  0.0 648.1 jit_solution(11852268486664007730)
XLA Ops:
  14.9 4.1 gather_fusion.1
  19.0 30.9 %all-gather.17.cloned.1.call-done = bf16[1024,768]{1,0:T(8,128)(2,1)} async-done(((bf16[256,768]{1,0:T(8,128)(2,1)}), bf16[1024,768]{1,0:T(8,128)(2,1)}) %all-gather.17.cloned.1.call-update) | async-done | bytes 1572880 | tf_op jit(solution)/shard_map/all_gather | solution.py:44
  50.0 3.6 convolution_bitcast_fusion.2
  65.4 3.5 all-to-all-start
  70.7 4.0 gather_fusion.9
  74.7 17.2 %all-to-all-done = bf16[4,256,192]{1,2,0:T(8,128)(2,1)S(1)} async-done(((bf16[4,256,192]{1,2,0:T(8,128)(2,1)}), bf16[4,256,192]{1,2,0:T(8,128)(2,1)S(1)}, u32[]{:S(2)}, u32[]{:S(2)}) %all-to-all-start) | async-done | bytes 393248 | tf_op jit(solution)/shard_map/all_to_all | solution.py:179
  91.9 4.3 all-to-all-start.1
  104.7 19.1 %all-to-all-done.1 = bf16[4,192,768]{2,1,0:T(8,128)(2,1)} async-done(((bf16[4,192,768]{2,1,0:T(8,128)(2,1)}), bf16[4,192,768]{2,1,0:T(8,128)(2,1)}, u32[]{:S(2)}, u32[]{:S(2)}) %all-to-all-start.1) | async-done | bytes 1179680 | tf_op jit(solution)/shard_map/all_to_all | solution.py:311
  128.5 3.6 convolution_bitcast_fusion.1
  150.1 4.1 all-to-all-start.2
  157.0 3.2 gather_fusion.14
  160.1 3.2 gather_fusion.7
  163.3 5.0 gather_fusion.12
  168.3 3.3 gather_fusion.5
  182.7 5.1 fusion.99
  187.8 7.3 %fusion.3 = bf16[4,256,768]{2,1,0:T(8,128)(2,1)S(1)} fusion(f32[4,256,768]{2,1,0:T(8,128)S(1)} %get-tuple-element.83, f32[4,768]{1,0:T(4,128)S(1)} %copy-done.74, u8[256,768]{1,0:T(8,128)(4,1)S(1)} %get-tuple-element.20, u8[256,768]{1,0:T(8,128)(4,1)S(1)} %get-tuple-element.19), kind=kLoop, calls=%fused_computation.27 | loop fusion | flops 55836672 | bytes 5124096 | tf_op jit(solution)/shard_map/convert_element_type | solution.py:193
  195.2 2.6 convolution_convert_fusion.5
  198.1 23.0 %all-gather.23.cloned.1.call-done = bf16[1024,768]{1,0:T(8,128)(2,1)} async-done(((bf16[256,768]{1,0:T(8,128)(2,1)}), bf16[1024,768]{1,0:T(8,128)(2,1)}) %all-gather.23.cloned.1.call-update) | async-done | bytes 1572880 | tf_op jit(solution)/shard_map/all_gather | solution.py:44
  221.1 5.1 fusion.100
  226.2 7.3 %fusion.6 = bf16[4,256,768]{2,1,0:T(8,128)(2,1)S(1)} fusion(f32[4,256,768]{2,1,0:T(8,128)S(1)} %get-tuple-element.80, f32[4,768]{1,0:T(4,128)S(1)} %copy-done.71, u8[256,768]{1,0:T(8,128)(4,1)S(1)} %get-tuple-element.22, u8[256,768]{1,0:T(8,128)(4,1)S(1)} %get-tuple-element.21), kind=kLoop, calls=%fused_computation.30 | loop fusion | flops 55836672 | bytes 5124096 | tf_op jit(solution)/shard_map/convert_element_type | solution.py:193
  233.6 2.6 convolution_convert_fusion.4
  238.1 19.5 %reduce-scatter.7.cloned.1.call-done = bf16[256,768]{1,0:T(8,128)(2,1)} async-done(((bf16[1024,768]{1,0:T(8,128)(2,1)}), bf16[256,768]{1,0:T(8,128)(2,1)}) %reduce-scatter.7.cloned.1.call-update) | async-done | bytes 393232 | tf_op jit(solution)/shard_map/reduce_scatter | solution.py:49
  260.1 34.0 %reduce-scatter.9.cloned.1.call-done = bf16[256,768]{1,0:T(8,128)(2,1)} async-done(((bf16[1024,768]{1,0:T(8,128)(2,1)}), bf16[256,768]{1,0:T(8,128)(2,1)}) %reduce-scatter.9.cloned.1.call-update) | async-done | bytes 393232 | tf_op jit(solution)/shard_map/reduce_scatter | solution.py:49
  299.9 2.8 gather_fusion.15
  309.2 2.6 copy.88
  311.8 2.6 copy.91
  314.5 2.6 copy.96
  317.1 2.6 copy.98
  319.6 2.6 copy.97
  322.2 2.6 copy.99
  335.9 7.5 %convert_reduce_fusion.1 = (f32[4,768]{1,0:T(4,128)}, bf16[4,256,768]{2,1,0:T(8,128)(2,1)}) fusion(f32[4,256,768]{2,1,0:T(8,128)} %copy-done.35, f32[4,768]{1,0:T(4,128)} %convert_element_type.516, bf16[4,256,768]{2,1,0:T(8,128)(2,1)} %bitcast.415, bf16[4,768,768]{2,1,0:T(8,128)(2,1)} %gather_fusion.7), kind=kOutput, calls=%fused_computation.64 | convolution fusion | flops 1219752960 | bytes 11034624 | tf_op jit(solution)/shard_map/srd,sfd->srf/dot_general | solution.py:208
  343.4 30.0 %all-gather.29.cloned.1.call-done = bf16[1024,768]{1,0:T(8,128)(2,1)} async-done(((bf16[256,768]{1,0:T(8,128)(2,1)}), bf16[1024,768]{1,0:T(8,128)(2,1)}) %all-gather.29.cloned.1.call-update) | async-done | bytes 1572880 | tf_op jit(solution)/shard_map/all_gather | solution.py:44
  373.4 6.4 convert_reduce_fusion
  379.8 5.5 convolution_convert_fusion
  385.8 4.7 fusion.25
  390.5 2.7 bitcast_add_fusion.1
  397.2 2.7 fusion.21
  400.0 2.8 bitcast_add_fusion
  407.3 2.6 convolution_convert_fusion.2
  410.1 3.1 bitcast_add_fusion.4
  414.9 3.1 bitcast_add_fusion.3
  419.7 9.9 %collective-permute-done.18 = bf16[384,768]{1,0:T(8,128)(2,1)S(1)} collective-permute-done((bf16[384,768]{1,0:T(8,128)(2,1)S(1)}, bf16[384,768]{1,0:T(8,128)(2,1)S(1)}, u32[]{:S(2)}, u32[]{:S(2)}) %collective-permute-start.18) | collective-permute-done | bytes 589856 | tf_op jit(solution)/shard_map/ppermute | solution.py:83
  431.4 10.4 %collective-permute-done.24 = bf16[384,768]{1,0:T(8,128)(2,1)S(1)} collective-permute-done((bf16[384,768]{1,0:T(8,128)(2,1)S(1)}, bf16[384,768]{1,0:T(8,128)(2,1)S(1)}, u32[]{:S(2)}, u32[]{:S(2)}) %collective-permute-start.24) | collective-permute-done | bytes 589856 | tf_op jit(solution)/shard_map/ppermute | solution.py:83
  444.5 7.5 %collective-permute-done.25 = bf16[192,768]{1,0:T(8,128)(2,1)S(1)} collective-permute-done((bf16[192,768]{1,0:T(8,128)(2,1)S(1)}, bf16[192,768]{1,0:T(8,128)(2,1)S(1)}, u32[]{:S(2)}, u32[]{:S(2)}) %collective-permute-start.25) | collective-permute-done | bytes 294944 | tf_op jit(solution)/shard_map/ppermute | solution.py:83
  454.5 3.9 collective-permute-done.20
  460.9 2.7 collective-permute-done.26
  466.0 2.9 fusion.212
  482.9 2.9 maximum_select_fusion.3
  485.8 3.0 collective-permute-done.6
  488.9 3.0 maximum_select_fusion.4
  492.2 4.3 collective-permute-done.7
  498.0 11.7 %all-gather.27.cloned.1.call-done = bf16[1024,768]{1,0:T(8,128)(2,1)} async-done(((bf16[256,768]{1,0:T(8,128)(2,1)}), bf16[1024,768]{1,0:T(8,128)(2,1)}) %all-gather.27.cloned.1.call-update) | async-done | bytes 1572880 | tf_op jit(solution)/shard_map/all_gather | solution.py:44
  522.1 4.6 convolution_bitcast_fusion
  526.7 21.0 %all-gather.31.cloned.1.call-done = bf16[1024,768]{1,0:T(8,128)(2,1)} async-done(((bf16[256,768]{1,0:T(8,128)(2,1)}), bf16[1024,768]{1,0:T(8,128)(2,1)}) %all-gather.31.cloned.1.call-update) | async-done | bytes 1572880 | tf_op jit(solution)/shard_map/all_gather | solution.py:44
  561.6 3.5 fusion.17
  573.9 2.7 bitcast_convert_fusion
  583.2 10.8 %collective-permute-done.1 = bf16[288,768]{1,0:T(8,128)(2,1)S(1)} collective-permute-done((bf16[288,768]{1,0:T(8,128)(2,1)S(1)}, bf16[288,768]{1,0:T(8,128)(2,1)S(1)}, u32[]{:S(2)}, u32[]{:S(2)}) %collective-permute-start.1) | collective-permute-done | bytes 442400 | tf_op jit(solution)/shard_map/ppermute | solution.py:83
  596.4 3.8 collective-permute-done.2
  602.5 3.8 collective-permute-done.3
  609.4 3.0 maximum_select_fusion
  613.8 2.9 collective-permute-done.4
  618.0 2.7 maximum_select_fusion.1
  620.6 2.5 convert.16
  623.2 2.5 convert.15
  (561 shorter events, 200.8 us)
Async XLA Ops:
  7.2 149.8 %copy-start = (bf16[2,768,768]{2,1,0:T(8,128)(2,1)S(1)}, bf16[2,768,768]{2,1,0:T(8,128)(2,1)}, u32[]{:S(2)}) copy-start(bf16[2,768,768]{2,1,0:T(8,128)(2,1)} %param.25) | copy-start | bytes 7077892
  7.2 42.7 %all-gather.17.cloned.1.call-start = ((), (), s32[]{:S(2)}) async-start(), calls=%async_computation.15 | async-start | bytes 1966080 | tf_op jit(solution)/shard_map/all_gather | solution.py:44
  9.5 119.0 %all-gather.21.cloned.1.call-start = ((), (), s32[]{:S(2)}) async-start(), calls=%async_computation.17 | async-start | bytes 1966080 | tf_op jit(solution)/shard_map/all_gather | solution.py:44
  13.2 48.9 %copy-start.67 = (f32[4,3,64]{2,1,0:T(4,128)}, f32[4,3,64]{2,1,0:T(4,128)S(1)}, u32[]{:S(2)}) copy-start(f32[4,3,64]{2,1,0:T(4,128)S(1)} %add.480) | copy-start | bytes 9220
  13.3 46.5 %copy-start.65 = (f32[4,3,64]{2,1,0:T(4,128)}, f32[4,3,64]{2,1,0:T(4,128)S(1)}, u32[]{:S(2)}) copy-start(f32[4,3,64]{2,1,0:T(4,128)S(1)} %add.487) | copy-start | bytes 9220
  65.4 26.5 %all-to-all-start = ((bf16[4,256,192]{1,2,0:T(8,128)(2,1)}), bf16[4,256,192]{1,2,0:T(8,128)(2,1)S(1)}, u32[]{:S(2)}, u32[]{:S(2)}) async-start(bf16[4,256,192]{1,2,0:T(8,128)(2,1)} %convert_element_type.514), calls=%async_computation | async-start | bytes 786432 | tf_op jit(solution)/shard_map/all_to_all | solution.py:179
  74.7 26.3 %copy-start.98 = (bf16[2,2,768]{2,1,0:T(2,128)(2,1)S(1)}, bf16[2,2,768]{2,1,0:T(2,128)(2,1)}, u32[]{:S(2)}) copy-start(bf16[2,2,768]{2,1,0:T(2,128)(2,1)} %param.20) | copy-start | bytes 18436
  74.7 27.5 %copy-start.99 = (bf16[2,2,768]{2,1,0:T(2,128)(2,1)S(1)}, bf16[2,2,768]{2,1,0:T(2,128)(2,1)}, u32[]{:S(2)}) copy-start(bf16[2,2,768]{2,1,0:T(2,128)(2,1)} %param.21) | copy-start | bytes 18436
  74.7 28.2 %copy-start.100 = (bf16[2,2,768]{2,1,0:T(2,128)(2,1)S(1)}, bf16[2,2,768]{2,1,0:T(2,128)(2,1)}, u32[]{:S(2)}) copy-start(bf16[2,2,768]{2,1,0:T(2,128)(2,1)} %param.22) | copy-start | bytes 18436
  91.9 31.9 %all-to-all-start.1 = ((bf16[4,192,768]{2,1,0:T(8,128)(2,1)}), bf16[4,192,768]{2,1,0:T(8,128)(2,1)}, u32[]{:S(2)}, u32[]{:S(2)}) async-start(bf16[4,192,768]{2,1,0:T(8,128)(2,1)} %gather_fusion.2), calls=%async_computation.1 | async-start | bytes 2359296 | tf_op jit(solution)/shard_map/all_to_all | solution.py:311
  96.2 86.5 %all-gather.19.cloned.1.call-start = ((), (), s32[]{:S(2)}) async-start(), calls=%async_computation.16 | async-start | bytes 1966080 | tf_op jit(solution)/shard_map/all_gather | solution.py:44
  97.9 40.5 %copy-start.68 = (f32[4,3,64]{2,1,0:T(4,128)}, f32[4,3,64]{2,1,0:T(4,128)S(1)}, u32[]{:S(2)}) copy-start(f32[4,3,64]{2,1,0:T(4,128)S(1)} %add.515) | copy-start | bytes 9220
  102.9 22.9 %copy-start.95 = (bf16[2,1,768]{2,1,0:T(2,128)(2,1)}, bf16[2,1,768]{2,1,0:T(2,128)(2,1)S(1)}, u32[]{:S(2)}) copy-start(bf16[2,1,768]{2,1,0:T(2,128)(2,1)S(1)} %get-tuple-element.62) | copy-start | bytes 9220
  150.1 26.9 %all-to-all-start.2 = ((bf16[4,256,192]{1,2,0:T(8,128)(2,1)}), bf16[4,256,192]{1,2,0:T(8,128)(2,1)}, u32[]{:S(2)}, u32[]{:S(2)}) async-start(bf16[4,256,192]{1,2,0:T(8,128)(2,1)} %convert_element_type.530), calls=%async_computation.3 | async-start | bytes 786432 | tf_op jit(solution)/shard_map/all_to_all | solution.py:179
  154.2 66.9 %all-gather.23.cloned.1.call-start = ((), (), s32[]{:S(2)}) async-start(), calls=%async_computation.18 | async-start | bytes 1966080 | tf_op jit(solution)/shard_map/all_gather | solution.py:44
  182.6 75.0 %reduce-scatter.7.cloned.1.call-start = ((), (), s32[]{:S(2)}) async-start(), calls=%async_computation.9 | async-start | bytes 1966080 | tf_op jit(solution)/shard_map/reduce_scatter | solution.py:49
  197.8 96.3 %reduce-scatter.9.cloned.1.call-start = ((), (), s32[]{:S(2)}) async-start(), calls=%async_computation.10 | async-start | bytes 1966080 | tf_op jit(solution)/shard_map/reduce_scatter | solution.py:49
  236.2 99.7 %all-gather.25.cloned.1.call-start = ((), (), s32[]{:S(2)}) async-start(), calls=%async_computation.19 | async-start | bytes 1966080 | tf_op jit(solution)/shard_map/all_gather | solution.py:44
  299.9 73.5 %all-gather.29.cloned.1.call-start = ((), (), s32[]{:S(2)}) async-start(), calls=%async_computation.21 | async-start | bytes 1966080 | tf_op jit(solution)/shard_map/all_gather | solution.py:44
  304.7 161.3 %reduce-scatter.15.cloned.1.call-start = ((), (), s32[]{:S(2)}) async-start(), calls=%async_computation.13 | async-start | bytes 1966080 | tf_op jit(solution)/shard_map/reduce_scatter | solution.py:49
  335.9 37.5 %copy-start.72 = (f32[4,768]{1,0:T(4,128)S(1)}, f32[4,768]{1,0:T(4,128)}, u32[]{:S(2)}) copy-start(f32[4,768]{1,0:T(4,128)} %convert_element_type.532) | copy-start | bytes 36868
  385.3 84.2 %reduce-scatter.11.cloned.1.call-start = ((), (), s32[]{:S(2)}) async-start(), calls=%async_computation.11 | async-start | bytes 1966080 | tf_op jit(solution)/shard_map/reduce_scatter | solution.py:49
  394.5 15.6 %collective-permute-start.17 = (bf16[768,768]{1,0:T(8,128)(2,1)}, bf16[768,768]{1,0:T(8,128)(2,1)}, u32[]{:S(2)}, u32[]{:S(2)}) collective-permute-start(bf16[768,768]{1,0:T(8,128)(2,1)} %fusion.85), channel_id=1, source_target_pairs={{0,4},{4,0},{8,12},{12,8},{16,20},{20,16},{24,28},{28,24},{1,5},{5... | collective-permute-start | bytes 3538952 | tf_op jit(solution)/shard_map/ppermute | solution.py:83
  406.2 8.7 %collective-permute-start.23 = (bf16[768,768]{1,0:T(8,128)(2,1)}, bf16[768,768]{1,0:T(8,128)(2,1)}, u32[]{:S(2)}, u32[]{:S(2)}) collective-permute-start(bf16[768,768]{1,0:T(8,128)(2,1)} %fusion.86), channel_id=1, source_target_pairs={{0,4},{4,0},{8,12},{12,8},{16,20},{20,16},{24,28},{28,24},{1,5},{5... | collective-permute-start | bytes 3538952 | tf_op jit(solution)/shard_map/ppermute | solution.py:83
  409.9 99.8 %all-gather.27.cloned.1.call-start = ((), (), s32[]{:S(2)}) async-start(), calls=%async_computation.20 | async-start | bytes 1966080 | tf_op jit(solution)/shard_map/all_gather | solution.py:44
  413.4 16.3 %collective-permute-start.18 = (bf16[384,768]{1,0:T(8,128)(2,1)S(1)}, bf16[384,768]{1,0:T(8,128)(2,1)S(1)}, u32[]{:S(2)}, u32[]{:S(2)}) collective-permute-start(bf16[384,768]{1,0:T(8,128)(2,1)S(1)} %select_convert_fusion.4), channel_id=1, source_target_pairs={{0,8},{4,12},{8,0},{12,4},{16,24},{20,28},{24,16},{28,20},{1,9},{5... | collective-permute-start | bytes 1769480 | tf_op jit(solution)/shard_map/ppermute | solution.py:83
  418.2 23.7 %collective-permute-start.24 = (bf16[384,768]{1,0:T(8,128)(2,1)S(1)}, bf16[384,768]{1,0:T(8,128)(2,1)S(1)}, u32[]{:S(2)}, u32[]{:S(2)}) collective-permute-start(bf16[384,768]{1,0:T(8,128)(2,1)S(1)} %select_convert_fusion.3), channel_id=1, source_target_pairs={{0,8},{4,12},{8,0},{12,4},{16,24},{20,28},{24,16},{28,20},{1,9},{5... | collective-permute-start | bytes 1769480 | tf_op jit(solution)/shard_map/ppermute | solution.py:83
  429.8 13.9 %copy-start.103 = (f32[4,768]{1,0:T(4,128)S(1)}, f32[4,768]{1,0:T(4,128)}, u32[]{:S(2)}) copy-start(f32[4,768]{1,0:T(4,128)} %get-tuple-element.99) | copy-start | bytes 36868
  429.8 13.9 %copy-start.106 = (s32[4]{0:T(128)S(1)}, s32[4]{0:T(128)}, u32[]{:S(2)}) copy-start(s32[4]{0:T(128)} %copy-done.105) | copy-start | bytes 52
  429.9 13.9 %collective-permute-start.19 = (bf16[192,768]{1,0:T(8,128)(2,1)S(1)}, bf16[192,768]{1,0:T(8,128)(2,1)S(1)}, u32[]{:S(2)}, u32[]{:S(2)}) collective-permute-start(bf16[192,768]{1,0:T(8,128)(2,1)S(1)} %select_convert_fusion.7), channel_id=1, source_target_pairs={{0,16},{4,20},{8,24},{12,28},{16,0},{20,4},{24,8},{28,12},{1,17},{... | collective-permute-start | bytes 884744 | tf_op jit(solution)/shard_map/ppermute | solution.py:83
  442.1 23.9 %copy-start.9 = (f32[256,768]{1,0:T(8,128)S(1)}, f32[256,768]{1,0:T(8,128)}, u32[]{:S(2)}) copy-start(f32[256,768]{1,0:T(8,128)} %get-tuple-element.52) | copy-start | bytes 2359300
  442.1 9.9 %collective-permute-start.25 = (bf16[192,768]{1,0:T(8,128)(2,1)S(1)}, bf16[192,768]{1,0:T(8,128)(2,1)S(1)}, u32[]{:S(2)}, u32[]{:S(2)}) collective-permute-start(bf16[192,768]{1,0:T(8,128)(2,1)S(1)} %select_convert_fusion.6), channel_id=1, source_target_pairs={{0,16},{4,20},{8,24},{12,28},{16,0},{20,4},{24,8},{28,12},{1,17},{... | collective-permute-start | bytes 884744 | tf_op jit(solution)/shard_map/ppermute | solution.py:83
  443.9 14.5 %collective-permute-start.20 = (bf16[192,768]{1,0:T(8,128)(2,1)S(1)}, bf16[192,768]{1,0:T(8,128)(2,1)S(1)}, u32[]{:S(2)}, u32[]{:S(2)}) collective-permute-start(bf16[192,768]{1,0:T(8,128)(2,1)S(1)} %add_convert_fusion.1), channel_id=1, source_target_pairs={{0,16},{4,20},{8,24},{12,28},{16,0},{20,4},{24,8},{28,12},{1,17},{... | collective-permute-start | bytes 884744 | tf_op jit(solution)/shard_map/ppermute | solution.py:88
  452.2 17.3 %copy-start.76 = (f32[256]{0:T(256)S(1)}, f32[256]{0:T(256)}, u32[]{:S(2)}) copy-start(f32[256]{0:T(256)} %copy-done.75) | copy-start | bytes 3076
  452.2 11.3 %collective-permute-start.26 = (bf16[192,768]{1,0:T(8,128)(2,1)S(1)}, bf16[192,768]{1,0:T(8,128)(2,1)S(1)}, u32[]{:S(2)}, u32[]{:S(2)}) collective-permute-start(bf16[192,768]{1,0:T(8,128)(2,1)S(1)} %add_convert_fusion), channel_id=1, source_target_pairs={{0,16},{4,20},{8,24},{12,28},{16,0},{20,4},{24,8},{28,12},{1,17},{... | collective-permute-start | bytes 884744 | tf_op jit(solution)/shard_map/ppermute | solution.py:88
  459.4 23.5 %collective-permute-start.21 = (bf16[384,768]{1,0:T(8,128)(2,1)}, bf16[384,768]{1,0:T(8,128)(2,1)}, u32[]{:S(2)}, u32[]{:S(2)}) collective-permute-start(bf16[384,768]{1,0:T(8,128)(2,1)} %maximum_select_fusion.7), channel_id=1, source_target_pairs={{0,8},{4,12},{8,0},{12,4},{16,24},{20,28},{24,16},{28,20},{1,9},{5... | collective-permute-start | bytes 1769480 | tf_op jit(solution)/shard_map/ppermute | solution.py:88
  464.5 24.4 %collective-permute-start.27 = (bf16[384,768]{1,0:T(8,128)(2,1)}, bf16[384,768]{1,0:T(8,128)(2,1)}, u32[]{:S(2)}, u32[]{:S(2)}) collective-permute-start(bf16[384,768]{1,0:T(8,128)(2,1)} %maximum_select_fusion.8), channel_id=1, source_target_pairs={{0,8},{4,12},{8,0},{12,4},{16,24},{20,28},{24,16},{28,20},{1,9},{5... | collective-permute-start | bytes 1769480 | tf_op jit(solution)/shard_map/ppermute | solution.py:88
  473.1 74.6 %all-gather.31.cloned.1.call-start = ((), (), s32[]{:S(2)}) async-start(), calls=%async_computation.22 | async-start | bytes 1966080 | tf_op jit(solution)/shard_map/all_gather | solution.py:44
  481.7 28.0 %copy-start.32 = (bf16[4,192,768]{2,1,0:T(8,128)(2,1)S(1)}, bf16[4,192,768]{2,1,0:T(8,128)(2,1)}, u32[]{:S(2)}) copy-start(bf16[4,192,768]{2,1,0:T(8,128)(2,1)} %gather_fusion.2) | copy-start | bytes 3538948
  482.2 6.6 %collective-permute-start.6 = (f32[3,2,2,768]{3,1,2,0:T(2,128)S(1)}, f32[3,2,2,768]{3,1,2,0:T(2,128)S(1)}, u32[]{:S(2)}, u32[]{:S(2)}) collective-permute-start(f32[3,2,2,768]{3,1,2,0:T(2,128)S(1)} %maximum_add_fusion), channel_id=1, source_target_pairs={{0,1},{1,0},{2,3},{3,2},{4,5},{5,4},{6,7},{7,6},{8,9},{9,8},{10,11... | collective-permute-start | bytes 110600 | tf_op jit(solution)/shard_map/ppermute | solution.py:102
  485.8 123.6 %collective-permute-start.22 = (bf16[768,768]{1,0:T(8,128)(2,1)}, bf16[768,768]{1,0:T(8,128)(2,1)}, u32[]{:S(2)}, u32[]{:S(2)}) collective-permute-start(bf16[768,768]{1,0:T(8,128)(2,1)} %maximum_select_fusion.3), channel_id=1, source_target_pairs={{0,4},{4,0},{8,12},{12,8},{16,20},{20,16},{24,28},{28,24},{1,5},{5... | collective-permute-start | bytes 3538952 | tf_op jit(solution)/shard_map/ppermute | solution.py:88
  488.8 23.1 %copy-start.5 = (f32[4,2,3,128,128]{3,4,2,1,0:T(8,128)S(1)}, f32[4,2,3,128,128]{3,4,2,1,0:T(8,128)}, u32[]{:S(2)}) copy-start(f32[4,2,3,128,128]{3,4,2,1,0:T(8,128)} %copy-done.4) | copy-start | bytes 4718596
  488.8 23.1 %copy-start.51 = (f32[4,2,3,128]{3,2,1,0:T(4,128)S(1)}, f32[4,2,3,128]{3,2,1,0:T(4,128)}, u32[]{:S(2)}) copy-start(f32[4,2,3,128]{3,2,1,0:T(4,128)} %copy-done.50) | copy-start | bytes 36868
  488.8 7.7 %collective-permute-start.7 = (f32[3,2,2,768]{3,1,2,0:T(2,128)S(1)}, f32[3,2,2,768]{3,1,2,0:T(2,128)S(1)}, u32[]{:S(2)}, u32[]{:S(2)}) collective-permute-start(f32[3,2,2,768]{3,1,2,0:T(2,128)S(1)} %fusion.281), channel_id=1, source_target_pairs={{0,2},{1,3},{2,0},{3,1},{4,6},{5,7},{6,4},{7,5},{8,10},{9,11},{10,... | collective-permute-start | bytes 110600 | tf_op jit(solution)/shard_map/ppermute | solution.py:102
  491.9 126.0 %collective-permute-start.28 = (bf16[768,768]{1,0:T(8,128)(2,1)}, bf16[768,768]{1,0:T(8,128)(2,1)}, u32[]{:S(2)}, u32[]{:S(2)}) collective-permute-start(bf16[768,768]{1,0:T(8,128)(2,1)} %maximum_select_fusion.4), channel_id=1, source_target_pairs={{0,4},{4,0},{8,12},{12,8},{16,20},{20,16},{24,28},{28,24},{1,5},{5... | collective-permute-start | bytes 3538952 | tf_op jit(solution)/shard_map/ppermute | solution.py:88
  491.9 143.4 %reduce-scatter.13.cloned.1.call-start = ((), (), s32[]{:S(2)}) async-start(), calls=%async_computation.12 | async-start | bytes 1966080 | tf_op jit(solution)/shard_map/reduce_scatter | solution.py:49
  526.7 23.6 %copy-start.7 = (f32[4,2,3,128,128]{3,4,2,1,0:T(8,128)S(1)}, f32[4,2,3,128,128]{3,4,2,1,0:T(8,128)}, u32[]{:S(2)}) copy-start(f32[4,2,3,128,128]{3,4,2,1,0:T(8,128)} %copy-done.6) | copy-start | bytes 4718596
  526.7 23.6 %copy-start.52 = (f32[4,2,3,128]{3,2,1,0:T(4,128)S(1)}, f32[4,2,3,128]{3,2,1,0:T(4,128)}, u32[]{:S(2)}) copy-start(f32[4,2,3,128]{3,2,1,0:T(4,128)} %log_add_fusion) | copy-start | bytes 36868
  555.8 81.6 %reduce-scatter.17.cloned.1.call-start = ((), (), s32[]{:S(2)}) async-start(), calls=%async_computation.14 | async-start | bytes 1966080 | tf_op jit(solution)/shard_map/reduce_scatter | solution.py:49
  561.6 15.8 %collective-permute-start.8 = (f32[15,768]{1,0:T(8,128)}, f32[15,768]{1,0:T(8,128)S(1)}, u32[]{:S(2)}, u32[]{:S(2)}) collective-permute-start(f32[15,768]{1,0:T(8,128)} %pad_maximum_fusion.6), channel_id=1, source_target_pairs={{0,4},{4,0},{8,12},{12,8},{16,20},{20,16},{24,28},{28,24},{1,5},{5... | collective-permute-start | bytes 138248 | tf_op jit(solution)/shard_map/ppermute | solution.py:102
  568.4 10.5 %collective-permute-start = (bf16[576,768]{1,0:T(8,128)(2,1)}, bf16[576,768]{1,0:T(8,128)(2,1)}, u32[]{:S(2)}, u32[]{:S(2)}) collective-permute-start(bf16[576,768]{1,0:T(8,128)(2,1)} %bitcast.62), channel_id=1, source_target_pairs={{0,4},{4,0},{8,12},{12,8},{16,20},{20,16},{24,28},{28,24},{1,5},{5... | collective-permute-start | bytes 2654216 | tf_op jit(solution)/shard_map/ppermute | solution.py:83
  577.3 4.2 collective-permute-start.11
  577.4 34.9 %collective-permute-start.9 = (f32[15,768]{1,0:T(8,128)S(1)}, f32[15,768]{1,0:T(8,128)S(1)}, u32[]{:S(2)}, u32[]{:S(2)}) collective-permute-start(f32[15,768]{1,0:T(8,128)S(1)} %fusion.280), channel_id=1, source_target_pairs={{0,8},{4,12},{8,0},{12,4},{16,24},{20,28},{24,16},{28,20},{1,9},{5... | collective-permute-start | bytes 138248 | tf_op jit(solution)/shard_map/ppermute | solution.py:102
  581.0 13.1 %collective-permute-start.1 = (bf16[288,768]{1,0:T(8,128)(2,1)S(1)}, bf16[288,768]{1,0:T(8,128)(2,1)S(1)}, u32[]{:S(2)}, u32[]{:S(2)}) collective-permute-start(bf16[288,768]{1,0:T(8,128)(2,1)S(1)} %select_convert_fusion.5), channel_id=1, source_target_pairs={{0,8},{4,12},{8,0},{12,4},{16,24},{20,28},{24,16},{28,20},{1,9},{5... | collective-permute-start | bytes 1327112 | tf_op jit(solution)/shard_map/ppermute | solution.py:83
  581.7 14.7 %collective-permute-start.12 = (bf16[96,768]{1,0:T(8,128)(2,1)S(1)}, bf16[96,768]{1,0:T(8,128)(2,1)S(1)}, u32[]{:S(2)}, u32[]{:S(2)}) collective-permute-start(bf16[96,768]{1,0:T(8,128)(2,1)S(1)} %select_convert_fusion.10), channel_id=1, source_target_pairs={{0,8},{4,12},{8,0},{12,4},{16,24},{20,28},{24,16},{28,20},{1,9},{5... | collective-permute-start | bytes 442376 | tf_op jit(solution)/shard_map/ppermute | solution.py:83
  594.2 6.0 collective-permute-start.2
  600.3 6.0 collective-permute-start.3
  601.9 5.9 collective-permute-start.13
  606.4 10.3 %collective-permute-start.4 = (bf16[288,768]{1,0:T(8,128)(2,1)S(1)}, bf16[288,768]{1,0:T(8,128)(2,1)S(1)}, u32[]{:S(2)}, u32[]{:S(2)}) collective-permute-start(bf16[288,768]{1,0:T(8,128)(2,1)S(1)} %maximum_select_fusion.9), channel_id=1, source_target_pairs={{0,8},{4,12},{8,0},{12,4},{16,24},{20,28},{24,16},{28,20},{1,9},{5... | collective-permute-start | bytes 1327112 | tf_op jit(solution)/shard_map/ppermute | solution.py:88
  607.8 5.2 collective-permute-start.14
  612.4 13.4 %collective-permute-start.10 = (f32[15,768]{1,0:T(8,128)S(1)}, f32[15,768]{1,0:T(8,128)S(1)}, u32[]{:S(2)}, u32[]{:S(2)}) collective-permute-start(f32[15,768]{1,0:T(8,128)S(1)} %add.555), channel_id=1, source_target_pairs={{0,16},{4,20},{8,24},{12,28},{16,0},{20,4},{24,8},{28,12},{1,17},{... | collective-permute-start | bytes 138248 | tf_op jit(solution)/shard_map/ppermute | solution.py:102
  613.0 13.4 %collective-permute-start.15 = (bf16[96,768]{1,0:T(8,128)(2,1)S(1)}, bf16[96,768]{1,0:T(8,128)(2,1)S(1)}, u32[]{:S(2)}, u32[]{:S(2)}) collective-permute-start(bf16[96,768]{1,0:T(8,128)(2,1)S(1)} %maximum_select_fusion.11), channel_id=1, source_target_pairs={{0,8},{4,12},{8,0},{12,4},{16,24},{20,28},{24,16},{28,20},{1,9},{5... | collective-permute-start | bytes 442376 | tf_op jit(solution)/shard_map/ppermute | solution.py:88
  617.9 12.9 %collective-permute-start.5 = (bf16[576,768]{1,0:T(8,128)(2,1)}, bf16[576,768]{1,0:T(8,128)(2,1)}, u32[]{:S(2)}, u32[]{:S(2)}) collective-permute-start(bf16[576,768]{1,0:T(8,128)(2,1)} %maximum_select_fusion.5), channel_id=1, source_target_pairs={{0,4},{4,0},{8,12},{12,8},{16,20},{20,16},{24,28},{28,24},{1,5},{5... | collective-permute-start | bytes 2654216 | tf_op jit(solution)/shard_map/ppermute | solution.py:88
  626.4 3.1 collective-permute-start.16
  (110 other events, 524.8 us)
Sparse Core Ops, SparseCore 0:
  10.2 39.7 all-gather.16
  52.1 44.3 all-gather.20
  128.6 43.7 all-gather.18
  182.7 38.3 all-gather.22
  223.3 34.2 reduce-scatter.6
  259.8 34.2 reduce-scatter.8
  300.0 35.8 all-gather.24
  337.5 35.8 all-gather.28
  385.4 34.2 reduce-scatter.14
  421.9 34.2 reduce-scatter.10
  473.2 36.4 all-gather.26
  511.7 35.9 all-gather.30
  555.9 34.2 reduce-scatter.12
  593.0 34.2 reduce-scatter.16

commit v11 on v10

--- a/solution.py
+++ b/solution.py
@@ -307,8 +307,7 @@
     peer_kind = block_kind[(jnp.arange(n_tensor) * tok_dev) // block_rows]
     row_parts = [slice(part * seg_rows, (part + 1) * seg_rows) for part in range(STREAMS)]
     gathered = [gather_rows(inputs[rows]) for rows in row_parts]
-    out_sel, gathered[0] = lax.optimization_barrier((w_out[peer_kind], gathered[0]))
-    out_rows_w = lax.all_to_all(out_sel, "tensor", 0, 0, tiled=True)
+    out_rows_w = lax.all_to_all(w_out[peer_kind], "tensor", 0, 0, tiled=True)
     marks = None
     outs, ins, grads, smalls = [], [], [], []
     for part in range(STREAMS):

time: 659 us -> 654 us (level)
  waiting for transfers between devices: 274 us -> 262 us
    all_to_all x1, waiting for transfers between devices: 19.1 us -> 0.01 us  [local(): out_rows_w = lax.all_to_all(w_out[peer_kind], 'tensor', 0, 0, tiled=True)]
    all_gather x8, waiting for transfers between devices: 119 us -> 132 us  [gather_rows(): return lax.all_gather(local_rows, 'tensor', axis=0, tiled=False)]
  transfers between devices with their start and end apart: 46 -> 46, of which waited for: 23 -> 22; matrix products, arithmetic and copies ran while one was open for 44% -> 45% of each run, Pallas kernels for 0% -> 0%
where the time goes in v11:
time: 654 us; the launch traced here: 643 us
  waiting for transfers between devices  262 us (40%)
  matrix products  132 us (20%)
  local copies, waits for them, and re-layouts  102 us (16%)
  other arithmetic  91 us (14%)
  starting transfers between devices  40.4 us (6%)
  between operations  16.3 us (2%)
    all_gather x8, waiting for transfers between devices, gather_rows(): return lax.all_gather(local_rows, 'tensor', axis=0, tiled=False)  132 us
    reduce_scatter x6, waiting for transfers between devices, scatter_sum(): lax.psum_scatter(seg_parts.reshape(n_seg * seg_rows, width).astype(jnp.bf...  53.5 us
    ppermute x12, waiting for transfers between devices, dp_sum_low(): gots = lax.ppermute(sends, 'dp', dp_perm(n_dp, 1 << b))  43.7 us
    select_n x12, other arithmetic, dp_sum_low(): jnp.where(upper, jnp.concatenate([g, c]), jnp.concatenate([c, g]))  17.5 us
    dot_general x12, matrix products, pick(): return jnp.dot(kind_hot, kind_table.astype(jnp.float32), precision=highest)  16.9 us
    dot_general x12, matrix products, type_sum(): jnp.einsum('rt,rd->td', kind_hot, values, precision=lax.Precision.HIGHEST)  16.3 us
    convert_element_type x2, other arithmetic, stream(): activ = jax.nn.gelu(pre_act, approximate=False).astype(jnp.bfloat16)  14.6 us
    dot_general x2, matrix products, stream(): jnp.einsum('srd,sfd->srf', two_segs, down_sel, preferred_element_type=jnp...  13.8 us
  transfers between devices with their start and end apart: 46, of which 22 were waited for; matrix products, arithmetic and copies ran while one was open for 45% of the time, Pallas kernels for 0%

profile of v11, /device:TPU:0, one launch (start us, length us, event | category | flops | bytes accessed | tf_op | source)
XLA Modules:
  0.0 643.2 jit_solution(13363460013688556410)
XLA Ops:
  13.0 6.5 %all-to-all-start.1 = ((bf16[4,192,768]{2,1,0:T(8,128)(2,1)}), bf16[4,192,768]{2,1,0:T(8,128)(2,1)}, u32[]{:S(2)}, u32[]{:S(2)}) async-start(bf16[4,192,768]{2,1,0:T(8,128)(2,1)} %gather_fusion.4), calls=%async_computation.1 | async-start | bytes 2359296 | tf_op jit(solution)/shard_map/all_to_all | solution.py:310
  26.2 4.1 gather_fusion.1
  30.3 43.4 %all-gather.17.cloned.1.call-done = bf16[1024,768]{1,0:T(8,128)(2,1)} async-done(((bf16[256,768]{1,0:T(8,128)(2,1)}), bf16[1024,768]{1,0:T(8,128)(2,1)}) %all-gather.17.cloned.1.call-update) | async-done | bytes 1572880 | tf_op jit(solution)/shard_map/all_gather | solution.py:44
  73.7 3.6 convolution_bitcast_fusion.2
  78.8 2.6 fusion.219
  91.9 4.1 all-to-all-start
  96.7 4.1 gather_fusion.9
  107.3 11.6 %all-to-all-done = bf16[4,256,192]{1,2,0:T(8,128)(2,1)} async-done(((bf16[4,256,192]{1,2,0:T(8,128)(2,1)}), bf16[4,256,192]{1,2,0:T(8,128)(2,1)}, u32[]{:S(2)}, u32[]{:S(2)}) %all-to-all-start) | async-done | bytes 393248 | tf_op jit(solution)/shard_map/all_to_all | solution.py:179
  123.6 3.6 convolution_bitcast_fusion.1
  145.1 4.1 all-to-all-start.2
  152.0 3.2 gather_fusion.14
  155.2 3.2 gather_fusion.7
  158.4 5.0 gather_fusion.12
  163.4 3.3 gather_fusion.5
  177.8 5.1 fusion.98
  182.9 7.3 %fusion.3 = bf16[4,256,768]{2,1,0:T(8,128)(2,1)S(1)} fusion(f32[4,256,768]{2,1,0:T(8,128)S(1)} %get-tuple-element.79, f32[4,768]{1,0:T(4,128)S(1)} %copy-done.76, u8[256,768]{1,0:T(8,128)(4,1)S(1)} %get-tuple-element.16, u8[256,768]{1,0:T(8,128)(4,1)S(1)} %get-tuple-element.15), kind=kLoop, calls=%fused_computation.27 | loop fusion | flops 55836672 | bytes 5124096 | tf_op jit(solution)/shard_map/convert_element_type | solution.py:193
  190.2 2.6 convolution_convert_fusion.5
  193.2 23.0 %all-gather.23.cloned.1.call-done = bf16[1024,768]{1,0:T(8,128)(2,1)} async-done(((bf16[256,768]{1,0:T(8,128)(2,1)}), bf16[1024,768]{1,0:T(8,128)(2,1)}) %all-gather.23.cloned.1.call-update) | async-done | bytes 1572880 | tf_op jit(solution)/shard_map/all_gather | solution.py:44
  216.2 5.1 fusion.99
  221.3 7.3 %fusion.6 = bf16[4,256,768]{2,1,0:T(8,128)(2,1)S(1)} fusion(f32[4,256,768]{2,1,0:T(8,128)S(1)} %get-tuple-element.76, f32[4,768]{1,0:T(4,128)S(1)} %copy-done.73, u8[256,768]{1,0:T(8,128)(4,1)S(1)} %get-tuple-element.18, u8[256,768]{1,0:T(8,128)(4,1)S(1)} %get-tuple-element.17), kind=kLoop, calls=%fused_computation.30 | loop fusion | flops 55836672 | bytes 5124096 | tf_op jit(solution)/shard_map/convert_element_type | solution.py:193
  228.7 2.6 convolution_convert_fusion.4
  233.2 19.5 %reduce-scatter.7.cloned.1.call-done = bf16[256,768]{1,0:T(8,128)(2,1)} async-done(((bf16[1024,768]{1,0:T(8,128)(2,1)}), bf16[256,768]{1,0:T(8,128)(2,1)}) %reduce-scatter.7.cloned.1.call-update) | async-done | bytes 393232 | tf_op jit(solution)/shard_map/reduce_scatter | solution.py:49
  255.2 34.0 %reduce-scatter.9.cloned.1.call-done = bf16[256,768]{1,0:T(8,128)(2,1)} async-done(((bf16[1024,768]{1,0:T(8,128)(2,1)}), bf16[256,768]{1,0:T(8,128)(2,1)}) %reduce-scatter.9.cloned.1.call-update) | async-done | bytes 393232 | tf_op jit(solution)/shard_map/reduce_scatter | solution.py:49
  295.0 2.8 gather_fusion.15
  304.3 2.6 copy.88
  306.9 2.6 copy.91
  309.6 2.6 copy.96
  312.2 2.6 copy.98
  314.7 2.6 copy.97
  317.3 2.6 copy.99
  331.0 7.5 %convert_reduce_fusion.1 = (f32[4,768]{1,0:T(4,128)}, bf16[4,256,768]{2,1,0:T(8,128)(2,1)}) fusion(f32[4,256,768]{2,1,0:T(8,128)} %copy-done.36, f32[4,768]{1,0:T(4,128)} %convert_element_type.516, bf16[4,256,768]{2,1,0:T(8,128)(2,1)} %bitcast.415, bf16[4,768,768]{2,1,0:T(8,128)(2,1)} %gather_fusion.7), kind=kOutput, calls=%fused_computation.64 | convolution fusion | flops 1219752960 | bytes 11034624 | tf_op jit(solution)/shard_map/srd,sfd->srf/dot_general | solution.py:208
  338.5 30.0 %all-gather.29.cloned.1.call-done = bf16[1024,768]{1,0:T(8,128)(2,1)} async-done(((bf16[256,768]{1,0:T(8,128)(2,1)}), bf16[1024,768]{1,0:T(8,128)(2,1)}) %all-gather.29.cloned.1.call-update) | async-done | bytes 1572880 | tf_op jit(solution)/shard_map/all_gather | solution.py:44
  368.5 6.4 convert_reduce_fusion
  374.9 5.5 convolution_convert_fusion
  380.9 4.7 fusion.25
  385.6 2.7 bitcast_add_fusion.1
  392.3 2.7 fusion.21
  395.1 2.8 bitcast_add_fusion
  402.4 2.6 convolution_convert_fusion.2
  405.2 3.1 bitcast_add_fusion.4
  410.0 3.1 bitcast_add_fusion.3
  414.8 9.9 %collective-permute-done.18 = bf16[384,768]{1,0:T(8,128)(2,1)S(1)} collective-permute-done((bf16[384,768]{1,0:T(8,128)(2,1)S(1)}, bf16[384,768]{1,0:T(8,128)(2,1)S(1)}, u32[]{:S(2)}, u32[]{:S(2)}) %collective-permute-start.18) | collective-permute-done | bytes 589856 | tf_op jit(solution)/shard_map/ppermute | solution.py:83
  426.5 10.4 %collective-permute-done.24 = bf16[384,768]{1,0:T(8,128)(2,1)S(1)} collective-permute-done((bf16[384,768]{1,0:T(8,128)(2,1)S(1)}, bf16[384,768]{1,0:T(8,128)(2,1)S(1)}, u32[]{:S(2)}, u32[]{:S(2)}) %collective-permute-start.24) | collective-permute-done | bytes 589856 | tf_op jit(solution)/shard_map/ppermute | solution.py:83
  439.6 7.5 %collective-permute-done.25 = bf16[192,768]{1,0:T(8,128)(2,1)S(1)} collective-permute-done((bf16[192,768]{1,0:T(8,128)(2,1)S(1)}, bf16[192,768]{1,0:T(8,128)(2,1)S(1)}, u32[]{:S(2)}, u32[]{:S(2)}) %collective-permute-start.25) | collective-permute-done | bytes 294944 | tf_op jit(solution)/shard_map/ppermute | solution.py:83
  449.6 3.9 collective-permute-done.20
  456.0 2.6 collective-permute-done.26
  461.1 2.9 fusion.211
  478.0 2.9 maximum_select_fusion.3
  480.9 3.0 collective-permute-done.6
  484.0 3.0 maximum_select_fusion.4
  487.3 4.1 collective-permute-done.7
  492.9 12.0 %all-gather.27.cloned.1.call-done = bf16[1024,768]{1,0:T(8,128)(2,1)} async-done(((bf16[256,768]{1,0:T(8,128)(2,1)}), bf16[1024,768]{1,0:T(8,128)(2,1)}) %all-gather.27.cloned.1.call-update) | async-done | bytes 1572880 | tf_op jit(solution)/shard_map/all_gather | solution.py:44
  517.2 4.6 convolution_bitcast_fusion
  521.8 20.9 %all-gather.31.cloned.1.call-done = bf16[1024,768]{1,0:T(8,128)(2,1)} async-done(((bf16[256,768]{1,0:T(8,128)(2,1)}), bf16[1024,768]{1,0:T(8,128)(2,1)}) %all-gather.31.cloned.1.call-update) | async-done | bytes 1572880 | tf_op jit(solution)/shard_map/all_gather | solution.py:44
  556.7 3.5 fusion.17
  569.0 2.7 bitcast_convert_fusion
  578.4 10.8 %collective-permute-done.1 = bf16[288,768]{1,0:T(8,128)(2,1)S(1)} collective-permute-done((bf16[288,768]{1,0:T(8,128)(2,1)S(1)}, bf16[288,768]{1,0:T(8,128)(2,1)S(1)}, u32[]{:S(2)}, u32[]{:S(2)}) %collective-permute-start.1) | collective-permute-done | bytes 442400 | tf_op jit(solution)/shard_map/ppermute | solution.py:83
  591.6 3.8 collective-permute-done.2
  597.6 3.8 collective-permute-done.3
  604.4 3.0 maximum_select_fusion
  608.9 2.9 collective-permute-done.4
  613.1 2.7 maximum_select_fusion.1
  615.8 2.5 convert.16
  618.3 2.5 convert.15
  (561 shorter events, 202.7 us)
Async XLA Ops:
  7.2 144.9 %copy-start = (bf16[2,768,768]{2,1,0:T(8,128)(2,1)S(1)}, bf16[2,768,768]{2,1,0:T(8,128)(2,1)}, u32[]{:S(2)}) copy-start(bf16[2,768,768]{2,1,0:T(8,128)(2,1)} %param.25) | copy-start | bytes 7077892
  7.2 66.5 %all-gather.17.cloned.1.call-start = ((), (), s32[]{:S(2)}) async-start(), calls=%async_computation.15 | async-start | bytes 1966080 | tf_op jit(solution)/shard_map/all_gather | solution.py:44
  11.4 14.8 %copy-start.102 = (s32[1024]{0:T(1024)}, s32[1024]{0:T(1024)S(1)}, u32[]{:S(2)}) copy-start(s32[1024]{0:T(1024)S(1)} %pad_clamp_fusion.4) | copy-start | bytes 12292
  13.0 78.8 %all-to-all-start.1 = ((bf16[4,192,768]{2,1,0:T(8,128)(2,1)}), bf16[4,192,768]{2,1,0:T(8,128)(2,1)}, u32[]{:S(2)}, u32[]{:S(2)}) async-start(bf16[4,192,768]{2,1,0:T(8,128)(2,1)} %gather_fusion.4), calls=%async_computation.1 | async-start | bytes 2359296 | tf_op jit(solution)/shard_map/all_to_all | solution.py:310
  19.5 104.0 %all-gather.21.cloned.1.call-start = ((), (), s32[]{:S(2)}) async-start(), calls=%async_computation.17 | async-start | bytes 1966080 | tf_op jit(solution)/shard_map/all_gather | solution.py:44
  23.5 73.1 %copy-start.101 = (s32[1024]{0:T(1024)}, s32[1024]{0:T(1024)S(1)}, u32[]{:S(2)}) copy-start(s32[1024]{0:T(1024)S(1)} %pad_clamp_fusion.1) | copy-start | bytes 12292
  24.9 63.7 %copy-start.69 = (f32[4,3,64]{2,1,0:T(4,128)}, f32[4,3,64]{2,1,0:T(4,128)S(1)}, u32[]{:S(2)}) copy-start(f32[4,3,64]{2,1,0:T(4,128)S(1)} %add.480) | copy-start | bytes 9220
  24.9 61.4 %copy-start.67 = (f32[4,3,64]{2,1,0:T(4,128)}, f32[4,3,64]{2,1,0:T(4,128)S(1)}, u32[]{:S(2)}) copy-start(f32[4,3,64]{2,1,0:T(4,128)S(1)} %add.487) | copy-start | bytes 9220
  91.9 27.0 %all-to-all-start = ((bf16[4,256,192]{1,2,0:T(8,128)(2,1)}), bf16[4,256,192]{1,2,0:T(8,128)(2,1)}, u32[]{:S(2)}, u32[]{:S(2)}) async-start(bf16[4,256,192]{1,2,0:T(8,128)(2,1)} %convert_element_type.514), calls=%async_computation | async-start | bytes 786432 | tf_op jit(solution)/shard_map/all_to_all | solution.py:179
  96.0 81.8 %all-gather.19.cloned.1.call-start = ((), (), s32[]{:S(2)}) async-start(), calls=%async_computation.16 | async-start | bytes 1966080 | tf_op jit(solution)/shard_map/all_gather | solution.py:44
  96.7 22.2 %copy-start.50 = (bf16[512,768]{1,0:T(8,128)(2,1)S(1)}, bf16[512,768]{1,0:T(8,128)(2,1)}, u32[]{:S(2)}) copy-start(bf16[512,768]{1,0:T(8,128)(2,1)} %param.13) | copy-start | bytes 2359300
  101.5 32.0 %copy-start.70 = (f32[4,3,64]{2,1,0:T(4,128)}, f32[4,3,64]{2,1,0:T(4,128)S(1)}, u32[]{:S(2)}) copy-start(f32[4,3,64]{2,1,0:T(4,128)S(1)} %add.515) | copy-start | bytes 9220
  145.1 26.9 %all-to-all-start.2 = ((bf16[4,256,192]{1,2,0:T(8,128)(2,1)}), bf16[4,256,192]{1,2,0:T(8,128)(2,1)}, u32[]{:S(2)}, u32[]{:S(2)}) async-start(bf16[4,256,192]{1,2,0:T(8,128)(2,1)} %convert_element_type.530), calls=%async_computation.3 | async-start | bytes 786432 | tf_op jit(solution)/shard_map/all_to_all | solution.py:179
  149.3 67.0 %all-gather.23.cloned.1.call-start = ((), (), s32[]{:S(2)}) async-start(), calls=%async_computation.18 | async-start | bytes 1966080 | tf_op jit(solution)/shard_map/all_gather | solution.py:44
  177.7 75.0 %reduce-scatter.7.cloned.1.call-start = ((), (), s32[]{:S(2)}) async-start(), calls=%async_computation.9 | async-start | bytes 1966080 | tf_op jit(solution)/shard_map/reduce_scatter | solution.py:49
  177.8 12.4 %slice-start.2 = ((s8[4718592]{0:T(1024)(128)(4,1)}), s8[4194304]{0:T(1024)(128)(4,1)S(1)}, s32[]{:S(2)}) async-start(s8[4718592]{0:T(1024)(128)(4,1)} %bitcast.349), calls=%async_computation.25 | async-start | bytes 8388608
  192.9 96.3 %reduce-scatter.9.cloned.1.call-start = ((), (), s32[]{:S(2)}) async-start(), calls=%async_computation.10 | async-start | bytes 1966080 | tf_op jit(solution)/shard_map/reduce_scatter | solution.py:49
  231.3 99.8 %all-gather.25.cloned.1.call-start = ((), (), s32[]{:S(2)}) async-start(), calls=%async_computation.19 | async-start | bytes 1966080 | tf_op jit(solution)/shard_map/all_gather | solution.py:44
  295.0 73.5 %all-gather.29.cloned.1.call-start = ((), (), s32[]{:S(2)}) async-start(), calls=%async_computation.21 | async-start | bytes 1966080 | tf_op jit(solution)/shard_map/all_gather | solution.py:44
  299.8 161.3 %reduce-scatter.15.cloned.1.call-start = ((), (), s32[]{:S(2)}) async-start(), calls=%async_computation.13 | async-start | bytes 1966080 | tf_op jit(solution)/shard_map/reduce_scatter | solution.py:49
  331.0 37.5 %copy-start.74 = (f32[4,768]{1,0:T(4,128)S(1)}, f32[4,768]{1,0:T(4,128)}, u32[]{:S(2)}) copy-start(f32[4,768]{1,0:T(4,128)} %convert_element_type.532) | copy-start | bytes 36868
  380.4 84.2 %reduce-scatter.11.cloned.1.call-start = ((), (), s32[]{:S(2)}) async-start(), calls=%async_computation.11 | async-start | bytes 1966080 | tf_op jit(solution)/shard_map/reduce_scatter | solution.py:49
  389.6 15.6 %collective-permute-start.17 = (bf16[768,768]{1,0:T(8,128)(2,1)}, bf16[768,768]{1,0:T(8,128)(2,1)}, u32[]{:S(2)}, u32[]{:S(2)}) collective-permute-start(bf16[768,768]{1,0:T(8,128)(2,1)} %fusion.84), channel_id=1, source_target_pairs={{0,4},{4,0},{8,12},{12,8},{16,20},{20,16},{24,28},{28,24},{1,5},{5... | collective-permute-start | bytes 3538952 | tf_op jit(solution)/shard_map/ppermute | solution.py:83
  401.3 8.7 %collective-permute-start.23 = (bf16[768,768]{1,0:T(8,128)(2,1)}, bf16[768,768]{1,0:T(8,128)(2,1)}, u32[]{:S(2)}, u32[]{:S(2)}) collective-permute-start(bf16[768,768]{1,0:T(8,128)(2,1)} %fusion.85), channel_id=1, source_target_pairs={{0,4},{4,0},{8,12},{12,8},{16,20},{20,16},{24,28},{28,24},{1,5},{5... | collective-permute-start | bytes 3538952 | tf_op jit(solution)/shard_map/ppermute | solution.py:83
  405.0 99.9 %all-gather.27.cloned.1.call-start = ((), (), s32[]{:S(2)}) async-start(), calls=%async_computation.20 | async-start | bytes 1966080 | tf_op jit(solution)/shard_map/all_gather | solution.py:44
  408.5 16.3 %collective-permute-start.18 = (bf16[384,768]{1,0:T(8,128)(2,1)S(1)}, bf16[384,768]{1,0:T(8,128)(2,1)S(1)}, u32[]{:S(2)}, u32[]{:S(2)}) collective-permute-start(bf16[384,768]{1,0:T(8,128)(2,1)S(1)} %select_convert_fusion.4), channel_id=1, source_target_pairs={{0,8},{4,12},{8,0},{12,4},{16,24},{20,28},{24,16},{28,20},{1,9},{5... | collective-permute-start | bytes 1769480 | tf_op jit(solution)/shard_map/ppermute | solution.py:83
  413.3 23.7 %collective-permute-start.24 = (bf16[384,768]{1,0:T(8,128)(2,1)S(1)}, bf16[384,768]{1,0:T(8,128)(2,1)S(1)}, u32[]{:S(2)}, u32[]{:S(2)}) collective-permute-start(bf16[384,768]{1,0:T(8,128)(2,1)S(1)} %select_convert_fusion.3), channel_id=1, source_target_pairs={{0,8},{4,12},{8,0},{12,4},{16,24},{20,28},{24,16},{28,20},{1,9},{5... | collective-permute-start | bytes 1769480 | tf_op jit(solution)/shard_map/ppermute | solution.py:83
  424.9 13.9 %copy-start.103 = (f32[4,768]{1,0:T(4,128)S(1)}, f32[4,768]{1,0:T(4,128)}, u32[]{:S(2)}) copy-start(f32[4,768]{1,0:T(4,128)} %get-tuple-element.95) | copy-start | bytes 36868
  424.9 13.9 %copy-start.106 = (s32[4]{0:T(128)S(1)}, s32[4]{0:T(128)}, u32[]{:S(2)}) copy-start(s32[4]{0:T(128)} %copy-done.105) | copy-start | bytes 52
  425.0 13.9 %collective-permute-start.19 = (bf16[192,768]{1,0:T(8,128)(2,1)S(1)}, bf16[192,768]{1,0:T(8,128)(2,1)S(1)}, u32[]{:S(2)}, u32[]{:S(2)}) collective-permute-start(bf16[192,768]{1,0:T(8,128)(2,1)S(1)} %select_convert_fusion.7), channel_id=1, source_target_pairs={{0,16},{4,20},{8,24},{12,28},{16,0},{20,4},{24,8},{28,12},{1,17},{... | collective-permute-start | bytes 884744 | tf_op jit(solution)/shard_map/ppermute | solution.py:83
  437.2 23.9 %copy-start.9 = (f32[256,768]{1,0:T(8,128)S(1)}, f32[256,768]{1,0:T(8,128)}, u32[]{:S(2)}) copy-start(f32[256,768]{1,0:T(8,128)} %get-tuple-element.48) | copy-start | bytes 2359300
  437.2 9.9 %collective-permute-start.25 = (bf16[192,768]{1,0:T(8,128)(2,1)S(1)}, bf16[192,768]{1,0:T(8,128)(2,1)S(1)}, u32[]{:S(2)}, u32[]{:S(2)}) collective-permute-start(bf16[192,768]{1,0:T(8,128)(2,1)S(1)} %select_convert_fusion.6), channel_id=1, source_target_pairs={{0,16},{4,20},{8,24},{12,28},{16,0},{20,4},{24,8},{28,12},{1,17},{... | collective-permute-start | bytes 884744 | tf_op jit(solution)/shard_map/ppermute | solution.py:83
  439.0 14.5 %collective-permute-start.20 = (bf16[192,768]{1,0:T(8,128)(2,1)S(1)}, bf16[192,768]{1,0:T(8,128)(2,1)S(1)}, u32[]{:S(2)}, u32[]{:S(2)}) collective-permute-start(bf16[192,768]{1,0:T(8,128)(2,1)S(1)} %add_convert_fusion.1), channel_id=1, source_target_pairs={{0,16},{4,20},{8,24},{12,28},{16,0},{20,4},{24,8},{28,12},{1,17},{... | collective-permute-start | bytes 884744 | tf_op jit(solution)/shard_map/ppermute | solution.py:88
  447.3 17.3 %copy-start.78 = (f32[256]{0:T(256)S(1)}, f32[256]{0:T(256)}, u32[]{:S(2)}) copy-start(f32[256]{0:T(256)} %copy-done.77) | copy-start | bytes 3076
  447.3 11.3 %collective-permute-start.26 = (bf16[192,768]{1,0:T(8,128)(2,1)S(1)}, bf16[192,768]{1,0:T(8,128)(2,1)S(1)}, u32[]{:S(2)}, u32[]{:S(2)}) collective-permute-start(bf16[192,768]{1,0:T(8,128)(2,1)S(1)} %add_convert_fusion), channel_id=1, source_target_pairs={{0,16},{4,20},{8,24},{12,28},{16,0},{20,4},{24,8},{28,12},{1,17},{... | collective-permute-start | bytes 884744 | tf_op jit(solution)/shard_map/ppermute | solution.py:88
  454.5 23.5 %collective-permute-start.21 = (bf16[384,768]{1,0:T(8,128)(2,1)}, bf16[384,768]{1,0:T(8,128)(2,1)}, u32[]{:S(2)}, u32[]{:S(2)}) collective-permute-start(bf16[384,768]{1,0:T(8,128)(2,1)} %maximum_select_fusion.7), channel_id=1, source_target_pairs={{0,8},{4,12},{8,0},{12,4},{16,24},{20,28},{24,16},{28,20},{1,9},{5... | collective-permute-start | bytes 1769480 | tf_op jit(solution)/shard_map/ppermute | solution.py:88
  459.6 24.4 %collective-permute-start.27 = (bf16[384,768]{1,0:T(8,128)(2,1)}, bf16[384,768]{1,0:T(8,128)(2,1)}, u32[]{:S(2)}, u32[]{:S(2)}) collective-permute-start(bf16[384,768]{1,0:T(8,128)(2,1)} %maximum_select_fusion.8), channel_id=1, source_target_pairs={{0,8},{4,12},{8,0},{12,4},{16,24},{20,28},{24,16},{28,20},{1,9},{5... | collective-permute-start | bytes 1769480 | tf_op jit(solution)/shard_map/ppermute | solution.py:88
  468.2 74.6 %all-gather.31.cloned.1.call-start = ((), (), s32[]{:S(2)}) async-start(), calls=%async_computation.22 | async-start | bytes 1966080 | tf_op jit(solution)/shard_map/all_gather | solution.py:44
  476.8 28.0 %copy-start.33 = (bf16[4,192,768]{2,1,0:T(8,128)(2,1)S(1)}, bf16[4,192,768]{2,1,0:T(8,128)(2,1)}, u32[]{:S(2)}) copy-start(bf16[4,192,768]{2,1,0:T(8,128)(2,1)} %gather_fusion.4) | copy-start | bytes 3538948
  477.3 6.5 %collective-permute-start.6 = (f32[3,2,2,768]{3,1,2,0:T(2,128)S(1)}, f32[3,2,2,768]{3,1,2,0:T(2,128)S(1)}, u32[]{:S(2)}, u32[]{:S(2)}) collective-permute-start(f32[3,2,2,768]{3,1,2,0:T(2,128)S(1)} %maximum_add_fusion), channel_id=1, source_target_pairs={{0,1},{1,0},{2,3},{3,2},{4,5},{5,4},{6,7},{7,6},{8,9},{9,8},{10,11... | collective-permute-start | bytes 110600 | tf_op jit(solution)/shard_map/ppermute | solution.py:102
  480.9 123.6 %collective-permute-start.22 = (bf16[768,768]{1,0:T(8,128)(2,1)}, bf16[768,768]{1,0:T(8,128)(2,1)}, u32[]{:S(2)}, u32[]{:S(2)}) collective-permute-start(bf16[768,768]{1,0:T(8,128)(2,1)} %maximum_select_fusion.3), channel_id=1, source_target_pairs={{0,4},{4,0},{8,12},{12,8},{16,20},{20,16},{24,28},{28,24},{1,5},{5... | collective-permute-start | bytes 3538952 | tf_op jit(solution)/shard_map/ppermute | solution.py:88
  483.9 23.1 %copy-start.5 = (f32[4,2,3,128,128]{3,4,2,1,0:T(8,128)S(1)}, f32[4,2,3,128,128]{3,4,2,1,0:T(8,128)}, u32[]{:S(2)}) copy-start(f32[4,2,3,128,128]{3,4,2,1,0:T(8,128)} %copy-done.4) | copy-start | bytes 4718596
  483.9 23.1 %copy-start.53 = (f32[4,2,3,128]{3,2,1,0:T(4,128)S(1)}, f32[4,2,3,128]{3,2,1,0:T(4,128)}, u32[]{:S(2)}) copy-start(f32[4,2,3,128]{3,2,1,0:T(4,128)} %copy-done.52) | copy-start | bytes 36868
  483.9 7.5 %collective-permute-start.7 = (f32[3,2,2,768]{3,1,2,0:T(2,128)S(1)}, f32[3,2,2,768]{3,1,2,0:T(2,128)S(1)}, u32[]{:S(2)}, u32[]{:S(2)}) collective-permute-start(f32[3,2,2,768]{3,1,2,0:T(2,128)S(1)} %fusion.281), channel_id=1, source_target_pairs={{0,2},{1,3},{2,0},{3,1},{4,6},{5,7},{6,4},{7,5},{8,10},{9,11},{10,... | collective-permute-start | bytes 110600 | tf_op jit(solution)/shard_map/ppermute | solution.py:102
  487.0 126.1 %collective-permute-start.28 = (bf16[768,768]{1,0:T(8,128)(2,1)}, bf16[768,768]{1,0:T(8,128)(2,1)}, u32[]{:S(2)}, u32[]{:S(2)}) collective-permute-start(bf16[768,768]{1,0:T(8,128)(2,1)} %maximum_select_fusion.4), channel_id=1, source_target_pairs={{0,4},{4,0},{8,12},{12,8},{16,20},{20,16},{24,28},{28,24},{1,5},{5... | collective-permute-start | bytes 3538952 | tf_op jit(solution)/shard_map/ppermute | solution.py:88
  487.0 143.4 %reduce-scatter.13.cloned.1.call-start = ((), (), s32[]{:S(2)}) async-start(), calls=%async_computation.12 | async-start | bytes 1966080 | tf_op jit(solution)/shard_map/reduce_scatter | solution.py:49
  521.8 23.5 %copy-start.7 = (f32[4,2,3,128,128]{3,4,2,1,0:T(8,128)S(1)}, f32[4,2,3,128,128]{3,4,2,1,0:T(8,128)}, u32[]{:S(2)}) copy-start(f32[4,2,3,128,128]{3,4,2,1,0:T(8,128)} %copy-done.6) | copy-start | bytes 4718596
  521.8 23.5 %copy-start.54 = (f32[4,2,3,128]{3,2,1,0:T(4,128)S(1)}, f32[4,2,3,128]{3,2,1,0:T(4,128)}, u32[]{:S(2)}) copy-start(f32[4,2,3,128]{3,2,1,0:T(4,128)} %log_add_fusion) | copy-start | bytes 36868
  550.9 81.6 %reduce-scatter.17.cloned.1.call-start = ((), (), s32[]{:S(2)}) async-start(), calls=%async_computation.14 | async-start | bytes 1966080 | tf_op jit(solution)/shard_map/reduce_scatter | solution.py:49
  556.7 15.8 %collective-permute-start.8 = (f32[15,768]{1,0:T(8,128)}, f32[15,768]{1,0:T(8,128)S(1)}, u32[]{:S(2)}, u32[]{:S(2)}) collective-permute-start(f32[15,768]{1,0:T(8,128)} %pad_maximum_fusion.6), channel_id=1, source_target_pairs={{0,4},{4,0},{8,12},{12,8},{16,20},{20,16},{24,28},{28,24},{1,5},{5... | collective-permute-start | bytes 138248 | tf_op jit(solution)/shard_map/ppermute | solution.py:102
  563.5 10.6 %collective-permute-start = (bf16[576,768]{1,0:T(8,128)(2,1)}, bf16[576,768]{1,0:T(8,128)(2,1)}, u32[]{:S(2)}, u32[]{:S(2)}) collective-permute-start(bf16[576,768]{1,0:T(8,128)(2,1)} %bitcast.62), channel_id=1, source_target_pairs={{0,4},{4,0},{8,12},{12,8},{16,20},{20,16},{24,28},{28,24},{1,5},{5... | collective-permute-start | bytes 2654216 | tf_op jit(solution)/shard_map/ppermute | solution.py:83
  572.4 4.2 collective-permute-start.11
  572.5 34.9 %collective-permute-start.9 = (f32[15,768]{1,0:T(8,128)S(1)}, f32[15,768]{1,0:T(8,128)S(1)}, u32[]{:S(2)}, u32[]{:S(2)}) collective-permute-start(f32[15,768]{1,0:T(8,128)S(1)} %fusion.280), channel_id=1, source_target_pairs={{0,8},{4,12},{8,0},{12,4},{16,24},{20,28},{24,16},{28,20},{1,9},{5... | collective-permute-start | bytes 138248 | tf_op jit(solution)/shard_map/ppermute | solution.py:102
  576.1 13.1 %collective-permute-start.1 = (bf16[288,768]{1,0:T(8,128)(2,1)S(1)}, bf16[288,768]{1,0:T(8,128)(2,1)S(1)}, u32[]{:S(2)}, u32[]{:S(2)}) collective-permute-start(bf16[288,768]{1,0:T(8,128)(2,1)S(1)} %select_convert_fusion.5), channel_id=1, source_target_pairs={{0,8},{4,12},{8,0},{12,4},{16,24},{20,28},{24,16},{28,20},{1,9},{5... | collective-permute-start | bytes 1327112 | tf_op jit(solution)/shard_map/ppermute | solution.py:83
  576.8 14.7 %collective-permute-start.12 = (bf16[96,768]{1,0:T(8,128)(2,1)S(1)}, bf16[96,768]{1,0:T(8,128)(2,1)S(1)}, u32[]{:S(2)}, u32[]{:S(2)}) collective-permute-start(bf16[96,768]{1,0:T(8,128)(2,1)S(1)} %select_convert_fusion.10), channel_id=1, source_target_pairs={{0,8},{4,12},{8,0},{12,4},{16,24},{20,28},{24,16},{28,20},{1,9},{5... | collective-permute-start | bytes 442376 | tf_op jit(solution)/shard_map/ppermute | solution.py:83
  589.4 6.0 collective-permute-start.2
  595.4 6.0 collective-permute-start.3
  597.0 5.8 collective-permute-start.13
  601.5 10.3 %collective-permute-start.4 = (bf16[288,768]{1,0:T(8,128)(2,1)S(1)}, bf16[288,768]{1,0:T(8,128)(2,1)S(1)}, u32[]{:S(2)}, u32[]{:S(2)}) collective-permute-start(bf16[288,768]{1,0:T(8,128)(2,1)S(1)} %maximum_select_fusion.9), channel_id=1, source_target_pairs={{0,8},{4,12},{8,0},{12,4},{16,24},{20,28},{24,16},{28,20},{1,9},{5... | collective-permute-start | bytes 1327112 | tf_op jit(solution)/shard_map/ppermute | solution.py:88
  602.8 5.2 collective-permute-start.14
  607.4 13.4 %collective-permute-start.10 = (f32[15,768]{1,0:T(8,128)S(1)}, f32[15,768]{1,0:T(8,128)S(1)}, u32[]{:S(2)}, u32[]{:S(2)}) collective-permute-start(f32[15,768]{1,0:T(8,128)S(1)} %add.555), channel_id=1, source_target_pairs={{0,16},{4,20},{8,24},{12,28},{16,0},{20,4},{24,8},{28,12},{1,17},{... | collective-permute-start | bytes 138248 | tf_op jit(solution)/shard_map/ppermute | solution.py:102
  608.0 13.4 %collective-permute-start.15 = (bf16[96,768]{1,0:T(8,128)(2,1)S(1)}, bf16[96,768]{1,0:T(8,128)(2,1)S(1)}, u32[]{:S(2)}, u32[]{:S(2)}) collective-permute-start(bf16[96,768]{1,0:T(8,128)(2,1)S(1)} %maximum_select_fusion.11), channel_id=1, source_target_pairs={{0,8},{4,12},{8,0},{12,4},{16,24},{20,28},{24,16},{28,20},{1,9},{5... | collective-permute-start | bytes 442376 | tf_op jit(solution)/shard_map/ppermute | solution.py:88
  613.1 12.9 %collective-permute-start.5 = (bf16[576,768]{1,0:T(8,128)(2,1)}, bf16[576,768]{1,0:T(8,128)(2,1)}, u32[]{:S(2)}, u32[]{:S(2)}) collective-permute-start(bf16[576,768]{1,0:T(8,128)(2,1)} %maximum_select_fusion.5), channel_id=1, source_target_pairs={{0,4},{4,0},{8,12},{12,8},{16,20},{20,16},{24,28},{28,24},{1,5},{5... | collective-permute-start | bytes 2654216 | tf_op jit(solution)/shard_map/ppermute | solution.py:88
  621.5 3.1 collective-permute-start.16
  (110 other events, 525.2 us)
Sparse Core Ops, SparseCore 0:
  10.2 63.4 all-gather.16
  75.8 44.5 all-gather.20
  123.7 43.0 all-gather.18
  177.8 38.3 all-gather.22
  218.4 34.2 reduce-scatter.6
  254.9 34.2 reduce-scatter.8
  295.1 35.8 all-gather.24
  332.6 35.8 all-gather.28
  380.5 34.2 reduce-scatter.14
  417.0 34.2 reduce-scatter.10
  468.3 36.4 all-gather.26
  506.8 35.8 all-gather.30
  551.0 34.3 reduce-scatter.12
  588.1 34.2 reduce-scatter.16

commit v12 on v11

--- a/solution.py
+++ b/solution.py
@@ -146,8 +146,6 @@
     ubias_sel = up_bias[seg_kind].astype(jnp.float32)
     down_sel = w_down[seg_kind]
 
-    if after is not None:
-        input_segs, _ = lax.optimization_barrier((input_segs, after["normed"]))
     projected = jnp.einsum(
         "srd,sjde->jsre", input_segs, qkv_sel, preferred_element_type=jnp.float32
     )
@@ -269,7 +267,7 @@
     )
     qkv_back = jnp.einsum("jsre,sjde->srd", d_proj, qkv_sel, preferred_element_type=jnp.float32)
     input_grad = scatter_sum(qkv_back) + d_one
-    marks = {"normed": normed_low, "qkv_back": qkv_back}
+    marks = {"qkv_back": qkv_back}
     small = jnp.stack([rbias_grads, gain_grads, shift_grads])
     return (
         layer_out,

time: 654 us -> 656 us (level)
  waiting for transfers between devices: 262 us -> 274 us
  local copies, waits for them, and re-layouts: 102 us -> 94.3 us
    all_gather x8, waiting for transfers between devices: 132 us -> 152 us  [gather_rows(): return lax.all_gather(local_rows, 'tensor', axis=0, tiled=False)]
    all_to_all x2, waiting for transfers between devices: 11.6 us -> 2.4 us  [stream(): mixed_rows = lax.all_to_all(mixed, 'tensor', 0, 0, tiled=True)]
  transfers between devices with their start and end apart: 46 -> 46, of which waited for: 22 -> 24; matrix products, arithmetic and copies ran while one was open for 45% -> 43% of each run, Pallas kernels for 0% -> 0%
where the time goes in v12:
time: 656 us; the launch traced here: 646 us
  waiting for transfers between devices  274 us (42%)
  matrix products  133 us (20%)
  local copies, waits for them, and re-layouts  94.3 us (14%)
  other arithmetic  89.1 us (14%)
  starting transfers between devices  39.8 us (6%)
  between operations  16.6 us (3%)
    all_gather x8, waiting for transfers between devices, gather_rows(): return lax.all_gather(local_rows, 'tensor', axis=0, tiled=False)  152 us
    reduce_scatter x6, waiting for transfers between devices, scatter_sum(): lax.psum_scatter(seg_parts.reshape(n_seg * seg_rows, width).astype(jnp.bf...  55.3 us
    ppermute x12, waiting for transfers between devices, dp_sum_low(): gots = lax.ppermute(sends, 'dp', dp_perm(n_dp, 1 << b))  42.6 us
    dot_general x12, matrix products, pick(): return jnp.dot(kind_hot, kind_table.astype(jnp.float32), precision=highest)  16.8 us
    select_n x12, other arithmetic, dp_sum_low(): jnp.where(upper, jnp.concatenate([g, c]), jnp.concatenate([c, g]))  16.5 us
    dot_general x12, matrix products, type_sum(): jnp.einsum('rt,rd->td', kind_hot, values, precision=lax.Precision.HIGHEST)  15 us
    convert_element_type x2, other arithmetic, stream(): activ = jax.nn.gelu(pre_act, approximate=False).astype(jnp.bfloat16)  14.6 us
    dot_general x2, matrix products, stream(): jnp.einsum('srd,sfd->srf', two_segs, down_sel, preferred_element_type=jnp...  13.9 us
  transfers between devices with their start and end apart: 46, of which 24 were waited for; matrix products, arithmetic and copies ran while one was open for 43% of the time, Pallas kernels for 0%

profile of v12, /device:TPU:0, one launch (start us, length us, event | category | flops | bytes accessed | tf_op | source)
XLA Modules:
  0.0 646.4 jit_solution(10815213591252686217)
XLA Ops:
  13.1 6.3 all-to-all-start.1
  22.7 4.0 gather_fusion.9
  26.7 4.1 gather_fusion.1
  41.1 32.5 %all-gather.21.cloned.1.call-done = bf16[1024,768]{1,0:T(8,128)(2,1)} async-done(((bf16[256,768]{1,0:T(8,128)(2,1)}), bf16[1024,768]{1,0:T(8,128)(2,1)}) %all-gather.21.cloned.1.call-update) | async-done | bytes 1572880 | tf_op jit(solution)/shard_map/all_gather | solution.py:44
  73.6 3.6 convolution_bitcast_fusion.1
  89.2 22.7 %all-gather.17.cloned.1.call-done = bf16[1024,768]{1,0:T(8,128)(2,1)} async-done(((bf16[256,768]{1,0:T(8,128)(2,1)}), bf16[1024,768]{1,0:T(8,128)(2,1)}) %all-gather.17.cloned.1.call-update) | async-done | bytes 1572880 | tf_op jit(solution)/shard_map/all_gather | solution.py:44
  111.9 5.0 convolution_bitcast_fusion.2
  116.9 4.1 all-to-all-start.2
  121.1 2.6 fusion.217
  143.0 3.5 all-to-all-start
  149.2 3.2 gather_fusion.14
  152.4 3.2 gather_fusion.7
  155.6 5.0 gather_fusion.12
  160.6 3.1 gather_fusion.5
  175.3 6.3 all-gather.23.cloned.1.call-done
  181.6 5.1 fusion.98
  186.7 7.3 %fusion.6 = bf16[4,256,768]{2,1,0:T(8,128)(2,1)S(1)} fusion(f32[4,256,768]{2,1,0:T(8,128)S(1)} %get-tuple-element.68, f32[4,768]{1,0:T(4,128)S(1)} %copy-done.82, u8[256,768]{1,0:T(8,128)(4,1)S(1)} %get-tuple-element.16, u8[256,768]{1,0:T(8,128)(4,1)S(1)} %get-tuple-element.15), kind=kLoop, calls=%fused_computation.30 | loop fusion | flops 55836672 | bytes 5124096 | tf_op jit(solution)/shard_map/convert_element_type | solution.py:191
  196.9 22.6 %all-gather.19.cloned.1.call-done = bf16[1024,768]{1,0:T(8,128)(2,1)} async-done(((bf16[256,768]{1,0:T(8,128)(2,1)}), bf16[1024,768]{1,0:T(8,128)(2,1)}) %all-gather.19.cloned.1.call-update) | async-done | bytes 1572880 | tf_op jit(solution)/shard_map/all_gather | solution.py:44
  219.5 5.1 fusion.97
  224.6 7.3 %fusion.3 = bf16[4,256,768]{2,1,0:T(8,128)(2,1)S(1)} fusion(f32[4,256,768]{2,1,0:T(8,128)S(1)} %get-tuple-element.77, f32[4,768]{1,0:T(4,128)S(1)} %copy-done.84, u8[256,768]{1,0:T(8,128)(4,1)S(1)} %get-tuple-element.14, u8[256,768]{1,0:T(8,128)(4,1)S(1)} %get-tuple-element.13), kind=kLoop, calls=%fused_computation.27 | loop fusion | flops 55836672 | bytes 5124096 | tf_op jit(solution)/shard_map/convert_element_type | solution.py:191
  232.0 2.6 convolution_convert_fusion.5
  235.9 20.7 %reduce-scatter.9.cloned.1.call-done = bf16[256,768]{1,0:T(8,128)(2,1)} async-done(((bf16[1024,768]{1,0:T(8,128)(2,1)}), bf16[256,768]{1,0:T(8,128)(2,1)}) %reduce-scatter.9.cloned.1.call-update) | async-done | bytes 393232 | tf_op jit(solution)/shard_map/reduce_scatter | solution.py:49
  258.5 34.6 %reduce-scatter.7.cloned.1.call-done = bf16[256,768]{1,0:T(8,128)(2,1)} async-done(((bf16[1024,768]{1,0:T(8,128)(2,1)}), bf16[256,768]{1,0:T(8,128)(2,1)}) %reduce-scatter.7.cloned.1.call-update) | async-done | bytes 393232 | tf_op jit(solution)/shard_map/reduce_scatter | solution.py:49
  298.9 2.8 gather_fusion.15
  306.9 2.6 copy.91
  309.6 2.6 copy.88
  312.1 2.6 copy.97
  314.7 2.6 copy.96
  317.4 2.6 copy.99
  320.0 2.6 copy.98
  331.9 3.0 all-gather.25.cloned.1.call-done
  334.9 7.5 %convert_reduce_fusion.1 = (f32[4,768]{1,0:T(4,128)}, bf16[4,256,768]{2,1,0:T(8,128)(2,1)}) fusion(f32[4,256,768]{2,1,0:T(8,128)} %copy-done.43, f32[4,768]{1,0:T(4,128)} %convert_element_type.516, bf16[4,256,768]{2,1,0:T(8,128)(2,1)} %bitcast.415, bf16[4,768,768]{2,1,0:T(8,128)(2,1)} %gather_fusion.7), kind=kOutput, calls=%fused_computation.64 | convolution fusion | flops 1219752960 | bytes 11034624 | tf_op jit(solution)/shard_map/srd,sfd->srf/dot_general | solution.py:206
  342.4 29.9 %all-gather.29.cloned.1.call-done = bf16[1024,768]{1,0:T(8,128)(2,1)} async-done(((bf16[256,768]{1,0:T(8,128)(2,1)}), bf16[1024,768]{1,0:T(8,128)(2,1)}) %all-gather.29.cloned.1.call-update) | async-done | bytes 1572880 | tf_op jit(solution)/shard_map/all_gather | solution.py:44
  372.4 6.4 convert_reduce_fusion
  378.7 5.5 convolution_convert_fusion
  384.8 4.7 fusion.25
  389.5 2.9 bitcast_add_fusion.1
  396.4 2.7 fusion.21
  399.1 2.8 bitcast_add_fusion
  406.4 2.6 convolution_convert_fusion.2
  409.2 3.1 bitcast_add_fusion.4
  414.0 3.1 bitcast_add_fusion.3
  418.8 9.9 %collective-permute-done.18 = bf16[384,768]{1,0:T(8,128)(2,1)S(1)} collective-permute-done((bf16[384,768]{1,0:T(8,128)(2,1)S(1)}, bf16[384,768]{1,0:T(8,128)(2,1)S(1)}, u32[]{:S(2)}, u32[]{:S(2)}) %collective-permute-start.18) | collective-permute-done | bytes 589856 | tf_op jit(solution)/shard_map/ppermute | solution.py:83
  430.6 10.4 %collective-permute-done.24 = bf16[384,768]{1,0:T(8,128)(2,1)S(1)} collective-permute-done((bf16[384,768]{1,0:T(8,128)(2,1)S(1)}, bf16[384,768]{1,0:T(8,128)(2,1)S(1)}, u32[]{:S(2)}, u32[]{:S(2)}) %collective-permute-start.24) | collective-permute-done | bytes 589856 | tf_op jit(solution)/shard_map/ppermute | solution.py:83
  443.7 7.5 %collective-permute-done.25 = bf16[192,768]{1,0:T(8,128)(2,1)S(1)} collective-permute-done((bf16[192,768]{1,0:T(8,128)(2,1)S(1)}, bf16[192,768]{1,0:T(8,128)(2,1)S(1)}, u32[]{:S(2)}, u32[]{:S(2)}) %collective-permute-start.25) | collective-permute-done | bytes 294944 | tf_op jit(solution)/shard_map/ppermute | solution.py:83
  453.6 4.0 collective-permute-done.20
  460.0 2.7 collective-permute-done.26
  465.1 2.9 fusion.210
  480.7 2.9 maximum_select_fusion.3
  483.7 3.4 collective-permute-done.6
  487.2 3.0 maximum_select_fusion.4
  490.5 3.7 collective-permute-done.7
  495.7 13.2 %all-gather.27.cloned.1.call-done = bf16[1024,768]{1,0:T(8,128)(2,1)} async-done(((bf16[256,768]{1,0:T(8,128)(2,1)}), bf16[1024,768]{1,0:T(8,128)(2,1)}) %all-gather.27.cloned.1.call-update) | async-done | bytes 1572880 | tf_op jit(solution)/shard_map/all_gather | solution.py:44
  508.9 2.8 convolution_convert_fusion.11
  520.7 4.6 convolution_bitcast_fusion
  525.3 21.5 %all-gather.31.cloned.1.call-done = bf16[1024,768]{1,0:T(8,128)(2,1)} async-done(((bf16[256,768]{1,0:T(8,128)(2,1)}), bf16[1024,768]{1,0:T(8,128)(2,1)}) %all-gather.31.cloned.1.call-update) | async-done | bytes 1572880 | tf_op jit(solution)/shard_map/all_gather | solution.py:44
  559.4 3.3 fusion.17
  572.6 2.7 bitcast_convert_fusion
  583.0 9.9 %collective-permute-done.1 = bf16[288,768]{1,0:T(8,128)(2,1)S(1)} collective-permute-done((bf16[288,768]{1,0:T(8,128)(2,1)S(1)}, bf16[288,768]{1,0:T(8,128)(2,1)S(1)}, u32[]{:S(2)}, u32[]{:S(2)}) %collective-permute-start.1) | collective-permute-done | bytes 442400 | tf_op jit(solution)/shard_map/ppermute | solution.py:83
  595.4 3.7 collective-permute-done.2
  601.3 3.8 collective-permute-done.3
  607.8 2.9 maximum_select_fusion
  612.6 3.4 collective-permute-done.4
  616.4 2.7 maximum_select_fusion.1
  (581 shorter events, 197.6 us)
Async XLA Ops:
  7.2 142.0 %copy-start = (bf16[2,768,768]{2,1,0:T(8,128)(2,1)S(1)}, bf16[2,768,768]{2,1,0:T(8,128)(2,1)}, u32[]{:S(2)}) copy-start(bf16[2,768,768]{2,1,0:T(8,128)(2,1)} %param.25) | copy-start | bytes 7077892
  7.2 66.4 %all-gather.21.cloned.1.call-start = ((), (), s32[]{:S(2)}) async-start(), calls=%async_computation.17 | async-start | bytes 1966080 | tf_op jit(solution)/shard_map/all_gather | solution.py:44
  11.4 15.3 %copy-start.110 = (s32[1024]{0:T(1024)}, s32[1024]{0:T(1024)S(1)}, u32[]{:S(2)}) copy-start(s32[1024]{0:T(1024)S(1)} %pad_clamp_fusion.4) | copy-start | bytes 12292
  13.1 103.8 %all-to-all-start.1 = ((bf16[4,192,768]{2,1,0:T(8,128)(2,1)}), bf16[4,192,768]{2,1,0:T(8,128)(2,1)}, u32[]{:S(2)}, u32[]{:S(2)}) async-start(bf16[4,192,768]{2,1,0:T(8,128)(2,1)} %gather_fusion.4), calls=%async_computation.1 | async-start | bytes 2359296 | tf_op jit(solution)/shard_map/all_to_all | solution.py:308
  19.4 92.5 %all-gather.17.cloned.1.call-start = ((), (), s32[]{:S(2)}) async-start(), calls=%async_computation.15 | async-start | bytes 1966080 | tf_op jit(solution)/shard_map/all_gather | solution.py:44
  32.9 53.4 %copy-start.76 = (f32[4,3,64]{2,1,0:T(4,128)}, f32[4,3,64]{2,1,0:T(4,128)S(1)}, u32[]{:S(2)}) copy-start(f32[4,3,64]{2,1,0:T(4,128)S(1)} %add.507) | copy-start | bytes 9220
  36.2 37.4 %copy-start.103 = (bf16[2,1,768]{2,1,0:T(2,128)(2,1)}, bf16[2,1,768]{2,1,0:T(2,128)(2,1)S(1)}, u32[]{:S(2)}) copy-start(bf16[2,1,768]{2,1,0:T(2,128)(2,1)S(1)} %get-tuple-element.56) | copy-start | bytes 9220
  116.9 15.3 %all-to-all-start.2 = ((bf16[4,256,192]{1,2,0:T(8,128)(2,1)}), bf16[4,256,192]{1,2,0:T(8,128)(2,1)}, u32[]{:S(2)}, u32[]{:S(2)}) async-start(bf16[4,256,192]{1,2,0:T(8,128)(2,1)} %convert_element_type.530), calls=%async_computation.3 | async-start | bytes 786432 | tf_op jit(solution)/shard_map/all_to_all | solution.py:177
  121.1 60.6 %all-gather.23.cloned.1.call-start = ((), (), s32[]{:S(2)}) async-start(), calls=%async_computation.18 | async-start | bytes 1966080 | tf_op jit(solution)/shard_map/all_gather | solution.py:44
  143.0 26.7 %all-to-all-start = ((bf16[4,256,192]{1,2,0:T(8,128)(2,1)}), bf16[4,256,192]{1,2,0:T(8,128)(2,1)S(1)}, u32[]{:S(2)}, u32[]{:S(2)}) async-start(bf16[4,256,192]{1,2,0:T(8,128)(2,1)} %convert_element_type.514), calls=%async_computation | async-start | bytes 786432 | tf_op jit(solution)/shard_map/all_to_all | solution.py:177
  146.4 73.1 %all-gather.19.cloned.1.call-start = ((), (), s32[]{:S(2)}) async-start(), calls=%async_computation.16 | async-start | bytes 1966080 | tf_op jit(solution)/shard_map/all_gather | solution.py:44
  175.2 81.3 %reduce-scatter.9.cloned.1.call-start = ((), (), s32[]{:S(2)}) async-start(), calls=%async_computation.10 | async-start | bytes 1966080 | tf_op jit(solution)/shard_map/reduce_scatter | solution.py:49
  194.1 25.5 %copy-start.84 = (f32[4,768]{1,0:T(4,128)S(1)}, f32[4,768]{1,0:T(4,128)}, u32[]{:S(2)}) copy-start(f32[4,768]{1,0:T(4,128)} %convert_element_type.516) | copy-start | bytes 36868
  196.7 96.4 %reduce-scatter.7.cloned.1.call-start = ((), (), s32[]{:S(2)}) async-start(), calls=%async_computation.9 | async-start | bytes 1966080 | tf_op jit(solution)/shard_map/reduce_scatter | solution.py:49
  231.9 24.6 %copy-start.101 = (bf16[2,1,768]{2,1,0:T(2,128)(2,1)S(1)}, bf16[2,1,768]{2,1,0:T(2,128)(2,1)}, u32[]{:S(2)}) copy-start(bf16[2,1,768]{2,1,0:T(2,128)(2,1)} %get-tuple-element.54) | copy-start | bytes 9220
  234.6 100.3 %all-gather.25.cloned.1.call-start = ((), (), s32[]{:S(2)}) async-start(), calls=%async_computation.19 | async-start | bytes 1966080 | tf_op jit(solution)/shard_map/all_gather | solution.py:44
  258.2 66.6 %copy-start.85 = (f32[256]{0:T(256)}, f32[256]{0:T(256)S(1)}, u32[]{:S(2)}) copy-start(f32[256]{0:T(256)S(1)} %broadcast_multiply_fusion.8) | copy-start | bytes 3076
  258.5 66.4 %copy-start.95 = (f32[256]{0:T(256)}, f32[256]{0:T(256)S(1)}, u32[]{:S(2)}) copy-start(f32[256]{0:T(256)S(1)} %add_rsqrt_fusion) | copy-start | bytes 3076
  294.8 32.2 %copy-start.86 = (f32[256]{0:T(256)}, f32[256]{0:T(256)S(1)}, u32[]{:S(2)}) copy-start(f32[256]{0:T(256)S(1)} %broadcast_multiply_fusion.10) | copy-start | bytes 3076
  295.1 31.9 %copy-start.96 = (f32[256]{0:T(256)}, f32[256]{0:T(256)S(1)}, u32[]{:S(2)}) copy-start(f32[256]{0:T(256)S(1)} %add_rsqrt_fusion.2) | copy-start | bytes 3076
  298.8 73.5 %all-gather.29.cloned.1.call-start = ((), (), s32[]{:S(2)}) async-start(), calls=%async_computation.21 | async-start | bytes 1966080 | tf_op jit(solution)/shard_map/all_gather | solution.py:44
  303.6 161.5 %reduce-scatter.15.cloned.1.call-start = ((), (), s32[]{:S(2)}) async-start(), calls=%async_computation.13 | async-start | bytes 1966080 | tf_op jit(solution)/shard_map/reduce_scatter | solution.py:49
  334.9 37.5 %copy-start.83 = (f32[4,768]{1,0:T(4,128)S(1)}, f32[4,768]{1,0:T(4,128)}, u32[]{:S(2)}) copy-start(f32[4,768]{1,0:T(4,128)} %convert_element_type.532) | copy-start | bytes 36868
  384.2 84.4 %reduce-scatter.11.cloned.1.call-start = ((), (), s32[]{:S(2)}) async-start(), calls=%async_computation.11 | async-start | bytes 1966080 | tf_op jit(solution)/shard_map/reduce_scatter | solution.py:49
  393.7 15.6 %collective-permute-start.17 = (bf16[768,768]{1,0:T(8,128)(2,1)}, bf16[768,768]{1,0:T(8,128)(2,1)}, u32[]{:S(2)}, u32[]{:S(2)}) collective-permute-start(bf16[768,768]{1,0:T(8,128)(2,1)} %fusion.83), channel_id=1, source_target_pairs={{0,4},{4,0},{8,12},{12,8},{16,20},{20,16},{24,28},{28,24},{1,5},{5... | collective-permute-start | bytes 3538952 | tf_op jit(solution)/shard_map/ppermute | solution.py:83
  405.4 8.6 %collective-permute-start.23 = (bf16[768,768]{1,0:T(8,128)(2,1)}, bf16[768,768]{1,0:T(8,128)(2,1)}, u32[]{:S(2)}, u32[]{:S(2)}) collective-permute-start(bf16[768,768]{1,0:T(8,128)(2,1)} %fusion.84), channel_id=1, source_target_pairs={{0,4},{4,0},{8,12},{12,8},{16,20},{20,16},{24,28},{28,24},{1,5},{5... | collective-permute-start | bytes 3538952 | tf_op jit(solution)/shard_map/ppermute | solution.py:83
  409.0 99.9 %all-gather.27.cloned.1.call-start = ((), (), s32[]{:S(2)}) async-start(), calls=%async_computation.20 | async-start | bytes 1966080 | tf_op jit(solution)/shard_map/all_gather | solution.py:44
  412.5 16.3 %collective-permute-start.18 = (bf16[384,768]{1,0:T(8,128)(2,1)S(1)}, bf16[384,768]{1,0:T(8,128)(2,1)S(1)}, u32[]{:S(2)}, u32[]{:S(2)}) collective-permute-start(bf16[384,768]{1,0:T(8,128)(2,1)S(1)} %select_convert_fusion.4), channel_id=1, source_target_pairs={{0,8},{4,12},{8,0},{12,4},{16,24},{20,28},{24,16},{28,20},{1,9},{5... | collective-permute-start | bytes 1769480 | tf_op jit(solution)/shard_map/ppermute | solution.py:83
  417.3 23.7 %collective-permute-start.24 = (bf16[384,768]{1,0:T(8,128)(2,1)S(1)}, bf16[384,768]{1,0:T(8,128)(2,1)S(1)}, u32[]{:S(2)}, u32[]{:S(2)}) collective-permute-start(bf16[384,768]{1,0:T(8,128)(2,1)S(1)} %select_convert_fusion.3), channel_id=1, source_target_pairs={{0,8},{4,12},{8,0},{12,4},{16,24},{20,28},{24,16},{28,20},{1,9},{5... | collective-permute-start | bytes 1769480 | tf_op jit(solution)/shard_map/ppermute | solution.py:83
  429.0 13.9 %collective-permute-start.19 = (bf16[192,768]{1,0:T(8,128)(2,1)S(1)}, bf16[192,768]{1,0:T(8,128)(2,1)S(1)}, u32[]{:S(2)}, u32[]{:S(2)}) collective-permute-start(bf16[192,768]{1,0:T(8,128)(2,1)S(1)} %select_convert_fusion.7), channel_id=1, source_target_pairs={{0,16},{4,20},{8,24},{12,28},{16,0},{20,4},{24,8},{28,12},{1,17},{... | collective-permute-start | bytes 884744 | tf_op jit(solution)/shard_map/ppermute | solution.py:83
  441.3 23.9 %copy-start.9 = (f32[256,768]{1,0:T(8,128)S(1)}, f32[256,768]{1,0:T(8,128)}, u32[]{:S(2)}) copy-start(f32[256,768]{1,0:T(8,128)} %get-tuple-element.46) | copy-start | bytes 2359300
  441.3 23.9 %copy-start.92 = (f32[256]{0:T(256)S(1)}, f32[256]{0:T(256)}, u32[]{:S(2)}) copy-start(f32[256]{0:T(256)} %copy-done.91) | copy-start | bytes 3076
  441.3 9.9 %collective-permute-start.25 = (bf16[192,768]{1,0:T(8,128)(2,1)S(1)}, bf16[192,768]{1,0:T(8,128)(2,1)S(1)}, u32[]{:S(2)}, u32[]{:S(2)}) collective-permute-start(bf16[192,768]{1,0:T(8,128)(2,1)S(1)} %select_convert_fusion.6), channel_id=1, source_target_pairs={{0,16},{4,20},{8,24},{12,28},{16,0},{20,4},{24,8},{28,12},{1,17},{... | collective-permute-start | bytes 884744 | tf_op jit(solution)/shard_map/ppermute | solution.py:83
  443.1 14.5 %collective-permute-start.20 = (bf16[192,768]{1,0:T(8,128)(2,1)S(1)}, bf16[192,768]{1,0:T(8,128)(2,1)S(1)}, u32[]{:S(2)}, u32[]{:S(2)}) collective-permute-start(bf16[192,768]{1,0:T(8,128)(2,1)S(1)} %add_convert_fusion.1), channel_id=1, source_target_pairs={{0,16},{4,20},{8,24},{12,28},{16,0},{20,4},{24,8},{28,12},{1,17},{... | collective-permute-start | bytes 884744 | tf_op jit(solution)/shard_map/ppermute | solution.py:88
  451.3 11.4 %collective-permute-start.26 = (bf16[192,768]{1,0:T(8,128)(2,1)S(1)}, bf16[192,768]{1,0:T(8,128)(2,1)S(1)}, u32[]{:S(2)}, u32[]{:S(2)}) collective-permute-start(bf16[192,768]{1,0:T(8,128)(2,1)S(1)} %add_convert_fusion), channel_id=1, source_target_pairs={{0,16},{4,20},{8,24},{12,28},{16,0},{20,4},{24,8},{28,12},{1,17},{... | collective-permute-start | bytes 884744 | tf_op jit(solution)/shard_map/ppermute | solution.py:88
  458.5 22.2 %collective-permute-start.21 = (bf16[384,768]{1,0:T(8,128)(2,1)}, bf16[384,768]{1,0:T(8,128)(2,1)}, u32[]{:S(2)}, u32[]{:S(2)}) collective-permute-start(bf16[384,768]{1,0:T(8,128)(2,1)} %maximum_select_fusion.7), channel_id=1, source_target_pairs={{0,8},{4,12},{8,0},{12,4},{16,24},{20,28},{24,16},{28,20},{1,9},{5... | collective-permute-start | bytes 1769480 | tf_op jit(solution)/shard_map/ppermute | solution.py:88
  463.7 23.5 %collective-permute-start.27 = (bf16[384,768]{1,0:T(8,128)(2,1)}, bf16[384,768]{1,0:T(8,128)(2,1)}, u32[]{:S(2)}, u32[]{:S(2)}) collective-permute-start(bf16[384,768]{1,0:T(8,128)(2,1)} %maximum_select_fusion.8), channel_id=1, source_target_pairs={{0,8},{4,12},{8,0},{12,4},{16,24},{20,28},{24,16},{28,20},{1,9},{5... | collective-permute-start | bytes 1769480 | tf_op jit(solution)/shard_map/ppermute | solution.py:88
  472.2 74.6 %all-gather.31.cloned.1.call-start = ((), (), s32[]{:S(2)}) async-start(), calls=%async_computation.22 | async-start | bytes 1966080 | tf_op jit(solution)/shard_map/all_gather | solution.py:44
  479.5 29.4 %copy-start.35 = (bf16[4,192,768]{2,1,0:T(8,128)(2,1)S(1)}, bf16[4,192,768]{2,1,0:T(8,128)(2,1)}, u32[]{:S(2)}) copy-start(bf16[4,192,768]{2,1,0:T(8,128)(2,1)} %gather_fusion.4) | copy-start | bytes 3538948
  480.0 7.0 %collective-permute-start.6 = (f32[3,2,2,768]{3,1,2,0:T(2,128)S(1)}, f32[3,2,2,768]{3,1,2,0:T(2,128)S(1)}, u32[]{:S(2)}, u32[]{:S(2)}) collective-permute-start(f32[3,2,2,768]{3,1,2,0:T(2,128)S(1)} %maximum_add_fusion), channel_id=1, source_target_pairs={{0,1},{1,0},{2,3},{3,2},{4,5},{5,4},{6,7},{7,6},{8,9},{9,8},{10,11... | collective-permute-start | bytes 110600 | tf_op jit(solution)/shard_map/ppermute | solution.py:102
  483.7 124.2 %collective-permute-start.22 = (bf16[768,768]{1,0:T(8,128)(2,1)}, bf16[768,768]{1,0:T(8,128)(2,1)}, u32[]{:S(2)}, u32[]{:S(2)}) collective-permute-start(bf16[768,768]{1,0:T(8,128)(2,1)} %maximum_select_fusion.3), channel_id=1, source_target_pairs={{0,4},{4,0},{8,12},{12,8},{16,20},{20,16},{24,28},{28,24},{1,5},{5... | collective-permute-start | bytes 3538952 | tf_op jit(solution)/shard_map/ppermute | solution.py:88
  487.1 25.8 %copy-start.7 = (f32[4,2,3,128,128]{3,4,2,1,0:T(8,128)S(1)}, f32[4,2,3,128,128]{3,4,2,1,0:T(8,128)}, u32[]{:S(2)}) copy-start(f32[4,2,3,128,128]{3,4,2,1,0:T(8,128)} %copy-done.6) | copy-start | bytes 4718596
  487.1 25.8 %copy-start.59 = (f32[4,2,3,128]{3,2,1,0:T(4,128)S(1)}, f32[4,2,3,128]{3,2,1,0:T(4,128)}, u32[]{:S(2)}) copy-start(f32[4,2,3,128]{3,2,1,0:T(4,128)} %copy-done.58) | copy-start | bytes 36868
  487.1 7.1 %collective-permute-start.7 = (f32[3,2,2,768]{3,1,2,0:T(2,128)S(1)}, f32[3,2,2,768]{3,1,2,0:T(2,128)S(1)}, u32[]{:S(2)}, u32[]{:S(2)}) collective-permute-start(f32[3,2,2,768]{3,1,2,0:T(2,128)S(1)} %fusion.281), channel_id=1, source_target_pairs={{0,2},{1,3},{2,0},{3,1},{4,6},{5,7},{6,4},{7,5},{8,10},{9,11},{10,... | collective-permute-start | bytes 110600 | tf_op jit(solution)/shard_map/ppermute | solution.py:102
  490.2 126.2 %collective-permute-start.28 = (bf16[768,768]{1,0:T(8,128)(2,1)}, bf16[768,768]{1,0:T(8,128)(2,1)}, u32[]{:S(2)}, u32[]{:S(2)}) collective-permute-start(bf16[768,768]{1,0:T(8,128)(2,1)} %maximum_select_fusion.4), channel_id=1, source_target_pairs={{0,4},{4,0},{8,12},{12,8},{16,20},{20,16},{24,28},{28,24},{1,5},{5... | collective-permute-start | bytes 3538952 | tf_op jit(solution)/shard_map/ppermute | solution.py:88
  490.3 143.4 %reduce-scatter.13.cloned.1.call-start = ((), (), s32[]{:S(2)}) async-start(), calls=%async_computation.12 | async-start | bytes 1966080 | tf_op jit(solution)/shard_map/reduce_scatter | solution.py:49
  525.3 24.1 %copy-start.5 = (f32[4,2,3,128,128]{3,4,2,1,0:T(8,128)S(1)}, f32[4,2,3,128,128]{3,4,2,1,0:T(8,128)}, u32[]{:S(2)}) copy-start(f32[4,2,3,128,128]{3,4,2,1,0:T(8,128)} %copy-done.4) | copy-start | bytes 4718596
  525.3 24.1 %copy-start.57 = (f32[4,2,3,128]{3,2,1,0:T(4,128)S(1)}, f32[4,2,3,128]{3,2,1,0:T(4,128)}, u32[]{:S(2)}) copy-start(f32[4,2,3,128]{3,2,1,0:T(4,128)} %copy-done.56) | copy-start | bytes 36868
  555.0 80.7 %reduce-scatter.17.cloned.1.call-start = ((), (), s32[]{:S(2)}) async-start(), calls=%async_computation.14 | async-start | bytes 1966080 | tf_op jit(solution)/shard_map/reduce_scatter | solution.py:49
  559.4 16.0 %collective-permute-start.8 = (f32[15,768]{1,0:T(8,128)}, f32[15,768]{1,0:T(8,128)}, u32[]{:S(2)}, u32[]{:S(2)}) collective-permute-start(f32[15,768]{1,0:T(8,128)} %pad_maximum_fusion.6), channel_id=1, source_target_pairs={{0,4},{4,0},{8,12},{12,8},{16,20},{20,16},{24,28},{28,24},{1,5},{5... | collective-permute-start | bytes 138248 | tf_op jit(solution)/shard_map/ppermute | solution.py:102
  566.0 11.8 %collective-permute-start = (bf16[576,768]{1,0:T(8,128)(2,1)}, bf16[576,768]{1,0:T(8,128)(2,1)}, u32[]{:S(2)}, u32[]{:S(2)}) collective-permute-start(bf16[576,768]{1,0:T(8,128)(2,1)} %bitcast.62), channel_id=1, source_target_pairs={{0,4},{4,0},{8,12},{12,8},{16,20},{20,16},{24,28},{28,24},{1,5},{5... | collective-permute-start | bytes 2654216 | tf_op jit(solution)/shard_map/ppermute | solution.py:83
  575.3 5.1 collective-permute-start.11
  576.2 34.5 %collective-permute-start.9 = (f32[15,768]{1,0:T(8,128)S(1)}, f32[15,768]{1,0:T(8,128)S(1)}, u32[]{:S(2)}, u32[]{:S(2)}) collective-permute-start(f32[15,768]{1,0:T(8,128)S(1)} %fusion.280), channel_id=1, source_target_pairs={{0,8},{4,12},{8,0},{12,4},{16,24},{20,28},{24,16},{28,20},{1,9},{5... | collective-permute-start | bytes 138248 | tf_op jit(solution)/shard_map/ppermute | solution.py:102
  579.8 13.1 %collective-permute-start.1 = (bf16[288,768]{1,0:T(8,128)(2,1)S(1)}, bf16[288,768]{1,0:T(8,128)(2,1)S(1)}, u32[]{:S(2)}, u32[]{:S(2)}) collective-permute-start(bf16[288,768]{1,0:T(8,128)(2,1)S(1)} %select_convert_fusion.5), channel_id=1, source_target_pairs={{0,8},{4,12},{8,0},{12,4},{16,24},{20,28},{24,16},{28,20},{1,9},{5... | collective-permute-start | bytes 1327112 | tf_op jit(solution)/shard_map/ppermute | solution.py:83
  581.5 13.9 %collective-permute-start.12 = (bf16[96,768]{1,0:T(8,128)(2,1)S(1)}, bf16[96,768]{1,0:T(8,128)(2,1)S(1)}, u32[]{:S(2)}, u32[]{:S(2)}) collective-permute-start(bf16[96,768]{1,0:T(8,128)(2,1)S(1)} %select_convert_fusion.10), channel_id=1, source_target_pairs={{0,8},{4,12},{8,0},{12,4},{16,24},{20,28},{24,16},{28,20},{1,9},{5... | collective-permute-start | bytes 442376 | tf_op jit(solution)/shard_map/ppermute | solution.py:83
  593.1 6.0 collective-permute-start.2
  599.2 6.0 collective-permute-start.3
  600.7 5.5 collective-permute-start.13
  605.3 10.7 %collective-permute-start.4 = (bf16[288,768]{1,0:T(8,128)(2,1)S(1)}, bf16[288,768]{1,0:T(8,128)(2,1)S(1)}, u32[]{:S(2)}, u32[]{:S(2)}) collective-permute-start(bf16[288,768]{1,0:T(8,128)(2,1)S(1)} %maximum_select_fusion.9), channel_id=1, source_target_pairs={{0,8},{4,12},{8,0},{12,4},{16,24},{20,28},{24,16},{28,20},{1,9},{5... | collective-permute-start | bytes 1327112 | tf_op jit(solution)/shard_map/ppermute | solution.py:88
  606.3 5.1 collective-permute-start.14
  610.8 13.5 %collective-permute-start.10 = (f32[15,768]{1,0:T(8,128)S(1)}, f32[15,768]{1,0:T(8,128)S(1)}, u32[]{:S(2)}, u32[]{:S(2)}) collective-permute-start(f32[15,768]{1,0:T(8,128)S(1)} %add.555), channel_id=1, source_target_pairs={{0,16},{4,20},{8,24},{12,28},{16,0},{20,4},{24,8},{28,12},{1,17},{... | collective-permute-start | bytes 138248 | tf_op jit(solution)/shard_map/ppermute | solution.py:102
  611.5 13.4 %collective-permute-start.15 = (bf16[96,768]{1,0:T(8,128)(2,1)S(1)}, bf16[96,768]{1,0:T(8,128)(2,1)S(1)}, u32[]{:S(2)}, u32[]{:S(2)}) collective-permute-start(bf16[96,768]{1,0:T(8,128)(2,1)S(1)} %maximum_select_fusion.11), channel_id=1, source_target_pairs={{0,8},{4,12},{8,0},{12,4},{16,24},{20,28},{24,16},{28,20},{1,9},{5... | collective-permute-start | bytes 442376 | tf_op jit(solution)/shard_map/ppermute | solution.py:88
  616.4 13.0 %collective-permute-start.5 = (bf16[576,768]{1,0:T(8,128)(2,1)S(1)}, bf16[576,768]{1,0:T(8,128)(2,1)}, u32[]{:S(2)}, u32[]{:S(2)}) collective-permute-start(bf16[576,768]{1,0:T(8,128)(2,1)S(1)} %maximum_select_fusion.5), channel_id=1, source_target_pairs={{0,4},{4,0},{8,12},{12,8},{16,20},{20,16},{24,28},{28,24},{1,5},{5... | collective-permute-start | bytes 2654216 | tf_op jit(solution)/shard_map/ppermute | solution.py:88
  625.0 3.1 collective-permute-start.16
  (120 other events, 597.1 us)
Sparse Core Ops, SparseCore 0:
  10.2 63.3 all-gather.20
  75.7 36.1 all-gather.16
  137.1 44.4 all-gather.22
  183.6 35.8 all-gather.18
  222.2 34.2 reduce-scatter.8
  258.7 34.2 reduce-scatter.6
  299.0 35.8 all-gather.24
  336.4 35.8 all-gather.28
  384.4 34.2 reduce-scatter.14
  420.8 34.2 reduce-scatter.10
  472.3 36.5 all-gather.26
  510.9 35.9 all-gather.30
  555.2 34.2 reduce-scatter.12
  592.2 34.2 reduce-scatter.16
